TPU v7x, 512 devices: a whole 4x4x16 slice. The times are simulated.
512 devices in a mesh: row: 32 (over z, core), col: 16 (over y, x).
Axes of the slice: x: 4, y: 4, z: 16, core: 2. Of those that a mesh axis runs over, the one named last changes fastest.
Arguments:
- pressure_in: float32 [1024, 256, 128], P('row', 'col'), may hold values from -6 to 6
- source: float32 [1024, 256, 128], P('row', 'col'), may hold values from -18 to 18
- permeability: float32 [1024, 256, 128], P('row', 'col'), may hold values from 0.2 to 5
Outputs:
- pressure_out: float32 [1024, 256, 128], P('row', 'col')
All inputs are finite; a program needn't handle non-finite values.
Results may differ from a plain program's by a relative error of at most 0.0001.
Values sent between devices are 32-bit elements; how exact they have to be, the bound alone decides.
No kernel may reach another device: no remote copies, remote signals or barrier semaphores. Data moves between devices by JAX's collectives and lax.ppermute only.
A program may use at most 128 MiB of HBM per device.

v0:
```python
import jax
import jax.numpy as jnp
from jax import lax
from jax.sharding import PartitionSpec as P

LEVELS = 3
NU1 = 2
NU2 = 2
CSWEEPS = 16

OMEGA = 0.8


def shift_from(x, axis, k):
    n = lax.axis_size(axis)
    return lax.ppermute(x, axis, [(i, (i + k) % n) for i in range(n)])


def halo(x, w):
    size_x = x.shape[-3]
    lower = shift_from(x[..., size_x - w :, :, :], "row", 1)
    upper = shift_from(x[..., :w, :, :], "row", -1)
    x = jnp.concatenate([lower, x, upper], axis=-3)
    size_y = x.shape[-2]
    lower = shift_from(x[..., :, size_y - w :, :], "col", 1)
    upper = shift_from(x[..., :, :w, :], "col", -1)
    return jnp.concatenate([lower, x, upper], axis=-2)


def trim(a, t, y=True):
    if t == 0:
        return a
    if y:
        return a[t:-t, t:-t]
    return a[t:-t]


def harmonic(left, right, scale):
    return 2.0 * left * right / (left + right) * scale


def faces_of(k, scale):
    c = k[1:-1, 1:-1]
    west_x = harmonic(k[:-2, 1:-1], c, scale)
    east_x = harmonic(c, k[2:, 1:-1], scale)
    west_y = harmonic(k[1:-1, :-2], c, scale)
    east_y = harmonic(c, k[1:-1, 2:], scale)
    inner = harmonic(c[:, :, :-1], c[:, :, 1:], scale)
    below = jnp.concatenate([2.0 * c[:, :, :1] * scale, inner], axis=2)
    above = jnp.concatenate([inner, 2.0 * c[:, :, -1:] * scale], axis=2)
    diagonal = west_x + east_x + west_y + east_y + below + above
    return (west_x, east_x, west_y, east_y, below, above, diagonal)


def apply_operator(v, faces):
    west_x, east_x, west_y, east_y, below, above, diagonal = faces
    c = v[1:-1, 1:-1]
    zero_plane = jnp.zeros_like(c[:, :, :1])
    under = jnp.concatenate([zero_plane, c[:, :, :-1]], axis=2)
    over = jnp.concatenate([c[:, :, 1:], zero_plane], axis=2)
    beside_all = west_x * v[:-2, 1:-1] + east_x * v[2:, 1:-1]
    beside_all = beside_all + west_y * v[1:-1, :-2] + east_y * v[1:-1, 2:]
    beside_all = beside_all + below * under + above * over
    return diagonal * c - beside_all


class Level:
    def __init__(self, faces, have, right_side, rhs_have):
        self.faces, self.have = faces, have
        self.right_side, self.rhs_have = right_side, rhs_have

    def faces_at(self, h, y=True):
        return tuple(trim(f, self.have - h, y) for f in self.faces)

    def rhs_at(self, h, y=True):
        return trim(self.right_side, self.rhs_have - h, y)

    def sweep(self, v, h):
        faces = self.faces_at(h)
        residual = self.rhs_at(h) - apply_operator(v, faces)
        return v[1:-1, 1:-1] + OMEGA * residual / faces[6]

    def first_sweep(self, h):
        return OMEGA * self.rhs_at(h) / self.faces_at(h)[6]

    def residual(self, v):
        return self.rhs_at(0) - apply_operator(v, self.faces_at(0))


def coarsen(field):
    size_x, size_y, size_z = field.shape
    t = field.reshape(size_x // 2, 2, size_y, size_z)
    t = t[:, 0] + t[:, 1]
    t = t[:, 0::2] + t[:, 1::2]
    t = t[:, :, 0::2] + t[:, :, 1::2]
    return t * 0.125


def prolong(field):
    return jnp.repeat(jnp.repeat(jnp.repeat(field, 2, axis=0), 2, axis=1), 2, axis=2)


def wrap_y(a, w=1):
    return jnp.concatenate([a[:, -w:], a, a[:, :w]], axis=1)


class Band(Level):
    def faces_at(self, h, y=False):
        return super().faces_at(h, False)

    def rhs_at(self, h, y=False):
        return super().rhs_at(h, False)

    def sweep(self, v, h):
        faces = self.faces_at(h)
        residual = self.rhs_at(h) - apply_operator(wrap_y(v), faces)
        return v[1:-1] + OMEGA * residual / faces[6]

    def residual(self, v):
        return self.rhs_at(0) - apply_operator(wrap_y(v), self.faces_at(0))


def x_halo(x, w):
    size_x = x.shape[-3]
    lower = shift_from(x[..., size_x - w :, :, :], "row", 1)
    upper = shift_from(x[..., :w, :, :], "row", -1)
    return jnp.concatenate([lower, x, upper], axis=-3)


def rows_around(x, steps, axis):
    lower = [shift_from(x, "row", k) for k in reversed(steps)]
    upper = [shift_from(x, "row", -k) for k in steps]
    return jnp.concatenate(lower + [x] + upper, axis=axis)


def lane_roll(a, k):
    return jnp.roll(a, k, axis=-1)


def coarse_solve(right_side, perm, scale):
    size_x, size_y, size_z = right_side.shape
    lanes = size_y * size_z
    pair = jnp.stack([right_side, perm]).reshape(2, size_x, lanes)
    need = CSWEEPS + 1
    near = rows_around(pair, (1, 2), 1)
    wide = rows_around(near, (5,), 1)
    assert 7 * size_x >= need
    cut = 7 * size_x - need
    wide = wide[:, cut : wide.shape[1] - cut]
    rhs_band, k = wide[0, 1:-1], wide[1]
    lane = lax.broadcasted_iota(jnp.int32, (1, lanes), 1) % size_z
    first, last = lane == 0, lane == size_z - 1
    c = k[1:-1]
    west_x = harmonic(k[:-2], c, scale)
    east_x = harmonic(c, k[2:], scale)
    west_y = harmonic(lane_roll(c, size_z), c, scale)
    east_y = harmonic(c, lane_roll(c, -size_z), scale)
    below = jnp.where(first, 2.0 * c * scale, harmonic(lane_roll(c, 1), c, scale))
    above = jnp.where(last, 2.0 * c * scale, harmonic(c, lane_roll(c, -1), scale))
    diagonal = west_x + east_x + west_y + east_y + below + above

    def one_sweep(i, v):
        ext = jnp.concatenate([v[:1], v, v[-1:]], axis=0)
        under = jnp.where(first, 0.0, lane_roll(v, 1))
        over = jnp.where(last, 0.0, lane_roll(v, -1))
        beside_all = west_x * ext[:-2] + east_x * ext[2:]
        beside_all = beside_all + west_y * lane_roll(v, size_z) + east_y * lane_roll(v, -size_z)
        beside_all = beside_all + below * under + above * over
        return v + OMEGA * (rhs_band - (diagonal * v - beside_all)) / diagonal

    v = OMEGA * rhs_band / diagonal
    v = lax.fori_loop(1, CSWEEPS, one_sweep, v)
    have = need - 1 - (CSWEEPS - 1)
    drop = need - 1 - have
    v = v[drop : v.shape[0] - drop]
    return v.reshape(v.shape[0], size_y, size_z)


def on_device(pressure_in, source, permeability):
    scales = [0.25**level for level in range(LEVELS + 1)]
    k0, p0, b0 = halo(jnp.stack([permeability, pressure_in, source]), 4)
    lev0 = Level(faces_of(k0, scales[0]), 3, b0, 4)
    p = lev0.sweep(p0, 3)
    s0 = lev0.sweep(p, 2)
    rhs = coarsen(lev0.residual(trim(s0, 1)))
    perm = coarsen(permeability)
    k1, b1 = halo(jnp.stack([perm, rhs]), 5)
    lev1 = Level(faces_of(k1, scales[1]), 4, b1, 5)
    p = lev1.first_sweep(4)
    s1 = lev1.sweep(p, 3)
    rhs = coarsen(lev1.residual(trim(s1, 2)))
    perm = coarsen(perm)
    size_y2 = rhs.shape[1]
    band = lax.all_gather(jnp.stack([perm, rhs]), "col", axis=2, tiled=True)
    k2, b2 = x_halo(band, 4)
    lev2 = Band(faces_of(wrap_y(k2), scales[2]), 3, b2, 4)
    p = lev2.first_sweep(3)
    s2 = lev2.sweep(p, 2)
    rhs = coarsen(lev2.residual(s2[1:-1]))
    perm = coarsen(band[0])
    correction = coarse_solve(rhs, perm, scales[3])
    q = s2 + prolong(correction)
    q = lev2.sweep(q, 1)
    u2 = lev2.sweep(q, 0)
    u2 = wrap_y(x_halo(u2, 2), 2)
    col = lax.axis_index("col")
    u2 = lax.dynamic_slice_in_dim(u2, col * size_y2, size_y2 + 4, axis=1)
    q = s1 + trim(prolong(u2), 1)
    q = lev1.sweep(q, 2)
    u1 = lev1.sweep(q, 1)
    q = s0 + prolong(u1)
    q = lev0.sweep(q, 1)
    return lev0.sweep(q, 0)


def solution(mesh):
    placed = (P("row", "col", None), P("row", "col", None), P("row", "col", None))
    return jax.shard_map(
        on_device, mesh=mesh, in_specs=placed, out_specs=P("row", "col", None), check_vma=False
    )
```

profile of v0, /device:TPU:1, one launch (start us, length us, event | category | flops | bytes accessed | tf_op | source)
XLA Modules:
  0.0 209.5 jit_solution(16676170689046436812)
XLA Ops:
  0.9 3.0 %collective-permute-start = (f32[3,4,16,128]{3,2,1,0:T(8,128)S(1)}, f32[3,4,16,128]{3,2,1,0:T(8,128)S(1)}, u32[]{:S(2)}, u32[]{:S(2)}) collective-permute-start(f32[3,4,16,128]{3,2,1,0:T(8,128)S(1)} %get-tuple-element.151), channel_id=1, source_target_pairs={{0,16},{16,32},{32,48},{48,64},{64,80},{80,96},{96,112},{112,128},... | collective-permute-start | bytes 294920 | tf_op jit(solution)/shard_map/ppermute | solution.py:16
  4.0 3.9 %collective-permute-start.1 = (f32[3,4,16,128]{3,2,1,0:T(8,128)S(1)}, f32[3,4,16,128]{3,2,1,0:T(8,128)S(1)}, u32[]{:S(2)}, u32[]{:S(2)}) collective-permute-start(f32[3,4,16,128]{3,2,1,0:T(8,128)S(1)} %get-tuple-element.152), channel_id=1, source_target_pairs={{0,496},{16,0},{32,16},{48,32},{64,48},{80,64},{96,80},{112,96},{1... | collective-permute-start | bytes 294920 | tf_op jit(solution)/shard_map/ppermute | solution.py:16
  10.1 2.3 %collective-permute-start.2 = (f32[3,40,4,128]{3,2,1,0:T(4,128)S(1)}, f32[3,40,4,128]{3,2,1,0:T(4,128)S(1)}, u32[]{:S(2)}, u32[]{:S(2)}) collective-permute-start(f32[3,40,4,128]{3,2,1,0:T(4,128)S(1)} %get-tuple-element.149), channel_id=1, source_target_pairs={{0,1},{1,2},{2,3},{3,4},{4,5},{5,6},{6,7},{7,8},{8,9},{9,10},{10,1... | collective-permute-start | bytes 737288 | tf_op jit(solution)/shard_map/ppermute | solution.py:16
  12.4 6.3 %collective-permute-start.3 = (f32[3,40,4,128]{3,2,1,0:T(4,128)S(1)}, f32[3,40,4,128]{3,2,1,0:T(4,128)S(1)}, u32[]{:S(2)}, u32[]{:S(2)}) collective-permute-start(f32[3,40,4,128]{3,2,1,0:T(4,128)S(1)} %get-tuple-element.150), channel_id=1, source_target_pairs={{0,15},{1,0},{2,1},{3,2},{4,3},{5,4},{6,5},{7,6},{8,7},{9,8},{10,9... | collective-permute-start | bytes 737288 | tf_op jit(solution)/shard_map/ppermute | solution.py:16
  30.3 2.1 collective-permute-start.4
  32.3 4.0 %collective-permute-start.5 = (f32[2,5,8,64]{3,2,1,0:T(8,128)}, f32[2,5,8,64]{3,2,1,0:T(8,128)S(1)}, u32[]{:S(2)}, u32[]{:S(2)}) collective-permute-start(f32[2,5,8,64]{3,2,1,0:T(8,128)} %get-tuple-element.208), channel_id=1, source_target_pairs={{0,496},{16,0},{32,16},{48,32},{64,48},{80,64},{96,80},{112,96},{1... | collective-permute-start | bytes 61448 | tf_op jit(solution)/shard_map/ppermute | solution.py:16
  37.5 1.9 collective-permute-start.6
  39.4 7.4 %collective-permute-start.7 = (f32[2,26,5,64]{3,2,1,0:T(8,128)S(1)}, f32[2,26,5,64]{3,2,1,0:T(8,128)S(1)}, u32[]{:S(2)}, u32[]{:S(2)}) collective-permute-start(f32[2,26,5,64]{3,2,1,0:T(8,128)S(1)} %get-tuple-element.182), channel_id=1, source_target_pairs={{0,15},{1,0},{2,1},{3,2},{4,3},{5,4},{6,5},{7,6},{8,7},{9,8},{10,9... | collective-permute-start | bytes 199688 | tf_op jit(solution)/shard_map/ppermute | solution.py:16
  52.1 21.4 %all_gather.3 = f32[2,8,64,32]{3,1,0,2:T(8,128)} all-gather(f32[2,8,4,32]{3,1,0,2:T(8,128)S(1)} %copy.41), channel_id=1, replica_groups=mesh['row'=32,'col'=16] {'col'}, dimensions={2}, use_global_device_ids=true | all-gather | bytes 139264 | tf_op jit(solution)/shard_map/all_gather | solution.py:194
  75.5 2.1 slice.1189
  77.5 2.1 slice.1190
  84.8 6.5 %collective-permute-start.8 = (f32[2,4,64,32]{2,3,1,0:T(8,128)}, f32[2,4,64,32]{2,3,1,0:T(8,128)}, u32[]{:S(2)}, u32[]{:S(2)}) collective-permute-start(f32[2,4,64,32]{2,3,1,0:T(8,128)} %get-tuple-element.173), channel_id=1, source_target_pairs={{0,16},{16,32},{32,48},{48,64},{64,80},{80,96},{96,112},{112,128},... | collective-permute-start | bytes 196616 | tf_op jit(solution)/shard_map/ppermute | solution.py:16
  91.3 5.2 %collective-permute-start.9 = (f32[2,4,64,32]{2,3,1,0:T(8,128)}, f32[2,4,64,32]{2,3,1,0:T(8,128)}, u32[]{:S(2)}, u32[]{:S(2)}) collective-permute-start(f32[2,4,64,32]{2,3,1,0:T(8,128)} %get-tuple-element.174), channel_id=1, source_target_pairs={{0,496},{16,0},{32,16},{48,32},{64,48},{80,64},{96,80},{112,96},{1... | collective-permute-start | bytes 196616 | tf_op jit(solution)/shard_map/ppermute | solution.py:16
  97.9 1.5 stack.50
  109.2 1.9 collective-permute-start.10
  111.1 3.0 %collective-permute-start.12 = (f32[2,4,512]{2,1,0:T(4,128)S(1)}, f32[2,4,512]{2,1,0:T(4,128)S(1)}, u32[]{:S(2)}, u32[]{:S(2)}) collective-permute-start(f32[2,4,512]{2,1,0:T(4,128)S(1)} %constant_dynamic-update-slice_fusion), channel_id=1, source_target_pairs={{0,496},{16,0},{32,16},{48,32},{64,48},{80,64},{96,80},{112,96},{1... | collective-permute-start | bytes 49160 | tf_op jit(solution)/shard_map/ppermute | solution.py:16
  114.1 4.9 %collective-permute-start.13 = (f32[2,4,512]{2,1,0:T(4,128)S(1)}, f32[2,4,512]{2,1,0:T(4,128)S(1)}, u32[]{:S(2)}, u32[]{:S(2)}) collective-permute-start(f32[2,4,512]{2,1,0:T(4,128)S(1)} %constant_dynamic-update-slice_fusion), channel_id=1, source_target_pairs={{0,480},{16,496},{32,0},{48,16},{64,32},{80,48},{96,64},{112,80},{... | collective-permute-start | bytes 49160 | tf_op jit(solution)/shard_map/ppermute | solution.py:16
  119.8 1.9 concatenate.226
  121.7 7.3 %collective-permute-start.14 = (f32[2,20,512]{2,1,0:T(8,128)}, f32[2,20,512]{2,1,0:T(8,128)}, u32[]{:S(2)}, u32[]{:S(2)}) collective-permute-start(f32[2,20,512]{2,1,0:T(8,128)} %concatenate.226), channel_id=1, source_target_pairs={{0,80},{16,96},{32,112},{48,128},{64,144},{80,160},{96,176},{112,1... | collective-permute-start | bytes 245768 | tf_op jit(solution)/shard_map/ppermute | solution.py:16
  129.0 2.2 %collective-permute-start.15 = (f32[2,20,512]{2,1,0:T(8,128)}, f32[2,20,512]{2,1,0:T(8,128)}, u32[]{:S(2)}, u32[]{:S(2)}) collective-permute-start(f32[2,20,512]{2,1,0:T(8,128)} %concatenate.226), channel_id=1, source_target_pairs={{0,432},{16,448},{32,464},{48,480},{64,496},{80,0},{96,16},{112,32... | collective-permute-start | bytes 245768 | tf_op jit(solution)/shard_map/ppermute | solution.py:16
  131.2 3.8 %collective-permute-done.14 = f32[2,20,512]{2,1,0:T(8,128)} collective-permute-done((f32[2,20,512]{2,1,0:T(8,128)}, f32[2,20,512]{2,1,0:T(8,128)}, u32[]{:S(2)}, u32[]{:S(2)}) %collective-permute-start.14) | collective-permute-done | bytes 81952 | tf_op jit(solution)/shard_map/ppermute | solution.py:16
  135.0 3.8 %collective-permute-done.15 = f32[2,20,512]{2,1,0:T(8,128)} collective-permute-done((f32[2,20,512]{2,1,0:T(8,128)}, f32[2,20,512]{2,1,0:T(8,128)}, u32[]{:S(2)}, u32[]{:S(2)}) %collective-permute-start.15) | collective-permute-done | bytes 81952 | tf_op jit(solution)/shard_map/ppermute | solution.py:16
  138.8 5.7 %concatenate.227 = f32[2,60,512]{2,1,0:T(8,128)} concatenate(f32[2,20,512]{2,1,0:T(8,128)} %collective-permute-done.14, f32[2,4,512]{2,1,0:T(4,128)S(1)} %collective-permute-done.10, f32[2,4,512]{2,1,0:T(4,128)S(1)} %collective-permute-done.11, f32[2,4,512]{2,1,0:T(4,128)S(1)} %constant_dynamic-update-slice_fusion, f32[2,4,512]{2,1,0:T(4,128)S(1)} %collective-permute-done.12, ...), dimensions={1} | concatenate | bytes 491520 | tf_op jit(solution)/shard_map/concatenate | solution.py:133
  144.5 1.6 slice_bitcast_fusion.17
  146.4 2.0 multiply_divide_fusion
  148.4 26.2 %while.11 = (s32[]{:T(128)}, f32[36,512]{1,0:T(8,128)S(1)}, f32[36,512]{1,0:T(8,128)}, f32[36,512]{1,0:T(8,128)}, f32[36,512]{1,0:T(8,128)}, /*index=5*/f32[36,5...) while((s32[]{:T(128)}, f32[36,512]{1,0:T(8,128)S(1)}, ...), condition=%wide.region_1.2_spmd.clone, body=%wide.region_0.1_spmd.clone.sunk | while | flops 467970 | bytes 1783917 | solution.py:172
  183.7 2.1 %collective-permute-done.17 = f32[2,64,32]{1,2,0:T(8,128)S(1)} collective-permute-done((f32[2,64,32]{1,2,0:T(8,128)S(1)}, f32[2,64,32]{1,2,0:T(8,128)S(1)}, u32[]{:S(2)}, u32[]{:S(2)}) %collective-permute-start.17) | collective-permute-done | bytes 16416 | tf_op jit(solution)/shard_map/ppermute | solution.py:16
  189.3 2.0 copy.64
  192.5 1.9 fusion.115
  198.4 2.1 %copy.56 = f32[36,20,64]{0,2,1:T(8,128)} copy(f32[36,20,64]{2,0,1:T(8,128)} %bitcast.168) | data formatting | bytes 368640 | tf_op jit(solution)/shard_map/reshape | solution.py:100
  200.5 2.6 %broadcast_in_dim.81 = f32[36,20,64,2]{0,3,2,1:T(2,128)} broadcast(f32[36,20,64]{0,2,1:T(8,128)} %copy.56), dimensions={0,1,2} | broadcast | bytes 552960 | tf_op jit(solution)/shard_map/broadcast_in_dim | solution.py:100
  203.1 2.6 %copy.57 = f32[36,20,128]{2,1,0:T(8,128)} copy(f32[36,20,128]{0,2,1:T(8,128)} %bitcast.156) | data formatting | bytes 737280 | tf_op jit(solution)/shard_map/reshape | solution.py:100
  (368 shorter events, 86.8 us)
Async XLA Ops:
  0.0 18.7 %copy-start.18 = (f32[32,16,128]{2,1,0:T(8,128)S(1)}, f32[32,16,128]{2,1,0:T(8,128)}, u32[]{:S(2)}) copy-start(f32[32,16,128]{2,1,0:T(8,128)} %param.7) | copy-start | bytes 786436
  0.9 20.9 %copy-start.41 = (f32[32,16,128]{2,1,0:T(8,128)S(1)}, f32[32,16,128]{2,1,0:T(8,128)}, u32[]{:S(2)}) copy-start(f32[32,16,128]{2,1,0:T(8,128)} %param.6) | copy-start | bytes 786436
  0.9 20.9 %copy-start.42 = (f32[32,16,128]{2,1,0:T(8,128)S(1)}, f32[32,16,128]{2,1,0:T(8,128)}, u32[]{:S(2)}) copy-start(f32[32,16,128]{2,1,0:T(8,128)} %param.5) | copy-start | bytes 786436
  0.9 7.7 %collective-permute-start = (f32[3,4,16,128]{3,2,1,0:T(8,128)S(1)}, f32[3,4,16,128]{3,2,1,0:T(8,128)S(1)}, u32[]{:S(2)}, u32[]{:S(2)}) collective-permute-start(f32[3,4,16,128]{3,2,1,0:T(8,128)S(1)} %get-tuple-element.151), channel_id=1, source_target_pairs={{0,16},{16,32},{32,48},{48,64},{64,80},{80,96},{96,112},{112,128},... | collective-permute-start | bytes 294920 | tf_op jit(solution)/shard_map/ppermute | solution.py:16
  4.0 4.8 %collective-permute-start.1 = (f32[3,4,16,128]{3,2,1,0:T(8,128)S(1)}, f32[3,4,16,128]{3,2,1,0:T(8,128)S(1)}, u32[]{:S(2)}, u32[]{:S(2)}) collective-permute-start(f32[3,4,16,128]{3,2,1,0:T(8,128)S(1)} %get-tuple-element.152), channel_id=1, source_target_pairs={{0,496},{16,0},{32,16},{48,32},{64,48},{80,64},{96,80},{112,96},{1... | collective-permute-start | bytes 294920 | tf_op jit(solution)/shard_map/ppermute | solution.py:16
  10.1 11.0 %collective-permute-start.2 = (f32[3,40,4,128]{3,2,1,0:T(4,128)S(1)}, f32[3,40,4,128]{3,2,1,0:T(4,128)S(1)}, u32[]{:S(2)}, u32[]{:S(2)}) collective-permute-start(f32[3,40,4,128]{3,2,1,0:T(4,128)S(1)} %get-tuple-element.149), channel_id=1, source_target_pairs={{0,1},{1,2},{2,3},{3,4},{4,5},{5,6},{6,7},{7,8},{8,9},{9,10},{10,1... | collective-permute-start | bytes 737288 | tf_op jit(solution)/shard_map/ppermute | solution.py:16
  12.4 9.4 %collective-permute-start.3 = (f32[3,40,4,128]{3,2,1,0:T(4,128)S(1)}, f32[3,40,4,128]{3,2,1,0:T(4,128)S(1)}, u32[]{:S(2)}, u32[]{:S(2)}) collective-permute-start(f32[3,40,4,128]{3,2,1,0:T(4,128)S(1)} %get-tuple-element.150), channel_id=1, source_target_pairs={{0,15},{1,0},{2,1},{3,2},{4,3},{5,4},{6,5},{7,6},{8,7},{9,8},{10,9... | collective-permute-start | bytes 737288 | tf_op jit(solution)/shard_map/ppermute | solution.py:16
  22.2 3.1 %copy-start.2 = (f32[40,24,128]{2,1,0:T(8,128)}, f32[40,24,128]{2,1,0:T(8,128)S(1)}, u32[]{:S(2)}) copy-start(f32[40,24,128]{2,1,0:T(8,128)S(1)} %get-tuple-element.146) | copy-start | bytes 1474564
  23.3 2.0 copy-start
  30.3 7.0 %collective-permute-start.4 = (f32[2,5,8,64]{3,2,1,0:T(8,128)}, f32[2,5,8,64]{3,2,1,0:T(8,128)S(1)}, u32[]{:S(2)}, u32[]{:S(2)}) collective-permute-start(f32[2,5,8,64]{3,2,1,0:T(8,128)} %get-tuple-element.207), channel_id=1, source_target_pairs={{0,16},{16,32},{32,48},{48,64},{64,80},{80,96},{96,112},{112,128},... | collective-permute-start | bytes 61448 | tf_op jit(solution)/shard_map/ppermute | solution.py:16
  32.3 5.0 %collective-permute-start.5 = (f32[2,5,8,64]{3,2,1,0:T(8,128)}, f32[2,5,8,64]{3,2,1,0:T(8,128)S(1)}, u32[]{:S(2)}, u32[]{:S(2)}) collective-permute-start(f32[2,5,8,64]{3,2,1,0:T(8,128)} %get-tuple-element.208), channel_id=1, source_target_pairs={{0,496},{16,0},{32,16},{48,32},{64,48},{80,64},{96,80},{112,96},{1... | collective-permute-start | bytes 61448 | tf_op jit(solution)/shard_map/ppermute | solution.py:16
  37.5 10.7 %collective-permute-start.6 = (f32[2,26,5,64]{3,2,1,0:T(8,128)S(1)}, f32[2,26,5,64]{3,2,1,0:T(8,128)S(1)}, u32[]{:S(2)}, u32[]{:S(2)}) collective-permute-start(f32[2,26,5,64]{3,2,1,0:T(8,128)S(1)} %get-tuple-element.181), channel_id=1, source_target_pairs={{0,1},{1,2},{2,3},{3,4},{4,5},{5,6},{6,7},{7,8},{8,9},{9,10},{10,1... | collective-permute-start | bytes 199688 | tf_op jit(solution)/shard_map/ppermute | solution.py:16
  39.4 10.2 %collective-permute-start.7 = (f32[2,26,5,64]{3,2,1,0:T(8,128)S(1)}, f32[2,26,5,64]{3,2,1,0:T(8,128)S(1)}, u32[]{:S(2)}, u32[]{:S(2)}) collective-permute-start(f32[2,26,5,64]{3,2,1,0:T(8,128)S(1)} %get-tuple-element.182), channel_id=1, source_target_pairs={{0,15},{1,0},{2,1},{3,2},{4,3},{5,4},{6,5},{7,6},{8,7},{9,8},{10,9... | collective-permute-start | bytes 199688 | tf_op jit(solution)/shard_map/ppermute | solution.py:16
  74.8 25.7 %copy-start.15 = (f32[2,8,64,32]{2,3,1,0:T(8,128)}, f32[2,8,64,32]{2,3,1,0:T(8,128)S(1)}, u32[]{:S(2)}) copy-start(f32[2,8,64,32]{2,3,1,0:T(8,128)S(1)} %copy.42) | copy-start | bytes 393220
  84.8 14.7 %collective-permute-start.8 = (f32[2,4,64,32]{2,3,1,0:T(8,128)}, f32[2,4,64,32]{2,3,1,0:T(8,128)}, u32[]{:S(2)}, u32[]{:S(2)}) collective-permute-start(f32[2,4,64,32]{2,3,1,0:T(8,128)} %get-tuple-element.173), channel_id=1, source_target_pairs={{0,16},{16,32},{32,48},{48,64},{64,80},{80,96},{96,112},{112,128},... | collective-permute-start | bytes 196616 | tf_op jit(solution)/shard_map/ppermute | solution.py:16
  91.3 8.2 %collective-permute-start.9 = (f32[2,4,64,32]{2,3,1,0:T(8,128)}, f32[2,4,64,32]{2,3,1,0:T(8,128)}, u32[]{:S(2)}, u32[]{:S(2)}) collective-permute-start(f32[2,4,64,32]{2,3,1,0:T(8,128)} %get-tuple-element.174), channel_id=1, source_target_pairs={{0,496},{16,0},{32,16},{48,32},{64,48},{80,64},{96,80},{112,96},{1... | collective-permute-start | bytes 196616 | tf_op jit(solution)/shard_map/ppermute | solution.py:16
  109.2 9.8 %collective-permute-start.10 = (f32[2,4,512]{2,1,0:T(4,128)S(1)}, f32[2,4,512]{2,1,0:T(4,128)S(1)}, u32[]{:S(2)}, u32[]{:S(2)}) collective-permute-start(f32[2,4,512]{2,1,0:T(4,128)S(1)} %constant_dynamic-update-slice_fusion), channel_id=1, source_target_pairs={{0,32},{16,48},{32,64},{48,80},{64,96},{80,112},{96,128},{112,144}... | collective-permute-start | bytes 49160 | tf_op jit(solution)/shard_map/ppermute | solution.py:16
  111.1 7.9 %collective-permute-start.11 = (f32[2,4,512]{2,1,0:T(4,128)S(1)}, f32[2,4,512]{2,1,0:T(4,128)S(1)}, u32[]{:S(2)}, u32[]{:S(2)}) collective-permute-start(f32[2,4,512]{2,1,0:T(4,128)S(1)} %constant_dynamic-update-slice_fusion), channel_id=1, source_target_pairs={{0,16},{16,32},{32,48},{48,64},{64,80},{80,96},{96,112},{112,128},... | collective-permute-start | bytes 49160 | tf_op jit(solution)/shard_map/ppermute | solution.py:16
  111.1 7.9 %collective-permute-start.12 = (f32[2,4,512]{2,1,0:T(4,128)S(1)}, f32[2,4,512]{2,1,0:T(4,128)S(1)}, u32[]{:S(2)}, u32[]{:S(2)}) collective-permute-start(f32[2,4,512]{2,1,0:T(4,128)S(1)} %constant_dynamic-update-slice_fusion), channel_id=1, source_target_pairs={{0,496},{16,0},{32,16},{48,32},{64,48},{80,64},{96,80},{112,96},{1... | collective-permute-start | bytes 49160 | tf_op jit(solution)/shard_map/ppermute | solution.py:16
  114.1 5.7 %collective-permute-start.13 = (f32[2,4,512]{2,1,0:T(4,128)S(1)}, f32[2,4,512]{2,1,0:T(4,128)S(1)}, u32[]{:S(2)}, u32[]{:S(2)}) collective-permute-start(f32[2,4,512]{2,1,0:T(4,128)S(1)} %constant_dynamic-update-slice_fusion), channel_id=1, source_target_pairs={{0,480},{16,496},{32,0},{48,16},{64,32},{80,48},{96,64},{112,80},{... | collective-permute-start | bytes 49160 | tf_op jit(solution)/shard_map/ppermute | solution.py:16
  121.7 13.3 %collective-permute-start.14 = (f32[2,20,512]{2,1,0:T(8,128)}, f32[2,20,512]{2,1,0:T(8,128)}, u32[]{:S(2)}, u32[]{:S(2)}) collective-permute-start(f32[2,20,512]{2,1,0:T(8,128)} %concatenate.226), channel_id=1, source_target_pairs={{0,80},{16,96},{32,112},{48,128},{64,144},{80,160},{96,176},{112,1... | collective-permute-start | bytes 245768 | tf_op jit(solution)/shard_map/ppermute | solution.py:16
  129.0 9.8 %collective-permute-start.15 = (f32[2,20,512]{2,1,0:T(8,128)}, f32[2,20,512]{2,1,0:T(8,128)}, u32[]{:S(2)}, u32[]{:S(2)}) collective-permute-start(f32[2,20,512]{2,1,0:T(8,128)} %concatenate.226), channel_id=1, source_target_pairs={{0,432},{16,448},{32,464},{48,480},{64,496},{80,0},{96,16},{112,32... | collective-permute-start | bytes 245768 | tf_op jit(solution)/shard_map/ppermute | solution.py:16
  181.2 2.5 %collective-permute-start.16 = (f32[2,64,32]{1,2,0:T(8,128)S(1)}, f32[2,64,32]{1,2,0:T(8,128)S(1)}, u32[]{:S(2)}, u32[]{:S(2)}) collective-permute-start(f32[2,64,32]{1,2,0:T(8,128)S(1)} %get-tuple-element.205), channel_id=1, source_target_pairs={{0,16},{16,32},{32,48},{48,64},{64,80},{80,96},{96,112},{112,128},... | collective-permute-start | bytes 49160 | tf_op jit(solution)/shard_map/ppermute | solution.py:16
  182.5 3.3 %collective-permute-start.17 = (f32[2,64,32]{1,2,0:T(8,128)S(1)}, f32[2,64,32]{1,2,0:T(8,128)S(1)}, u32[]{:S(2)}, u32[]{:S(2)}) collective-permute-start(f32[2,64,32]{1,2,0:T(8,128)S(1)} %get-tuple-element.206), channel_id=1, source_target_pairs={{0,496},{16,0},{32,16},{48,32},{64,48},{80,64},{96,80},{112,96},{1... | collective-permute-start | bytes 49160 | tf_op jit(solution)/shard_map/ppermute | solution.py:16
  188.3 4.1 %copy-start.10 = (f32[24,16,1]{2,1,0:T(8,128)S(1)}, f32[24,16,1]{2,1,0:T(8,128)}, u32[]{:S(2)}) copy-start(f32[24,16,1]{2,1,0:T(8,128)} %copy-done.9) | copy-start | bytes 4612
  192.4 2.0 copy-start.12
  192.5 2.0 copy-start.14
  192.5 2.0 copy-start.32
  192.5 2.0 copy-start.34
  192.5 2.0 copy-start.36
  192.5 2.0 copy-start.38
  192.5 2.0 copy-start.40
  (29 other events, 31.1 us)
where the time goes:
time: 214 us; the launch traced here: 210 us
  starting transfers between devices  63.7 us (30%)
  local copies, waits for them, and re-layouts  58.6 us (27%)
  other arithmetic  47.8 us (22%)
  blocking collectives  21.4 us (10%)
  waiting for transfers between devices  16.2 us (8%)
    ppermute x18, starting transfers between devices, shift_from(): return lax.ppermute(x, axis, [(i, (i + k) % n) for i in range(n)])  63.7 us
    all_gather x1, blocking collectives, on_device(): band = lax.all_gather(jnp.stack([perm, rhs]), 'col', axis=2, tiled=True)  21.4 us
    add x15, other arithmetic, one_sweep(): return v + OMEGA * (rhs_band - (diagonal * v - beside_all)) / diagonal  19.7 us
    ppermute x18, waiting for transfers between devices, shift_from(): return lax.ppermute(x, axis, [(i, (i + k) % n) for i in range(n)])  16.2 us
    slice x12, local copies, waits for them, and re-layouts, coarsen(): t = t[:, :, 0::2] + t[:, :, 1::2]  9.58 us
    concatenate x2, local copies, waits for them, and re-layouts, rows_around(): return jnp.concatenate(lower + [x] + upper, axis=axis)  7.6 us
    slice x12, local copies, waits for them, and re-layouts, coarsen(): t = t[:, 0::2] + t[:, 1::2]  7.34 us
    add x7, other arithmetic, sweep(): return v[1:-1, 1:-1] + OMEGA * residual / faces[6]  7.26 us
  transfers between devices with their start and end apart: 18, of which 12 were waited for; matrix products, arithmetic and copies ran while one was open for 3% of the time, Pallas kernels for 0%

commit v1 on v0

--- a/solution.py
+++ b/solution.py
@@ -87,17 +87,40 @@
         return self.rhs_at(0) - apply_operator(v, self.faces_at(0))
 
 
+def pairs(n):
+    i = lax.broadcasted_iota(jnp.int32, (n, n // 2), 0)
+    j = lax.broadcasted_iota(jnp.int32, (n, n // 2), 1)
+    return (i // 2 == j).astype(jnp.float32)
+
+
+def along_z(field, matrix):
+    size_x, size_y, size_z = field.shape
+    flat = field.reshape(size_x * size_y, size_z)
+    out = jnp.dot(flat, matrix, precision=lax.Precision.HIGHEST)
+    return out.reshape(size_x, size_y, matrix.shape[1])
+
+
+def along_y(field, matrix):
+    size_x = field.shape[0]
+    batched = jnp.broadcast_to(matrix, (size_x,) + matrix.shape)
+    return jnp.einsum("xjy,xyz->xjz", batched, field, precision=lax.Precision.HIGHEST)
+
+
 def coarsen(field):
     size_x, size_y, size_z = field.shape
     t = field.reshape(size_x // 2, 2, size_y, size_z)
     t = t[:, 0] + t[:, 1]
-    t = t[:, 0::2] + t[:, 1::2]
-    t = t[:, :, 0::2] + t[:, :, 1::2]
+    t = along_z(t, pairs(size_z))
+    t = along_y(t, pairs(size_y).T)
     return t * 0.125
 
 
 def prolong(field):
-    return jnp.repeat(jnp.repeat(jnp.repeat(field, 2, axis=0), 2, axis=1), 2, axis=2)
+    size_x, size_y, size_z = field.shape
+    t = along_z(field, pairs(2 * size_z).T)
+    t = along_y(t, pairs(2 * size_y))
+    t = jnp.broadcast_to(t[:, None], (size_x, 2) + t.shape[1:])
+    return t.reshape(2 * size_x, 2 * size_y, 2 * size_z)
 
 
 def wrap_y(a, w=1):

time: 214 us -> 184 us (0.86)
  local copies, waits for them, and re-layouts: 58.6 us -> 32.9 us
  matrix products: 0 us -> 9.93 us
  other arithmetic: 47.8 us -> 39.8 us
  blocking collectives: 21.4 us -> 18.5 us
    slice x25 -> x1, local copies, waits for them, and re-layouts: 17.9 us -> 2.05 us  [coarsen(): t = t[:, 0] + t[:, 1]]
    dot_general x0 -> x18, matrix products: none -> 9.93 us  [the longest x9 6.07 us: along_z(): out = jnp.dot(flat, matrix, precision=lax.Precision.HIGHEST)]
    reshape x6 -> x0, local copies, waits for them, and re-layouts: 7.8 us -> none  [the longest x2 3.25 us: prolong(): jnp.repeat(jnp.repeat(field, 2, axis=0), 2, axis=1)]
    broadcast_in_dim x9 -> x1, local copies, waits for them, and re-layouts: 5.29 us -> 0.01 us  [prolong(): t = jnp.broadcast_to(t[:, None], (size_x, 2) + t.shape[1:])]
    add x12 -> x0, other arithmetic: 4 us -> none  [the longest x6 3.26 us: coarsen(): t = t[:, 0::2] + t[:, 1::2]]
    all_gather x1, blocking collectives: 21.4 us -> 18.5 us  [on_device(): band = lax.all_gather(jnp.stack([perm, rhs]), 'col', axis=2, tiled=True)]
    add x7 -> x6, other arithmetic: 7.26 us -> 4.52 us  [sweep(): return v[1:-1, 1:-1] + OMEGA * residual / faces[6]]
    unnamed x88 -> x145, local copies, waits for them, and re-layouts: 4.46 us -> 7.02 us
  transfers between devices with their start and end apart: 18 -> 18, of which waited for: 12 -> 10; matrix products, arithmetic and copies ran while one was open for 3% -> 5% of each run, Pallas kernels for 0% -> 0%
where the time goes in v1:
time: 184 us; the launch traced here: 181 us
  starting transfers between devices  61.8 us (34%)
  other arithmetic  39.8 us (22%)
  local copies, waits for them, and re-layouts  32.9 us (18%)
  blocking collectives  18.5 us (10%)
  waiting for transfers between devices  15.7 us (9%)
  matrix products  9.93 us (5%)
    ppermute x18, starting transfers between devices, shift_from(): return lax.ppermute(x, axis, [(i, (i + k) % n) for i in range(n)])  61.8 us
    add x15, other arithmetic, one_sweep(): return v + OMEGA * (rhs_band - (diagonal * v - beside_all)) / diagonal  19.7 us
    all_gather x1, blocking collectives, on_device(): band = lax.all_gather(jnp.stack([perm, rhs]), 'col', axis=2, tiled=True)  18.5 us
    ppermute x18, waiting for transfers between devices, shift_from(): return lax.ppermute(x, axis, [(i, (i + k) % n) for i in range(n)])  15.7 us
    concatenate x2, local copies, waits for them, and re-layouts, rows_around(): return jnp.concatenate(lower + [x] + upper, axis=axis)  7.61 us
    unnamed x145, local copies, waits for them, and re-layouts  7.02 us
    dot_general x9, matrix products, along_z(): out = jnp.dot(flat, matrix, precision=lax.Precision.HIGHEST)  6.07 us
    slice x64, local copies, waits for them, and re-layouts, lane_roll(): return jnp.roll(a, k, axis=-1)  4.98 us
  transfers between devices with their start and end apart: 18, of which 10 were waited for; matrix products, arithmetic and copies ran while one was open for 5% of the time, Pallas kernels for 0%

profile of v1, /device:TPU:1, one launch (start us, length us, event | category | flops | bytes accessed | tf_op | source)
XLA Modules:
  0.0 180.8 jit_solution(8115204299811840319)
XLA Ops:
  0.9 3.0 %collective-permute-start = (f32[3,4,16,128]{3,2,1,0:T(8,128)S(1)}, f32[3,4,16,128]{3,2,1,0:T(8,128)S(1)}, u32[]{:S(2)}, u32[]{:S(2)}) collective-permute-start(f32[3,4,16,128]{3,2,1,0:T(8,128)S(1)} %get-tuple-element.151), channel_id=1, source_target_pairs={{0,16},{16,32},{32,48},{48,64},{64,80},{80,96},{96,112},{112,128},... | collective-permute-start | bytes 294920 | tf_op jit(solution)/shard_map/ppermute | solution.py:16
  4.0 3.9 %collective-permute-start.1 = (f32[3,4,16,128]{3,2,1,0:T(8,128)S(1)}, f32[3,4,16,128]{3,2,1,0:T(8,128)S(1)}, u32[]{:S(2)}, u32[]{:S(2)}) collective-permute-start(f32[3,4,16,128]{3,2,1,0:T(8,128)S(1)} %get-tuple-element.152), channel_id=1, source_target_pairs={{0,496},{16,0},{32,16},{48,32},{64,48},{80,64},{96,80},{112,96},{1... | collective-permute-start | bytes 294920 | tf_op jit(solution)/shard_map/ppermute | solution.py:16
  10.5 1.9 %collective-permute-start.2 = (f32[3,40,4,128]{3,2,1,0:T(4,128)S(1)}, f32[3,40,4,128]{3,2,1,0:T(4,128)S(1)}, u32[]{:S(2)}, u32[]{:S(2)}) collective-permute-start(f32[3,40,4,128]{3,2,1,0:T(4,128)S(1)} %get-tuple-element.149), channel_id=1, source_target_pairs={{0,1},{1,2},{2,3},{3,4},{4,5},{5,6},{6,7},{7,8},{8,9},{9,10},{10,1... | collective-permute-start | bytes 737288 | tf_op jit(solution)/shard_map/ppermute | solution.py:16
  12.4 6.7 %collective-permute-start.3 = (f32[3,40,4,128]{3,2,1,0:T(4,128)S(1)}, f32[3,40,4,128]{3,2,1,0:T(4,128)S(1)}, u32[]{:S(2)}, u32[]{:S(2)}) collective-permute-start(f32[3,40,4,128]{3,2,1,0:T(4,128)S(1)} %get-tuple-element.150), channel_id=1, source_target_pairs={{0,15},{1,0},{2,1},{3,2},{4,3},{5,4},{6,5},{7,6},{8,7},{9,8},{10,9... | collective-permute-start | bytes 737288 | tf_op jit(solution)/shard_map/ppermute | solution.py:16
  20.7 1.5 collective-permute-done.3
  27.6 3.8 %collective-permute-start.5 = (f32[2,5,8,64]{3,2,1,0:T(8,128)S(1)}, f32[2,5,8,64]{3,2,1,0:T(8,128)S(1)}, u32[]{:S(2)}, u32[]{:S(2)}) collective-permute-start(f32[2,5,8,64]{3,2,1,0:T(8,128)S(1)} %get-tuple-element.210), channel_id=1, source_target_pairs={{0,496},{16,0},{32,16},{48,32},{64,48},{80,64},{96,80},{112,96},{1... | collective-permute-start | bytes 61448 | tf_op jit(solution)/shard_map/ppermute | solution.py:16
  32.3 1.9 %collective-permute-start.6 = (f32[2,26,5,64]{3,2,1,0:T(8,128)S(1)}, f32[2,26,5,64]{3,2,1,0:T(8,128)S(1)}, u32[]{:S(2)}, u32[]{:S(2)}) collective-permute-start(f32[2,26,5,64]{3,2,1,0:T(8,128)S(1)} %get-tuple-element.183), channel_id=1, source_target_pairs={{0,1},{1,2},{2,3},{3,4},{4,5},{5,6},{6,7},{7,8},{8,9},{9,10},{10,1... | collective-permute-start | bytes 199688 | tf_op jit(solution)/shard_map/ppermute | solution.py:16
  34.3 7.4 %collective-permute-start.7 = (f32[2,26,5,64]{3,2,1,0:T(8,128)S(1)}, f32[2,26,5,64]{3,2,1,0:T(8,128)S(1)}, u32[]{:S(2)}, u32[]{:S(2)}) collective-permute-start(f32[2,26,5,64]{3,2,1,0:T(8,128)S(1)} %get-tuple-element.184), channel_id=1, source_target_pairs={{0,15},{1,0},{2,1},{3,2},{4,3},{5,4},{6,5},{7,6},{8,7},{9,8},{10,9... | collective-permute-start | bytes 199688 | tf_op jit(solution)/shard_map/ppermute | solution.py:16
  43.0 1.5 collective-permute-done.7
  46.8 18.5 %all_gather.3 = f32[2,8,64,32]{3,1,0,2:T(8,128)S(1)} all-gather(f32[2,8,4,32]{3,1,0,2:T(8,128)S(1)} %copy.71), channel_id=1, replica_groups=mesh['row'=32,'col'=16] {'col'}, dimensions={2}, use_global_device_ids=true | all-gather | bytes 139264 | tf_op jit(solution)/shard_map/all_gather | solution.py:217
  68.1 2.1 %fusion.262 = (f32[4,1,64,32]{3,1,0,2:T(1,128)}, f32[4,1,64,32]{3,1,0,2:T(1,128)}) fusion(f32[4,2,64,32]{3,1,0,2:T(2,128)} %bitcast.226), kind=kLoop, calls=%fused_computation.477 | loop fusion | bytes 131072 | tf_op jit(solution)/shard_map/slice | solution.py:112
  70.2 1.6 copy.97
  71.8 1.6 copy.98
  74.1 6.4 %collective-permute-start.8 = (f32[2,4,64,32]{2,3,1,0:T(8,128)}, f32[2,4,64,32]{2,3,1,0:T(8,128)}, u32[]{:S(2)}, u32[]{:S(2)}) collective-permute-start(f32[2,4,64,32]{2,3,1,0:T(8,128)} %get-tuple-element.175), channel_id=1, source_target_pairs={{0,16},{16,32},{32,48},{48,64},{64,80},{80,96},{96,112},{112,128},... | collective-permute-start | bytes 196616 | tf_op jit(solution)/shard_map/ppermute | solution.py:16
  80.5 4.9 %collective-permute-start.9 = (f32[2,4,64,32]{2,3,1,0:T(8,128)}, f32[2,4,64,32]{2,3,1,0:T(8,128)}, u32[]{:S(2)}, u32[]{:S(2)}) collective-permute-start(f32[2,4,64,32]{2,3,1,0:T(8,128)} %get-tuple-element.176), channel_id=1, source_target_pairs={{0,496},{16,0},{32,16},{48,32},{64,48},{80,64},{96,80},{112,96},{1... | collective-permute-start | bytes 196616 | tf_op jit(solution)/shard_map/ppermute | solution.py:16
  93.9 1.9 %collective-permute-start.10 = (f32[2,4,512]{2,1,0:T(4,128)S(1)}, f32[2,4,512]{2,1,0:T(4,128)S(1)}, u32[]{:S(2)}, u32[]{:S(2)}) collective-permute-start(f32[2,4,512]{2,1,0:T(4,128)S(1)} %constant_dynamic-update-slice_fusion), channel_id=1, source_target_pairs={{0,32},{16,48},{32,64},{48,80},{64,96},{80,112},{96,128},{112,144}... | collective-permute-start | bytes 49160 | tf_op jit(solution)/shard_map/ppermute | solution.py:16
  95.8 3.0 %collective-permute-start.12 = (f32[2,4,512]{2,1,0:T(4,128)S(1)}, f32[2,4,512]{2,1,0:T(4,128)S(1)}, u32[]{:S(2)}, u32[]{:S(2)}) collective-permute-start(f32[2,4,512]{2,1,0:T(4,128)S(1)} %constant_dynamic-update-slice_fusion), channel_id=1, source_target_pairs={{0,496},{16,0},{32,16},{48,32},{64,48},{80,64},{96,80},{112,96},{1... | collective-permute-start | bytes 49160 | tf_op jit(solution)/shard_map/ppermute | solution.py:16
  98.8 4.9 %collective-permute-start.13 = (f32[2,4,512]{2,1,0:T(4,128)S(1)}, f32[2,4,512]{2,1,0:T(4,128)S(1)}, u32[]{:S(2)}, u32[]{:S(2)}) collective-permute-start(f32[2,4,512]{2,1,0:T(4,128)S(1)} %constant_dynamic-update-slice_fusion), channel_id=1, source_target_pairs={{0,480},{16,496},{32,0},{48,16},{64,32},{80,48},{96,64},{112,80},{... | collective-permute-start | bytes 49160 | tf_op jit(solution)/shard_map/ppermute | solution.py:16
  105.1 1.9 %concatenate.226 = f32[2,20,512]{2,1,0:T(8,128)} concatenate(f32[2,4,512]{2,1,0:T(4,128)S(1)} %collective-permute-done.10, f32[2,4,512]{2,1,0:T(4,128)S(1)} %collective-permute-done.11, f32[2,4,512]{2,1,0:T(4,128)S(1)} %constant_dynamic-update-slice_fusion, f32[2,4,512]{2,1,0:T(4,128)S(1)} %collective-permute-done.12, f32[2,4,512]{2,1,0:T(4,128)S(1)} %collective-permute-done.13), dimensions={1} | concatenate | bytes 163840 | tf_op jit(solution)/shard_map/concatenate | solution.py:156
  107.0 7.6 %collective-permute-start.14 = (f32[2,20,512]{2,1,0:T(8,128)}, f32[2,20,512]{2,1,0:T(8,128)}, u32[]{:S(2)}, u32[]{:S(2)}) collective-permute-start(f32[2,20,512]{2,1,0:T(8,128)} %concatenate.226), channel_id=1, source_target_pairs={{0,80},{16,96},{32,112},{48,128},{64,144},{80,160},{96,176},{112,1... | collective-permute-start | bytes 245768 | tf_op jit(solution)/shard_map/ppermute | solution.py:16
  114.5 2.1 %collective-permute-start.15 = (f32[2,20,512]{2,1,0:T(8,128)}, f32[2,20,512]{2,1,0:T(8,128)}, u32[]{:S(2)}, u32[]{:S(2)}) collective-permute-start(f32[2,20,512]{2,1,0:T(8,128)} %concatenate.226), channel_id=1, source_target_pairs={{0,432},{16,448},{32,464},{48,480},{64,496},{80,0},{96,16},{112,32... | collective-permute-start | bytes 245768 | tf_op jit(solution)/shard_map/ppermute | solution.py:16
  116.7 3.1 %collective-permute-done.14 = f32[2,20,512]{2,1,0:T(8,128)} collective-permute-done((f32[2,20,512]{2,1,0:T(8,128)}, f32[2,20,512]{2,1,0:T(8,128)}, u32[]{:S(2)}, u32[]{:S(2)}) %collective-permute-start.14) | collective-permute-done | bytes 81952 | tf_op jit(solution)/shard_map/ppermute | solution.py:16
  119.7 5.0 %collective-permute-done.15 = f32[2,20,512]{2,1,0:T(8,128)} collective-permute-done((f32[2,20,512]{2,1,0:T(8,128)}, f32[2,20,512]{2,1,0:T(8,128)}, u32[]{:S(2)}, u32[]{:S(2)}) %collective-permute-start.15) | collective-permute-done | bytes 81952 | tf_op jit(solution)/shard_map/ppermute | solution.py:16
  124.7 5.7 %concatenate.227 = f32[2,60,512]{2,1,0:T(8,128)} concatenate(f32[2,20,512]{2,1,0:T(8,128)} %collective-permute-done.14, f32[2,4,512]{2,1,0:T(4,128)S(1)} %collective-permute-done.10, f32[2,4,512]{2,1,0:T(4,128)S(1)} %collective-permute-done.11, f32[2,4,512]{2,1,0:T(4,128)S(1)} %constant_dynamic-update-slice_fusion, f32[2,4,512]{2,1,0:T(4,128)S(1)} %collective-permute-done.12, ...), dimensions={1} | concatenate | bytes 491520 | tf_op jit(solution)/shard_map/concatenate | solution.py:156
  130.5 1.6 slice_bitcast_fusion.21
  132.4 2.0 %multiply_divide_fusion = (f32[36,512]{1,0:T(8,128)S(1)}, f32[36,512]{1,0:T(8,128)}, f32[36,512]{1,0:T(8,128)}, f32[36,512]{1,0:T(8,128)}, f32[36,512]{1,0:T(8,1...) fusion(f32[2,60,512]{2,1,0:T(8,128)} %concatenate.227, f32[36,496]{1,0:T(8,128)S(1)} %get-tuple-element.216, ...), kind=kLoop, calls=%fused_computation.352 | loop fusion | flops 774144 | bytes 1180672 | tf_op jit(solution)/shard_map/div | solution.py:194
  134.4 26.2 %while.11 = (s32[]{:T(128)}, f32[36,512]{1,0:T(8,128)S(1)}, f32[36,512]{1,0:T(8,128)}, f32[36,512]{1,0:T(8,128)}, f32[36,512]{1,0:T(8,128)}, /*index=5*/f32[36,5...) while((s32[]{:T(128)}, f32[36,512]{1,0:T(8,128)S(1)}, ...), condition=%wide.region_1.2_spmd.clone, body=%wide.region_0.1_spmd.clone.sunk | while | flops 467970 | bytes 1783917 | solution.py:195
  136.6 1.3 fusion.305
  141.8 1.3 fusion.305
  147.1 1.3 fusion.305
  169.9 2.2 %collective-permute-done.17 = f32[2,64,32]{1,2,0:T(8,128)} collective-permute-done((f32[2,64,32]{1,2,0:T(8,128)}, f32[2,64,32]{1,2,0:T(8,128)}, u32[]{:S(2)}, u32[]{:S(2)}) %collective-permute-start.17) | collective-permute-done | bytes 16416 | tf_op jit(solution)/shard_map/ppermute | solution.py:16
  173.1 1.5 fusion.85
  (402 shorter events, 65.4 us)
Async XLA Ops:
  0.0 10.4 %copy-start.34 = (f32[32,16,128]{2,1,0:T(8,128)S(1)}, f32[32,16,128]{2,1,0:T(8,128)}, u32[]{:S(2)}) copy-start(f32[32,16,128]{2,1,0:T(8,128)} %param.6) | copy-start | bytes 786436
  0.9 9.4 %collective-permute-start = (f32[3,4,16,128]{3,2,1,0:T(8,128)S(1)}, f32[3,4,16,128]{3,2,1,0:T(8,128)S(1)}, u32[]{:S(2)}, u32[]{:S(2)}) collective-permute-start(f32[3,4,16,128]{3,2,1,0:T(8,128)S(1)} %get-tuple-element.151), channel_id=1, source_target_pairs={{0,16},{16,32},{32,48},{48,64},{64,80},{80,96},{96,112},{112,128},... | collective-permute-start | bytes 294920 | tf_op jit(solution)/shard_map/ppermute | solution.py:16
  4.0 6.4 %collective-permute-start.1 = (f32[3,4,16,128]{3,2,1,0:T(8,128)S(1)}, f32[3,4,16,128]{3,2,1,0:T(8,128)S(1)}, u32[]{:S(2)}, u32[]{:S(2)}) collective-permute-start(f32[3,4,16,128]{3,2,1,0:T(8,128)S(1)} %get-tuple-element.152), channel_id=1, source_target_pairs={{0,496},{16,0},{32,16},{48,32},{64,48},{80,64},{96,80},{112,96},{1... | collective-permute-start | bytes 294920 | tf_op jit(solution)/shard_map/ppermute | solution.py:16
  7.9 18.3 %copy-start.59 = (s32[128]{0:T(128)}, s32[128]{0:T(128)S(1)}, u32[]{:S(2)}) copy-start(s32[128]{0:T(128)S(1)} %get-tuple-element.222) | copy-start | bytes 1540
  7.9 18.3 %copy-start.61 = (s32[128]{0:T(128)}, s32[128]{0:T(128)S(1)}, u32[]{:S(2)}) copy-start(s32[128]{0:T(128)S(1)} %get-tuple-element.223) | copy-start | bytes 1540
  7.9 18.3 %copy-start.63 = (pred[128]{0:T(512)(128)(4,1)}, pred[128]{0:T(512)(128)(4,1)S(1)}, u32[]{:S(2)}) copy-start(pred[128]{0:T(512)(128)(4,1)S(1)} %compare_and_fusion.3) | copy-start | bytes 388
  7.9 38.4 %copy-start.50 = (s32[64]{0:T(128)}, s32[64]{0:T(128)S(1)}, u32[]{:S(2)}) copy-start(s32[64]{0:T(128)S(1)} %get-tuple-element.226) | copy-start | bytes 772
  8.0 38.4 %copy-start.51 = (s32[64]{0:T(128)}, s32[64]{0:T(128)S(1)}, u32[]{:S(2)}) copy-start(s32[64]{0:T(128)S(1)} %get-tuple-element.227) | copy-start | bytes 772
  8.0 38.4 %copy-start.52 = (pred[64]{0:T(512)(128)(4,1)}, pred[64]{0:T(512)(128)(4,1)S(1)}, u32[]{:S(2)}) copy-start(pred[64]{0:T(512)(128)(4,1)S(1)} %compare_and_fusion.1) | copy-start | bytes 196
  10.3 75.2 %copy-start.53 = (s32[32]{0:T(128)}, s32[32]{0:T(128)S(1)}, u32[]{:S(2)}) copy-start(s32[32]{0:T(128)S(1)} %get-tuple-element.230) | copy-start | bytes 388
  10.3 75.2 %copy-start.55 = (s32[32]{0:T(128)}, s32[32]{0:T(128)S(1)}, u32[]{:S(2)}) copy-start(s32[32]{0:T(128)S(1)} %get-tuple-element.231) | copy-start | bytes 388
  10.5 10.3 %collective-permute-start.2 = (f32[3,40,4,128]{3,2,1,0:T(4,128)S(1)}, f32[3,40,4,128]{3,2,1,0:T(4,128)S(1)}, u32[]{:S(2)}, u32[]{:S(2)}) collective-permute-start(f32[3,40,4,128]{3,2,1,0:T(4,128)S(1)} %get-tuple-element.149), channel_id=1, source_target_pairs={{0,1},{1,2},{2,3},{3,4},{4,5},{5,6},{6,7},{7,8},{8,9},{9,10},{10,1... | collective-permute-start | bytes 737288 | tf_op jit(solution)/shard_map/ppermute | solution.py:16
  12.4 9.8 %collective-permute-start.3 = (f32[3,40,4,128]{3,2,1,0:T(4,128)S(1)}, f32[3,40,4,128]{3,2,1,0:T(4,128)S(1)}, u32[]{:S(2)}, u32[]{:S(2)}) collective-permute-start(f32[3,40,4,128]{3,2,1,0:T(4,128)S(1)} %get-tuple-element.150), channel_id=1, source_target_pairs={{0,15},{1,0},{2,1},{3,2},{4,3},{5,4},{6,5},{7,6},{8,7},{9,8},{10,9... | collective-permute-start | bytes 737288 | tf_op jit(solution)/shard_map/ppermute | solution.py:16
  26.7 5.4 %collective-permute-start.4 = (f32[2,5,8,64]{3,2,1,0:T(8,128)S(1)}, f32[2,5,8,64]{3,2,1,0:T(8,128)S(1)}, u32[]{:S(2)}, u32[]{:S(2)}) collective-permute-start(f32[2,5,8,64]{3,2,1,0:T(8,128)S(1)} %get-tuple-element.209), channel_id=1, source_target_pairs={{0,16},{16,32},{32,48},{48,64},{64,80},{80,96},{96,112},{112,128},... | collective-permute-start | bytes 61448 | tf_op jit(solution)/shard_map/ppermute | solution.py:16
  27.6 4.6 %collective-permute-start.5 = (f32[2,5,8,64]{3,2,1,0:T(8,128)S(1)}, f32[2,5,8,64]{3,2,1,0:T(8,128)S(1)}, u32[]{:S(2)}, u32[]{:S(2)}) collective-permute-start(f32[2,5,8,64]{3,2,1,0:T(8,128)S(1)} %get-tuple-element.210), channel_id=1, source_target_pairs={{0,496},{16,0},{32,16},{48,32},{64,48},{80,64},{96,80},{112,96},{1... | collective-permute-start | bytes 61448 | tf_op jit(solution)/shard_map/ppermute | solution.py:16
  31.4 54.1 %copy-start.57 = (pred[32]{0:T(512)(128)(4,1)}, pred[32]{0:T(512)(128)(4,1)S(1)}, u32[]{:S(2)}) copy-start(pred[32]{0:T(512)(128)(4,1)S(1)} %compare_and_fusion) | copy-start | bytes 100
  32.3 10.7 %collective-permute-start.6 = (f32[2,26,5,64]{3,2,1,0:T(8,128)S(1)}, f32[2,26,5,64]{3,2,1,0:T(8,128)S(1)}, u32[]{:S(2)}, u32[]{:S(2)}) collective-permute-start(f32[2,26,5,64]{3,2,1,0:T(8,128)S(1)} %get-tuple-element.183), channel_id=1, source_target_pairs={{0,1},{1,2},{2,3},{3,4},{4,5},{5,6},{6,7},{7,8},{8,9},{9,10},{10,1... | collective-permute-start | bytes 199688 | tf_op jit(solution)/shard_map/ppermute | solution.py:16
  34.3 10.2 %collective-permute-start.7 = (f32[2,26,5,64]{3,2,1,0:T(8,128)S(1)}, f32[2,26,5,64]{3,2,1,0:T(8,128)S(1)}, u32[]{:S(2)}, u32[]{:S(2)}) collective-permute-start(f32[2,26,5,64]{3,2,1,0:T(8,128)S(1)} %get-tuple-element.184), channel_id=1, source_target_pairs={{0,15},{1,0},{2,1},{3,2},{4,3},{5,4},{6,5},{7,6},{8,7},{9,8},{10,9... | collective-permute-start | bytes 199688 | tf_op jit(solution)/shard_map/ppermute | solution.py:16
  45.7 19.5 %copy-start.18 = (f32[22,14,64]{2,1,0:T(8,128)}, f32[22,14,64]{2,1,0:T(8,128)S(1)}, u32[]{:S(2)}) copy-start(f32[22,14,64]{2,1,0:T(8,128)S(1)} %fusion.104) | copy-start | bytes 236548
  68.1 21.3 %copy-start.15 = (f32[2,8,64,32]{2,3,1,0:T(8,128)}, f32[2,8,64,32]{2,3,1,0:T(8,128)S(1)}, u32[]{:S(2)}) copy-start(f32[2,8,64,32]{2,3,1,0:T(8,128)S(1)} %copy.72) | copy-start | bytes 393220
  74.1 14.2 %collective-permute-start.8 = (f32[2,4,64,32]{2,3,1,0:T(8,128)}, f32[2,4,64,32]{2,3,1,0:T(8,128)}, u32[]{:S(2)}, u32[]{:S(2)}) collective-permute-start(f32[2,4,64,32]{2,3,1,0:T(8,128)} %get-tuple-element.175), channel_id=1, source_target_pairs={{0,16},{16,32},{32,48},{48,64},{64,80},{80,96},{96,112},{112,128},... | collective-permute-start | bytes 196616 | tf_op jit(solution)/shard_map/ppermute | solution.py:16
  80.5 7.9 %collective-permute-start.9 = (f32[2,4,64,32]{2,3,1,0:T(8,128)}, f32[2,4,64,32]{2,3,1,0:T(8,128)}, u32[]{:S(2)}, u32[]{:S(2)}) collective-permute-start(f32[2,4,64,32]{2,3,1,0:T(8,128)} %get-tuple-element.176), channel_id=1, source_target_pairs={{0,496},{16,0},{32,16},{48,32},{64,48},{80,64},{96,80},{112,96},{1... | collective-permute-start | bytes 196616 | tf_op jit(solution)/shard_map/ppermute | solution.py:16
  89.6 74.8 %copy-start.46 = (f32[14,64,1]{1,2,0:T(1,128)}, f32[14,64,1]{1,2,0:T(1,128)S(1)}, u32[]{:S(2)}) copy-start(f32[14,64,1]{1,2,0:T(1,128)S(1)} %get-tuple-element.181) | copy-start | bytes 10756
  89.6 74.8 %copy-start.47 = (f32[14,64,1]{1,2,0:T(1,128)}, f32[14,64,1]{1,2,0:T(1,128)S(1)}, u32[]{:S(2)}) copy-start(f32[14,64,1]{1,2,0:T(1,128)S(1)} %get-tuple-element.182) | copy-start | bytes 10756
  93.9 11.2 %collective-permute-start.10 = (f32[2,4,512]{2,1,0:T(4,128)S(1)}, f32[2,4,512]{2,1,0:T(4,128)S(1)}, u32[]{:S(2)}, u32[]{:S(2)}) collective-permute-start(f32[2,4,512]{2,1,0:T(4,128)S(1)} %constant_dynamic-update-slice_fusion), channel_id=1, source_target_pairs={{0,32},{16,48},{32,64},{48,80},{64,96},{80,112},{96,128},{112,144}... | collective-permute-start | bytes 49160 | tf_op jit(solution)/shard_map/ppermute | solution.py:16
  95.8 9.3 %collective-permute-start.11 = (f32[2,4,512]{2,1,0:T(4,128)S(1)}, f32[2,4,512]{2,1,0:T(4,128)S(1)}, u32[]{:S(2)}, u32[]{:S(2)}) collective-permute-start(f32[2,4,512]{2,1,0:T(4,128)S(1)} %constant_dynamic-update-slice_fusion), channel_id=1, source_target_pairs={{0,16},{16,32},{32,48},{48,64},{64,80},{80,96},{96,112},{112,128},... | collective-permute-start | bytes 49160 | tf_op jit(solution)/shard_map/ppermute | solution.py:16
  95.8 9.2 %collective-permute-start.12 = (f32[2,4,512]{2,1,0:T(4,128)S(1)}, f32[2,4,512]{2,1,0:T(4,128)S(1)}, u32[]{:S(2)}, u32[]{:S(2)}) collective-permute-start(f32[2,4,512]{2,1,0:T(4,128)S(1)} %constant_dynamic-update-slice_fusion), channel_id=1, source_target_pairs={{0,496},{16,0},{32,16},{48,32},{64,48},{80,64},{96,80},{112,96},{1... | collective-permute-start | bytes 49160 | tf_op jit(solution)/shard_map/ppermute | solution.py:16
  98.8 6.3 %collective-permute-start.13 = (f32[2,4,512]{2,1,0:T(4,128)S(1)}, f32[2,4,512]{2,1,0:T(4,128)S(1)}, u32[]{:S(2)}, u32[]{:S(2)}) collective-permute-start(f32[2,4,512]{2,1,0:T(4,128)S(1)} %constant_dynamic-update-slice_fusion), channel_id=1, source_target_pairs={{0,480},{16,496},{32,0},{48,16},{64,32},{80,48},{96,64},{112,80},{... | collective-permute-start | bytes 49160 | tf_op jit(solution)/shard_map/ppermute | solution.py:16
  107.0 12.7 %collective-permute-start.14 = (f32[2,20,512]{2,1,0:T(8,128)}, f32[2,20,512]{2,1,0:T(8,128)}, u32[]{:S(2)}, u32[]{:S(2)}) collective-permute-start(f32[2,20,512]{2,1,0:T(8,128)} %concatenate.226), channel_id=1, source_target_pairs={{0,80},{16,96},{32,112},{48,128},{64,144},{80,160},{96,176},{112,1... | collective-permute-start | bytes 245768 | tf_op jit(solution)/shard_map/ppermute | solution.py:16
  114.5 10.2 %collective-permute-start.15 = (f32[2,20,512]{2,1,0:T(8,128)}, f32[2,20,512]{2,1,0:T(8,128)}, u32[]{:S(2)}, u32[]{:S(2)}) collective-permute-start(f32[2,20,512]{2,1,0:T(8,128)} %concatenate.226), channel_id=1, source_target_pairs={{0,432},{16,448},{32,464},{48,480},{64,496},{80,0},{96,16},{112,32... | collective-permute-start | bytes 245768 | tf_op jit(solution)/shard_map/ppermute | solution.py:16
  167.5 2.4 %collective-permute-start.16 = (f32[2,64,32]{1,2,0:T(8,128)}, f32[2,64,32]{1,2,0:T(8,128)}, u32[]{:S(2)}, u32[]{:S(2)}) collective-permute-start(f32[2,64,32]{1,2,0:T(8,128)} %get-tuple-element.207), channel_id=1, source_target_pairs={{0,16},{16,32},{32,48},{48,64},{64,80},{80,96},{96,112},{112,128},... | collective-permute-start | bytes 49160 | tf_op jit(solution)/shard_map/ppermute | solution.py:16
  168.4 3.7 %collective-permute-start.17 = (f32[2,64,32]{1,2,0:T(8,128)}, f32[2,64,32]{1,2,0:T(8,128)}, u32[]{:S(2)}, u32[]{:S(2)}) collective-permute-start(f32[2,64,32]{1,2,0:T(8,128)} %get-tuple-element.208), channel_id=1, source_target_pairs={{0,496},{16,0},{32,16},{48,32},{64,48},{80,64},{96,80},{112,96},{1... | collective-permute-start | bytes 49160 | tf_op jit(solution)/shard_map/ppermute | solution.py:16
  (57 other events, 116.1 us)

commit v2 on v1

--- a/solution.py
+++ b/solution.py
@@ -1,6 +1,8 @@
 import jax
 import jax.numpy as jnp
 from jax import lax
+from jax.experimental import pallas as pl
+from jax.experimental.pallas import tpu as pltpu
 from jax.sharding import PartitionSpec as P
 
 LEVELS = 3
@@ -156,46 +158,73 @@
     return jnp.concatenate(lower + [x] + upper, axis=axis)
 
 
-def lane_roll(a, k):
-    return jnp.roll(a, k, axis=-1)
+def coarse_kernel(scale, size_z, k_ref, b_ref, out_ref):
+    k = k_ref[...]
+    b = b_ref[...]
+    rows, lanes = k.shape
+    lane = lax.broadcasted_iota(jnp.int32, (rows, lanes), 1) % size_z
+    first, last = lane == 0, lane == size_z - 1
+
+    def x_lower(a):
+        return pltpu.roll(a, 1, 0)
+
+    def x_upper(a):
+        return pltpu.roll(a, rows - 1, 0)
+
+    def y_lower(a):
+        return pltpu.roll(a, size_z, 1)
+
+    def y_upper(a):
+        return pltpu.roll(a, lanes - size_z, 1)
+
+    def z_lower(a):
+        return pltpu.roll(a, 1, 1)
+
+    def z_upper(a):
+        return pltpu.roll(a, lanes - 1, 1)
+
+    west_x = harmonic(x_lower(k), k, scale)
+    east_x = harmonic(k, x_upper(k), scale)
+    west_y = harmonic(y_lower(k), k, scale)
+    east_y = harmonic(k, y_upper(k), scale)
+    below = jnp.where(first, 2.0 * k * scale, harmonic(z_lower(k), k, scale))
+    above = jnp.where(last, 2.0 * k * scale, harmonic(k, z_upper(k), scale))
+    diagonal = west_x + east_x + west_y + east_y + below + above
+
+    def one_sweep(i, v):
+        under = jnp.where(first, 0.0, z_lower(v))
+        over = jnp.where(last, 0.0, z_upper(v))
+        beside_all = west_x * x_lower(v) + east_x * x_upper(v)
+        beside_all = beside_all + west_y * y_lower(v) + east_y * y_upper(v)
+        beside_all = beside_all + below * under + above * over
+        return v + OMEGA * (b - (diagonal * v - beside_all)) / diagonal
+
+    v = OMEGA * b / diagonal
+    out_ref[...] = lax.fori_loop(1, CSWEEPS, one_sweep, v)
 
 
 def coarse_solve(right_side, perm, scale):
     size_x, size_y, size_z = right_side.shape
     lanes = size_y * size_z
     pair = jnp.stack([right_side, perm]).reshape(2, size_x, lanes)
-    need = CSWEEPS + 1
     near = rows_around(pair, (1, 2), 1)
     wide = rows_around(near, (5,), 1)
-    assert 7 * size_x >= need
-    cut = 7 * size_x - need
+    keep = CSWEEPS + 2
+    keep += (-(size_x + 2 * keep)) % 8 // 2
+    cut = 7 * size_x - keep
+    assert cut >= 0
     wide = wide[:, cut : wide.shape[1] - cut]
-    rhs_band, k = wide[0, 1:-1], wide[1]
-    lane = lax.broadcasted_iota(jnp.int32, (1, lanes), 1) % size_z
-    first, last = lane == 0, lane == size_z - 1
-    c = k[1:-1]
-    west_x = harmonic(k[:-2], c, scale)
-    east_x = harmonic(c, k[2:], scale)
-    west_y = harmonic(lane_roll(c, size_z), c, scale)
-    east_y = harmonic(c, lane_roll(c, -size_z), scale)
-    below = jnp.where(first, 2.0 * c * scale, harmonic(lane_roll(c, 1), c, scale))
-    above = jnp.where(last, 2.0 * c * scale, harmonic(c, lane_roll(c, -1), scale))
-    diagonal = west_x + east_x + west_y + east_y + below + above
-
-    def one_sweep(i, v):
-        ext = jnp.concatenate([v[:1], v, v[-1:]], axis=0)
-        under = jnp.where(first, 0.0, lane_roll(v, 1))
-        over = jnp.where(last, 0.0, lane_roll(v, -1))
-        beside_all = west_x * ext[:-2] + east_x * ext[2:]
-        beside_all = beside_all + west_y * lane_roll(v, size_z) + east_y * lane_roll(v, -size_z)
-        beside_all = beside_all + below * under + above * over
-        return v + OMEGA * (rhs_band - (diagonal * v - beside_all)) / diagonal
-
-    v = OMEGA * rhs_band / diagonal
-    v = lax.fori_loop(1, CSWEEPS, one_sweep, v)
-    have = need - 1 - (CSWEEPS - 1)
-    drop = need - 1 - have
-    v = v[drop : v.shape[0] - drop]
+    rows = wide.shape[1]
+    call = pl.pallas_call(
+        lambda k_ref, b_ref, out_ref: coarse_kernel(scale, size_z, k_ref, b_ref, out_ref),
+        out_shape=jax.ShapeDtypeStruct((rows, lanes), jnp.float32),
+        cost_estimate=pl.CostEstimate(
+            flops=40 * CSWEEPS * rows * lanes, transcendentals=0, bytes_accessed=12 * rows * lanes
+        ),
+    )
+    v = call(wide[1], wide[0])
+    drop = keep - 1
+    v = v[drop : rows - drop]
     return v.reshape(v.shape[0], size_y, size_z)
 
 

time: 184 us -> 160 us (0.87)
  the two profiles are of different devices: /device:TPU:1 before, /device:TPU:35 now
where the time goes in v2:
time: 160 us; the launch traced here: 159 us
  starting transfers between devices  47.5 us (30%)
  waiting for transfers between devices  29.9 us (19%)
  local copies, waits for them, and re-layouts  28 us (18%)
  blocking collectives  21.4 us (13%)
  other arithmetic  16.4 us (10%)
  matrix products  9.86 us (6%)
  Pallas kernels  4.54 us (3%)
    ppermute x18, starting transfers between devices, shift_from(): return lax.ppermute(x, axis, [(i, (i + k) % n) for i in range(n)])  47.5 us
    ppermute x18, waiting for transfers between devices, shift_from(): return lax.ppermute(x, axis, [(i, (i + k) % n) for i in range(n)])  29.9 us
    all_gather x1, blocking collectives, on_device(): band = lax.all_gather(jnp.stack([perm, rhs]), 'col', axis=2, tiled=True)  21.4 us
    concatenate x2, local copies, waits for them, and re-layouts, rows_around(): return jnp.concatenate(lower + [x] + upper, axis=axis)  7.6 us
    unnamed x145, local copies, waits for them, and re-layouts  6.56 us
    dot_general x9, matrix products, along_z(): out = jnp.dot(flat, matrix, precision=lax.Precision.HIGHEST)  6 us
    pallas_call x1, Pallas kernels, coarse_solve(): v = call(wide[1], wide[0])  4.54 us
    add x6, other arithmetic, sweep(): return v[1:-1, 1:-1] + OMEGA * residual / faces[6]  4.51 us
  transfers between devices with their start and end apart: 18, of which 14 were waited for; matrix products, arithmetic and copies ran while one was open for 5% of the time, Pallas kernels for 0%

profile of v2, /device:TPU:35, one launch (start us, length us, event | category | flops | bytes accessed | tf_op | source)
XLA Modules:
  0.0 159.1 jit_solution(460217581944168939)
XLA Ops:
  0.9 2.2 %collective-permute-start = (f32[3,4,16,128]{3,2,1,0:T(8,128)S(1)}, f32[3,4,16,128]{3,2,1,0:T(8,128)S(1)}, u32[]{:S(2)}, u32[]{:S(2)}) collective-permute-start(f32[3,4,16,128]{3,2,1,0:T(8,128)S(1)} %get-tuple-element.27), channel_id=1, source_target_pairs={{0,16},{16,32},{32,48},{48,64},{64,80},{80,96},{96,112},{112,128},... | collective-permute-start | bytes 294920 | tf_op jit(solution)/shard_map/ppermute | solution.py:18
  5.2 2.0 %collective-permute-done.1 = f32[3,4,16,128]{3,2,1,0:T(8,128)S(1)} collective-permute-done((f32[3,4,16,128]{3,2,1,0:T(8,128)S(1)}, f32[3,4,16,128]{3,2,1,0:T(8,128)S(1)}, u32[]{:S(2)}, u32[]{:S(2)}) %collective-permute-start.1) | collective-permute-done | bytes 98336 | tf_op jit(solution)/shard_map/ppermute | solution.py:18
  7.3 3.1 %collective-permute-start.2 = (f32[3,40,4,128]{3,2,1,0:T(4,128)S(1)}, f32[3,40,4,128]{3,2,1,0:T(4,128)S(1)}, u32[]{:S(2)}, u32[]{:S(2)}) collective-permute-start(f32[3,40,4,128]{3,2,1,0:T(4,128)S(1)} %get-tuple-element.25), channel_id=1, source_target_pairs={{0,1},{1,2},{2,3},{3,4},{4,5},{5,6},{6,7},{7,8},{8,9},{9,10},{10,1... | collective-permute-start | bytes 737288 | tf_op jit(solution)/shard_map/ppermute | solution.py:18
  10.4 2.2 %collective-permute-start.3 = (f32[3,40,4,128]{3,2,1,0:T(4,128)S(1)}, f32[3,40,4,128]{3,2,1,0:T(4,128)S(1)}, u32[]{:S(2)}, u32[]{:S(2)}) collective-permute-start(f32[3,40,4,128]{3,2,1,0:T(4,128)S(1)} %get-tuple-element.26), channel_id=1, source_target_pairs={{0,15},{1,0},{2,1},{3,2},{4,3},{5,4},{6,5},{7,6},{8,7},{9,8},{10,9... | collective-permute-start | bytes 737288 | tf_op jit(solution)/shard_map/ppermute | solution.py:18
  13.2 2.9 %collective-permute-done.2 = f32[3,40,4,128]{3,2,1,0:T(4,128)S(1)} collective-permute-done((f32[3,40,4,128]{3,2,1,0:T(4,128)S(1)}, f32[3,40,4,128]{3,2,1,0:T(4,128)S(1)}, u32[]{:S(2)}, u32[]{:S(2)}) %collective-permute-start.2) | collective-permute-done | bytes 245792 | tf_op jit(solution)/shard_map/ppermute | solution.py:18
  16.1 3.1 %collective-permute-done.3 = f32[3,40,4,128]{3,2,1,0:T(4,128)S(1)} collective-permute-done((f32[3,40,4,128]{3,2,1,0:T(4,128)S(1)}, f32[3,40,4,128]{3,2,1,0:T(4,128)S(1)}, u32[]{:S(2)}, u32[]{:S(2)}) %collective-permute-start.3) | collective-permute-done | bytes 245792 | tf_op jit(solution)/shard_map/ppermute | solution.py:18
  23.7 1.5 collective-permute-start.4
  26.3 2.3 %collective-permute-done.5 = f32[2,5,8,64]{3,2,1,0:T(8,128)S(1)} collective-permute-done((f32[2,5,8,64]{3,2,1,0:T(8,128)S(1)}, f32[2,5,8,64]{3,2,1,0:T(8,128)S(1)}, u32[]{:S(2)}, u32[]{:S(2)}) %collective-permute-start.5) | collective-permute-done | bytes 20512 | tf_op jit(solution)/shard_map/ppermute | solution.py:18
  28.7 2.8 %collective-permute-start.6 = (f32[2,26,5,64]{3,2,1,0:T(8,128)S(1)}, f32[2,26,5,64]{3,2,1,0:T(8,128)S(1)}, u32[]{:S(2)}, u32[]{:S(2)}) collective-permute-start(f32[2,26,5,64]{3,2,1,0:T(8,128)S(1)} %get-tuple-element.59), channel_id=1, source_target_pairs={{0,1},{1,2},{2,3},{3,4},{4,5},{5,6},{6,7},{7,8},{8,9},{9,10},{10,1... | collective-permute-start | bytes 199688 | tf_op jit(solution)/shard_map/ppermute | solution.py:18
  31.5 2.5 %collective-permute-start.7 = (f32[2,26,5,64]{3,2,1,0:T(8,128)S(1)}, f32[2,26,5,64]{3,2,1,0:T(8,128)S(1)}, u32[]{:S(2)}, u32[]{:S(2)}) collective-permute-start(f32[2,26,5,64]{3,2,1,0:T(8,128)S(1)} %get-tuple-element.60), channel_id=1, source_target_pairs={{0,15},{1,0},{2,1},{3,2},{4,3},{5,4},{6,5},{7,6},{8,7},{9,8},{10,9... | collective-permute-start | bytes 199688 | tf_op jit(solution)/shard_map/ppermute | solution.py:18
  34.0 2.5 %collective-permute-done.6 = f32[2,26,5,64]{3,2,1,0:T(8,128)S(1)} collective-permute-done((f32[2,26,5,64]{3,2,1,0:T(8,128)S(1)}, f32[2,26,5,64]{3,2,1,0:T(8,128)S(1)}, u32[]{:S(2)}, u32[]{:S(2)}) %collective-permute-start.6) | collective-permute-done | bytes 66592 | tf_op jit(solution)/shard_map/ppermute | solution.py:18
  36.5 4.7 %collective-permute-done.7 = f32[2,26,5,64]{3,2,1,0:T(8,128)S(1)} collective-permute-done((f32[2,26,5,64]{3,2,1,0:T(8,128)S(1)}, f32[2,26,5,64]{3,2,1,0:T(8,128)S(1)}, u32[]{:S(2)}, u32[]{:S(2)}) %collective-permute-start.7) | collective-permute-done | bytes 66592 | tf_op jit(solution)/shard_map/ppermute | solution.py:18
  43.5 21.4 %all_gather.3 = f32[2,8,64,32]{3,1,0,2:T(8,128)S(1)} all-gather(f32[2,8,4,32]{3,1,0,2:T(8,128)S(1)} %copy.73), channel_id=1, replica_groups=mesh['row'=32,'col'=16] {'col'}, dimensions={2}, use_global_device_ids=true | all-gather | bytes 139264 | tf_op jit(solution)/shard_map/all_gather | solution.py:246
  67.7 2.1 %fusion.234 = (f32[4,1,64,32]{3,1,0,2:T(1,128)}, f32[4,1,64,32]{3,1,0,2:T(1,128)}) fusion(f32[4,2,64,32]{3,1,0,2:T(2,128)} %bitcast.196), kind=kLoop, calls=%fused_computation.426 | loop fusion | bytes 131072 | tf_op jit(solution)/shard_map/slice | solution.py:114
  69.7 1.6 %copy.100 = f32[4,1,64,32]{2,3,0,1:T(8,128)} copy(f32[4,1,64,32]{3,1,0,2:T(1,128)} %get-tuple-element.47) | data formatting | bytes 65536
  71.3 1.6 %copy.99 = f32[4,1,64,32]{2,3,0,1:T(8,128)} copy(f32[4,1,64,32]{3,1,0,2:T(1,128)} %get-tuple-element.48) | data formatting | bytes 65536
  73.7 6.4 %collective-permute-start.8 = (f32[2,4,64,32]{2,3,1,0:T(8,128)}, f32[2,4,64,32]{2,3,1,0:T(8,128)}, u32[]{:S(2)}, u32[]{:S(2)}) collective-permute-start(f32[2,4,64,32]{2,3,1,0:T(8,128)} %get-tuple-element.51), channel_id=1, source_target_pairs={{0,16},{16,32},{32,48},{48,64},{64,80},{80,96},{96,112},{112,128},... | collective-permute-start | bytes 196616 | tf_op jit(solution)/shard_map/ppermute | solution.py:18
  83.0 1.8 %collective-permute-done.9 = f32[2,4,64,32]{2,3,1,0:T(8,128)} collective-permute-done((f32[2,4,64,32]{2,3,1,0:T(8,128)}, f32[2,4,64,32]{2,3,1,0:T(8,128)}, u32[]{:S(2)}, u32[]{:S(2)}) %collective-permute-start.9) | collective-permute-done | bytes 65568 | tf_op jit(solution)/shard_map/ppermute | solution.py:18
  90.2 4.5 %collective-permute-start.10 = (f32[2,4,512]{2,1,0:T(4,128)S(1)}, f32[2,4,512]{2,1,0:T(4,128)S(1)}, u32[]{:S(2)}, u32[]{:S(2)}) collective-permute-start(f32[2,4,512]{2,1,0:T(4,128)S(1)} %constant_dynamic-update-slice_fusion), channel_id=1, source_target_pairs={{0,32},{16,48},{32,64},{48,80},{64,96},{80,112},{96,128},{112,144}... | collective-permute-start | bytes 49160 | tf_op jit(solution)/shard_map/ppermute | solution.py:18
  95.7 4.7 %collective-permute-start.13 = (f32[2,4,512]{2,1,0:T(4,128)S(1)}, f32[2,4,512]{2,1,0:T(4,128)S(1)}, u32[]{:S(2)}, u32[]{:S(2)}) collective-permute-start(f32[2,4,512]{2,1,0:T(4,128)S(1)} %constant_dynamic-update-slice_fusion), channel_id=1, source_target_pairs={{0,480},{16,496},{32,0},{48,16},{64,32},{80,48},{96,64},{112,80},{... | collective-permute-start | bytes 49160 | tf_op jit(solution)/shard_map/ppermute | solution.py:18
  101.6 1.7 %collective-permute-done.13 = f32[2,4,512]{2,1,0:T(4,128)S(1)} collective-permute-done((f32[2,4,512]{2,1,0:T(4,128)S(1)}, f32[2,4,512]{2,1,0:T(4,128)S(1)}, u32[]{:S(2)}, u32[]{:S(2)}) %collective-permute-start.13) | collective-permute-done | bytes 16416 | tf_op jit(solution)/shard_map/ppermute | solution.py:18
  103.3 1.9 %concatenate.191 = f32[2,20,512]{2,1,0:T(8,128)} concatenate(f32[2,4,512]{2,1,0:T(4,128)S(1)} %collective-permute-done.10, f32[2,4,512]{2,1,0:T(4,128)S(1)} %collective-permute-done.11, f32[2,4,512]{2,1,0:T(4,128)S(1)} %constant_dynamic-update-slice_fusion, f32[2,4,512]{2,1,0:T(4,128)S(1)} %collective-permute-done.12, f32[2,4,512]{2,1,0:T(4,128)S(1)} %collective-permute-done.13), dimensions={1} | concatenate | bytes 163840 | tf_op jit(solution)/shard_map/concatenate | solution.py:158
  105.2 6.4 %collective-permute-start.14 = (f32[2,20,512]{2,1,0:T(8,128)}, f32[2,20,512]{2,1,0:T(8,128)}, u32[]{:S(2)}, u32[]{:S(2)}) collective-permute-start(f32[2,20,512]{2,1,0:T(8,128)} %concatenate.191), channel_id=1, source_target_pairs={{0,80},{16,96},{32,112},{48,128},{64,144},{80,160},{96,176},{112,1... | collective-permute-start | bytes 245768 | tf_op jit(solution)/shard_map/ppermute | solution.py:18
  111.6 3.9 %collective-permute-start.15 = (f32[2,20,512]{2,1,0:T(8,128)}, f32[2,20,512]{2,1,0:T(8,128)}, u32[]{:S(2)}, u32[]{:S(2)}) collective-permute-start(f32[2,20,512]{2,1,0:T(8,128)} %concatenate.191), channel_id=1, source_target_pairs={{0,432},{16,448},{32,464},{48,480},{64,496},{80,0},{96,16},{112,32... | collective-permute-start | bytes 245768 | tf_op jit(solution)/shard_map/ppermute | solution.py:18
  116.8 2.2 %collective-permute-done.14 = f32[2,20,512]{2,1,0:T(8,128)} collective-permute-done((f32[2,20,512]{2,1,0:T(8,128)}, f32[2,20,512]{2,1,0:T(8,128)}, u32[]{:S(2)}, u32[]{:S(2)}) %collective-permute-start.14) | collective-permute-done | bytes 81952 | tf_op jit(solution)/shard_map/ppermute | solution.py:18
  119.1 2.0 %collective-permute-done.15 = f32[2,20,512]{2,1,0:T(8,128)} collective-permute-done((f32[2,20,512]{2,1,0:T(8,128)}, f32[2,20,512]{2,1,0:T(8,128)}, u32[]{:S(2)}, u32[]{:S(2)}) %collective-permute-start.15) | collective-permute-done | bytes 81952 | tf_op jit(solution)/shard_map/ppermute | solution.py:18
  121.1 5.7 %concatenate.192 = f32[2,60,512]{2,1,0:T(8,128)} concatenate(f32[2,20,512]{2,1,0:T(8,128)} %collective-permute-done.14, f32[2,4,512]{2,1,0:T(4,128)S(1)} %collective-permute-done.10, f32[2,4,512]{2,1,0:T(4,128)S(1)} %collective-permute-done.11, f32[2,4,512]{2,1,0:T(4,128)S(1)} %constant_dynamic-update-slice_fusion, f32[2,4,512]{2,1,0:T(4,128)S(1)} %collective-permute-done.12, ...), dimensions={1} | concatenate | bytes 491520 | tf_op jit(solution)/shard_map/concatenate | solution.py:158
  126.8 1.6 %slice_bitcast_fusion.18 = (f32[40,512]{1,0:T(8,128)}, f32[40,512]{1,0:T(8,128)}) fusion(f32[2,60,512]{2,1,0:T(8,128)} %concatenate.192), kind=kLoop, calls=%fused_computation.312 | loop fusion | bytes 327680 | tf_op jit(solution)/shard_map/squeeze | solution.py:225
  128.4 4.5 %shard_map.37 = f32[40,512]{1,0:T(8,128)} custom-call(f32[40,512]{1,0:T(8,128)} %get-tuple-element.46.k_ref, f32[40,512]{1,0:T(8,128)} %get-tuple-element.45.b_ref), custom_call_target="tpu_custom_call" | custom-call | flops 13107200 | bytes 245760 | tf_op jit(solution)/shard_map/pallas_call | solution.py:225
  140.4 6.3 %collective-permute-start.16 = (f32[2,64,32]{1,2,0:T(8,128)}, f32[2,64,32]{1,2,0:T(8,128)}, u32[]{:S(2)}, u32[]{:S(2)}) collective-permute-start(f32[2,64,32]{1,2,0:T(8,128)} %get-tuple-element.83), channel_id=1, source_target_pairs={{0,16},{16,32},{32,48},{48,64},{64,80},{80,96},{96,112},{112,128},... | collective-permute-start | bytes 49160 | tf_op jit(solution)/shard_map/ppermute | solution.py:18
  148.0 2.3 %collective-permute-done.17 = f32[2,64,32]{1,2,0:T(8,128)} collective-permute-done((f32[2,64,32]{1,2,0:T(8,128)}, f32[2,64,32]{1,2,0:T(8,128)}, u32[]{:S(2)}, u32[]{:S(2)}) %collective-permute-start.17) | collective-permute-done | bytes 16416 | tf_op jit(solution)/shard_map/ppermute | solution.py:18
  151.3 1.5 fusion.67
  (261 shorter events, 41.4 us)
Async XLA Ops:
  0.9 4.3 %collective-permute-start = (f32[3,4,16,128]{3,2,1,0:T(8,128)S(1)}, f32[3,4,16,128]{3,2,1,0:T(8,128)S(1)}, u32[]{:S(2)}, u32[]{:S(2)}) collective-permute-start(f32[3,4,16,128]{3,2,1,0:T(8,128)S(1)} %get-tuple-element.27), channel_id=1, source_target_pairs={{0,16},{16,32},{32,48},{48,64},{64,80},{80,96},{96,112},{112,128},... | collective-permute-start | bytes 294920 | tf_op jit(solution)/shard_map/ppermute | solution.py:18
  3.2 4.0 %collective-permute-start.1 = (f32[3,4,16,128]{3,2,1,0:T(8,128)S(1)}, f32[3,4,16,128]{3,2,1,0:T(8,128)S(1)}, u32[]{:S(2)}, u32[]{:S(2)}) collective-permute-start(f32[3,4,16,128]{3,2,1,0:T(8,128)S(1)} %get-tuple-element.28), channel_id=1, source_target_pairs={{0,496},{16,0},{32,16},{48,32},{64,48},{80,64},{96,80},{112,96},{1... | collective-permute-start | bytes 294920 | tf_op jit(solution)/shard_map/ppermute | solution.py:18
  3.2 20.0 %copy-start.59 = (s32[128]{0:T(128)}, s32[128]{0:T(128)S(1)}, u32[]{:S(2)}) copy-start(s32[128]{0:T(128)S(1)} %get-tuple-element.88) | copy-start | bytes 1540
  3.2 20.0 %copy-start.61 = (s32[128]{0:T(128)}, s32[128]{0:T(128)S(1)}, u32[]{:S(2)}) copy-start(s32[128]{0:T(128)S(1)} %get-tuple-element.89) | copy-start | bytes 1540
  3.2 20.0 %copy-start.63 = (pred[128]{0:T(512)(128)(4,1)}, pred[128]{0:T(512)(128)(4,1)S(1)}, u32[]{:S(2)}) copy-start(pred[128]{0:T(512)(128)(4,1)S(1)} %compare_and_fusion.3) | copy-start | bytes 388
  3.3 39.8 %copy-start.50 = (s32[64]{0:T(128)}, s32[64]{0:T(128)S(1)}, u32[]{:S(2)}) copy-start(s32[64]{0:T(128)S(1)} %get-tuple-element.92) | copy-start | bytes 772
  3.3 39.8 %copy-start.51 = (s32[64]{0:T(128)}, s32[64]{0:T(128)S(1)}, u32[]{:S(2)}) copy-start(s32[64]{0:T(128)S(1)} %get-tuple-element.93) | copy-start | bytes 772
  3.3 39.8 %copy-start.52 = (pred[64]{0:T(512)(128)(4,1)}, pred[64]{0:T(512)(128)(4,1)S(1)}, u32[]{:S(2)}) copy-start(pred[64]{0:T(512)(128)(4,1)S(1)} %compare_and_fusion.1) | copy-start | bytes 196
  7.3 8.8 %collective-permute-start.2 = (f32[3,40,4,128]{3,2,1,0:T(4,128)S(1)}, f32[3,40,4,128]{3,2,1,0:T(4,128)S(1)}, u32[]{:S(2)}, u32[]{:S(2)}) collective-permute-start(f32[3,40,4,128]{3,2,1,0:T(4,128)S(1)} %get-tuple-element.25), channel_id=1, source_target_pairs={{0,1},{1,2},{2,3},{3,4},{4,5},{5,6},{6,7},{7,8},{8,9},{9,10},{10,1... | collective-permute-start | bytes 737288 | tf_op jit(solution)/shard_map/ppermute | solution.py:18
  10.4 8.8 %collective-permute-start.3 = (f32[3,40,4,128]{3,2,1,0:T(4,128)S(1)}, f32[3,40,4,128]{3,2,1,0:T(4,128)S(1)}, u32[]{:S(2)}, u32[]{:S(2)}) collective-permute-start(f32[3,40,4,128]{3,2,1,0:T(4,128)S(1)} %get-tuple-element.26), channel_id=1, source_target_pairs={{0,15},{1,0},{2,1},{3,2},{4,3},{5,4},{6,5},{7,6},{8,7},{9,8},{10,9... | collective-permute-start | bytes 737288 | tf_op jit(solution)/shard_map/ppermute | solution.py:18
  12.6 67.5 %copy-start.53 = (s32[32]{0:T(128)}, s32[32]{0:T(128)S(1)}, u32[]{:S(2)}) copy-start(s32[32]{0:T(128)S(1)} %get-tuple-element.96) | copy-start | bytes 388
  12.6 67.5 %copy-start.55 = (s32[32]{0:T(128)}, s32[32]{0:T(128)S(1)}, u32[]{:S(2)}) copy-start(s32[32]{0:T(128)S(1)} %get-tuple-element.97) | copy-start | bytes 388
  23.7 2.6 %collective-permute-start.4 = (f32[2,5,8,64]{3,2,1,0:T(8,128)S(1)}, f32[2,5,8,64]{3,2,1,0:T(8,128)S(1)}, u32[]{:S(2)}, u32[]{:S(2)}) collective-permute-start(f32[2,5,8,64]{3,2,1,0:T(8,128)S(1)} %get-tuple-element.85), channel_id=1, source_target_pairs={{0,16},{16,32},{32,48},{48,64},{64,80},{80,96},{96,112},{112,128},... | collective-permute-start | bytes 61448 | tf_op jit(solution)/shard_map/ppermute | solution.py:18
  25.2 3.4 %collective-permute-start.5 = (f32[2,5,8,64]{3,2,1,0:T(8,128)S(1)}, f32[2,5,8,64]{3,2,1,0:T(8,128)S(1)}, u32[]{:S(2)}, u32[]{:S(2)}) collective-permute-start(f32[2,5,8,64]{3,2,1,0:T(8,128)S(1)} %get-tuple-element.86), channel_id=1, source_target_pairs={{0,496},{16,0},{32,16},{48,32},{64,48},{80,64},{96,80},{112,96},{1... | collective-permute-start | bytes 61448 | tf_op jit(solution)/shard_map/ppermute | solution.py:18
  28.7 7.8 %collective-permute-start.6 = (f32[2,26,5,64]{3,2,1,0:T(8,128)S(1)}, f32[2,26,5,64]{3,2,1,0:T(8,128)S(1)}, u32[]{:S(2)}, u32[]{:S(2)}) collective-permute-start(f32[2,26,5,64]{3,2,1,0:T(8,128)S(1)} %get-tuple-element.59), channel_id=1, source_target_pairs={{0,1},{1,2},{2,3},{3,4},{4,5},{5,6},{6,7},{7,8},{8,9},{9,10},{10,1... | collective-permute-start | bytes 199688 | tf_op jit(solution)/shard_map/ppermute | solution.py:18
  31.5 9.7 %collective-permute-start.7 = (f32[2,26,5,64]{3,2,1,0:T(8,128)S(1)}, f32[2,26,5,64]{3,2,1,0:T(8,128)S(1)}, u32[]{:S(2)}, u32[]{:S(2)}) collective-permute-start(f32[2,26,5,64]{3,2,1,0:T(8,128)S(1)} %get-tuple-element.60), channel_id=1, source_target_pairs={{0,15},{1,0},{2,1},{3,2},{4,3},{5,4},{6,5},{7,6},{8,7},{9,8},{10,9... | collective-permute-start | bytes 199688 | tf_op jit(solution)/shard_map/ppermute | solution.py:18
  34.0 46.1 %copy-start.57 = (pred[32]{0:T(512)(128)(4,1)}, pred[32]{0:T(512)(128)(4,1)S(1)}, u32[]{:S(2)}) copy-start(pred[32]{0:T(512)(128)(4,1)S(1)} %compare_and_fusion) | copy-start | bytes 100
  42.5 22.4 %copy-start.18 = (f32[22,14,64]{2,1,0:T(8,128)}, f32[22,14,64]{2,1,0:T(8,128)S(1)}, u32[]{:S(2)}) copy-start(f32[22,14,64]{2,1,0:T(8,128)S(1)} %fusion.86) | copy-start | bytes 236548
  67.7 18.2 %copy-start.15 = (f32[2,8,64,32]{2,3,1,0:T(8,128)}, f32[2,8,64,32]{2,3,1,0:T(8,128)S(1)}, u32[]{:S(2)}) copy-start(f32[2,8,64,32]{2,3,1,0:T(8,128)S(1)} %copy.74) | copy-start | bytes 393220
  73.7 9.3 %collective-permute-start.8 = (f32[2,4,64,32]{2,3,1,0:T(8,128)}, f32[2,4,64,32]{2,3,1,0:T(8,128)}, u32[]{:S(2)}, u32[]{:S(2)}) collective-permute-start(f32[2,4,64,32]{2,3,1,0:T(8,128)} %get-tuple-element.51), channel_id=1, source_target_pairs={{0,16},{16,32},{32,48},{48,64},{64,80},{80,96},{96,112},{112,128},... | collective-permute-start | bytes 196616 | tf_op jit(solution)/shard_map/ppermute | solution.py:18
  80.1 4.7 %collective-permute-start.9 = (f32[2,4,64,32]{2,3,1,0:T(8,128)}, f32[2,4,64,32]{2,3,1,0:T(8,128)}, u32[]{:S(2)}, u32[]{:S(2)}) collective-permute-start(f32[2,4,64,32]{2,3,1,0:T(8,128)} %get-tuple-element.52), channel_id=1, source_target_pairs={{0,496},{16,0},{32,16},{48,32},{64,48},{80,64},{96,80},{112,96},{1... | collective-permute-start | bytes 196616 | tf_op jit(solution)/shard_map/ppermute | solution.py:18
  86.0 51.4 %copy-start.46 = (f32[14,64,1]{1,2,0:T(1,128)}, f32[14,64,1]{1,2,0:T(1,128)S(1)}, u32[]{:S(2)}) copy-start(f32[14,64,1]{1,2,0:T(1,128)S(1)} %get-tuple-element.57) | copy-start | bytes 10756
  86.0 51.4 %copy-start.47 = (f32[14,64,1]{1,2,0:T(1,128)}, f32[14,64,1]{1,2,0:T(1,128)S(1)}, u32[]{:S(2)}) copy-start(f32[14,64,1]{1,2,0:T(1,128)S(1)} %get-tuple-element.58) | copy-start | bytes 10756
  90.2 10.2 %collective-permute-start.10 = (f32[2,4,512]{2,1,0:T(4,128)S(1)}, f32[2,4,512]{2,1,0:T(4,128)S(1)}, u32[]{:S(2)}, u32[]{:S(2)}) collective-permute-start(f32[2,4,512]{2,1,0:T(4,128)S(1)} %constant_dynamic-update-slice_fusion), channel_id=1, source_target_pairs={{0,32},{16,48},{32,64},{48,80},{64,96},{80,112},{96,128},{112,144}... | collective-permute-start | bytes 49160 | tf_op jit(solution)/shard_map/ppermute | solution.py:18
  94.8 5.7 %collective-permute-start.11 = (f32[2,4,512]{2,1,0:T(4,128)S(1)}, f32[2,4,512]{2,1,0:T(4,128)S(1)}, u32[]{:S(2)}, u32[]{:S(2)}) collective-permute-start(f32[2,4,512]{2,1,0:T(4,128)S(1)} %constant_dynamic-update-slice_fusion), channel_id=1, source_target_pairs={{0,16},{16,32},{32,48},{48,64},{64,80},{80,96},{96,112},{112,128},... | collective-permute-start | bytes 49160 | tf_op jit(solution)/shard_map/ppermute | solution.py:18
  95.7 5.9 %collective-permute-start.12 = (f32[2,4,512]{2,1,0:T(4,128)S(1)}, f32[2,4,512]{2,1,0:T(4,128)S(1)}, u32[]{:S(2)}, u32[]{:S(2)}) collective-permute-start(f32[2,4,512]{2,1,0:T(4,128)S(1)} %constant_dynamic-update-slice_fusion), channel_id=1, source_target_pairs={{0,496},{16,0},{32,16},{48,32},{64,48},{80,64},{96,80},{112,96},{1... | collective-permute-start | bytes 49160 | tf_op jit(solution)/shard_map/ppermute | solution.py:18
  95.7 7.6 %collective-permute-start.13 = (f32[2,4,512]{2,1,0:T(4,128)S(1)}, f32[2,4,512]{2,1,0:T(4,128)S(1)}, u32[]{:S(2)}, u32[]{:S(2)}) collective-permute-start(f32[2,4,512]{2,1,0:T(4,128)S(1)} %constant_dynamic-update-slice_fusion), channel_id=1, source_target_pairs={{0,480},{16,496},{32,0},{48,16},{64,32},{80,48},{96,64},{112,80},{... | collective-permute-start | bytes 49160 | tf_op jit(solution)/shard_map/ppermute | solution.py:18
  105.2 13.9 %collective-permute-start.14 = (f32[2,20,512]{2,1,0:T(8,128)}, f32[2,20,512]{2,1,0:T(8,128)}, u32[]{:S(2)}, u32[]{:S(2)}) collective-permute-start(f32[2,20,512]{2,1,0:T(8,128)} %concatenate.191), channel_id=1, source_target_pairs={{0,80},{16,96},{32,112},{48,128},{64,144},{80,160},{96,176},{112,1... | collective-permute-start | bytes 245768 | tf_op jit(solution)/shard_map/ppermute | solution.py:18
  111.6 9.5 %collective-permute-start.15 = (f32[2,20,512]{2,1,0:T(8,128)}, f32[2,20,512]{2,1,0:T(8,128)}, u32[]{:S(2)}, u32[]{:S(2)}) collective-permute-start(f32[2,20,512]{2,1,0:T(8,128)} %concatenate.191), channel_id=1, source_target_pairs={{0,432},{16,448},{32,464},{48,480},{64,496},{80,0},{96,16},{112,32... | collective-permute-start | bytes 245768 | tf_op jit(solution)/shard_map/ppermute | solution.py:18
  139.8 13.6 %copy-start.19 = (f32[22,14,64]{2,1,0:T(8,128)S(1)}, f32[22,14,64]{2,1,0:T(8,128)}, u32[]{:S(2)}) copy-start(f32[22,14,64]{2,1,0:T(8,128)} %copy-done.18) | copy-start | bytes 236548
  140.4 7.6 %collective-permute-start.16 = (f32[2,64,32]{1,2,0:T(8,128)}, f32[2,64,32]{1,2,0:T(8,128)}, u32[]{:S(2)}, u32[]{:S(2)}) collective-permute-start(f32[2,64,32]{1,2,0:T(8,128)} %get-tuple-element.83), channel_id=1, source_target_pairs={{0,16},{16,32},{32,48},{48,64},{64,80},{80,96},{96,112},{112,128},... | collective-permute-start | bytes 49160 | tf_op jit(solution)/shard_map/ppermute | solution.py:18
  146.7 3.7 %collective-permute-start.17 = (f32[2,64,32]{1,2,0:T(8,128)}, f32[2,64,32]{1,2,0:T(8,128)}, u32[]{:S(2)}, u32[]{:S(2)}) collective-permute-start(f32[2,64,32]{1,2,0:T(8,128)} %get-tuple-element.84), channel_id=1, source_target_pairs={{0,496},{16,0},{32,16},{48,32},{64,48},{80,64},{96,80},{112,96},{1... | collective-permute-start | bytes 49160 | tf_op jit(solution)/shard_map/ppermute | solution.py:18
  (57 other events, 125.4 us)

commit v3 on v2

--- a/solution.py
+++ b/solution.py
@@ -158,9 +158,14 @@
     return jnp.concatenate(lower + [x] + upper, axis=axis)
 
 
-def coarse_kernel(scale, size_z, k_ref, b_ref, out_ref):
-    k = k_ref[...]
-    b = b_ref[...]
+def coarse_kernel(scale, size_z, spans, keep, lower_ref, own_ref, upper_ref, out_ref, tile_ref):
+    span, extra = spans
+    for f in range(2):
+        tile_ref[f, 0:extra] = lower_ref[f, span - extra : span]
+        tile_ref[f, extra : extra + span] = own_ref[f]
+        tile_ref[f, extra + span : 2 * extra + span] = upper_ref[f, 0:extra]
+    b = tile_ref[0]
+    k = tile_ref[1]
     rows, lanes = k.shape
     lane = lax.broadcasted_iota(jnp.int32, (rows, lanes), 1) % size_z
     first, last = lane == 0, lane == size_z - 1
@@ -200,7 +205,8 @@
         return v + OMEGA * (b - (diagonal * v - beside_all)) / diagonal
 
     v = OMEGA * b / diagonal
-    out_ref[...] = lax.fori_loop(1, CSWEEPS, one_sweep, v)
+    v = lax.fori_loop(1, CSWEEPS, one_sweep, v)
+    out_ref[...] = v[(rows - keep) // 2 : (rows + keep) // 2]
 
 
 def coarse_solve(right_side, perm, scale):
@@ -208,24 +214,24 @@
     lanes = size_y * size_z
     pair = jnp.stack([right_side, perm]).reshape(2, size_x, lanes)
     near = rows_around(pair, (1, 2), 1)
-    wide = rows_around(near, (5,), 1)
-    keep = CSWEEPS + 2
-    keep += (-(size_x + 2 * keep)) % 8 // 2
-    cut = 7 * size_x - keep
-    assert cut >= 0
-    wide = wide[:, cut : wide.shape[1] - cut]
-    rows = wide.shape[1]
+    span = near.shape[1]
+    extra = CSWEEPS + 2 - (span - size_x) // 2
+    extra += (-(span + 2 * extra)) % 8 // 2
+    assert 0 < extra <= span
+    rows = span + 2 * extra
+    keep = 8
+    assert (rows - keep) // 2 >= CSWEEPS
+    lower, upper = shift_from(near, "row", 5), shift_from(near, "row", -5)
     call = pl.pallas_call(
-        lambda k_ref, b_ref, out_ref: coarse_kernel(scale, size_z, k_ref, b_ref, out_ref),
-        out_shape=jax.ShapeDtypeStruct((rows, lanes), jnp.float32),
+        lambda *refs: coarse_kernel(scale, size_z, (span, extra), keep, *refs),
+        out_shape=jax.ShapeDtypeStruct((keep, lanes), jnp.float32),
+        scratch_shapes=[pltpu.VMEM((2, rows, lanes), jnp.float32)],
         cost_estimate=pl.CostEstimate(
-            flops=40 * CSWEEPS * rows * lanes, transcendentals=0, bytes_accessed=12 * rows * lanes
+            flops=40 * CSWEEPS * rows * lanes, transcendentals=0, bytes_accessed=24 * rows * lanes
         ),
     )
-    v = call(wide[1], wide[0])
-    drop = keep - 1
-    v = v[drop : rows - drop]
-    return v.reshape(v.shape[0], size_y, size_z)
+    v = call(lower, near, upper)
+    return v.reshape(keep, size_y, size_z)
 
 
 def on_device(pressure_in, source, permeability):
@@ -251,7 +257,7 @@
     rhs = coarsen(lev2.residual(s2[1:-1]))
     perm = coarsen(band[0])
     correction = coarse_solve(rhs, perm, scales[3])
-    q = s2 + prolong(correction)
+    q = s2 + prolong(correction)[2:-2]
     q = lev2.sweep(q, 1)
     u2 = lev2.sweep(q, 0)
     u2 = wrap_y(x_halo(u2, 2), 2)

time: 160 us -> 153 us (0.956)
  local copies, waits for them, and re-layouts: 28 us -> 21.6 us
  waiting for transfers between devices: 29.9 us -> 28.1 us
    concatenate x2 -> x1, local copies, waits for them, and re-layouts: 7.6 us -> 2.24 us  [rows_around(): return jnp.concatenate(lower + [x] + upper, axis=axis)]
    ppermute x18, waiting for transfers between devices: 29.9 us -> 28.1 us  [shift_from(): return lax.ppermute(x, axis, [(i, (i + k) % n) for i in range(n)])]
    squeeze x1 -> x0, local copies, waits for them, and re-layouts: 1.62 us -> none  [coarse_solve(): v = call(wide[1], wide[0])]
    unnamed x145 -> x157, local copies, waits for them, and re-layouts: 6.56 us -> 7.87 us
    dot_general x9 -> x8, matrix products: 3.86 us -> 2.91 us  [along_y(): jnp.einsum('xjy,xyz->xjz', batched, field, precision=lax.Precision.HIGHEST)]
where the time goes in v3:
time: 153 us; the launch traced here: 152 us
  starting transfers between devices  47.5 us (31%)
  waiting for transfers between devices  28.1 us (18%)
  local copies, waits for them, and re-layouts  21.6 us (14%)
  blocking collectives  21.4 us (14%)
  other arithmetic  16.9 us (11%)
  matrix products  10.2 us (7%)
  Pallas kernels  4.56 us (3%)
    ppermute x18, starting transfers between devices, shift_from(): return lax.ppermute(x, axis, [(i, (i + k) % n) for i in range(n)])  47.5 us
    ppermute x18, waiting for transfers between devices, shift_from(): return lax.ppermute(x, axis, [(i, (i + k) % n) for i in range(n)])  28.1 us
    all_gather x1, blocking collectives, on_device(): band = lax.all_gather(jnp.stack([perm, rhs]), 'col', axis=2, tiled=True)  21.4 us
    unnamed x157, local copies, waits for them, and re-layouts  7.87 us
    dot_general x9, matrix products, along_z(): out = jnp.dot(flat, matrix, precision=lax.Precision.HIGHEST)  6.36 us
    pallas_call x1, Pallas kernels, coarse_solve(): v = call(lower, near, upper)  4.56 us
    add x6, other arithmetic, sweep(): return v[1:-1, 1:-1] + OMEGA * residual / faces[6]  4.51 us
  transfers between devices with their start and end apart: 18, of which 14 were waited for; matrix products, arithmetic and copies ran while one was open for 5% of the time, Pallas kernels for 0%

profile of v3, /device:TPU:35, one launch (start us, length us, event | category | flops | bytes accessed | tf_op | source)
XLA Modules:
  0.0 151.7 jit_solution(27854183678038707)
XLA Ops:
  0.9 2.2 %collective-permute-start = (f32[3,4,16,128]{3,2,1,0:T(8,128)S(1)}, f32[3,4,16,128]{3,2,1,0:T(8,128)S(1)}, u32[]{:S(2)}, u32[]{:S(2)}) collective-permute-start(f32[3,4,16,128]{3,2,1,0:T(8,128)S(1)} %get-tuple-element.27), channel_id=1, source_target_pairs={{0,16},{16,32},{32,48},{48,64},{64,80},{80,96},{96,112},{112,128},... | collective-permute-start | bytes 294920 | tf_op jit(solution)/shard_map/ppermute | solution.py:18
  5.2 2.0 %collective-permute-done.1 = f32[3,4,16,128]{3,2,1,0:T(8,128)S(1)} collective-permute-done((f32[3,4,16,128]{3,2,1,0:T(8,128)S(1)}, f32[3,4,16,128]{3,2,1,0:T(8,128)S(1)}, u32[]{:S(2)}, u32[]{:S(2)}) %collective-permute-start.1) | collective-permute-done | bytes 98336 | tf_op jit(solution)/shard_map/ppermute | solution.py:18
  7.3 3.1 %collective-permute-start.2 = (f32[3,40,4,128]{3,2,1,0:T(4,128)S(1)}, f32[3,40,4,128]{3,2,1,0:T(4,128)S(1)}, u32[]{:S(2)}, u32[]{:S(2)}) collective-permute-start(f32[3,40,4,128]{3,2,1,0:T(4,128)S(1)} %get-tuple-element.25), channel_id=1, source_target_pairs={{0,1},{1,2},{2,3},{3,4},{4,5},{5,6},{6,7},{7,8},{8,9},{9,10},{10,1... | collective-permute-start | bytes 737288 | tf_op jit(solution)/shard_map/ppermute | solution.py:18
  10.4 2.2 %collective-permute-start.3 = (f32[3,40,4,128]{3,2,1,0:T(4,128)S(1)}, f32[3,40,4,128]{3,2,1,0:T(4,128)S(1)}, u32[]{:S(2)}, u32[]{:S(2)}) collective-permute-start(f32[3,40,4,128]{3,2,1,0:T(4,128)S(1)} %get-tuple-element.26), channel_id=1, source_target_pairs={{0,15},{1,0},{2,1},{3,2},{4,3},{5,4},{6,5},{7,6},{8,7},{9,8},{10,9... | collective-permute-start | bytes 737288 | tf_op jit(solution)/shard_map/ppermute | solution.py:18
  13.2 2.9 %collective-permute-done.2 = f32[3,40,4,128]{3,2,1,0:T(4,128)S(1)} collective-permute-done((f32[3,40,4,128]{3,2,1,0:T(4,128)S(1)}, f32[3,40,4,128]{3,2,1,0:T(4,128)S(1)}, u32[]{:S(2)}, u32[]{:S(2)}) %collective-permute-start.2) | collective-permute-done | bytes 245792 | tf_op jit(solution)/shard_map/ppermute | solution.py:18
  16.1 3.1 %collective-permute-done.3 = f32[3,40,4,128]{3,2,1,0:T(4,128)S(1)} collective-permute-done((f32[3,40,4,128]{3,2,1,0:T(4,128)S(1)}, f32[3,40,4,128]{3,2,1,0:T(4,128)S(1)}, u32[]{:S(2)}, u32[]{:S(2)}) %collective-permute-start.3) | collective-permute-done | bytes 245792 | tf_op jit(solution)/shard_map/ppermute | solution.py:18
  23.7 1.5 collective-permute-start.4
  26.3 2.3 %collective-permute-done.5 = f32[2,5,8,64]{3,2,1,0:T(8,128)S(1)} collective-permute-done((f32[2,5,8,64]{3,2,1,0:T(8,128)S(1)}, f32[2,5,8,64]{3,2,1,0:T(8,128)S(1)}, u32[]{:S(2)}, u32[]{:S(2)}) %collective-permute-start.5) | collective-permute-done | bytes 20512 | tf_op jit(solution)/shard_map/ppermute | solution.py:18
  28.7 2.8 %collective-permute-start.6 = (f32[2,26,5,64]{3,2,1,0:T(8,128)S(1)}, f32[2,26,5,64]{3,2,1,0:T(8,128)S(1)}, u32[]{:S(2)}, u32[]{:S(2)}) collective-permute-start(f32[2,26,5,64]{3,2,1,0:T(8,128)S(1)} %get-tuple-element.57), channel_id=1, source_target_pairs={{0,1},{1,2},{2,3},{3,4},{4,5},{5,6},{6,7},{7,8},{8,9},{9,10},{10,1... | collective-permute-start | bytes 199688 | tf_op jit(solution)/shard_map/ppermute | solution.py:18
  31.5 2.5 %collective-permute-start.7 = (f32[2,26,5,64]{3,2,1,0:T(8,128)S(1)}, f32[2,26,5,64]{3,2,1,0:T(8,128)S(1)}, u32[]{:S(2)}, u32[]{:S(2)}) collective-permute-start(f32[2,26,5,64]{3,2,1,0:T(8,128)S(1)} %get-tuple-element.58), channel_id=1, source_target_pairs={{0,15},{1,0},{2,1},{3,2},{4,3},{5,4},{6,5},{7,6},{8,7},{9,8},{10,9... | collective-permute-start | bytes 199688 | tf_op jit(solution)/shard_map/ppermute | solution.py:18
  34.0 2.5 %collective-permute-done.6 = f32[2,26,5,64]{3,2,1,0:T(8,128)S(1)} collective-permute-done((f32[2,26,5,64]{3,2,1,0:T(8,128)S(1)}, f32[2,26,5,64]{3,2,1,0:T(8,128)S(1)}, u32[]{:S(2)}, u32[]{:S(2)}) %collective-permute-start.6) | collective-permute-done | bytes 66592 | tf_op jit(solution)/shard_map/ppermute | solution.py:18
  36.5 4.7 %collective-permute-done.7 = f32[2,26,5,64]{3,2,1,0:T(8,128)S(1)} collective-permute-done((f32[2,26,5,64]{3,2,1,0:T(8,128)S(1)}, f32[2,26,5,64]{3,2,1,0:T(8,128)S(1)}, u32[]{:S(2)}, u32[]{:S(2)}) %collective-permute-start.7) | collective-permute-done | bytes 66592 | tf_op jit(solution)/shard_map/ppermute | solution.py:18
  43.5 21.4 %all_gather.3 = f32[2,8,64,32]{3,1,0,2:T(8,128)S(1)} all-gather(f32[2,8,4,32]{3,1,0,2:T(8,128)S(1)} %copy.73), channel_id=1, replica_groups=mesh['row'=32,'col'=16] {'col'}, dimensions={2}, use_global_device_ids=true | all-gather | bytes 139264 | tf_op jit(solution)/shard_map/all_gather | solution.py:252
  66.4 1.3 copy.74
  67.7 2.0 %fusion.234 = (f32[4,1,64,32]{3,1,0,2:T(1,128)}, f32[4,1,64,32]{3,1,0,2:T(1,128)}) fusion(f32[4,2,64,32]{3,1,0,2:T(2,128)} %bitcast.192), kind=kLoop, calls=%fused_computation.424 | loop fusion | bytes 131072 | tf_op jit(solution)/shard_map/slice | solution.py:114
  69.7 1.6 %copy.100 = f32[4,1,64,32]{2,3,0,1:T(8,128)} copy(f32[4,1,64,32]{3,1,0,2:T(1,128)} %get-tuple-element.45) | data formatting | bytes 65536
  71.3 1.6 %copy.99 = f32[4,1,64,32]{2,3,0,1:T(8,128)} copy(f32[4,1,64,32]{3,1,0,2:T(1,128)} %get-tuple-element.46) | data formatting | bytes 65536
  73.7 6.4 %collective-permute-start.8 = (f32[2,4,64,32]{2,3,1,0:T(8,128)}, f32[2,4,64,32]{2,3,1,0:T(8,128)}, u32[]{:S(2)}, u32[]{:S(2)}) collective-permute-start(f32[2,4,64,32]{2,3,1,0:T(8,128)} %get-tuple-element.49), channel_id=1, source_target_pairs={{0,16},{16,32},{32,48},{48,64},{64,80},{80,96},{96,112},{112,128},... | collective-permute-start | bytes 196616 | tf_op jit(solution)/shard_map/ppermute | solution.py:18
  83.0 1.8 %collective-permute-done.9 = f32[2,4,64,32]{2,3,1,0:T(8,128)} collective-permute-done((f32[2,4,64,32]{2,3,1,0:T(8,128)}, f32[2,4,64,32]{2,3,1,0:T(8,128)}, u32[]{:S(2)}, u32[]{:S(2)}) %collective-permute-start.9) | collective-permute-done | bytes 65568 | tf_op jit(solution)/shard_map/ppermute | solution.py:18
  90.2 4.5 %collective-permute-start.10 = (f32[2,4,512]{2,1,0:T(4,128)S(1)}, f32[2,4,512]{2,1,0:T(4,128)S(1)}, u32[]{:S(2)}, u32[]{:S(2)}) collective-permute-start(f32[2,4,512]{2,1,0:T(4,128)S(1)} %constant_dynamic-update-slice_fusion), channel_id=1, source_target_pairs={{0,32},{16,48},{32,64},{48,80},{64,96},{80,112},{96,128},{112,144}... | collective-permute-start | bytes 49160 | tf_op jit(solution)/shard_map/ppermute | solution.py:18
  95.7 4.7 %collective-permute-start.13 = (f32[2,4,512]{2,1,0:T(4,128)S(1)}, f32[2,4,512]{2,1,0:T(4,128)}, u32[]{:S(2)}, u32[]{:S(2)}) collective-permute-start(f32[2,4,512]{2,1,0:T(4,128)S(1)} %constant_dynamic-update-slice_fusion), channel_id=1, source_target_pairs={{0,480},{16,496},{32,0},{48,16},{64,32},{80,48},{96,64},{112,80},{... | collective-permute-start | bytes 49160 | tf_op jit(solution)/shard_map/ppermute | solution.py:18
  103.4 2.2 %concatenate.187.refs_1_ = f32[2,20,512]{2,1,0:T(8,128)S(1)} concatenate(f32[2,4,512]{2,1,0:T(4,128)} %copy-done.53, f32[2,4,512]{2,1,0:T(4,128)} %copy-done.54, f32[2,4,512]{2,1,0:T(4,128)} %copy-done.50, f32[2,4,512]{2,1,0:T(4,128)} %copy-done.55, f32[2,4,512]{2,1,0:T(4,128)} %collective-permute-done.13), dimensions={1} | concatenate | bytes 163840 | tf_op jit(solution)/shard_map/concatenate | solution.py:158
  105.6 6.4 %collective-permute-start.14 = (f32[2,20,512]{2,1,0:T(8,128)S(1)}, f32[2,20,512]{2,1,0:T(8,128)S(1)}, u32[]{:S(2)}, u32[]{:S(2)}) collective-permute-start(f32[2,20,512]{2,1,0:T(8,128)S(1)} %concatenate.187.refs_1_), channel_id=1, source_target_pairs={{0,80},{16,96},{32,112},{48,128},{64,144},{80,160},{96,176},{112,1... | collective-permute-start | bytes 245768 | tf_op jit(solution)/shard_map/ppermute | solution.py:18
  112.0 3.9 %collective-permute-start.15 = (f32[2,20,512]{2,1,0:T(8,128)S(1)}, f32[2,20,512]{2,1,0:T(8,128)}, u32[]{:S(2)}, u32[]{:S(2)}) collective-permute-start(f32[2,20,512]{2,1,0:T(8,128)S(1)} %concatenate.187.refs_1_), channel_id=1, source_target_pairs={{0,432},{16,448},{32,464},{48,480},{64,496},{80,0},{96,16},{112,32... | collective-permute-start | bytes 245768 | tf_op jit(solution)/shard_map/ppermute | solution.py:18
  117.2 2.2 %collective-permute-done.14.refs_0_ = f32[2,20,512]{2,1,0:T(8,128)S(1)} collective-permute-done((f32[2,20,512]{2,1,0:T(8,128)S(1)}, f32[2,20,512]{2,1,0:T(8,128)S(1)}, u32[]{:S(2)}, u32[]{:S(2)}) %collective-permute-start.14) | collective-permute-done | bytes 81952 | tf_op jit(solution)/shard_map/ppermute | solution.py:18
  121.3 4.6 %shard_map.37 = f32[8,512]{1,0:T(8,128)} custom-call(f32[2,20,512]{2,1,0:T(8,128)} %copy-done.49, f32[2,20,512]{2,1,0:T(8,128)} %copy-done.46, f32[2,20,512]{2,1,0:T(8,128)} %collective-permute-done.15.refs_2_), custom_call_target="tpu_custom_call" | custom-call | flops 13107200 | bytes 491520 | tf_op jit(solution)/shard_map/pallas_call | solution.py:233
  125.9 1.5 dot_general.68
  127.4 1.5 fusion.223
  133.0 6.3 %collective-permute-start.16 = (f32[2,64,32]{1,2,0:T(8,128)}, f32[2,64,32]{1,2,0:T(8,128)}, u32[]{:S(2)}, u32[]{:S(2)}) collective-permute-start(f32[2,64,32]{1,2,0:T(8,128)} %get-tuple-element.81), channel_id=1, source_target_pairs={{0,16},{16,32},{32,48},{48,64},{64,80},{80,96},{96,112},{112,128},... | collective-permute-start | bytes 49160 | tf_op jit(solution)/shard_map/ppermute | solution.py:18
  140.6 2.3 %collective-permute-done.17 = f32[2,64,32]{1,2,0:T(8,128)} collective-permute-done((f32[2,64,32]{1,2,0:T(8,128)}, f32[2,64,32]{1,2,0:T(8,128)}, u32[]{:S(2)}, u32[]{:S(2)}) %collective-permute-start.17) | collective-permute-done | bytes 16416 | tf_op jit(solution)/shard_map/ppermute | solution.py:18
  144.0 1.5 %fusion.67 = f32[12,8,64]{2,1,0:T(8,128)S(1)} fusion(s32[]{:T(128)S(6)} %select_n.80, f32[12,2,32]{1,2,0:T(8,128)S(1)} %get-tuple-element.60, f32[2,64,32]{1,2,0:T(8,128)} %collective-permute-done.17, f32[8,64,32]{1,2,0:T(8,128)S(1)} %fusion.143, f32[2,64,32]{1,2,0:T(8,128)} %collective-permute-done.16, f32[12,2,32]{1,2,0:T(8,128)S(1)} %get-tuple-element.59, ...), kind=kOutput, calls=%fused_computation.148 | convolution fusion | flops 2375680 | bytes 129604 | tf_op jit(solution)/shard_map/dot_general | solution.py:101
  150.4 1.3 fusion.42
  (270 shorter events, 39.3 us)
Async XLA Ops:
  0.9 4.3 %collective-permute-start = (f32[3,4,16,128]{3,2,1,0:T(8,128)S(1)}, f32[3,4,16,128]{3,2,1,0:T(8,128)S(1)}, u32[]{:S(2)}, u32[]{:S(2)}) collective-permute-start(f32[3,4,16,128]{3,2,1,0:T(8,128)S(1)} %get-tuple-element.27), channel_id=1, source_target_pairs={{0,16},{16,32},{32,48},{48,64},{64,80},{80,96},{96,112},{112,128},... | collective-permute-start | bytes 294920 | tf_op jit(solution)/shard_map/ppermute | solution.py:18
  3.2 4.0 %collective-permute-start.1 = (f32[3,4,16,128]{3,2,1,0:T(8,128)S(1)}, f32[3,4,16,128]{3,2,1,0:T(8,128)S(1)}, u32[]{:S(2)}, u32[]{:S(2)}) collective-permute-start(f32[3,4,16,128]{3,2,1,0:T(8,128)S(1)} %get-tuple-element.28), channel_id=1, source_target_pairs={{0,496},{16,0},{32,16},{48,32},{64,48},{80,64},{96,80},{112,96},{1... | collective-permute-start | bytes 294920 | tf_op jit(solution)/shard_map/ppermute | solution.py:18
  3.2 20.0 %copy-start.65 = (s32[128]{0:T(128)}, s32[128]{0:T(128)S(1)}, u32[]{:S(2)}) copy-start(s32[128]{0:T(128)S(1)} %get-tuple-element.86) | copy-start | bytes 1540
  3.2 20.0 %copy-start.67 = (s32[128]{0:T(128)}, s32[128]{0:T(128)S(1)}, u32[]{:S(2)}) copy-start(s32[128]{0:T(128)S(1)} %get-tuple-element.87) | copy-start | bytes 1540
  3.2 20.0 %copy-start.69 = (pred[128]{0:T(512)(128)(4,1)}, pred[128]{0:T(512)(128)(4,1)S(1)}, u32[]{:S(2)}) copy-start(pred[128]{0:T(512)(128)(4,1)S(1)} %compare_and_fusion.3) | copy-start | bytes 388
  3.3 39.8 %copy-start.56 = (s32[64]{0:T(128)}, s32[64]{0:T(128)S(1)}, u32[]{:S(2)}) copy-start(s32[64]{0:T(128)S(1)} %get-tuple-element.90) | copy-start | bytes 772
  3.3 39.8 %copy-start.57 = (s32[64]{0:T(128)}, s32[64]{0:T(128)S(1)}, u32[]{:S(2)}) copy-start(s32[64]{0:T(128)S(1)} %get-tuple-element.91) | copy-start | bytes 772
  3.3 39.8 %copy-start.58 = (pred[64]{0:T(512)(128)(4,1)}, pred[64]{0:T(512)(128)(4,1)S(1)}, u32[]{:S(2)}) copy-start(pred[64]{0:T(512)(128)(4,1)S(1)} %compare_and_fusion.1) | copy-start | bytes 196
  7.3 8.8 %collective-permute-start.2 = (f32[3,40,4,128]{3,2,1,0:T(4,128)S(1)}, f32[3,40,4,128]{3,2,1,0:T(4,128)S(1)}, u32[]{:S(2)}, u32[]{:S(2)}) collective-permute-start(f32[3,40,4,128]{3,2,1,0:T(4,128)S(1)} %get-tuple-element.25), channel_id=1, source_target_pairs={{0,1},{1,2},{2,3},{3,4},{4,5},{5,6},{6,7},{7,8},{8,9},{9,10},{10,1... | collective-permute-start | bytes 737288 | tf_op jit(solution)/shard_map/ppermute | solution.py:18
  10.4 8.8 %collective-permute-start.3 = (f32[3,40,4,128]{3,2,1,0:T(4,128)S(1)}, f32[3,40,4,128]{3,2,1,0:T(4,128)S(1)}, u32[]{:S(2)}, u32[]{:S(2)}) collective-permute-start(f32[3,40,4,128]{3,2,1,0:T(4,128)S(1)} %get-tuple-element.26), channel_id=1, source_target_pairs={{0,15},{1,0},{2,1},{3,2},{4,3},{5,4},{6,5},{7,6},{8,7},{9,8},{10,9... | collective-permute-start | bytes 737288 | tf_op jit(solution)/shard_map/ppermute | solution.py:18
  12.6 67.5 %copy-start.59 = (s32[32]{0:T(128)}, s32[32]{0:T(128)S(1)}, u32[]{:S(2)}) copy-start(s32[32]{0:T(128)S(1)} %get-tuple-element.94) | copy-start | bytes 388
  12.6 67.4 %copy-start.61 = (s32[32]{0:T(128)}, s32[32]{0:T(128)S(1)}, u32[]{:S(2)}) copy-start(s32[32]{0:T(128)S(1)} %get-tuple-element.95) | copy-start | bytes 388
  23.7 2.6 %collective-permute-start.4 = (f32[2,5,8,64]{3,2,1,0:T(8,128)S(1)}, f32[2,5,8,64]{3,2,1,0:T(8,128)S(1)}, u32[]{:S(2)}, u32[]{:S(2)}) collective-permute-start(f32[2,5,8,64]{3,2,1,0:T(8,128)S(1)} %get-tuple-element.83), channel_id=1, source_target_pairs={{0,16},{16,32},{32,48},{48,64},{64,80},{80,96},{96,112},{112,128},... | collective-permute-start | bytes 61448 | tf_op jit(solution)/shard_map/ppermute | solution.py:18
  25.2 3.4 %collective-permute-start.5 = (f32[2,5,8,64]{3,2,1,0:T(8,128)S(1)}, f32[2,5,8,64]{3,2,1,0:T(8,128)S(1)}, u32[]{:S(2)}, u32[]{:S(2)}) collective-permute-start(f32[2,5,8,64]{3,2,1,0:T(8,128)S(1)} %get-tuple-element.84), channel_id=1, source_target_pairs={{0,496},{16,0},{32,16},{48,32},{64,48},{80,64},{96,80},{112,96},{1... | collective-permute-start | bytes 61448 | tf_op jit(solution)/shard_map/ppermute | solution.py:18
  28.7 7.8 %collective-permute-start.6 = (f32[2,26,5,64]{3,2,1,0:T(8,128)S(1)}, f32[2,26,5,64]{3,2,1,0:T(8,128)S(1)}, u32[]{:S(2)}, u32[]{:S(2)}) collective-permute-start(f32[2,26,5,64]{3,2,1,0:T(8,128)S(1)} %get-tuple-element.57), channel_id=1, source_target_pairs={{0,1},{1,2},{2,3},{3,4},{4,5},{5,6},{6,7},{7,8},{8,9},{9,10},{10,1... | collective-permute-start | bytes 199688 | tf_op jit(solution)/shard_map/ppermute | solution.py:18
  31.5 9.7 %collective-permute-start.7 = (f32[2,26,5,64]{3,2,1,0:T(8,128)S(1)}, f32[2,26,5,64]{3,2,1,0:T(8,128)S(1)}, u32[]{:S(2)}, u32[]{:S(2)}) collective-permute-start(f32[2,26,5,64]{3,2,1,0:T(8,128)S(1)} %get-tuple-element.58), channel_id=1, source_target_pairs={{0,15},{1,0},{2,1},{3,2},{4,3},{5,4},{6,5},{7,6},{8,7},{9,8},{10,9... | collective-permute-start | bytes 199688 | tf_op jit(solution)/shard_map/ppermute | solution.py:18
  34.0 46.1 %copy-start.63 = (pred[32]{0:T(512)(128)(4,1)}, pred[32]{0:T(512)(128)(4,1)S(1)}, u32[]{:S(2)}) copy-start(pred[32]{0:T(512)(128)(4,1)S(1)} %compare_and_fusion) | copy-start | bytes 100
  42.5 22.4 %copy-start.18 = (f32[22,14,64]{2,1,0:T(8,128)}, f32[22,14,64]{2,1,0:T(8,128)S(1)}, u32[]{:S(2)}) copy-start(f32[22,14,64]{2,1,0:T(8,128)S(1)} %fusion.86) | copy-start | bytes 236548
  67.7 18.2 %copy-start.15 = (f32[2,8,64,32]{2,3,1,0:T(8,128)}, f32[2,8,64,32]{2,3,1,0:T(8,128)S(1)}, u32[]{:S(2)}) copy-start(f32[2,8,64,32]{2,3,1,0:T(8,128)S(1)} %copy.74) | copy-start | bytes 393220
  73.7 9.3 %collective-permute-start.8 = (f32[2,4,64,32]{2,3,1,0:T(8,128)}, f32[2,4,64,32]{2,3,1,0:T(8,128)}, u32[]{:S(2)}, u32[]{:S(2)}) collective-permute-start(f32[2,4,64,32]{2,3,1,0:T(8,128)} %get-tuple-element.49), channel_id=1, source_target_pairs={{0,16},{16,32},{32,48},{48,64},{64,80},{80,96},{96,112},{112,128},... | collective-permute-start | bytes 196616 | tf_op jit(solution)/shard_map/ppermute | solution.py:18
  80.1 4.7 %collective-permute-start.9 = (f32[2,4,64,32]{2,3,1,0:T(8,128)}, f32[2,4,64,32]{2,3,1,0:T(8,128)}, u32[]{:S(2)}, u32[]{:S(2)}) collective-permute-start(f32[2,4,64,32]{2,3,1,0:T(8,128)} %get-tuple-element.50), channel_id=1, source_target_pairs={{0,496},{16,0},{32,16},{48,32},{64,48},{80,64},{96,80},{112,96},{1... | collective-permute-start | bytes 196616 | tf_op jit(solution)/shard_map/ppermute | solution.py:18
  86.0 44.0 %copy-start.47 = (f32[14,64,1]{1,2,0:T(1,128)}, f32[14,64,1]{1,2,0:T(1,128)S(1)}, u32[]{:S(2)}) copy-start(f32[14,64,1]{1,2,0:T(1,128)S(1)} %get-tuple-element.55) | copy-start | bytes 10756
  86.0 44.0 %copy-start.48 = (f32[14,64,1]{1,2,0:T(1,128)}, f32[14,64,1]{1,2,0:T(1,128)S(1)}, u32[]{:S(2)}) copy-start(f32[14,64,1]{1,2,0:T(1,128)S(1)} %get-tuple-element.56) | copy-start | bytes 10756
  90.2 10.7 %collective-permute-start.10 = (f32[2,4,512]{2,1,0:T(4,128)S(1)}, f32[2,4,512]{2,1,0:T(4,128)S(1)}, u32[]{:S(2)}, u32[]{:S(2)}) collective-permute-start(f32[2,4,512]{2,1,0:T(4,128)S(1)} %constant_dynamic-update-slice_fusion), channel_id=1, source_target_pairs={{0,32},{16,48},{32,64},{48,80},{64,96},{80,112},{96,128},{112,144}... | collective-permute-start | bytes 49160 | tf_op jit(solution)/shard_map/ppermute | solution.py:18
  94.8 6.2 %collective-permute-start.11 = (f32[2,4,512]{2,1,0:T(4,128)S(1)}, f32[2,4,512]{2,1,0:T(4,128)S(1)}, u32[]{:S(2)}, u32[]{:S(2)}) collective-permute-start(f32[2,4,512]{2,1,0:T(4,128)S(1)} %constant_dynamic-update-slice_fusion), channel_id=1, source_target_pairs={{0,16},{16,32},{32,48},{48,64},{64,80},{80,96},{96,112},{112,128},... | collective-permute-start | bytes 49160 | tf_op jit(solution)/shard_map/ppermute | solution.py:18
  95.7 5.9 %collective-permute-start.12 = (f32[2,4,512]{2,1,0:T(4,128)S(1)}, f32[2,4,512]{2,1,0:T(4,128)S(1)}, u32[]{:S(2)}, u32[]{:S(2)}) collective-permute-start(f32[2,4,512]{2,1,0:T(4,128)S(1)} %constant_dynamic-update-slice_fusion), channel_id=1, source_target_pairs={{0,496},{16,0},{32,16},{48,32},{64,48},{80,64},{96,80},{112,96},{1... | collective-permute-start | bytes 49160 | tf_op jit(solution)/shard_map/ppermute | solution.py:18
  95.7 7.7 %collective-permute-start.13 = (f32[2,4,512]{2,1,0:T(4,128)S(1)}, f32[2,4,512]{2,1,0:T(4,128)}, u32[]{:S(2)}, u32[]{:S(2)}) collective-permute-start(f32[2,4,512]{2,1,0:T(4,128)S(1)} %constant_dynamic-update-slice_fusion), channel_id=1, source_target_pairs={{0,480},{16,496},{32,0},{48,16},{64,32},{80,48},{96,64},{112,80},{... | collective-permute-start | bytes 49160 | tf_op jit(solution)/shard_map/ppermute | solution.py:18
  105.6 15.7 %copy-start.46 = (f32[2,20,512]{2,1,0:T(8,128)}, f32[2,20,512]{2,1,0:T(8,128)S(1)}, u32[]{:S(2)}) copy-start(f32[2,20,512]{2,1,0:T(8,128)S(1)} %concatenate.187.refs_1_) | copy-start | bytes 245764
  105.6 13.8 %collective-permute-start.14 = (f32[2,20,512]{2,1,0:T(8,128)S(1)}, f32[2,20,512]{2,1,0:T(8,128)S(1)}, u32[]{:S(2)}, u32[]{:S(2)}) collective-permute-start(f32[2,20,512]{2,1,0:T(8,128)S(1)} %concatenate.187.refs_1_), channel_id=1, source_target_pairs={{0,80},{16,96},{32,112},{48,128},{64,144},{80,160},{96,176},{112,1... | collective-permute-start | bytes 245768 | tf_op jit(solution)/shard_map/ppermute | solution.py:18
  112.0 9.3 %collective-permute-start.15 = (f32[2,20,512]{2,1,0:T(8,128)S(1)}, f32[2,20,512]{2,1,0:T(8,128)}, u32[]{:S(2)}, u32[]{:S(2)}) collective-permute-start(f32[2,20,512]{2,1,0:T(8,128)S(1)} %concatenate.187.refs_1_), channel_id=1, source_target_pairs={{0,432},{16,448},{32,464},{48,480},{64,496},{80,0},{96,16},{112,32... | collective-permute-start | bytes 245768 | tf_op jit(solution)/shard_map/ppermute | solution.py:18
  133.0 7.6 %collective-permute-start.16 = (f32[2,64,32]{1,2,0:T(8,128)}, f32[2,64,32]{1,2,0:T(8,128)}, u32[]{:S(2)}, u32[]{:S(2)}) collective-permute-start(f32[2,64,32]{1,2,0:T(8,128)} %get-tuple-element.81), channel_id=1, source_target_pairs={{0,16},{16,32},{32,48},{48,64},{64,80},{80,96},{96,112},{112,128},... | collective-permute-start | bytes 49160 | tf_op jit(solution)/shard_map/ppermute | solution.py:18
  139.3 3.7 %collective-permute-start.17 = (f32[2,64,32]{1,2,0:T(8,128)}, f32[2,64,32]{1,2,0:T(8,128)}, u32[]{:S(2)}, u32[]{:S(2)}) collective-permute-start(f32[2,64,32]{1,2,0:T(8,128)} %get-tuple-element.82), channel_id=1, source_target_pairs={{0,496},{16,0},{32,16},{48,32},{64,48},{80,64},{96,80},{112,96},{1... | collective-permute-start | bytes 49160 | tf_op jit(solution)/shard_map/ppermute | solution.py:18
  (63 other events, 154.8 us)

commit v4 on v3

--- a/solution.py
+++ b/solution.py
@@ -19,22 +19,28 @@
 
 
 def halo(x, w):
+    wx, wy = w
     size_x = x.shape[-3]
-    lower = shift_from(x[..., size_x - w :, :, :], "row", 1)
-    upper = shift_from(x[..., :w, :, :], "row", -1)
+    lower = shift_from(x[..., size_x - wx :, :, :], "row", 1)
+    upper = shift_from(x[..., :wx, :, :], "row", -1)
     x = jnp.concatenate([lower, x, upper], axis=-3)
     size_y = x.shape[-2]
-    lower = shift_from(x[..., :, size_y - w :, :], "col", 1)
-    upper = shift_from(x[..., :, :w, :], "col", -1)
+    lower = shift_from(x[..., :, size_y - wy :, :], "col", 1)
+    upper = shift_from(x[..., :, :wy, :], "col", -1)
     return jnp.concatenate([lower, x, upper], axis=-2)
 
 
-def trim(a, t, y=True):
-    if t == 0:
-        return a
-    if y:
-        return a[t:-t, t:-t]
-    return a[t:-t]
+def trim(a, t):
+    tx, ty = t if isinstance(t, tuple) else (t, 0)
+    return a[tx : a.shape[0] - tx, ty : a.shape[1] - ty]
+
+
+def less(a, b):
+    return tuple(i - j for i, j in zip(a, b))
+
+
+def more(a, k):
+    return tuple(i + k for i in a)
 
 
 def harmonic(left, right, scale):
@@ -71,11 +77,11 @@
         self.faces, self.have = faces, have
         self.right_side, self.rhs_have = right_side, rhs_have
 
-    def faces_at(self, h, y=True):
-        return tuple(trim(f, self.have - h, y) for f in self.faces)
-
-    def rhs_at(self, h, y=True):
-        return trim(self.right_side, self.rhs_have - h, y)
+    def faces_at(self, h):
+        return tuple(trim(f, less(self.have, h)) for f in self.faces)
+
+    def rhs_at(self, h):
+        return trim(self.right_side, less(self.rhs_have, h))
 
     def sweep(self, v, h):
         faces = self.faces_at(h)
@@ -85,8 +91,8 @@
     def first_sweep(self, h):
         return OMEGA * self.rhs_at(h) / self.faces_at(h)[6]
 
-    def residual(self, v):
-        return self.rhs_at(0) - apply_operator(v, self.faces_at(0))
+    def residual(self, v, h):
+        return self.rhs_at(h) - apply_operator(v, self.faces_at(h))
 
 
 def pairs(n):
@@ -129,27 +135,27 @@
     return jnp.concatenate([a[:, -w:], a, a[:, :w]], axis=1)
 
 
-class Band(Level):
-    def faces_at(self, h, y=False):
-        return super().faces_at(h, False)
-
-    def rhs_at(self, h, y=False):
-        return super().rhs_at(h, False)
+class Band:
+    def __init__(self, faces, have, right_side, rhs_have):
+        self.faces, self.have = faces, have
+        self.right_side, self.rhs_have = right_side, rhs_have
+
+    def faces_at(self, h):
+        return tuple(trim(f, self.have - h) for f in self.faces)
+
+    def rhs_at(self, h):
+        return trim(self.right_side, self.rhs_have - h)
 
     def sweep(self, v, h):
         faces = self.faces_at(h)
         residual = self.rhs_at(h) - apply_operator(wrap_y(v), faces)
         return v[1:-1] + OMEGA * residual / faces[6]
 
+    def first_sweep(self, h):
+        return OMEGA * self.rhs_at(h) / self.faces_at(h)[6]
+
     def residual(self, v):
         return self.rhs_at(0) - apply_operator(wrap_y(v), self.faces_at(0))
-
-
-def x_halo(x, w):
-    size_x = x.shape[-3]
-    lower = shift_from(x[..., size_x - w :, :, :], "row", 1)
-    upper = shift_from(x[..., :w, :, :], "row", -1)
-    return jnp.concatenate([lower, x, upper], axis=-3)
 
 
 def rows_around(x, steps, axis):
@@ -236,39 +242,38 @@
 
 def on_device(pressure_in, source, permeability):
     scales = [0.25**level for level in range(LEVELS + 1)]
-    k0, p0, b0 = halo(jnp.stack([permeability, pressure_in, source]), 4)
-    lev0 = Level(faces_of(k0, scales[0]), 3, b0, 4)
-    p = lev0.sweep(p0, 3)
-    s0 = lev0.sweep(p, 2)
-    rhs = coarsen(lev0.residual(trim(s0, 1)))
+    k0, p0, b0 = halo(jnp.stack([permeability, pressure_in, source]), (4, 4))
+    lev0 = Level(faces_of(k0, scales[0]), (3, 3), b0, (4, 4))
+    p = lev0.sweep(p0, (3, 3))
+    s0 = lev0.sweep(p, (2, 2))
+    rhs = coarsen(lev0.residual(trim(s0, (1, 1)), (0, 0)))
     perm = coarsen(permeability)
-    k1, b1 = halo(jnp.stack([perm, rhs]), 5)
-    lev1 = Level(faces_of(k1, scales[1]), 4, b1, 5)
-    p = lev1.first_sweep(4)
-    s1 = lev1.sweep(p, 3)
-    rhs = coarsen(lev1.residual(trim(s1, 2)))
-    perm = coarsen(perm)
+    k1, b1 = halo(jnp.stack([perm, rhs]), (13, 5))
+    lev1 = Level(faces_of(k1, scales[1]), (12, 4), b1, (13, 5))
+    p = lev1.first_sweep((12, 4))
+    s1 = lev1.sweep(p, (11, 3))
+    rhs = coarsen(lev1.residual(trim(s1, (0, 2)), (10, 0)))
+    rhs = jnp.pad(rhs, ((1, 1), (0, 0), (0, 0)))
+    perm = coarsen(trim(k1, (1, 5)))
     size_y2 = rhs.shape[1]
-    band = lax.all_gather(jnp.stack([perm, rhs]), "col", axis=2, tiled=True)
-    k2, b2 = x_halo(band, 4)
-    lev2 = Band(faces_of(wrap_y(k2), scales[2]), 3, b2, 4)
-    p = lev2.first_sweep(3)
-    s2 = lev2.sweep(p, 2)
-    rhs = coarsen(lev2.residual(s2[1:-1]))
-    perm = coarsen(band[0])
+    k2, b2 = lax.all_gather(jnp.stack([perm, rhs]), "col", axis=2, tiled=True)
+    lev2 = Band(faces_of(wrap_y(k2), scales[2]), 5, b2, 6)
+    p = lev2.first_sweep(5)
+    s2 = lev2.sweep(p, 4)
+    rhs = coarsen(lev2.residual(s2[3:-3]))
+    perm = coarsen(trim(k2, 6))
     correction = coarse_solve(rhs, perm, scales[3])
-    q = s2 + prolong(correction)[2:-2]
-    q = lev2.sweep(q, 1)
-    u2 = lev2.sweep(q, 0)
-    u2 = wrap_y(x_halo(u2, 2), 2)
+    q = s2 + prolong(correction)
+    q = lev2.sweep(q, 3)
+    u2 = lev2.sweep(q, 2)
     col = lax.axis_index("col")
-    u2 = lax.dynamic_slice_in_dim(u2, col * size_y2, size_y2 + 4, axis=1)
-    q = s1 + trim(prolong(u2), 1)
-    q = lev1.sweep(q, 2)
-    u1 = lev1.sweep(q, 1)
+    u2 = lax.dynamic_slice_in_dim(wrap_y(u2, 2), col * size_y2, size_y2 + 4, axis=1)
+    q = trim(s1, (8, 0)) + trim(prolong(u2), (1, 1))
+    q = lev1.sweep(q, (2, 2))
+    u1 = lev1.sweep(q, (1, 1))
     q = s0 + prolong(u1)
-    q = lev0.sweep(q, 1)
-    return lev0.sweep(q, 0)
+    q = lev0.sweep(q, (1, 1))
+    return lev0.sweep(q, (0, 0))
 
 
 def solution(mesh):

time: 153 us -> 158 us (1.033)
  the two profiles are of different devices: /device:TPU:35 before, /device:TPU:1 now
where the time goes in v4:
time: 158 us; the launch traced here: 157 us
  starting transfers between devices  53.9 us (34%)
  local copies, waits for them, and re-layouts  33 us (21%)
  other arithmetic  20.5 us (13%)
  waiting for transfers between devices  19.2 us (12%)
  blocking collectives  18.2 us (12%)
  matrix products  6.21 us (4%)
  Pallas kernels  4.57 us (3%)
    ppermute x14, starting transfers between devices, shift_from(): return lax.ppermute(x, axis, [(i, (i + k) % n) for i in range(n)])  53.9 us
    ppermute x14, waiting for transfers between devices, shift_from(): return lax.ppermute(x, axis, [(i, (i + k) % n) for i in range(n)])  19.2 us
    all_gather x1, blocking collectives, on_device(): k2, b2 = lax.all_gather(jnp.stack([perm, rhs]), 'col', axis=2, tiled=True)  18.2 us
    unnamed x166, local copies, waits for them, and re-layouts  16.9 us
    slice x5, local copies, waits for them, and re-layouts, trim(): return a[tx:a.shape[0] - tx, ty:a.shape[1] - ty]  4.99 us
    add x6, other arithmetic, sweep(): return v[1:-1, 1:-1] + OMEGA * residual / faces[6]  4.75 us
    pallas_call x1, Pallas kernels, coarse_solve(): v = call(lower, near, upper)  4.57 us
    dot_general x9, matrix products, along_z(): out = jnp.dot(flat, matrix, precision=lax.Precision.HIGHEST)  3.49 us
  transfers between devices with their start and end apart: 14, of which 8 were waited for; matrix products, arithmetic and copies ran while one was open for 6% of the time, Pallas kernels for 0%

profile of v4, /device:TPU:1, one launch (start us, length us, event | category | flops | bytes accessed | tf_op | source)
XLA Modules:
  0.0 157.0 jit_solution(10438981724082778392)
XLA Ops:
  0.9 6.9 %collective-permute-start.1 = (f32[3,4,16,128]{3,2,1,0:T(8,128)S(1)}, f32[3,4,16,128]{3,2,1,0:T(8,128)S(1)}, u32[]{:S(2)}, u32[]{:S(2)}) collective-permute-start(f32[3,4,16,128]{3,2,1,0:T(8,128)S(1)} %get-tuple-element.36), channel_id=1, source_target_pairs={{0,496},{16,0},{32,16},{48,32},{64,48},{80,64},{96,80},{112,96},{1... | collective-permute-start | bytes 294920 | tf_op jit(solution)/shard_map/ppermute | solution.py:18
  9.5 2.6 %collective-permute-done = f32[3,4,16,128]{3,2,1,0:T(8,128)S(1)} collective-permute-done((f32[3,4,16,128]{3,2,1,0:T(8,128)S(1)}, f32[3,4,16,128]{3,2,1,0:T(8,128)S(1)}, u32[]{:S(2)}, u32[]{:S(2)}) %collective-permute-start) | collective-permute-done | bytes 98336 | tf_op jit(solution)/shard_map/ppermute | solution.py:18
  12.3 6.8 %collective-permute-start.3 = (f32[3,40,4,128]{3,2,1,0:T(4,128)S(1)}, f32[3,40,4,128]{3,2,1,0:T(4,128)S(1)}, u32[]{:S(2)}, u32[]{:S(2)}) collective-permute-start(f32[3,40,4,128]{3,2,1,0:T(4,128)S(1)} %get-tuple-element.34), channel_id=1, source_target_pairs={{0,15},{1,0},{2,1},{3,2},{4,3},{5,4},{6,5},{7,6},{8,7},{9,8},{10,9... | collective-permute-start | bytes 737288 | tf_op jit(solution)/shard_map/ppermute | solution.py:18
  19.1 1.9 %collective-permute-start.2 = (f32[3,40,4,128]{3,2,1,0:T(4,128)S(1)}, f32[3,40,4,128]{3,2,1,0:T(4,128)S(1)}, u32[]{:S(2)}, u32[]{:S(2)}) collective-permute-start(f32[3,40,4,128]{3,2,1,0:T(4,128)S(1)} %get-tuple-element.33), channel_id=1, source_target_pairs={{0,1},{1,2},{2,3},{3,4},{4,5},{5,6},{6,7},{7,8},{8,9},{9,10},{10,1... | collective-permute-start | bytes 737288 | tf_op jit(solution)/shard_map/ppermute | solution.py:18
  22.3 7.1 %collective-permute-done.2 = f32[3,40,4,128]{3,2,1,0:T(4,128)S(1)} collective-permute-done((f32[3,40,4,128]{3,2,1,0:T(4,128)S(1)}, f32[3,40,4,128]{3,2,1,0:T(4,128)S(1)}, u32[]{:S(2)}, u32[]{:S(2)}) %collective-permute-start.2) | collective-permute-done | bytes 245792 | tf_op jit(solution)/shard_map/ppermute | solution.py:18
  34.0 5.9 %collective-permute-start.5 = (f32[2,13,8,64]{3,2,1,0:T(8,128)S(1)}, f32[2,13,8,64]{3,2,1,0:T(8,128)S(1)}, u32[]{:S(2)}, u32[]{:S(2)}) collective-permute-start(f32[2,13,8,64]{3,2,1,0:T(8,128)S(1)} %get-tuple-element.90), channel_id=1, source_target_pairs={{0,496},{16,0},{32,16},{48,32},{64,48},{80,64},{96,80},{112,96},{1... | collective-permute-start | bytes 159752 | tf_op jit(solution)/shard_map/ppermute | solution.py:18
  41.7 1.9 %collective-permute-start.7 = (f32[2,42,5,64]{3,2,1,0:T(8,128)S(1)}, f32[2,42,5,64]{3,2,1,0:T(8,128)S(1)}, u32[]{:S(2)}, u32[]{:S(2)}) collective-permute-start(f32[2,42,5,64]{3,2,1,0:T(8,128)S(1)} %get-tuple-element.52), channel_id=1, source_target_pairs={{0,15},{1,0},{2,1},{3,2},{4,3},{5,4},{6,5},{7,6},{8,7},{9,8},{10,9... | collective-permute-start | bytes 322568 | tf_op jit(solution)/shard_map/ppermute | solution.py:18
  43.6 3.4 %collective-permute-start.6 = (f32[2,42,5,64]{3,2,1,0:T(8,128)S(1)}, f32[2,42,5,64]{3,2,1,0:T(8,128)S(1)}, u32[]{:S(2)}, u32[]{:S(2)}) collective-permute-start(f32[2,42,5,64]{3,2,1,0:T(8,128)S(1)} %get-tuple-element.51), channel_id=1, source_target_pairs={{0,1},{1,2},{2,3},{3,4},{4,5},{5,6},{6,7},{7,8},{8,9},{9,10},{10,1... | collective-permute-start | bytes 322568 | tf_op jit(solution)/shard_map/ppermute | solution.py:18
  47.5 2.2 %collective-permute-done.7 = f32[2,42,5,64]{3,2,1,0:T(8,128)S(1)} collective-permute-done((f32[2,42,5,64]{3,2,1,0:T(8,128)S(1)}, f32[2,42,5,64]{3,2,1,0:T(8,128)S(1)}, u32[]{:S(2)}, u32[]{:S(2)}) %collective-permute-start.7) | collective-permute-done | bytes 107552 | tf_op jit(solution)/shard_map/ppermute | solution.py:18
  49.7 5.2 %collective-permute-done.6 = f32[2,42,5,64]{3,2,1,0:T(8,128)S(1)} collective-permute-done((f32[2,42,5,64]{3,2,1,0:T(8,128)S(1)}, f32[2,42,5,64]{3,2,1,0:T(8,128)S(1)}, u32[]{:S(2)}, u32[]{:S(2)}) %collective-permute-start.6) | collective-permute-done | bytes 107552 | tf_op jit(solution)/shard_map/ppermute | solution.py:18
  58.8 18.2 %all_gather.3 = f32[2,20,64,32]{3,0,1,2:T(2,128)S(1)} all-gather(f32[2,20,4,32]{3,0,1,2:T(2,128)S(1)} %copy.81), channel_id=1, replica_groups=mesh['row'=32,'col'=16] {'col'}, dimensions={2}, use_global_device_ids=true | all-gather | bytes 348160 | tf_op jit(solution)/shard_map/all_gather | solution.py:259
  77.0 2.6 %fusion.246 = (f32[1,18,64,32]{3,0,1,2:T(1,128)}, f32[1,18,64,32]{3,0,1,2:T(1,128)}, f32[1,18,64,32]{3,0,1,2:T(1,128)}, f32[1,18,64,32]{3,0,1,2:T(1,128)}) fusion(f32[2,20,64,32]{3,0,1,2:T(2,128)S(1)} %all_gather.3), kind=kLoop, calls=%fused_computation.429 | loop fusion | bytes 1179648 | tf_op jit(solution)/shard_map/slice | solution.py:52
  79.6 1.3 copy.112
  81.7 1.4 slice.1222
  83.1 2.0 %copy.110 = f32[1,18,64,32]{2,3,1,0:T(8,128)} copy(f32[1,18,64,32]{3,0,1,2:T(1,128)} %get-tuple-element.30) | data formatting | bytes 294912
  85.0 1.9 %copy.113 = f32[1,18,64,32]{2,3,1,0:T(8,128)} copy(f32[1,18,64,32]{3,0,1,2:T(1,128)} %get-tuple-element.28) | data formatting | bytes 294912
  87.0 1.9 %copy.111 = f32[1,18,64,32]{2,3,1,0:T(8,128)} copy(f32[1,18,64,32]{3,0,1,2:T(1,128)} %get-tuple-element.27) | data formatting | bytes 294912
  90.3 2.8 %bitcast_divide_fusion = (f32[18,64,32]{1,2,0:T(8,128)S(1)}, f32[18,64,32]{1,2,0:T(8,128)}, f32[18,64,32]{1,2,0:T(8,128)}, f32[18,64,32]{1,2,0:T(8,128)}, f32[18,64,32]{1,2,0:T(8,128)}, /*index=5*/f32[18,64,32]{1,2,0:T(8,128)}) fusion(f32[1,18,64,32]{2,3,1,0:T(8,128)} %copy.110, f32[18,64,1]{1,2,0:T(1,128)S(1)} %get-tuple-element.64, ...), kind=kLoop, calls=%fused_computation.128 | loop fusion | flops 1105920 | bytes 1795584 | tf_op jit(solution)/shard_map/div | solution.py:155
  95.8 2.4 %fusion.61 = f32[16,64,32]{1,2,0:T(8,128)S(1)} fusion(f32[18,64,1]{1,2,0:T(1,128)S(1)} %get-tuple-element.64, f32[18,64,1]{1,2,0:T(1,128)S(1)} %get-tuple-element.63, f32[18,1,32]{1,2,0:T(8,128)} %get-tuple-element.62, f32[18,64,32]{1,2,0:T(8,128)S(1)} %get-tuple-element.5, f32[18,64,32]{1,2,0:T(8,128)} %get-tuple-element.10, ...), kind=kLoop, calls=%fused_computation.141 | loop fusion | flops 688128 | bytes 2418688 | tf_op jit(solution)/shard_map/add | solution.py:152
  101.6 1.7 %copy.116 = f32[1,8,64,32]{2,3,1,0:T(8,128)} copy(f32[1,8,64,32]{3,0,1,2:T(1,128)} %get-tuple-element.26) | data formatting | bytes 131072
  103.3 1.8 %fusion.169 = f32[8,64,32]{1,2,0:T(8,128)S(1)} fusion(f32[18,64,31]{1,2,0:T(8,128)S(1)} %copy-done.15, f32[18,64,1]{1,2,0:T(1,128)S(1)} %get-tuple-element.64, f32[18,64,1]{1,2,0:T(1,128)S(1)} %get-tuple-element.63, f32[10,1,32]{1,2,0:T(8,128)} %get-tuple-element.74, f32[10,64,32]{1,2,0:T(8,128)} %slice.1247, f32[18,64,32]{1,2,0:T(8,128)} %get-tuple-element.10, ...), kind=kLoop, calls=%fused_computation.307 | loop fusion | flops 294912 | bytes 1018880 | tf_op jit(solution)/shard_map/sub | solution.py:158
  105.7 1.3 fusion.260
  107.7 1.9 %collective-permute-start.8 = (f32[2,4,512]{2,1,0:T(4,128)S(1)}, f32[2,4,512]{2,1,0:T(4,128)S(1)}, u32[]{:S(2)}, u32[]{:S(2)}) collective-permute-start(f32[2,4,512]{2,1,0:T(4,128)S(1)} %constant_dynamic-update-slice_fusion), channel_id=1, source_target_pairs={{0,32},{16,48},{32,64},{48,80},{64,96},{80,112},{96,128},{112,144}... | collective-permute-start | bytes 49160 | tf_op jit(solution)/shard_map/ppermute | solution.py:18
  109.7 7.9 %collective-permute-start.9 = (f32[2,4,512]{2,1,0:T(4,128)S(1)}, f32[2,4,512]{2,1,0:T(4,128)S(1)}, u32[]{:S(2)}, u32[]{:S(2)}) collective-permute-start(f32[2,4,512]{2,1,0:T(4,128)S(1)} %constant_dynamic-update-slice_fusion), channel_id=1, source_target_pairs={{0,16},{16,32},{32,48},{48,64},{64,80},{80,96},{96,112},{112,128},... | collective-permute-start | bytes 49160 | tf_op jit(solution)/shard_map/ppermute | solution.py:18
  117.6 1.7 %collective-permute-start.10 = (f32[2,4,512]{2,1,0:T(4,128)S(1)}, f32[2,4,512]{2,1,0:T(4,128)S(1)}, u32[]{:S(2)}, u32[]{:S(2)}) collective-permute-start(f32[2,4,512]{2,1,0:T(4,128)S(1)} %constant_dynamic-update-slice_fusion), channel_id=1, source_target_pairs={{0,496},{16,0},{32,16},{48,32},{64,48},{80,64},{96,80},{112,96},{1... | collective-permute-start | bytes 49160 | tf_op jit(solution)/shard_map/ppermute | solution.py:18
  119.3 5.5 %collective-permute-start.11 = (f32[2,4,512]{2,1,0:T(4,128)S(1)}, f32[2,4,512]{2,1,0:T(4,128)S(1)}, u32[]{:S(2)}, u32[]{:S(2)}) collective-permute-start(f32[2,4,512]{2,1,0:T(4,128)S(1)} %constant_dynamic-update-slice_fusion), channel_id=1, source_target_pairs={{0,480},{16,496},{32,0},{48,16},{64,32},{80,48},{96,64},{112,80},{... | collective-permute-start | bytes 49160 | tf_op jit(solution)/shard_map/ppermute | solution.py:18
  125.8 4.6 %collective-permute-start.12 = (f32[2,20,512]{2,1,0:T(8,128)S(1)}, f32[2,20,512]{2,1,0:T(8,128)}, u32[]{:S(2)}, u32[]{:S(2)}) collective-permute-start(f32[2,20,512]{2,1,0:T(8,128)S(1)} %concatenate.180.refs_1_), channel_id=1, source_target_pairs={{0,80},{16,96},{32,112},{48,128},{64,144},{80,160},{96,176},{112,1... | collective-permute-start | bytes 245768 | tf_op jit(solution)/shard_map/ppermute | solution.py:18
  130.4 5.4 %collective-permute-start.13 = (f32[2,20,512]{2,1,0:T(8,128)S(1)}, f32[2,20,512]{2,1,0:T(8,128)}, u32[]{:S(2)}, u32[]{:S(2)}) collective-permute-start(f32[2,20,512]{2,1,0:T(8,128)S(1)} %concatenate.180.refs_1_), channel_id=1, source_target_pairs={{0,432},{16,448},{32,464},{48,480},{64,496},{80,0},{96,16},{112,32... | collective-permute-start | bytes 245768 | tf_op jit(solution)/shard_map/ppermute | solution.py:18
  136.4 1.2 slice.1262
  138.8 1.2 copy.121
  141.2 4.6 %shard_map.37 = f32[8,512]{1,0:T(8,128)} custom-call(f32[2,20,512]{2,1,0:T(8,128)} %collective-permute-done.12.refs_0_, f32[2,20,512]{2,1,0:T(8,128)} %copy-done.50, f32[2,20,512]{2,1,0:T(8,128)} %collective-permute-done.13.refs_2_), custom_call_target="tpu_custom_call" | custom-call | flops 13107200 | bytes 491520 | tf_op jit(solution)/shard_map/pallas_call | solution.py:239
  155.7 1.3 fusion.72
  (274 shorter events, 37.0 us)
Async XLA Ops:
  0.0 12.2 %copy-start.46 = (f32[32,16,128]{2,1,0:T(8,128)S(1)}, f32[32,16,128]{2,1,0:T(8,128)}, u32[]{:S(2)}) copy-start(f32[32,16,128]{2,1,0:T(8,128)} %param.4) | copy-start | bytes 786436
  0.0 12.2 %copy-start.47 = (f32[32,16,128]{2,1,0:T(8,128)S(1)}, f32[32,16,128]{2,1,0:T(8,128)}, u32[]{:S(2)}) copy-start(f32[32,16,128]{2,1,0:T(8,128)} %param.3) | copy-start | bytes 786436
  0.0 12.2 %copy-start.35 = (f32[32,16,128]{2,1,0:T(8,128)S(1)}, f32[32,16,128]{2,1,0:T(8,128)}, u32[]{:S(2)}) copy-start(f32[32,16,128]{2,1,0:T(8,128)} %param.5) | copy-start | bytes 786436
  0.9 8.6 %collective-permute-start.1 = (f32[3,4,16,128]{3,2,1,0:T(8,128)S(1)}, f32[3,4,16,128]{3,2,1,0:T(8,128)S(1)}, u32[]{:S(2)}, u32[]{:S(2)}) collective-permute-start(f32[3,4,16,128]{3,2,1,0:T(8,128)S(1)} %get-tuple-element.36), channel_id=1, source_target_pairs={{0,496},{16,0},{32,16},{48,32},{64,48},{80,64},{96,80},{112,96},{1... | collective-permute-start | bytes 294920 | tf_op jit(solution)/shard_map/ppermute | solution.py:18
  7.8 4.4 %collective-permute-start = (f32[3,4,16,128]{3,2,1,0:T(8,128)S(1)}, f32[3,4,16,128]{3,2,1,0:T(8,128)S(1)}, u32[]{:S(2)}, u32[]{:S(2)}) collective-permute-start(f32[3,4,16,128]{3,2,1,0:T(8,128)S(1)} %get-tuple-element.35), channel_id=1, source_target_pairs={{0,16},{16,32},{32,48},{48,64},{64,80},{80,96},{96,112},{112,128},... | collective-permute-start | bytes 294920 | tf_op jit(solution)/shard_map/ppermute | solution.py:18
  7.8 25.6 %copy-start.68 = (s32[128]{0:T(128)}, s32[128]{0:T(128)S(1)}, u32[]{:S(2)}) copy-start(s32[128]{0:T(128)S(1)} %get-tuple-element.92) | copy-start | bytes 1540
  7.8 25.6 %copy-start.70 = (s32[128]{0:T(128)}, s32[128]{0:T(128)S(1)}, u32[]{:S(2)}) copy-start(s32[128]{0:T(128)S(1)} %get-tuple-element.93) | copy-start | bytes 1540
  7.9 25.6 %copy-start.72 = (pred[128]{0:T(512)(128)(4,1)}, pred[128]{0:T(512)(128)(4,1)S(1)}, u32[]{:S(2)}) copy-start(pred[128]{0:T(512)(128)(4,1)S(1)} %compare_and_fusion.3) | copy-start | bytes 388
  7.9 21.8 %copy-start.74 = (s32[16]{0:T(128)}, s32[16]{0:T(128)S(1)}, u32[]{:S(2)}) copy-start(s32[16]{0:T(128)S(1)} %get-tuple-element.94) | copy-start | bytes 196
  7.9 21.8 %copy-start.75 = (s32[16]{0:T(128)}, s32[16]{0:T(128)S(1)}, u32[]{:S(2)}) copy-start(s32[16]{0:T(128)S(1)} %get-tuple-element.95) | copy-start | bytes 196
  7.9 50.2 %copy-start.56 = (s32[64]{0:T(128)}, s32[64]{0:T(128)S(1)}, u32[]{:S(2)}) copy-start(s32[64]{0:T(128)S(1)} %get-tuple-element.96) | copy-start | bytes 772
  7.9 50.2 %copy-start.58 = (s32[64]{0:T(128)}, s32[64]{0:T(128)S(1)}, u32[]{:S(2)}) copy-start(s32[64]{0:T(128)S(1)} %get-tuple-element.97) | copy-start | bytes 772
  8.0 50.2 %copy-start.60 = (pred[64]{0:T(512)(128)(4,1)}, pred[64]{0:T(512)(128)(4,1)S(1)}, u32[]{:S(2)}) copy-start(pred[64]{0:T(512)(128)(4,1)S(1)} %compare_and_fusion.1) | copy-start | bytes 196
  9.5 97.6 %copy-start.62 = (s32[32]{0:T(128)}, s32[32]{0:T(128)S(1)}, u32[]{:S(2)}) copy-start(s32[32]{0:T(128)S(1)} %get-tuple-element.100) | copy-start | bytes 388
  9.5 97.6 %copy-start.64 = (s32[32]{0:T(128)}, s32[32]{0:T(128)S(1)}, u32[]{:S(2)}) copy-start(s32[32]{0:T(128)S(1)} %get-tuple-element.101) | copy-start | bytes 388
  12.3 10.0 %collective-permute-start.3 = (f32[3,40,4,128]{3,2,1,0:T(4,128)S(1)}, f32[3,40,4,128]{3,2,1,0:T(4,128)S(1)}, u32[]{:S(2)}, u32[]{:S(2)}) collective-permute-start(f32[3,40,4,128]{3,2,1,0:T(4,128)S(1)} %get-tuple-element.34), channel_id=1, source_target_pairs={{0,15},{1,0},{2,1},{3,2},{4,3},{5,4},{6,5},{7,6},{8,7},{9,8},{10,9... | collective-permute-start | bytes 737288 | tf_op jit(solution)/shard_map/ppermute | solution.py:18
  19.1 10.3 %collective-permute-start.2 = (f32[3,40,4,128]{3,2,1,0:T(4,128)S(1)}, f32[3,40,4,128]{3,2,1,0:T(4,128)S(1)}, u32[]{:S(2)}, u32[]{:S(2)}) collective-permute-start(f32[3,40,4,128]{3,2,1,0:T(4,128)S(1)} %get-tuple-element.33), channel_id=1, source_target_pairs={{0,1},{1,2},{2,3},{3,4},{4,5},{5,6},{6,7},{7,8},{8,9},{9,10},{10,1... | collective-permute-start | bytes 737288 | tf_op jit(solution)/shard_map/ppermute | solution.py:18
  34.0 6.9 %collective-permute-start.5 = (f32[2,13,8,64]{3,2,1,0:T(8,128)S(1)}, f32[2,13,8,64]{3,2,1,0:T(8,128)S(1)}, u32[]{:S(2)}, u32[]{:S(2)}) collective-permute-start(f32[2,13,8,64]{3,2,1,0:T(8,128)S(1)} %get-tuple-element.90), channel_id=1, source_target_pairs={{0,496},{16,0},{32,16},{48,32},{64,48},{80,64},{96,80},{112,96},{1... | collective-permute-start | bytes 159752 | tf_op jit(solution)/shard_map/ppermute | solution.py:18
  39.9 1.7 %collective-permute-start.4 = (f32[2,13,8,64]{3,2,1,0:T(8,128)S(1)}, f32[2,13,8,64]{3,2,1,0:T(8,128)S(1)}, u32[]{:S(2)}, u32[]{:S(2)}) collective-permute-start(f32[2,13,8,64]{3,2,1,0:T(8,128)S(1)} %get-tuple-element.89), channel_id=1, source_target_pairs={{0,16},{16,32},{32,48},{48,64},{64,80},{80,96},{96,112},{112,128},... | collective-permute-start | bytes 159752 | tf_op jit(solution)/shard_map/ppermute | solution.py:18
  39.9 67.2 %copy-start.66 = (pred[32]{0:T(512)(128)(4,1)}, pred[32]{0:T(512)(128)(4,1)S(1)}, u32[]{:S(2)}) copy-start(pred[32]{0:T(512)(128)(4,1)S(1)} %compare_and_fusion) | copy-start | bytes 100
  41.7 8.0 %collective-permute-start.7 = (f32[2,42,5,64]{3,2,1,0:T(8,128)S(1)}, f32[2,42,5,64]{3,2,1,0:T(8,128)S(1)}, u32[]{:S(2)}, u32[]{:S(2)}) collective-permute-start(f32[2,42,5,64]{3,2,1,0:T(8,128)S(1)} %get-tuple-element.52), channel_id=1, source_target_pairs={{0,15},{1,0},{2,1},{3,2},{4,3},{5,4},{6,5},{7,6},{8,7},{9,8},{10,9... | collective-permute-start | bytes 322568 | tf_op jit(solution)/shard_map/ppermute | solution.py:18
  43.6 11.3 %collective-permute-start.6 = (f32[2,42,5,64]{3,2,1,0:T(8,128)S(1)}, f32[2,42,5,64]{3,2,1,0:T(8,128)S(1)}, u32[]{:S(2)}, u32[]{:S(2)}) collective-permute-start(f32[2,42,5,64]{3,2,1,0:T(8,128)S(1)} %get-tuple-element.51), channel_id=1, source_target_pairs={{0,1},{1,2},{2,3},{3,4},{4,5},{5,6},{6,7},{7,8},{8,9},{9,10},{10,1... | collective-permute-start | bytes 322568 | tf_op jit(solution)/shard_map/ppermute | solution.py:18
  81.7 21.7 %copy-start.51 = (f32[18,64,1]{1,2,0:T(1,128)}, f32[18,64,1]{1,2,0:T(1,128)S(1)}, u32[]{:S(2)}) copy-start(f32[18,64,1]{1,2,0:T(1,128)S(1)} %get-tuple-element.63) | copy-start | bytes 13828
  81.7 21.6 %copy-start.53 = (f32[18,64,1]{1,2,0:T(1,128)}, f32[18,64,1]{1,2,0:T(1,128)S(1)}, u32[]{:S(2)}) copy-start(f32[18,64,1]{1,2,0:T(1,128)S(1)} %get-tuple-element.64) | copy-start | bytes 13828
  107.7 17.7 %collective-permute-start.8 = (f32[2,4,512]{2,1,0:T(4,128)S(1)}, f32[2,4,512]{2,1,0:T(4,128)S(1)}, u32[]{:S(2)}, u32[]{:S(2)}) collective-permute-start(f32[2,4,512]{2,1,0:T(4,128)S(1)} %constant_dynamic-update-slice_fusion), channel_id=1, source_target_pairs={{0,32},{16,48},{32,64},{48,80},{64,96},{80,112},{96,128},{112,144}... | collective-permute-start | bytes 49160 | tf_op jit(solution)/shard_map/ppermute | solution.py:18
  109.7 15.8 %collective-permute-start.9 = (f32[2,4,512]{2,1,0:T(4,128)S(1)}, f32[2,4,512]{2,1,0:T(4,128)S(1)}, u32[]{:S(2)}, u32[]{:S(2)}) collective-permute-start(f32[2,4,512]{2,1,0:T(4,128)S(1)} %constant_dynamic-update-slice_fusion), channel_id=1, source_target_pairs={{0,16},{16,32},{32,48},{48,64},{64,80},{80,96},{96,112},{112,128},... | collective-permute-start | bytes 49160 | tf_op jit(solution)/shard_map/ppermute | solution.py:18
  117.6 7.9 %collective-permute-start.10 = (f32[2,4,512]{2,1,0:T(4,128)S(1)}, f32[2,4,512]{2,1,0:T(4,128)S(1)}, u32[]{:S(2)}, u32[]{:S(2)}) collective-permute-start(f32[2,4,512]{2,1,0:T(4,128)S(1)} %constant_dynamic-update-slice_fusion), channel_id=1, source_target_pairs={{0,496},{16,0},{32,16},{48,32},{64,48},{80,64},{96,80},{112,96},{1... | collective-permute-start | bytes 49160 | tf_op jit(solution)/shard_map/ppermute | solution.py:18
  119.3 6.4 %collective-permute-start.11 = (f32[2,4,512]{2,1,0:T(4,128)S(1)}, f32[2,4,512]{2,1,0:T(4,128)S(1)}, u32[]{:S(2)}, u32[]{:S(2)}) collective-permute-start(f32[2,4,512]{2,1,0:T(4,128)S(1)} %constant_dynamic-update-slice_fusion), channel_id=1, source_target_pairs={{0,480},{16,496},{32,0},{48,16},{64,32},{80,48},{96,64},{112,80},{... | collective-permute-start | bytes 49160 | tf_op jit(solution)/shard_map/ppermute | solution.py:18
  125.8 15.4 %copy-start.50 = (f32[2,20,512]{2,1,0:T(8,128)}, f32[2,20,512]{2,1,0:T(8,128)S(1)}, u32[]{:S(2)}) copy-start(f32[2,20,512]{2,1,0:T(8,128)S(1)} %concatenate.180.refs_1_) | copy-start | bytes 245764
  125.8 15.4 %collective-permute-start.12 = (f32[2,20,512]{2,1,0:T(8,128)S(1)}, f32[2,20,512]{2,1,0:T(8,128)}, u32[]{:S(2)}, u32[]{:S(2)}) collective-permute-start(f32[2,20,512]{2,1,0:T(8,128)S(1)} %concatenate.180.refs_1_), channel_id=1, source_target_pairs={{0,80},{16,96},{32,112},{48,128},{64,144},{80,160},{96,176},{112,1... | collective-permute-start | bytes 245768 | tf_op jit(solution)/shard_map/ppermute | solution.py:18
  130.4 10.8 %collective-permute-start.13 = (f32[2,20,512]{2,1,0:T(8,128)S(1)}, f32[2,20,512]{2,1,0:T(8,128)}, u32[]{:S(2)}, u32[]{:S(2)}) collective-permute-start(f32[2,20,512]{2,1,0:T(8,128)S(1)} %concatenate.180.refs_1_), channel_id=1, source_target_pairs={{0,432},{16,448},{32,464},{48,480},{64,496},{80,0},{96,16},{112,32... | collective-permute-start | bytes 245768 | tf_op jit(solution)/shard_map/ppermute | solution.py:18
  137.6 9.8 %copy-start.13 = (f32[16,64,32]{1,2,0:T(8,128)S(1)}, f32[16,64,32]{1,2,0:T(8,128)}, u32[]{:S(2)}) copy-start(f32[16,64,32]{1,2,0:T(8,128)} %copy-done.12) | copy-start | bytes 393220
  (60 other events, 128.3 us)

commit v5 on v3

--- a/solution.py
+++ b/solution.py
@@ -19,14 +19,14 @@
 
 
 def halo(x, w):
+    size_y = x.shape[-2]
+    lower = shift_from(x[..., :, size_y - w :, :], "col", 1)
+    upper = shift_from(x[..., :, :w, :], "col", -1)
+    x = jnp.concatenate([lower, x, upper], axis=-2)
     size_x = x.shape[-3]
     lower = shift_from(x[..., size_x - w :, :, :], "row", 1)
     upper = shift_from(x[..., :w, :, :], "row", -1)
-    x = jnp.concatenate([lower, x, upper], axis=-3)
-    size_y = x.shape[-2]
-    lower = shift_from(x[..., :, size_y - w :, :], "col", 1)
-    upper = shift_from(x[..., :, :w, :], "col", -1)
-    return jnp.concatenate([lower, x, upper], axis=-2)
+    return jnp.concatenate([lower, x, upper], axis=-3)
 
 
 def trim(a, t, y=True):
@@ -161,9 +161,9 @@
 def coarse_kernel(scale, size_z, spans, keep, lower_ref, own_ref, upper_ref, out_ref, tile_ref):
     span, extra = spans
     for f in range(2):
-        tile_ref[f, 0:extra] = lower_ref[f, span - extra : span]
+        tile_ref[f, 0:extra] = lower_ref[f]
         tile_ref[f, extra : extra + span] = own_ref[f]
-        tile_ref[f, extra + span : 2 * extra + span] = upper_ref[f, 0:extra]
+        tile_ref[f, extra + span : 2 * extra + span] = upper_ref[f]
     b = tile_ref[0]
     k = tile_ref[1]
     rows, lanes = k.shape
@@ -221,7 +221,8 @@
     rows = span + 2 * extra
     keep = 8
     assert (rows - keep) // 2 >= CSWEEPS
-    lower, upper = shift_from(near, "row", 5), shift_from(near, "row", -5)
+    lower = shift_from(near[:, span - extra :], "row", 5)
+    upper = shift_from(near[:, :extra], "row", -5)
     call = pl.pallas_call(
         lambda *refs: coarse_kernel(scale, size_z, (span, extra), keep, *refs),
         out_shape=jax.ShapeDtypeStruct((keep, lanes), jnp.float32),

time: 153 us -> 148 us (0.967)
  the two profiles are of different devices: /device:TPU:35 before, /device:TPU:1 now
where the time goes in v5:
time: 148 us; the launch traced here: 147 us
  starting transfers between devices  62.4 us (42%)
  local copies, waits for them, and re-layouts  20.7 us (14%)
  blocking collectives  19.2 us (13%)
  other arithmetic  17.4 us (12%)
  matrix products  10.8 us (7%)
  waiting for transfers between devices  10.8 us (7%)
  Pallas kernels  4.47 us (3%)
    ppermute x18, starting transfers between devices, shift_from(): return lax.ppermute(x, axis, [(i, (i + k) % n) for i in range(n)])  62.4 us
    all_gather x1, blocking collectives, on_device(): band = lax.all_gather(jnp.stack([perm, rhs]), 'col', axis=2, tiled=True)  19.2 us
    ppermute x18, waiting for transfers between devices, shift_from(): return lax.ppermute(x, axis, [(i, (i + k) % n) for i in range(n)])  10.8 us
    unnamed x137, local copies, waits for them, and re-layouts  6.56 us
    dot_general x9, matrix products, along_z(): out = jnp.dot(flat, matrix, precision=lax.Precision.HIGHEST)  6.35 us
    add x6, other arithmetic, sweep(): return v[1:-1, 1:-1] + OMEGA * residual / faces[6]  4.51 us
    pallas_call x1, Pallas kernels, coarse_solve(): v = call(lower, near, upper)  4.47 us
    dot_general x8, matrix products, along_y(): jnp.einsum('xjy,xyz->xjz', batched, field, precision=lax.Precision.HIGHEST)  3.55 us
  transfers between devices with their start and end apart: 18, of which 10 were waited for; matrix products, arithmetic and copies ran while one was open for 7% of the time, Pallas kernels for 0%

profile of v5, /device:TPU:1, one launch (start us, length us, event | category | flops | bytes accessed | tf_op | source)
XLA Modules:
  0.0 147.1 jit_solution(7444500863665262737)
XLA Ops:
  0.0 1.3 pad_maximum_fusion.13
  1.4 3.9 %collective-permute-start = (f32[3,32,4,128]{3,2,1,0:T(4,128)S(1)}, f32[3,32,4,128]{3,2,1,0:T(4,128)S(1)}, u32[]{:S(2)}, u32[]{:S(2)}) collective-permute-start(f32[3,32,4,128]{3,2,1,0:T(4,128)S(1)} %get-tuple-element.27), channel_id=1, source_target_pairs={{0,1},{1,2},{2,3},{3,4},{4,5},{5,6},{6,7},{7,8},{8,9},{9,10},{10,1... | collective-permute-start | bytes 589832 | tf_op jit(solution)/shard_map/ppermute | solution.py:18
  5.3 5.6 %collective-permute-start.1 = (f32[3,32,4,128]{3,2,1,0:T(4,128)S(1)}, f32[3,32,4,128]{3,2,1,0:T(4,128)S(1)}, u32[]{:S(2)}, u32[]{:S(2)}) collective-permute-start(f32[3,32,4,128]{3,2,1,0:T(4,128)S(1)} %get-tuple-element.28), channel_id=1, source_target_pairs={{0,15},{1,0},{2,1},{3,2},{4,3},{5,4},{6,5},{7,6},{8,7},{9,8},{10,9... | collective-permute-start | bytes 589832 | tf_op jit(solution)/shard_map/ppermute | solution.py:18
  13.6 4.0 %collective-permute-start.2 = (f32[3,4,24,128]{3,2,1,0:T(8,128)S(1)}, f32[3,4,24,128]{3,2,1,0:T(8,128)S(1)}, u32[]{:S(2)}, u32[]{:S(2)}) collective-permute-start(f32[3,4,24,128]{3,2,1,0:T(8,128)S(1)} %get-tuple-element.25), channel_id=1, source_target_pairs={{0,16},{16,32},{32,48},{48,64},{64,80},{80,96},{96,112},{112,128},... | collective-permute-start | bytes 442376 | tf_op jit(solution)/shard_map/ppermute | solution.py:18
  17.6 3.0 %collective-permute-start.3 = (f32[3,4,24,128]{3,2,1,0:T(8,128)S(1)}, f32[3,4,24,128]{3,2,1,0:T(8,128)S(1)}, u32[]{:S(2)}, u32[]{:S(2)}) collective-permute-start(f32[3,4,24,128]{3,2,1,0:T(8,128)S(1)} %get-tuple-element.26), channel_id=1, source_target_pairs={{0,496},{16,0},{32,16},{48,32},{64,48},{80,64},{96,80},{112,96},{1... | collective-permute-start | bytes 442376 | tf_op jit(solution)/shard_map/ppermute | solution.py:18
  26.7 1.9 %collective-permute-start.4 = (f32[2,16,5,64]{3,2,1,0:T(8,128)S(1)}, f32[2,16,5,64]{3,2,1,0:T(8,128)S(1)}, u32[]{:S(2)}, u32[]{:S(2)}) collective-permute-start(f32[2,16,5,64]{3,2,1,0:T(8,128)S(1)} %get-tuple-element.83), channel_id=1, source_target_pairs={{0,1},{1,2},{2,3},{3,4},{4,5},{5,6},{6,7},{7,8},{8,9},{9,10},{10,1... | collective-permute-start | bytes 122888 | tf_op jit(solution)/shard_map/ppermute | solution.py:18
  28.6 7.4 %collective-permute-start.5 = (f32[2,16,5,64]{3,2,1,0:T(8,128)S(1)}, f32[2,16,5,64]{3,2,1,0:T(8,128)S(1)}, u32[]{:S(2)}, u32[]{:S(2)}) collective-permute-start(f32[2,16,5,64]{3,2,1,0:T(8,128)S(1)} %get-tuple-element.84), channel_id=1, source_target_pairs={{0,15},{1,0},{2,1},{3,2},{4,3},{5,4},{6,5},{7,6},{8,7},{9,8},{10,9... | collective-permute-start | bytes 122888 | tf_op jit(solution)/shard_map/ppermute | solution.py:18
  36.6 1.4 collective-permute-done.5
  39.2 4.4 %collective-permute-start.7 = (f32[2,5,18,64]{3,2,1,0:T(8,128)S(1)}, f32[2,5,18,64]{3,2,1,0:T(8,128)S(1)}, u32[]{:S(2)}, u32[]{:S(2)}) collective-permute-start(f32[2,5,18,64]{3,2,1,0:T(8,128)S(1)} %get-tuple-element.44), channel_id=1, source_target_pairs={{0,496},{16,0},{32,16},{48,32},{64,48},{80,64},{96,80},{112,96},{1... | collective-permute-start | bytes 138248 | tf_op jit(solution)/shard_map/ppermute | solution.py:18
  46.8 19.2 %all_gather.3 = f32[2,8,64,32]{3,1,0,2:T(8,128)S(1)} all-gather(f32[2,8,4,32]{3,1,0,2:T(8,128)S(1)} %copy.73), channel_id=1, replica_groups=mesh['row'=32,'col'=16] {'col'}, dimensions={2}, use_global_device_ids=true | all-gather | bytes 139264 | tf_op jit(solution)/shard_map/all_gather | solution.py:253
  67.5 1.3 copy.74
  68.8 2.1 %fusion.234 = (f32[4,1,64,32]{3,1,0,2:T(1,128)}, f32[4,1,64,32]{3,1,0,2:T(1,128)}) fusion(f32[4,2,64,32]{3,1,0,2:T(2,128)} %bitcast.192), kind=kLoop, calls=%fused_computation.431 | loop fusion | bytes 131072 | tf_op jit(solution)/shard_map/slice | solution.py:114
  70.9 1.6 %copy.100 = f32[4,1,64,32]{2,3,0,1:T(8,128)} copy(f32[4,1,64,32]{3,1,0,2:T(1,128)} %get-tuple-element.47) | data formatting | bytes 65536
  72.5 1.6 %copy.99 = f32[4,1,64,32]{2,3,0,1:T(8,128)} copy(f32[4,1,64,32]{3,1,0,2:T(1,128)} %get-tuple-element.48) | data formatting | bytes 65536
  74.8 3.8 %collective-permute-start.8 = (f32[2,4,64,32]{2,3,1,0:T(8,128)}, f32[2,4,64,32]{2,3,1,0:T(8,128)}, u32[]{:S(2)}, u32[]{:S(2)}) collective-permute-start(f32[2,4,64,32]{2,3,1,0:T(8,128)} %get-tuple-element.51), channel_id=1, source_target_pairs={{0,16},{16,32},{32,48},{48,64},{64,80},{80,96},{96,112},{112,128},... | collective-permute-start | bytes 196616 | tf_op jit(solution)/shard_map/ppermute | solution.py:18
  78.6 5.5 %collective-permute-start.9 = (f32[2,4,64,32]{2,3,1,0:T(8,128)}, f32[2,4,64,32]{2,3,1,0:T(8,128)}, u32[]{:S(2)}, u32[]{:S(2)}) collective-permute-start(f32[2,4,64,32]{2,3,1,0:T(8,128)} %get-tuple-element.52), channel_id=1, source_target_pairs={{0,496},{16,0},{32,16},{48,32},{64,48},{80,64},{96,80},{112,96},{1... | collective-permute-start | bytes 196616 | tf_op jit(solution)/shard_map/ppermute | solution.py:18
  86.0 1.5 copy.83
  93.9 3.0 %collective-permute-start.10 = (f32[2,4,512]{2,1,0:T(4,128)S(1)}, f32[2,4,512]{2,1,0:T(4,128)S(1)}, u32[]{:S(2)}, u32[]{:S(2)}) collective-permute-start(f32[2,4,512]{2,1,0:T(4,128)S(1)} %constant_dynamic-update-slice_fusion), channel_id=1, source_target_pairs={{0,496},{16,0},{32,16},{48,32},{64,48},{80,64},{96,80},{112,96},{1... | collective-permute-start | bytes 49160 | tf_op jit(solution)/shard_map/ppermute | solution.py:18
  96.9 3.2 %collective-permute-start.11 = (f32[2,4,512]{2,1,0:T(4,128)S(1)}, f32[2,4,512]{2,1,0:T(4,128)S(1)}, u32[]{:S(2)}, u32[]{:S(2)}) collective-permute-start(f32[2,4,512]{2,1,0:T(4,128)S(1)} %constant_dynamic-update-slice_fusion), channel_id=1, source_target_pairs={{0,480},{16,496},{32,0},{48,16},{64,32},{80,48},{96,64},{112,80},{... | collective-permute-start | bytes 49160 | tf_op jit(solution)/shard_map/ppermute | solution.py:18
  100.0 2.1 %collective-permute-start.13 = (f32[2,4,512]{2,1,0:T(4,128)S(1)}, f32[2,4,512]{2,1,0:T(4,128)S(1)}, u32[]{:S(2)}, u32[]{:S(2)}) collective-permute-start(f32[2,4,512]{2,1,0:T(4,128)S(1)} %constant_dynamic-update-slice_fusion), channel_id=1, source_target_pairs={{0,32},{16,48},{32,64},{48,80},{64,96},{80,112},{96,128},{112,144}... | collective-permute-start | bytes 49160 | tf_op jit(solution)/shard_map/ppermute | solution.py:18
  102.1 1.8 %collective-permute-start.14 = (f32[2,4,512]{2,1,0:T(4,128)S(1)}, f32[2,4,512]{2,1,0:T(4,128)S(1)}, u32[]{:S(2)}, u32[]{:S(2)}) collective-permute-start(f32[2,4,512]{2,1,0:T(4,128)S(1)} %constant_dynamic-update-slice_fusion), channel_id=1, source_target_pairs={{0,16},{16,32},{32,48},{48,64},{64,80},{80,96},{96,112},{112,128},... | collective-permute-start | bytes 49160 | tf_op jit(solution)/shard_map/ppermute | solution.py:18
  104.0 1.7 %collective-permute-done.13 = f32[2,4,512]{2,1,0:T(4,128)S(1)} collective-permute-done((f32[2,4,512]{2,1,0:T(4,128)S(1)}, f32[2,4,512]{2,1,0:T(4,128)S(1)}, u32[]{:S(2)}, u32[]{:S(2)}) %collective-permute-start.13) | collective-permute-done | bytes 16416 | tf_op jit(solution)/shard_map/ppermute | solution.py:18
  106.4 5.3 %collective-permute-start.12 = (f32[2,10,512]{2,1,0:T(8,128)}, f32[2,10,512]{2,1,0:T(8,128)}, u32[]{:S(2)}, u32[]{:S(2)}) collective-permute-start(f32[2,10,512]{2,1,0:T(8,128)} %get-tuple-element.86), channel_id=1, source_target_pairs={{0,80},{16,96},{32,112},{48,128},{64,144},{80,160},{96,176},{112,1... | collective-permute-start | bytes 122888 | tf_op jit(solution)/shard_map/ppermute | solution.py:18
  111.7 4.4 %collective-permute-start.15 = (f32[2,10,512]{2,1,0:T(8,128)}, f32[2,10,512]{2,1,0:T(8,128)}, u32[]{:S(2)}, u32[]{:S(2)}) collective-permute-start(f32[2,10,512]{2,1,0:T(8,128)} %get-tuple-element.85), channel_id=1, source_target_pairs={{0,432},{16,448},{32,464},{48,480},{64,496},{80,0},{96,16},{112,32... | collective-permute-start | bytes 122888 | tf_op jit(solution)/shard_map/ppermute | solution.py:18
  116.1 1.2 fusion.207
  117.3 1.9 %concatenate.194.refs_1_ = f32[2,20,512]{2,1,0:T(8,128)} concatenate(f32[2,4,512]{2,1,0:T(4,128)S(1)} %collective-permute-done.13, f32[2,4,512]{2,1,0:T(4,128)S(1)} %collective-permute-done.14, f32[2,4,512]{2,1,0:T(4,128)S(1)} %constant_dynamic-update-slice_fusion, f32[2,4,512]{2,1,0:T(4,128)S(1)} %collective-permute-done.10, f32[2,4,512]{2,1,0:T(4,128)S(1)} %collective-permute-done.11), dimensions={1} | concatenate | bytes 163840 | tf_op jit(solution)/shard_map/concatenate | solution.py:158
  119.6 4.5 %shard_map.37 = f32[8,512]{1,0:T(8,128)} custom-call(f32[2,10,512]{2,1,0:T(8,128)} %collective-permute-done.12.refs_0_, f32[2,20,512]{2,1,0:T(8,128)} %concatenate.194.refs_1_, f32[2,10,512]{2,1,0:T(8,128)} %collective-permute-done.15.refs_2_), custom_call_target="tpu_custom_call" | custom-call | flops 13107200 | bytes 491520 | tf_op jit(solution)/shard_map/pallas_call | solution.py:234
  124.1 1.5 dot_general.68
  125.6 1.4 fusion.223
  134.0 4.4 %collective-permute-done.17 = f32[2,64,32]{1,2,0:T(8,128)} collective-permute-done((f32[2,64,32]{1,2,0:T(8,128)}, f32[2,64,32]{1,2,0:T(8,128)}, u32[]{:S(2)}, u32[]{:S(2)}) %collective-permute-start.17) | collective-permute-done | bytes 16416 | tf_op jit(solution)/shard_map/ppermute | solution.py:18
  139.4 1.5 %fusion.67 = f32[12,8,64]{2,1,0:T(8,128)S(1)} fusion(s32[]{:T(128)S(6)} %select_n.80, f32[12,2,32]{1,2,0:T(8,128)S(1)} %get-tuple-element.60, f32[2,64,32]{1,2,0:T(8,128)} %collective-permute-done.17, f32[8,64,32]{1,2,0:T(8,128)S(1)} %fusion.143, f32[2,64,32]{1,2,0:T(8,128)} %collective-permute-done.16, f32[12,2,32]{1,2,0:T(8,128)S(1)} %get-tuple-element.59, ...), kind=kOutput, calls=%fused_computation.142 | convolution fusion | flops 2375680 | bytes 129604 | tf_op jit(solution)/shard_map/dot_general | solution.py:101
  145.8 1.3 fusion.42
  (250 shorter events, 36.8 us)
Async XLA Ops:
  0.0 13.5 %copy-start.21 = (f32[32,16,128]{2,1,0:T(8,128)S(1)}, f32[32,16,128]{2,1,0:T(8,128)}, u32[]{:S(2)}) copy-start(f32[32,16,128]{2,1,0:T(8,128)} %param.5) | copy-start | bytes 786436
  0.0 13.6 %copy-start.35 = (f32[32,16,128]{2,1,0:T(8,128)S(1)}, f32[32,16,128]{2,1,0:T(8,128)}, u32[]{:S(2)}) copy-start(f32[32,16,128]{2,1,0:T(8,128)} %param.3) | copy-start | bytes 786436
  0.0 13.6 %copy-start.34 = (f32[32,16,128]{2,1,0:T(8,128)S(1)}, f32[32,16,128]{2,1,0:T(8,128)}, u32[]{:S(2)}) copy-start(f32[32,16,128]{2,1,0:T(8,128)} %param.4) | copy-start | bytes 786436
  1.4 12.1 %collective-permute-start = (f32[3,32,4,128]{3,2,1,0:T(4,128)S(1)}, f32[3,32,4,128]{3,2,1,0:T(4,128)S(1)}, u32[]{:S(2)}, u32[]{:S(2)}) collective-permute-start(f32[3,32,4,128]{3,2,1,0:T(4,128)S(1)} %get-tuple-element.27), channel_id=1, source_target_pairs={{0,1},{1,2},{2,3},{3,4},{4,5},{5,6},{6,7},{7,8},{8,9},{9,10},{10,1... | collective-permute-start | bytes 589832 | tf_op jit(solution)/shard_map/ppermute | solution.py:18
  5.3 8.2 %collective-permute-start.1 = (f32[3,32,4,128]{3,2,1,0:T(4,128)S(1)}, f32[3,32,4,128]{3,2,1,0:T(4,128)S(1)}, u32[]{:S(2)}, u32[]{:S(2)}) collective-permute-start(f32[3,32,4,128]{3,2,1,0:T(4,128)S(1)} %get-tuple-element.28), channel_id=1, source_target_pairs={{0,15},{1,0},{2,1},{3,2},{4,3},{5,4},{6,5},{7,6},{8,7},{9,8},{10,9... | collective-permute-start | bytes 589832 | tf_op jit(solution)/shard_map/ppermute | solution.py:18
  11.0 15.2 %copy-start.55 = (s32[128]{0:T(128)}, s32[128]{0:T(128)S(1)}, u32[]{:S(2)}) copy-start(s32[128]{0:T(128)S(1)} %get-tuple-element.88) | copy-start | bytes 1540
  11.0 15.2 %copy-start.57 = (s32[128]{0:T(128)}, s32[128]{0:T(128)S(1)}, u32[]{:S(2)}) copy-start(s32[128]{0:T(128)S(1)} %get-tuple-element.89) | copy-start | bytes 1540
  11.0 15.2 %copy-start.59 = (pred[128]{0:T(512)(128)(4,1)}, pred[128]{0:T(512)(128)(4,1)S(1)}, u32[]{:S(2)}) copy-start(pred[128]{0:T(512)(128)(4,1)S(1)} %compare_and_fusion.3) | copy-start | bytes 388
  11.1 35.3 %copy-start.50 = (s32[64]{0:T(128)}, s32[64]{0:T(128)S(1)}, u32[]{:S(2)}) copy-start(s32[64]{0:T(128)S(1)} %get-tuple-element.92) | copy-start | bytes 772
  11.1 35.3 %copy-start.51 = (s32[64]{0:T(128)}, s32[64]{0:T(128)S(1)}, u32[]{:S(2)}) copy-start(s32[64]{0:T(128)S(1)} %get-tuple-element.93) | copy-start | bytes 772
  11.1 35.3 %copy-start.52 = (pred[64]{0:T(512)(128)(4,1)}, pred[64]{0:T(512)(128)(4,1)S(1)}, u32[]{:S(2)}) copy-start(pred[64]{0:T(512)(128)(4,1)S(1)} %compare_and_fusion.1) | copy-start | bytes 196
  13.6 7.9 %collective-permute-start.2 = (f32[3,4,24,128]{3,2,1,0:T(8,128)S(1)}, f32[3,4,24,128]{3,2,1,0:T(8,128)S(1)}, u32[]{:S(2)}, u32[]{:S(2)}) collective-permute-start(f32[3,4,24,128]{3,2,1,0:T(8,128)S(1)} %get-tuple-element.25), channel_id=1, source_target_pairs={{0,16},{16,32},{32,48},{48,64},{64,80},{80,96},{96,112},{112,128},... | collective-permute-start | bytes 442376 | tf_op jit(solution)/shard_map/ppermute | solution.py:18
  17.6 4.6 %collective-permute-start.3 = (f32[3,4,24,128]{3,2,1,0:T(8,128)S(1)}, f32[3,4,24,128]{3,2,1,0:T(8,128)S(1)}, u32[]{:S(2)}, u32[]{:S(2)}) collective-permute-start(f32[3,4,24,128]{3,2,1,0:T(8,128)S(1)} %get-tuple-element.26), channel_id=1, source_target_pairs={{0,496},{16,0},{32,16},{48,32},{64,48},{80,64},{96,80},{112,96},{1... | collective-permute-start | bytes 442376 | tf_op jit(solution)/shard_map/ppermute | solution.py:18
  26.7 9.9 %collective-permute-start.4 = (f32[2,16,5,64]{3,2,1,0:T(8,128)S(1)}, f32[2,16,5,64]{3,2,1,0:T(8,128)S(1)}, u32[]{:S(2)}, u32[]{:S(2)}) collective-permute-start(f32[2,16,5,64]{3,2,1,0:T(8,128)S(1)} %get-tuple-element.83), channel_id=1, source_target_pairs={{0,1},{1,2},{2,3},{3,4},{4,5},{5,6},{6,7},{7,8},{8,9},{9,10},{10,1... | collective-permute-start | bytes 122888 | tf_op jit(solution)/shard_map/ppermute | solution.py:18
  28.6 9.4 %collective-permute-start.5 = (f32[2,16,5,64]{3,2,1,0:T(8,128)S(1)}, f32[2,16,5,64]{3,2,1,0:T(8,128)S(1)}, u32[]{:S(2)}, u32[]{:S(2)}) collective-permute-start(f32[2,16,5,64]{3,2,1,0:T(8,128)S(1)} %get-tuple-element.84), channel_id=1, source_target_pairs={{0,15},{1,0},{2,1},{3,2},{4,3},{5,4},{6,5},{7,6},{8,7},{9,8},{10,9... | collective-permute-start | bytes 122888 | tf_op jit(solution)/shard_map/ppermute | solution.py:18
  38.0 6.4 %collective-permute-start.6 = (f32[2,5,18,64]{3,2,1,0:T(8,128)S(1)}, f32[2,5,18,64]{3,2,1,0:T(8,128)S(1)}, u32[]{:S(2)}, u32[]{:S(2)}) collective-permute-start(f32[2,5,18,64]{3,2,1,0:T(8,128)S(1)} %get-tuple-element.43), channel_id=1, source_target_pairs={{0,16},{16,32},{32,48},{48,64},{64,80},{80,96},{96,112},{112,128},... | collective-permute-start | bytes 138248 | tf_op jit(solution)/shard_map/ppermute | solution.py:18
  39.2 5.4 %collective-permute-start.7 = (f32[2,5,18,64]{3,2,1,0:T(8,128)S(1)}, f32[2,5,18,64]{3,2,1,0:T(8,128)S(1)}, u32[]{:S(2)}, u32[]{:S(2)}) collective-permute-start(f32[2,5,18,64]{3,2,1,0:T(8,128)S(1)} %get-tuple-element.44), channel_id=1, source_target_pairs={{0,496},{16,0},{32,16},{48,32},{64,48},{80,64},{96,80},{112,96},{1... | collective-permute-start | bytes 138248 | tf_op jit(solution)/shard_map/ppermute | solution.py:18
  43.6 40.6 %copy-start.53 = (pred[32]{0:T(512)(128)(4,1)}, pred[32]{0:T(512)(128)(4,1)S(1)}, u32[]{:S(2)}) copy-start(pred[32]{0:T(512)(128)(4,1)S(1)} %compare_and_fusion) | copy-start | bytes 100
  45.8 20.2 %copy-start.18 = (f32[22,14,64]{2,1,0:T(8,128)}, f32[22,14,64]{2,1,0:T(8,128)S(1)}, u32[]{:S(2)}) copy-start(f32[22,14,64]{2,1,0:T(8,128)S(1)} %fusion.86) | copy-start | bytes 236548
  68.8 20.7 %copy-start.15 = (f32[2,8,64,32]{2,3,1,0:T(8,128)}, f32[2,8,64,32]{2,3,1,0:T(8,128)S(1)}, u32[]{:S(2)}) copy-start(f32[2,8,64,32]{2,3,1,0:T(8,128)S(1)} %copy.74) | copy-start | bytes 393220
  74.8 13.6 %collective-permute-start.8 = (f32[2,4,64,32]{2,3,1,0:T(8,128)}, f32[2,4,64,32]{2,3,1,0:T(8,128)}, u32[]{:S(2)}, u32[]{:S(2)}) collective-permute-start(f32[2,4,64,32]{2,3,1,0:T(8,128)} %get-tuple-element.51), channel_id=1, source_target_pairs={{0,16},{16,32},{32,48},{48,64},{64,80},{80,96},{96,112},{112,128},... | collective-permute-start | bytes 196616 | tf_op jit(solution)/shard_map/ppermute | solution.py:18
  78.6 9.8 %collective-permute-start.9 = (f32[2,4,64,32]{2,3,1,0:T(8,128)}, f32[2,4,64,32]{2,3,1,0:T(8,128)}, u32[]{:S(2)}, u32[]{:S(2)}) collective-permute-start(f32[2,4,64,32]{2,3,1,0:T(8,128)} %get-tuple-element.52), channel_id=1, source_target_pairs={{0,496},{16,0},{32,16},{48,32},{64,48},{80,64},{96,80},{112,96},{1... | collective-permute-start | bytes 196616 | tf_op jit(solution)/shard_map/ppermute | solution.py:18
  89.6 38.6 %copy-start.46 = (f32[14,64,1]{1,2,0:T(1,128)}, f32[14,64,1]{1,2,0:T(1,128)S(1)}, u32[]{:S(2)}) copy-start(f32[14,64,1]{1,2,0:T(1,128)S(1)} %get-tuple-element.57) | copy-start | bytes 10756
  89.6 38.6 %copy-start.47 = (f32[14,64,1]{1,2,0:T(1,128)}, f32[14,64,1]{1,2,0:T(1,128)S(1)}, u32[]{:S(2)}) copy-start(f32[14,64,1]{1,2,0:T(1,128)S(1)} %get-tuple-element.58) | copy-start | bytes 10756
  93.9 10.1 %collective-permute-start.10 = (f32[2,4,512]{2,1,0:T(4,128)S(1)}, f32[2,4,512]{2,1,0:T(4,128)S(1)}, u32[]{:S(2)}, u32[]{:S(2)}) collective-permute-start(f32[2,4,512]{2,1,0:T(4,128)S(1)} %constant_dynamic-update-slice_fusion), channel_id=1, source_target_pairs={{0,496},{16,0},{32,16},{48,32},{64,48},{80,64},{96,80},{112,96},{1... | collective-permute-start | bytes 49160 | tf_op jit(solution)/shard_map/ppermute | solution.py:18
  96.9 7.1 %collective-permute-start.11 = (f32[2,4,512]{2,1,0:T(4,128)S(1)}, f32[2,4,512]{2,1,0:T(4,128)S(1)}, u32[]{:S(2)}, u32[]{:S(2)}) collective-permute-start(f32[2,4,512]{2,1,0:T(4,128)S(1)} %constant_dynamic-update-slice_fusion), channel_id=1, source_target_pairs={{0,480},{16,496},{32,0},{48,16},{64,32},{80,48},{96,64},{112,80},{... | collective-permute-start | bytes 49160 | tf_op jit(solution)/shard_map/ppermute | solution.py:18
  100.0 5.7 %collective-permute-start.13 = (f32[2,4,512]{2,1,0:T(4,128)S(1)}, f32[2,4,512]{2,1,0:T(4,128)S(1)}, u32[]{:S(2)}, u32[]{:S(2)}) collective-permute-start(f32[2,4,512]{2,1,0:T(4,128)S(1)} %constant_dynamic-update-slice_fusion), channel_id=1, source_target_pairs={{0,32},{16,48},{32,64},{48,80},{64,96},{80,112},{96,128},{112,144}... | collective-permute-start | bytes 49160 | tf_op jit(solution)/shard_map/ppermute | solution.py:18
  102.1 3.6 %collective-permute-start.14 = (f32[2,4,512]{2,1,0:T(4,128)S(1)}, f32[2,4,512]{2,1,0:T(4,128)S(1)}, u32[]{:S(2)}, u32[]{:S(2)}) collective-permute-start(f32[2,4,512]{2,1,0:T(4,128)S(1)} %constant_dynamic-update-slice_fusion), channel_id=1, source_target_pairs={{0,16},{16,32},{32,48},{48,64},{64,80},{80,96},{96,112},{112,128},... | collective-permute-start | bytes 49160 | tf_op jit(solution)/shard_map/ppermute | solution.py:18
  106.4 12.8 %collective-permute-start.12 = (f32[2,10,512]{2,1,0:T(8,128)}, f32[2,10,512]{2,1,0:T(8,128)}, u32[]{:S(2)}, u32[]{:S(2)}) collective-permute-start(f32[2,10,512]{2,1,0:T(8,128)} %get-tuple-element.86), channel_id=1, source_target_pairs={{0,80},{16,96},{32,112},{48,128},{64,144},{80,160},{96,176},{112,1... | collective-permute-start | bytes 122888 | tf_op jit(solution)/shard_map/ppermute | solution.py:18
  111.7 7.9 %collective-permute-start.15 = (f32[2,10,512]{2,1,0:T(8,128)}, f32[2,10,512]{2,1,0:T(8,128)}, u32[]{:S(2)}, u32[]{:S(2)}) collective-permute-start(f32[2,10,512]{2,1,0:T(8,128)} %get-tuple-element.85), channel_id=1, source_target_pairs={{0,432},{16,448},{32,464},{48,480},{64,496},{80,0},{96,16},{112,32... | collective-permute-start | bytes 122888 | tf_op jit(solution)/shard_map/ppermute | solution.py:18
  131.2 2.8 %collective-permute-start.16 = (f32[2,64,32]{1,2,0:T(8,128)}, f32[2,64,32]{1,2,0:T(8,128)}, u32[]{:S(2)}, u32[]{:S(2)}) collective-permute-start(f32[2,64,32]{1,2,0:T(8,128)} %get-tuple-element.81), channel_id=1, source_target_pairs={{0,16},{16,32},{32,48},{48,64},{64,80},{80,96},{96,112},{112,128},... | collective-permute-start | bytes 49160 | tf_op jit(solution)/shard_map/ppermute | solution.py:18
  132.4 6.0 %collective-permute-start.17 = (f32[2,64,32]{1,2,0:T(8,128)}, f32[2,64,32]{1,2,0:T(8,128)}, u32[]{:S(2)}, u32[]{:S(2)}) collective-permute-start(f32[2,64,32]{1,2,0:T(8,128)} %get-tuple-element.82), channel_id=1, source_target_pairs={{0,496},{16,0},{32,16},{48,32},{64,48},{80,64},{96,80},{112,96},{1... | collective-permute-start | bytes 49160 | tf_op jit(solution)/shard_map/ppermute | solution.py:18
  (53 other events, 101.3 us)

commit v6 on v5

--- a/solution.py
+++ b/solution.py
@@ -129,6 +129,31 @@
     return jnp.concatenate([a[:, -w:], a, a[:, :w]], axis=1)
 
 
+def faces_band(k, scale):
+    c = k[1:-1]
+    west_x = harmonic(k[:-2], c, scale)
+    east_x = harmonic(c, k[2:], scale)
+    west_y = harmonic(jnp.roll(c, 1, axis=2), c, scale)
+    east_y = harmonic(c, jnp.roll(c, -1, axis=2), scale)
+    inner = harmonic(c[:, :-1], c[:, 1:], scale)
+    below = jnp.concatenate([2.0 * c[:, :1] * scale, inner], axis=1)
+    above = jnp.concatenate([inner, 2.0 * c[:, -1:] * scale], axis=1)
+    diagonal = west_x + east_x + west_y + east_y + below + above
+    return (west_x, east_x, west_y, east_y, below, above, diagonal)
+
+
+def apply_band(v, faces):
+    west_x, east_x, west_y, east_y, below, above, diagonal = faces
+    c = v[1:-1]
+    zero_plane = jnp.zeros_like(c[:, :1])
+    under = jnp.concatenate([zero_plane, c[:, :-1]], axis=1)
+    over = jnp.concatenate([c[:, 1:], zero_plane], axis=1)
+    beside_all = west_x * v[:-2] + east_x * v[2:]
+    beside_all = beside_all + west_y * jnp.roll(c, 1, axis=2) + east_y * jnp.roll(c, -1, axis=2)
+    beside_all = beside_all + below * under + above * over
+    return diagonal * c - beside_all
+
+
 class Band(Level):
     def faces_at(self, h, y=False):
         return super().faces_at(h, False)
@@ -138,11 +163,11 @@
 
     def sweep(self, v, h):
         faces = self.faces_at(h)
-        residual = self.rhs_at(h) - apply_operator(wrap_y(v), faces)
+        residual = self.rhs_at(h) - apply_band(v, faces)
         return v[1:-1] + OMEGA * residual / faces[6]
 
     def residual(self, v):
-        return self.rhs_at(0) - apply_operator(wrap_y(v), self.faces_at(0))
+        return self.rhs_at(0) - apply_band(v, self.faces_at(0))
 
 
 def x_halo(x, w):
@@ -158,7 +183,7 @@
     return jnp.concatenate(lower + [x] + upper, axis=axis)
 
 
-def coarse_kernel(scale, size_z, spans, keep, lower_ref, own_ref, upper_ref, out_ref, tile_ref):
+def coarse_kernel(scale, size_y, spans, keep, lower_ref, own_ref, upper_ref, out_ref, tile_ref):
     span, extra = spans
     for f in range(2):
         tile_ref[f, 0:extra] = lower_ref[f]
@@ -167,8 +192,9 @@
     b = tile_ref[0]
     k = tile_ref[1]
     rows, lanes = k.shape
-    lane = lax.broadcasted_iota(jnp.int32, (rows, lanes), 1) % size_z
-    first, last = lane == 0, lane == size_z - 1
+    lane = lax.broadcasted_iota(jnp.int32, (rows, lanes), 1)
+    first, last = lane < size_y, lane >= lanes - size_y
+    y_first, y_last = lane % size_y == 0, lane % size_y == size_y - 1
 
     def x_lower(a):
         return pltpu.roll(a, 1, 0)
@@ -177,16 +203,16 @@
         return pltpu.roll(a, rows - 1, 0)
 
     def y_lower(a):
-        return pltpu.roll(a, size_z, 1)
+        return jnp.where(y_first, pltpu.roll(a, lanes - (size_y - 1), 1), pltpu.roll(a, 1, 1))
 
     def y_upper(a):
-        return pltpu.roll(a, lanes - size_z, 1)
+        return jnp.where(y_last, pltpu.roll(a, size_y - 1, 1), pltpu.roll(a, lanes - 1, 1))
 
     def z_lower(a):
-        return pltpu.roll(a, 1, 1)
+        return pltpu.roll(a, size_y, 1)
 
     def z_upper(a):
-        return pltpu.roll(a, lanes - 1, 1)
+        return pltpu.roll(a, lanes - size_y, 1)
 
     west_x = harmonic(x_lower(k), k, scale)
     east_x = harmonic(k, x_upper(k), scale)
@@ -210,7 +236,7 @@
 
 
 def coarse_solve(right_side, perm, scale):
-    size_x, size_y, size_z = right_side.shape
+    size_x, size_z, size_y = right_side.shape
     lanes = size_y * size_z
     pair = jnp.stack([right_side, perm]).reshape(2, size_x, lanes)
     near = rows_around(pair, (1, 2), 1)
@@ -224,7 +250,7 @@
     lower = shift_from(near[:, span - extra :], "row", 5)
     upper = shift_from(near[:, :extra], "row", -5)
     call = pl.pallas_call(
-        lambda *refs: coarse_kernel(scale, size_z, (span, extra), keep, *refs),
+        lambda *refs: coarse_kernel(scale, size_y, (span, extra), keep, *refs),
         out_shape=jax.ShapeDtypeStruct((keep, lanes), jnp.float32),
         scratch_shapes=[pltpu.VMEM((2, rows, lanes), jnp.float32)],
         cost_estimate=pl.CostEstimate(
@@ -232,7 +258,7 @@
         ),
     )
     v = call(lower, near, upper)
-    return v.reshape(keep, size_y, size_z)
+    return v.reshape(keep, size_z, size_y)
 
 
 def on_device(pressure_in, source, permeability):
@@ -250,9 +276,10 @@
     rhs = coarsen(lev1.residual(trim(s1, 2)))
     perm = coarsen(perm)
     size_y2 = rhs.shape[1]
-    band = lax.all_gather(jnp.stack([perm, rhs]), "col", axis=2, tiled=True)
+    block = jnp.swapaxes(jnp.stack([perm, rhs]), 2, 3)
+    band = lax.all_gather(block, "col", axis=3, tiled=True)
     k2, b2 = x_halo(band, 4)
-    lev2 = Band(faces_of(wrap_y(k2), scales[2]), 3, b2, 4)
+    lev2 = Band(faces_band(k2, scales[2]), 3, b2, 4)
     p = lev2.first_sweep(3)
     s2 = lev2.sweep(p, 2)
     rhs = coarsen(lev2.residual(s2[1:-1]))
@@ -261,9 +288,11 @@
     q = s2 + prolong(correction)[2:-2]
     q = lev2.sweep(q, 1)
     u2 = lev2.sweep(q, 0)
-    u2 = wrap_y(x_halo(u2, 2), 2)
+    u2 = x_halo(u2, 2)
+    u2 = jnp.concatenate([u2[..., -2:], u2, u2[..., :2]], axis=2)
     col = lax.axis_index("col")
-    u2 = lax.dynamic_slice_in_dim(u2, col * size_y2, size_y2 + 4, axis=1)
+    u2 = lax.dynamic_slice_in_dim(u2, col * size_y2, size_y2 + 4, axis=2)
+    u2 = jnp.swapaxes(u2, 1, 2)
     q = s1 + trim(prolong(u2), 1)
     q = lev1.sweep(q, 2)
     u1 = lev1.sweep(q, 1)

time: 148 us -> 148 us (level)
  starting transfers between devices: 62.4 us -> 65.4 us
  matrix products: 10.8 us -> 8.48 us
  local copies, waits for them, and re-layouts: 20.7 us -> 18.4 us
    ppermute x18, starting transfers between devices: 62.4 us -> 65.4 us  [shift_from(): return lax.ppermute(x, axis, [(i, (i + k) % n) for i in range(n)])]
    mul x2 -> x0, local copies, waits for them, and re-layouts: 2.29 us -> none  [coarsen(): return t * 0.125]
    concatenate x0 -> x1, other arithmetic: none -> 1.94 us  [on_device(): u2 = jnp.concatenate([u2[..., -2:], u2, u2[..., :2]], axis=2)]
    unnamed x137 -> x138, local copies, waits for them, and re-layouts: 6.56 us -> 8.22 us
  transfers between devices with their start and end apart: 18 -> 18, of which waited for: 10 -> 11; matrix products, arithmetic and copies ran while one was open for 7% -> 5% of each run, Pallas kernels for 0% -> 0%
where the time goes in v6:
time: 148 us; the launch traced here: 147 us
  starting transfers between devices  65.4 us (44%)
  blocking collectives  19.2 us (13%)
  local copies, waits for them, and re-layouts  18.4 us (12%)
  other arithmetic  18.2 us (12%)
  waiting for transfers between devices  11 us (7%)
  matrix products  8.48 us (6%)
  Pallas kernels  5.3 us (4%)
    ppermute x18, starting transfers between devices, shift_from(): return lax.ppermute(x, axis, [(i, (i + k) % n) for i in range(n)])  65.4 us
    all_gather x1, blocking collectives, on_device(): band = lax.all_gather(block, 'col', axis=3, tiled=True)  19.2 us
    ppermute x18, waiting for transfers between devices, shift_from(): return lax.ppermute(x, axis, [(i, (i + k) % n) for i in range(n)])  11 us
    unnamed x138, local copies, waits for them, and re-layouts  8.22 us
    pallas_call x1, Pallas kernels, coarse_solve(): v = call(lower, near, upper)  5.3 us
    dot_general x9, matrix products, along_z(): out = jnp.dot(flat, matrix, precision=lax.Precision.HIGHEST)  5.22 us
    add x6, other arithmetic, sweep(): return v[1:-1, 1:-1] + OMEGA * residual / faces[6]  4.48 us
  transfers between devices with their start and end apart: 18, of which 11 were waited for; matrix products, arithmetic and copies ran while one was open for 5% of the time, Pallas kernels for 0%

profile of v6, /device:TPU:1, one launch (start us, length us, event | category | flops | bytes accessed | tf_op | source)
XLA Modules:
  0.0 147.3 jit_solution(16655342909043347631)
XLA Ops:
  0.0 1.3 pad_maximum_fusion.11
  1.4 3.9 %collective-permute-start = (f32[3,32,4,128]{3,2,1,0:T(4,128)S(1)}, f32[3,32,4,128]{3,2,1,0:T(4,128)S(1)}, u32[]{:S(2)}, u32[]{:S(2)}) collective-permute-start(f32[3,32,4,128]{3,2,1,0:T(4,128)S(1)} %get-tuple-element.27), channel_id=1, source_target_pairs={{0,1},{1,2},{2,3},{3,4},{4,5},{5,6},{6,7},{7,8},{8,9},{9,10},{10,1... | collective-permute-start | bytes 589832 | tf_op jit(solution)/shard_map/ppermute | solution.py:18
  5.3 5.6 %collective-permute-start.1 = (f32[3,32,4,128]{3,2,1,0:T(4,128)S(1)}, f32[3,32,4,128]{3,2,1,0:T(4,128)S(1)}, u32[]{:S(2)}, u32[]{:S(2)}) collective-permute-start(f32[3,32,4,128]{3,2,1,0:T(4,128)S(1)} %get-tuple-element.28), channel_id=1, source_target_pairs={{0,15},{1,0},{2,1},{3,2},{4,3},{5,4},{6,5},{7,6},{8,7},{9,8},{10,9... | collective-permute-start | bytes 589832 | tf_op jit(solution)/shard_map/ppermute | solution.py:18
  11.2 1.2 fusion.147
  13.6 4.0 %collective-permute-start.2 = (f32[3,4,24,128]{3,2,1,0:T(8,128)S(1)}, f32[3,4,24,128]{3,2,1,0:T(8,128)S(1)}, u32[]{:S(2)}, u32[]{:S(2)}) collective-permute-start(f32[3,4,24,128]{3,2,1,0:T(8,128)S(1)} %get-tuple-element.25), channel_id=1, source_target_pairs={{0,16},{16,32},{32,48},{48,64},{64,80},{80,96},{96,112},{112,128},... | collective-permute-start | bytes 442376 | tf_op jit(solution)/shard_map/ppermute | solution.py:18
  17.7 3.0 %collective-permute-start.3 = (f32[3,4,24,128]{3,2,1,0:T(8,128)S(1)}, f32[3,4,24,128]{3,2,1,0:T(8,128)S(1)}, u32[]{:S(2)}, u32[]{:S(2)}) collective-permute-start(f32[3,4,24,128]{3,2,1,0:T(8,128)S(1)} %get-tuple-element.26), channel_id=1, source_target_pairs={{0,496},{16,0},{32,16},{48,32},{64,48},{80,64},{96,80},{112,96},{1... | collective-permute-start | bytes 442376 | tf_op jit(solution)/shard_map/ppermute | solution.py:18
  26.7 1.9 %collective-permute-start.4 = (f32[2,16,5,64]{3,2,1,0:T(8,128)S(1)}, f32[2,16,5,64]{3,2,1,0:T(8,128)S(1)}, u32[]{:S(2)}, u32[]{:S(2)}) collective-permute-start(f32[2,16,5,64]{3,2,1,0:T(8,128)S(1)} %get-tuple-element.93), channel_id=1, source_target_pairs={{0,1},{1,2},{2,3},{3,4},{4,5},{5,6},{6,7},{7,8},{8,9},{9,10},{10,1... | collective-permute-start | bytes 122888 | tf_op jit(solution)/shard_map/ppermute | solution.py:18
  28.6 7.4 %collective-permute-start.5 = (f32[2,16,5,64]{3,2,1,0:T(8,128)S(1)}, f32[2,16,5,64]{3,2,1,0:T(8,128)S(1)}, u32[]{:S(2)}, u32[]{:S(2)}) collective-permute-start(f32[2,16,5,64]{3,2,1,0:T(8,128)S(1)} %get-tuple-element.94), channel_id=1, source_target_pairs={{0,15},{1,0},{2,1},{3,2},{4,3},{5,4},{6,5},{7,6},{8,7},{9,8},{10,9... | collective-permute-start | bytes 122888 | tf_op jit(solution)/shard_map/ppermute | solution.py:18
  36.5 1.5 %collective-permute-done.5 = f32[2,16,5,64]{3,2,1,0:T(8,128)S(1)} collective-permute-done((f32[2,16,5,64]{3,2,1,0:T(8,128)S(1)}, f32[2,16,5,64]{3,2,1,0:T(8,128)S(1)}, u32[]{:S(2)}, u32[]{:S(2)}) %collective-permute-start.5) | collective-permute-done | bytes 40992 | tf_op jit(solution)/shard_map/ppermute | solution.py:18
  38.0 1.2 collective-permute-start.6
  39.2 4.4 %collective-permute-start.7 = (f32[2,5,18,64]{3,2,1,0:T(8,128)S(1)}, f32[2,5,18,64]{3,2,1,0:T(8,128)S(1)}, u32[]{:S(2)}, u32[]{:S(2)}) collective-permute-start(f32[2,5,18,64]{3,2,1,0:T(8,128)S(1)} %get-tuple-element.44), channel_id=1, source_target_pairs={{0,496},{16,0},{32,16},{48,32},{64,48},{80,64},{96,80},{112,96},{1... | collective-permute-start | bytes 138248 | tf_op jit(solution)/shard_map/ppermute | solution.py:18
  46.8 19.2 %all_gather.3 = f32[2,8,32,64]{2,1,0,3:T(8,128)S(1)} all-gather(f32[2,8,32,4]{2,1,0,3:T(8,128)S(1)} %copy.21), channel_id=1, replica_groups=mesh['row'=32,'col'=16] {'col'}, dimensions={3}, use_global_device_ids=true | all-gather | bytes 139264 | tf_op jit(solution)/shard_map/all_gather | solution.py:280
  67.5 1.3 copy.22
  68.8 2.1 %fusion.218 = (f32[4,1,32,64]{2,1,0,3:T(1,128)}, f32[4,1,32,64]{2,1,0,3:T(1,128)}) fusion(f32[4,2,32,64]{2,1,0,3:T(2,128)} %bitcast.193), kind=kLoop, calls=%fused_computation.414 | loop fusion | bytes 131072 | tf_op jit(solution)/shard_map/slice | solution.py:114
  70.9 1.6 %copy.41 = f32[4,1,32,64]{3,2,0,1:T(8,128)} copy(f32[4,1,32,64]{2,1,0,3:T(1,128)} %get-tuple-element.48) | data formatting | bytes 65536
  72.5 1.6 %copy.42 = f32[4,1,32,64]{3,2,0,1:T(8,128)} copy(f32[4,1,32,64]{2,1,0,3:T(1,128)} %get-tuple-element.47) | data formatting | bytes 65536
  74.8 3.8 %collective-permute-start.8 = (f32[2,4,32,64]{3,2,1,0:T(8,128)}, f32[2,4,32,64]{3,2,1,0:T(8,128)}, u32[]{:S(2)}, u32[]{:S(2)}) collective-permute-start(f32[2,4,32,64]{3,2,1,0:T(8,128)} %get-tuple-element.49), channel_id=1, source_target_pairs={{0,16},{16,32},{32,48},{48,64},{64,80},{80,96},{96,112},{112,128},... | collective-permute-start | bytes 196616 | tf_op jit(solution)/shard_map/ppermute | solution.py:18
  78.6 5.5 %collective-permute-start.9 = (f32[2,4,32,64]{3,2,1,0:T(8,128)}, f32[2,4,32,64]{3,2,1,0:T(8,128)}, u32[]{:S(2)}, u32[]{:S(2)}) collective-permute-start(f32[2,4,32,64]{3,2,1,0:T(8,128)} %get-tuple-element.50), channel_id=1, source_target_pairs={{0,496},{16,0},{32,16},{48,32},{64,48},{80,64},{96,80},{112,96},{1... | collective-permute-start | bytes 196616 | tf_op jit(solution)/shard_map/ppermute | solution.py:18
  89.7 4.6 %collective-permute-start.10 = (f32[2,4,512]{2,1,0:T(4,128)S(1)}, f32[2,4,512]{2,1,0:T(4,128)S(1)}, u32[]{:S(2)}, u32[]{:S(2)}) collective-permute-start(f32[2,4,512]{2,1,0:T(4,128)S(1)} %constant_dynamic-update-slice_fusion), channel_id=1, source_target_pairs={{0,496},{16,0},{32,16},{48,32},{64,48},{80,64},{96,80},{112,96},{1... | collective-permute-start | bytes 49160 | tf_op jit(solution)/shard_map/ppermute | solution.py:18
  94.3 4.5 %collective-permute-start.11 = (f32[2,4,512]{2,1,0:T(4,128)S(1)}, f32[2,4,512]{2,1,0:T(4,128)S(1)}, u32[]{:S(2)}, u32[]{:S(2)}) collective-permute-start(f32[2,4,512]{2,1,0:T(4,128)S(1)} %constant_dynamic-update-slice_fusion), channel_id=1, source_target_pairs={{0,480},{16,496},{32,0},{48,16},{64,32},{80,48},{96,64},{112,80},{... | collective-permute-start | bytes 49160 | tf_op jit(solution)/shard_map/ppermute | solution.py:18
  98.8 1.9 %collective-permute-start.13 = (f32[2,4,512]{2,1,0:T(4,128)S(1)}, f32[2,4,512]{2,1,0:T(4,128)S(1)}, u32[]{:S(2)}, u32[]{:S(2)}) collective-permute-start(f32[2,4,512]{2,1,0:T(4,128)S(1)} %constant_dynamic-update-slice_fusion), channel_id=1, source_target_pairs={{0,32},{16,48},{32,64},{48,80},{64,96},{80,112},{96,128},{112,144}... | collective-permute-start | bytes 49160 | tf_op jit(solution)/shard_map/ppermute | solution.py:18
  100.7 2.0 %collective-permute-start.14 = (f32[2,4,512]{2,1,0:T(4,128)S(1)}, f32[2,4,512]{2,1,0:T(4,128)S(1)}, u32[]{:S(2)}, u32[]{:S(2)}) collective-permute-start(f32[2,4,512]{2,1,0:T(4,128)S(1)} %constant_dynamic-update-slice_fusion), channel_id=1, source_target_pairs={{0,16},{16,32},{32,48},{48,64},{64,80},{80,96},{96,112},{112,128},... | collective-permute-start | bytes 49160 | tf_op jit(solution)/shard_map/ppermute | solution.py:18
  102.7 1.7 %collective-permute-done.13 = f32[2,4,512]{2,1,0:T(4,128)S(1)} collective-permute-done((f32[2,4,512]{2,1,0:T(4,128)S(1)}, f32[2,4,512]{2,1,0:T(4,128)S(1)}, u32[]{:S(2)}, u32[]{:S(2)}) %collective-permute-start.13) | collective-permute-done | bytes 16416 | tf_op jit(solution)/shard_map/ppermute | solution.py:18
  105.2 5.3 %collective-permute-start.12 = (f32[2,10,512]{2,1,0:T(8,128)}, f32[2,10,512]{2,1,0:T(8,128)}, u32[]{:S(2)}, u32[]{:S(2)}) collective-permute-start(f32[2,10,512]{2,1,0:T(8,128)} %get-tuple-element.96), channel_id=1, source_target_pairs={{0,80},{16,96},{32,112},{48,128},{64,144},{80,160},{96,176},{112,1... | collective-permute-start | bytes 122888 | tf_op jit(solution)/shard_map/ppermute | solution.py:18
  110.5 4.4 %collective-permute-start.15 = (f32[2,10,512]{2,1,0:T(8,128)}, f32[2,10,512]{2,1,0:T(8,128)}, u32[]{:S(2)}, u32[]{:S(2)}) collective-permute-start(f32[2,10,512]{2,1,0:T(8,128)} %get-tuple-element.95), channel_id=1, source_target_pairs={{0,432},{16,448},{32,464},{48,480},{64,496},{80,0},{96,16},{112,32... | collective-permute-start | bytes 122888 | tf_op jit(solution)/shard_map/ppermute | solution.py:18
  115.5 1.9 %concatenate.197.refs_1_ = f32[2,20,512]{2,1,0:T(8,128)} concatenate(f32[2,4,512]{2,1,0:T(4,128)S(1)} %collective-permute-done.13, f32[2,4,512]{2,1,0:T(4,128)S(1)} %collective-permute-done.14, f32[2,4,512]{2,1,0:T(4,128)S(1)} %constant_dynamic-update-slice_fusion, f32[2,4,512]{2,1,0:T(4,128)S(1)} %collective-permute-done.10, f32[2,4,512]{2,1,0:T(4,128)S(1)} %collective-permute-done.11), dimensions={1} | concatenate | bytes 163840 | tf_op jit(solution)/shard_map/concatenate | solution.py:183
  118.4 5.3 %shard_map.37 = f32[8,512]{1,0:T(8,128)} custom-call(f32[2,10,512]{2,1,0:T(8,128)} %collective-permute-done.12.refs_0_, f32[2,20,512]{2,1,0:T(8,128)} %concatenate.197.refs_1_, f32[2,10,512]{2,1,0:T(8,128)} %collective-permute-done.15.refs_2_), custom_call_target="tpu_custom_call" | custom-call | flops 13107200 | bytes 491520 | tf_op jit(solution)/shard_map/pallas_call | solution.py:260
  126.9 1.2 fusion.89
  129.3 1.2 collective-permute-start.16
  131.7 4.4 %collective-permute-done.17 = f32[2,32,64]{2,1,0:T(8,128)S(1)} collective-permute-done((f32[2,32,64]{2,1,0:T(8,128)S(1)}, f32[2,32,64]{2,1,0:T(8,128)S(1)}, u32[]{:S(2)}, u32[]{:S(2)}) %collective-permute-start.17) | collective-permute-done | bytes 16416 | tf_op jit(solution)/shard_map/ppermute | solution.py:18
  136.3 1.9 %dynamic-slice_maximum_fusion = f32[12,32,8]{2,1,0:T(8,128)} fusion(s32[]{:T(128)S(6)} %select_n.80, f32[12,32,2]{2,1,0:T(8,128)S(1)} %get-tuple-element.64, f32[2,32,64]{2,1,0:T(8,128)S(1)} %collective-permute-done.17, f32[8,32,64]{2,1,0:T(8,128)} %copy-done.45, f32[2,32,64]{2,1,0:T(8,128)S(1)} %collective-permute-done.16, ...), kind=kLoop, calls=%fused_computation.140 | loop fusion | flops 12288 | bytes 116740 | tf_op jit(solution)/shard_map/concatenate | solution.py:292
  146.0 1.3 fusion.42
  (253 shorter events, 33.5 us)
Async XLA Ops:
  0.0 13.5 %copy-start.20 = (f32[32,16,128]{2,1,0:T(8,128)S(1)}, f32[32,16,128]{2,1,0:T(8,128)}, u32[]{:S(2)}) copy-start(f32[32,16,128]{2,1,0:T(8,128)} %param.5) | copy-start | bytes 786436
  0.0 13.6 %copy-start.34 = (f32[32,16,128]{2,1,0:T(8,128)S(1)}, f32[32,16,128]{2,1,0:T(8,128)}, u32[]{:S(2)}) copy-start(f32[32,16,128]{2,1,0:T(8,128)} %param.3) | copy-start | bytes 786436
  0.0 13.6 %copy-start.33 = (f32[32,16,128]{2,1,0:T(8,128)S(1)}, f32[32,16,128]{2,1,0:T(8,128)}, u32[]{:S(2)}) copy-start(f32[32,16,128]{2,1,0:T(8,128)} %param.4) | copy-start | bytes 786436
  1.4 12.1 %collective-permute-start = (f32[3,32,4,128]{3,2,1,0:T(4,128)S(1)}, f32[3,32,4,128]{3,2,1,0:T(4,128)S(1)}, u32[]{:S(2)}, u32[]{:S(2)}) collective-permute-start(f32[3,32,4,128]{3,2,1,0:T(4,128)S(1)} %get-tuple-element.27), channel_id=1, source_target_pairs={{0,1},{1,2},{2,3},{3,4},{4,5},{5,6},{6,7},{7,8},{8,9},{9,10},{10,1... | collective-permute-start | bytes 589832 | tf_op jit(solution)/shard_map/ppermute | solution.py:18
  5.3 8.2 %collective-permute-start.1 = (f32[3,32,4,128]{3,2,1,0:T(4,128)S(1)}, f32[3,32,4,128]{3,2,1,0:T(4,128)S(1)}, u32[]{:S(2)}, u32[]{:S(2)}) collective-permute-start(f32[3,32,4,128]{3,2,1,0:T(4,128)S(1)} %get-tuple-element.28), channel_id=1, source_target_pairs={{0,15},{1,0},{2,1},{3,2},{4,3},{5,4},{6,5},{7,6},{8,7},{9,8},{10,9... | collective-permute-start | bytes 589832 | tf_op jit(solution)/shard_map/ppermute | solution.py:18
  11.0 15.2 %copy-start.55 = (s32[128]{0:T(128)}, s32[128]{0:T(128)S(1)}, u32[]{:S(2)}) copy-start(s32[128]{0:T(128)S(1)} %get-tuple-element.98) | copy-start | bytes 1540
  11.0 15.2 %copy-start.57 = (s32[128]{0:T(128)}, s32[128]{0:T(128)S(1)}, u32[]{:S(2)}) copy-start(s32[128]{0:T(128)S(1)} %get-tuple-element.99) | copy-start | bytes 1540
  11.0 15.2 %copy-start.59 = (pred[128]{0:T(512)(128)(4,1)}, pred[128]{0:T(512)(128)(4,1)S(1)}, u32[]{:S(2)}) copy-start(pred[128]{0:T(512)(128)(4,1)S(1)} %compare_and_fusion.3) | copy-start | bytes 388
  11.1 73.1 %copy-start.46 = (s32[64]{0:T(128)}, s32[64]{0:T(128)S(1)}, u32[]{:S(2)}) copy-start(s32[64]{0:T(128)S(1)} %get-tuple-element.102) | copy-start | bytes 772
  11.1 73.1 %copy-start.49 = (s32[64]{0:T(128)}, s32[64]{0:T(128)S(1)}, u32[]{:S(2)}) copy-start(s32[64]{0:T(128)S(1)} %get-tuple-element.103) | copy-start | bytes 772
  11.1 73.1 %copy-start.52 = (pred[64]{0:T(512)(128)(4,1)}, pred[64]{0:T(512)(128)(4,1)S(1)}, u32[]{:S(2)}) copy-start(pred[64]{0:T(512)(128)(4,1)S(1)} %compare_and_fusion.1) | copy-start | bytes 196
  13.6 7.9 %collective-permute-start.2 = (f32[3,4,24,128]{3,2,1,0:T(8,128)S(1)}, f32[3,4,24,128]{3,2,1,0:T(8,128)S(1)}, u32[]{:S(2)}, u32[]{:S(2)}) collective-permute-start(f32[3,4,24,128]{3,2,1,0:T(8,128)S(1)} %get-tuple-element.25), channel_id=1, source_target_pairs={{0,16},{16,32},{32,48},{48,64},{64,80},{80,96},{96,112},{112,128},... | collective-permute-start | bytes 442376 | tf_op jit(solution)/shard_map/ppermute | solution.py:18
  17.7 4.6 %collective-permute-start.3 = (f32[3,4,24,128]{3,2,1,0:T(8,128)S(1)}, f32[3,4,24,128]{3,2,1,0:T(8,128)S(1)}, u32[]{:S(2)}, u32[]{:S(2)}) collective-permute-start(f32[3,4,24,128]{3,2,1,0:T(8,128)S(1)} %get-tuple-element.26), channel_id=1, source_target_pairs={{0,496},{16,0},{32,16},{48,32},{64,48},{80,64},{96,80},{112,96},{1... | collective-permute-start | bytes 442376 | tf_op jit(solution)/shard_map/ppermute | solution.py:18
  26.7 9.8 %collective-permute-start.4 = (f32[2,16,5,64]{3,2,1,0:T(8,128)S(1)}, f32[2,16,5,64]{3,2,1,0:T(8,128)S(1)}, u32[]{:S(2)}, u32[]{:S(2)}) collective-permute-start(f32[2,16,5,64]{3,2,1,0:T(8,128)S(1)} %get-tuple-element.93), channel_id=1, source_target_pairs={{0,1},{1,2},{2,3},{3,4},{4,5},{5,6},{6,7},{7,8},{8,9},{9,10},{10,1... | collective-permute-start | bytes 122888 | tf_op jit(solution)/shard_map/ppermute | solution.py:18
  28.6 9.4 %collective-permute-start.5 = (f32[2,16,5,64]{3,2,1,0:T(8,128)S(1)}, f32[2,16,5,64]{3,2,1,0:T(8,128)S(1)}, u32[]{:S(2)}, u32[]{:S(2)}) collective-permute-start(f32[2,16,5,64]{3,2,1,0:T(8,128)S(1)} %get-tuple-element.94), channel_id=1, source_target_pairs={{0,15},{1,0},{2,1},{3,2},{4,3},{5,4},{6,5},{7,6},{8,7},{9,8},{10,9... | collective-permute-start | bytes 122888 | tf_op jit(solution)/shard_map/ppermute | solution.py:18
  38.0 6.4 %collective-permute-start.6 = (f32[2,5,18,64]{3,2,1,0:T(8,128)S(1)}, f32[2,5,18,64]{3,2,1,0:T(8,128)S(1)}, u32[]{:S(2)}, u32[]{:S(2)}) collective-permute-start(f32[2,5,18,64]{3,2,1,0:T(8,128)S(1)} %get-tuple-element.43), channel_id=1, source_target_pairs={{0,16},{16,32},{32,48},{48,64},{64,80},{80,96},{96,112},{112,128},... | collective-permute-start | bytes 138248 | tf_op jit(solution)/shard_map/ppermute | solution.py:18
  39.2 5.4 %collective-permute-start.7 = (f32[2,5,18,64]{3,2,1,0:T(8,128)S(1)}, f32[2,5,18,64]{3,2,1,0:T(8,128)S(1)}, u32[]{:S(2)}, u32[]{:S(2)}) collective-permute-start(f32[2,5,18,64]{3,2,1,0:T(8,128)S(1)} %get-tuple-element.44), channel_id=1, source_target_pairs={{0,496},{16,0},{32,16},{48,32},{64,48},{80,64},{96,80},{112,96},{1... | collective-permute-start | bytes 138248 | tf_op jit(solution)/shard_map/ppermute | solution.py:18
  45.8 20.2 %copy-start.18 = (f32[22,14,64]{2,1,0:T(8,128)}, f32[22,14,64]{2,1,0:T(8,128)S(1)}, u32[]{:S(2)}) copy-start(f32[22,14,64]{2,1,0:T(8,128)S(1)} %fusion.77) | copy-start | bytes 236548
  68.8 17.8 %copy-start.15 = (f32[2,8,32,64]{3,2,1,0:T(8,128)}, f32[2,8,32,64]{3,2,1,0:T(8,128)S(1)}, u32[]{:S(2)}) copy-start(f32[2,8,32,64]{3,2,1,0:T(8,128)S(1)} %copy.22) | copy-start | bytes 393220
  74.8 10.7 %collective-permute-start.8 = (f32[2,4,32,64]{3,2,1,0:T(8,128)}, f32[2,4,32,64]{3,2,1,0:T(8,128)}, u32[]{:S(2)}, u32[]{:S(2)}) collective-permute-start(f32[2,4,32,64]{3,2,1,0:T(8,128)} %get-tuple-element.49), channel_id=1, source_target_pairs={{0,16},{16,32},{32,48},{48,64},{64,80},{80,96},{96,112},{112,128},... | collective-permute-start | bytes 196616 | tf_op jit(solution)/shard_map/ppermute | solution.py:18
  78.6 6.9 %collective-permute-start.9 = (f32[2,4,32,64]{3,2,1,0:T(8,128)}, f32[2,4,32,64]{3,2,1,0:T(8,128)}, u32[]{:S(2)}, u32[]{:S(2)}) collective-permute-start(f32[2,4,32,64]{3,2,1,0:T(8,128)} %get-tuple-element.50), channel_id=1, source_target_pairs={{0,496},{16,0},{32,16},{48,32},{64,48},{80,64},{96,80},{112,96},{1... | collective-permute-start | bytes 196616 | tf_op jit(solution)/shard_map/ppermute | solution.py:18
  89.7 13.0 %collective-permute-start.10 = (f32[2,4,512]{2,1,0:T(4,128)S(1)}, f32[2,4,512]{2,1,0:T(4,128)S(1)}, u32[]{:S(2)}, u32[]{:S(2)}) collective-permute-start(f32[2,4,512]{2,1,0:T(4,128)S(1)} %constant_dynamic-update-slice_fusion), channel_id=1, source_target_pairs={{0,496},{16,0},{32,16},{48,32},{64,48},{80,64},{96,80},{112,96},{1... | collective-permute-start | bytes 49160 | tf_op jit(solution)/shard_map/ppermute | solution.py:18
  94.3 8.4 %collective-permute-start.11 = (f32[2,4,512]{2,1,0:T(4,128)S(1)}, f32[2,4,512]{2,1,0:T(4,128)S(1)}, u32[]{:S(2)}, u32[]{:S(2)}) collective-permute-start(f32[2,4,512]{2,1,0:T(4,128)S(1)} %constant_dynamic-update-slice_fusion), channel_id=1, source_target_pairs={{0,480},{16,496},{32,0},{48,16},{64,32},{80,48},{96,64},{112,80},{... | collective-permute-start | bytes 49160 | tf_op jit(solution)/shard_map/ppermute | solution.py:18
  98.8 5.7 %collective-permute-start.13 = (f32[2,4,512]{2,1,0:T(4,128)S(1)}, f32[2,4,512]{2,1,0:T(4,128)S(1)}, u32[]{:S(2)}, u32[]{:S(2)}) collective-permute-start(f32[2,4,512]{2,1,0:T(4,128)S(1)} %constant_dynamic-update-slice_fusion), channel_id=1, source_target_pairs={{0,32},{16,48},{32,64},{48,80},{64,96},{80,112},{96,128},{112,144}... | collective-permute-start | bytes 49160 | tf_op jit(solution)/shard_map/ppermute | solution.py:18
  100.7 3.8 %collective-permute-start.14 = (f32[2,4,512]{2,1,0:T(4,128)S(1)}, f32[2,4,512]{2,1,0:T(4,128)S(1)}, u32[]{:S(2)}, u32[]{:S(2)}) collective-permute-start(f32[2,4,512]{2,1,0:T(4,128)S(1)} %constant_dynamic-update-slice_fusion), channel_id=1, source_target_pairs={{0,16},{16,32},{32,48},{48,64},{64,80},{80,96},{96,112},{112,128},... | collective-permute-start | bytes 49160 | tf_op jit(solution)/shard_map/ppermute | solution.py:18
  105.2 12.3 %collective-permute-start.12 = (f32[2,10,512]{2,1,0:T(8,128)}, f32[2,10,512]{2,1,0:T(8,128)}, u32[]{:S(2)}, u32[]{:S(2)}) collective-permute-start(f32[2,10,512]{2,1,0:T(8,128)} %get-tuple-element.96), channel_id=1, source_target_pairs={{0,80},{16,96},{32,112},{48,128},{64,144},{80,160},{96,176},{112,1... | collective-permute-start | bytes 122888 | tf_op jit(solution)/shard_map/ppermute | solution.py:18
  110.5 7.9 %collective-permute-start.15 = (f32[2,10,512]{2,1,0:T(8,128)}, f32[2,10,512]{2,1,0:T(8,128)}, u32[]{:S(2)}, u32[]{:S(2)}) collective-permute-start(f32[2,10,512]{2,1,0:T(8,128)} %get-tuple-element.95), channel_id=1, source_target_pairs={{0,432},{16,448},{32,464},{48,480},{64,496},{80,0},{96,16},{112,32... | collective-permute-start | bytes 122888 | tf_op jit(solution)/shard_map/ppermute | solution.py:18
  129.2 6.9 %copy-start.45 = (f32[8,32,64]{2,1,0:T(8,128)}, f32[8,32,64]{2,1,0:T(8,128)S(1)}, u32[]{:S(2)}) copy-start(f32[8,32,64]{2,1,0:T(8,128)S(1)} %fusion.133) | copy-start | bytes 196612
  129.2 10.0 %copy-start.48 = (s32[64]{0:T(128)S(1)}, s32[64]{0:T(128)}, u32[]{:S(2)}) copy-start(s32[64]{0:T(128)} %copy-done.46) | copy-start | bytes 772
  129.3 10.0 %copy-start.51 = (s32[64]{0:T(128)S(1)}, s32[64]{0:T(128)}, u32[]{:S(2)}) copy-start(s32[64]{0:T(128)} %copy-done.49) | copy-start | bytes 772
  129.3 2.5 %collective-permute-start.16 = (f32[2,32,64]{2,1,0:T(8,128)S(1)}, f32[2,32,64]{2,1,0:T(8,128)S(1)}, u32[]{:S(2)}, u32[]{:S(2)}) collective-permute-start(f32[2,32,64]{2,1,0:T(8,128)S(1)} %get-tuple-element.91), channel_id=1, source_target_pairs={{0,16},{16,32},{32,48},{48,64},{64,80},{80,96},{96,112},{112,128},... | collective-permute-start | bytes 49160 | tf_op jit(solution)/shard_map/ppermute | solution.py:18
  130.5 5.7 %collective-permute-start.17 = (f32[2,32,64]{2,1,0:T(8,128)S(1)}, f32[2,32,64]{2,1,0:T(8,128)S(1)}, u32[]{:S(2)}, u32[]{:S(2)}) collective-permute-start(f32[2,32,64]{2,1,0:T(8,128)S(1)} %get-tuple-element.92), channel_id=1, source_target_pairs={{0,496},{16,0},{32,16},{48,32},{64,48},{80,64},{96,80},{112,96},{1... | collective-permute-start | bytes 49160 | tf_op jit(solution)/shard_map/ppermute | solution.py:18
  (53 other events, 93.7 us)

commit v7 on v5

--- a/solution.py
+++ b/solution.py
@@ -129,20 +129,101 @@
     return jnp.concatenate([a[:, -w:], a, a[:, :w]], axis=1)
 
 
-class Band(Level):
-    def faces_at(self, h, y=False):
-        return super().faces_at(h, False)
-
-    def rhs_at(self, h, y=False):
-        return super().rhs_at(h, False)
+def lane_band_ops(size_z):
+    def roll(a, k, axis):
+        return jnp.roll(a, k, axis=axis)
+
+    def masks(a):
+        lane = lax.broadcasted_iota(jnp.int32, a.shape, 2)
+        size_l = a.shape[2]
+        return lane % size_z == 0, lane % size_z == size_z - 1, lane < size_z, lane >= size_l - size_z
+
+    def y_lower(a):
+        _, _, y_first, _ = masks(a)
+        inside = roll(a, size_z, 2)
+        return jnp.where(y_first, roll(inside, 1, 0), inside)
+
+    def y_upper(a):
+        _, _, _, y_last = masks(a)
+        inside = roll(a, -size_z, 2)
+        return jnp.where(y_last, roll(inside, -1, 0), inside)
+
+    def faces(k, scale):
+        first, last, _, _ = masks(k[:, 1:-1])
+        c = k[:, 1:-1]
+        west_x = harmonic(k[:, :-2], c, scale)
+        east_x = harmonic(c, k[:, 2:], scale)
+        west_y = harmonic(y_lower(c), c, scale)
+        east_y = harmonic(c, y_upper(c), scale)
+        below = jnp.where(first, 2.0 * c * scale, harmonic(roll(c, 1, 2), c, scale))
+        above = jnp.where(last, 2.0 * c * scale, harmonic(c, roll(c, -1, 2), scale))
+        diagonal = west_x + east_x + west_y + east_y + below + above
+        return (west_x, east_x, west_y, east_y, below, above, diagonal)
+
+    def apply(v, faces):
+        west_x, east_x, west_y, east_y, below, above, diagonal = faces
+        c = v[:, 1:-1]
+        first, last, _, _ = masks(c)
+        under = jnp.where(first, 0.0, roll(c, 1, 2))
+        over = jnp.where(last, 0.0, roll(c, -1, 2))
+        beside_all = west_x * v[:, :-2] + east_x * v[:, 2:]
+        beside_all = beside_all + west_y * y_lower(c) + east_y * y_upper(c)
+        beside_all = beside_all + below * under + above * over
+        return diagonal * c - beside_all
+
+    return faces, apply
+
+
+class LaneBand:
+    def __init__(self, ops, k, scale, have, right_side, rhs_have):
+        faces, self.apply = ops
+        self.faces, self.have = faces(k, scale), have
+        self.right_side, self.rhs_have = right_side, rhs_have
+
+    def faces_at(self, h):
+        t = self.have - h
+        return tuple(f[:, t : f.shape[1] - t] for f in self.faces)
+
+    def rhs_at(self, h):
+        t = self.rhs_have - h
+        return self.right_side[:, t : self.right_side.shape[1] - t]
 
     def sweep(self, v, h):
         faces = self.faces_at(h)
-        residual = self.rhs_at(h) - apply_operator(wrap_y(v), faces)
-        return v[1:-1] + OMEGA * residual / faces[6]
+        residual = self.rhs_at(h) - self.apply(v, faces)
+        return v[:, 1:-1] + OMEGA * residual / faces[6]
+
+    def first_sweep(self, h):
+        return OMEGA * self.rhs_at(h) / self.faces_at(h)[6]
 
     def residual(self, v):
-        return self.rhs_at(0) - apply_operator(wrap_y(v), self.faces_at(0))
+        return self.rhs_at(0) - self.apply(v, self.faces_at(0))
+
+
+def lane_pairs(size_y, size_z):
+    n = size_y * size_z
+    i = lax.broadcasted_iota(jnp.int32, (n, n // 4), 0)
+    j = lax.broadcasted_iota(jnp.int32, (n, n // 4), 1)
+    coarse = (i // size_z // 2) * (size_z // 2) + (i % size_z) // 2
+    return (coarse == j).astype(jnp.float32)
+
+
+def band_coarsen(field, size_y, size_z):
+    t = along_y(field, pairs(field.shape[1]).T)
+    t = jnp.einsum("cxl,lm->cxm", t, lane_pairs(size_y, size_z), precision=lax.Precision.HIGHEST)
+    return t * 0.125
+
+
+def band_prolong(field, size_y, size_z):
+    t = jnp.einsum("cxm,lm->cxl", field, lane_pairs(size_y, size_z), precision=lax.Precision.HIGHEST)
+    return along_y(t, pairs(2 * field.shape[1]))
+
+
+def rows_halo(x, w, axis):
+    size_x = x.shape[axis]
+    lower = shift_from(lax.slice_in_dim(x, size_x - w, size_x, axis=axis), "row", 1)
+    upper = shift_from(lax.slice_in_dim(x, 0, w, axis=axis), "row", -1)
+    return jnp.concatenate([lower, x, upper], axis=axis)
 
 
 def x_halo(x, w):
@@ -209,10 +290,8 @@
     out_ref[...] = v[(rows - keep) // 2 : (rows + keep) // 2]
 
 
-def coarse_solve(right_side, perm, scale):
-    size_x, size_y, size_z = right_side.shape
-    lanes = size_y * size_z
-    pair = jnp.stack([right_side, perm]).reshape(2, size_x, lanes)
+def coarse_solve(pair, size_z, scale):
+    size_x, lanes = pair.shape[1:]
     near = rows_around(pair, (1, 2), 1)
     span = near.shape[1]
     extra = CSWEEPS + 2 - (span - size_x) // 2
@@ -231,8 +310,7 @@
             flops=40 * CSWEEPS * rows * lanes, transcendentals=0, bytes_accessed=24 * rows * lanes
         ),
     )
-    v = call(lower, near, upper)
-    return v.reshape(keep, size_y, size_z)
+    return call(lower, near, upper)
 
 
 def on_device(pressure_in, source, permeability):
@@ -249,21 +327,31 @@
     s1 = lev1.sweep(p, 3)
     rhs = coarsen(lev1.residual(trim(s1, 2)))
     perm = coarsen(perm)
-    size_y2 = rhs.shape[1]
-    band = lax.all_gather(jnp.stack([perm, rhs]), "col", axis=2, tiled=True)
-    k2, b2 = x_halo(band, 4)
-    lev2 = Band(faces_of(wrap_y(k2), scales[2]), 3, b2, 4)
+    _, size_y2, size_z2 = rhs.shape
+    block = jnp.stack([perm, rhs]).reshape(2, rhs.shape[0], size_y2 * size_z2)
+    band = lax.all_gather(block, "col", axis=0, tiled=False)
+    k2, b2 = jnp.moveaxis(rows_halo(band, 4, 2), 1, 0)
+    ops = lane_band_ops(size_z2)
+    lev2 = LaneBand(ops, k2, scales[2], 3, b2, 4)
     p = lev2.first_sweep(3)
     s2 = lev2.sweep(p, 2)
-    rhs = coarsen(lev2.residual(s2[1:-1]))
-    perm = coarsen(band[0])
-    correction = coarse_solve(rhs, perm, scales[3])
-    q = s2 + prolong(correction)[2:-2]
+    rhs = band_coarsen(lev2.residual(s2[:, 1:-1]), size_y2, size_z2)
+    perm = band_coarsen(band[:, 0], size_y2, size_z2)
+    blocks, size_x3, lanes3 = rhs.shape
+    pair = jnp.stack([rhs, perm], axis=1)
+    pair = jnp.transpose(pair, (1, 2, 0, 3)).reshape(2, size_x3, blocks * lanes3)
+    correction = coarse_solve(pair, size_z2 // 2, scales[3])
+    correction = jnp.transpose(correction.reshape(-1, blocks, lanes3), (1, 0, 2))
+    q = s2 + band_prolong(correction, size_y2, size_z2)[:, 2:-2]
     q = lev2.sweep(q, 1)
     u2 = lev2.sweep(q, 0)
-    u2 = wrap_y(x_halo(u2, 2), 2)
+    u2 = rows_halo(u2, 2, 1)
+    u2 = jnp.concatenate([u2[-1:], u2, u2[:1]], axis=0)
     col = lax.axis_index("col")
-    u2 = lax.dynamic_slice_in_dim(u2, col * size_y2, size_y2 + 4, axis=1)
+    u2 = lax.dynamic_slice_in_dim(u2, col, 3, axis=0)
+    edge = 2 * size_z2
+    u2 = jnp.concatenate([u2[0, :, -edge:], u2[1], u2[2, :, :edge]], axis=1)
+    u2 = u2.reshape(u2.shape[0], size_y2 + 4, size_z2)
     q = s1 + trim(prolong(u2), 1)
     q = lev1.sweep(q, 2)
     u1 = lev1.sweep(q, 1)

time: 148 us -> 138 us (0.932)
  local copies, waits for them, and re-layouts: 20.7 us -> 12 us
  matrix products: 10.8 us -> 8.66 us
  waiting for transfers between devices: 10.8 us -> 12.3 us
    unnamed x137 -> x148, local copies, waits for them, and re-layouts: 6.56 us -> 2.43 us
    dot_general x9 -> x6, matrix products: 6.35 us -> 3.63 us  [along_z(): out = jnp.dot(flat, matrix, precision=lax.Precision.HIGHEST)]
    mul x2 -> x0, local copies, waits for them, and re-layouts: 2.29 us -> none  [coarsen(): return t * 0.125]
    convert_element_type x6 -> x4, other arithmetic: 2.44 us -> 0.62 us  [pairs(): return (i // 2 == j).astype(jnp.float32)]
    add x4 -> x3, other arithmetic: 2.5 us -> 0.85 us  [sweep(): return v[:, 1:-1] + OMEGA * residual / faces[6]]
    ppermute x18, waiting for transfers between devices: 10.8 us -> 12.3 us  [shift_from(): return lax.ppermute(x, axis, [(i, (i + k) % n) for i in range(n)])]
    slice x12 -> x23, local copies, waits for them, and re-layouts: 4.85 us -> 3.85 us  [the longest x20 1.86 us: roll(): return jnp.roll(a, k, axis=axis)]
    dot_general x8 -> x9, matrix products: 3.55 us -> 3.85 us  [along_y(): jnp.einsum('xjy,xyz->xjz', batched, field, precision=lax.Precision.HIGHEST)]
  transfers between devices with their start and end apart: 18 -> 18, of which waited for: 10 -> 11; matrix products, arithmetic and copies ran while one was open for 7% -> 6% of each run, Pallas kernels for 0% -> 0%
where the time goes in v7:
time: 138 us; the launch traced here: 136 us
  starting transfers between devices  61.1 us (44%)
  blocking collectives  19 us (14%)
  other arithmetic  16.8 us (12%)
  waiting for transfers between devices  12.3 us (9%)
  local copies, waits for them, and re-layouts  12 us (9%)
  matrix products  8.66 us (6%)
  Pallas kernels  4.48 us (3%)
  between operations  1.52 us (1%)
    ppermute x18, starting transfers between devices, shift_from(): return lax.ppermute(x, axis, [(i, (i + k) % n) for i in range(n)])  61.1 us
    all_gather x1, blocking collectives, on_device(): band = lax.all_gather(block, 'col', axis=0, tiled=False)  19 us
    ppermute x18, waiting for transfers between devices, shift_from(): return lax.ppermute(x, axis, [(i, (i + k) % n) for i in range(n)])  12.3 us
    add x6, other arithmetic, sweep(): return v[1:-1, 1:-1] + OMEGA * residual / faces[6]  4.52 us
    pallas_call x1, Pallas kernels, coarse_solve(): return call(lower, near, upper)  4.48 us
    dot_general x9, matrix products, along_y(): jnp.einsum('xjy,xyz->xjz', batched, field, precision=lax.Precision.HIGHEST)  3.85 us
    dot_general x6, matrix products, along_z(): out = jnp.dot(flat, matrix, precision=lax.Precision.HIGHEST)  3.63 us
    concatenate x1, local copies, waits for them, and re-layouts, rows_around(): return jnp.concatenate(lower + [x] + upper, axis=axis)  3.31 us
  transfers between devices with their start and end apart: 18, of which 11 were waited for; matrix products, arithmetic and copies ran while one was open for 6% of the time, Pallas kernels for 0%

profile of v7, /device:TPU:1, one launch (start us, length us, event | category | flops | bytes accessed | tf_op | source)
XLA Modules:
  0.0 135.9 jit_solution(12629632024482411413)
XLA Ops:
  0.0 1.3 pad_maximum_fusion.6
  1.4 3.9 %collective-permute-start = (f32[3,32,4,128]{3,2,1,0:T(4,128)S(1)}, f32[3,32,4,128]{3,2,1,0:T(4,128)S(1)}, u32[]{:S(2)}, u32[]{:S(2)}) collective-permute-start(f32[3,32,4,128]{3,2,1,0:T(4,128)S(1)} %get-tuple-element.29), channel_id=1, source_target_pairs={{0,1},{1,2},{2,3},{3,4},{4,5},{5,6},{6,7},{7,8},{8,9},{9,10},{10,1... | collective-permute-start | bytes 589832 | tf_op jit(solution)/shard_map/ppermute | solution.py:18
  5.3 5.6 %collective-permute-start.1 = (f32[3,32,4,128]{3,2,1,0:T(4,128)S(1)}, f32[3,32,4,128]{3,2,1,0:T(4,128)S(1)}, u32[]{:S(2)}, u32[]{:S(2)}) collective-permute-start(f32[3,32,4,128]{3,2,1,0:T(4,128)S(1)} %get-tuple-element.30), channel_id=1, source_target_pairs={{0,15},{1,0},{2,1},{3,2},{4,3},{5,4},{6,5},{7,6},{8,7},{9,8},{10,9... | collective-permute-start | bytes 589832 | tf_op jit(solution)/shard_map/ppermute | solution.py:18
  11.1 1.3 fusion.116
  13.8 3.8 %collective-permute-start.2 = (f32[3,4,24,128]{3,2,1,0:T(8,128)S(1)}, f32[3,4,24,128]{3,2,1,0:T(8,128)S(1)}, u32[]{:S(2)}, u32[]{:S(2)}) collective-permute-start(f32[3,4,24,128]{3,2,1,0:T(8,128)S(1)} %get-tuple-element.27), channel_id=1, source_target_pairs={{0,16},{16,32},{32,48},{48,64},{64,80},{80,96},{96,112},{112,128},... | collective-permute-start | bytes 442376 | tf_op jit(solution)/shard_map/ppermute | solution.py:18
  17.6 3.0 %collective-permute-start.3 = (f32[3,4,24,128]{3,2,1,0:T(8,128)S(1)}, f32[3,4,24,128]{3,2,1,0:T(8,128)S(1)}, u32[]{:S(2)}, u32[]{:S(2)}) collective-permute-start(f32[3,4,24,128]{3,2,1,0:T(8,128)S(1)} %get-tuple-element.28), channel_id=1, source_target_pairs={{0,496},{16,0},{32,16},{48,32},{64,48},{80,64},{96,80},{112,96},{1... | collective-permute-start | bytes 442376 | tf_op jit(solution)/shard_map/ppermute | solution.py:18
  26.8 1.9 %collective-permute-start.4 = (f32[2,16,5,64]{3,2,1,0:T(8,128)S(1)}, f32[2,16,5,64]{3,2,1,0:T(8,128)S(1)}, u32[]{:S(2)}, u32[]{:S(2)}) collective-permute-start(f32[2,16,5,64]{3,2,1,0:T(8,128)S(1)} %get-tuple-element.101), channel_id=1, source_target_pairs={{0,1},{1,2},{2,3},{3,4},{4,5},{5,6},{6,7},{7,8},{8,9},{9,10},{10,1... | collective-permute-start | bytes 122888 | tf_op jit(solution)/shard_map/ppermute | solution.py:18
  28.7 7.4 %collective-permute-start.5 = (f32[2,16,5,64]{3,2,1,0:T(8,128)S(1)}, f32[2,16,5,64]{3,2,1,0:T(8,128)S(1)}, u32[]{:S(2)}, u32[]{:S(2)}) collective-permute-start(f32[2,16,5,64]{3,2,1,0:T(8,128)S(1)} %get-tuple-element.102), channel_id=1, source_target_pairs={{0,15},{1,0},{2,1},{3,2},{4,3},{5,4},{6,5},{7,6},{8,7},{9,8},{10,9... | collective-permute-start | bytes 122888 | tf_op jit(solution)/shard_map/ppermute | solution.py:18
  36.6 1.5 %collective-permute-done.5 = f32[2,16,5,64]{3,2,1,0:T(8,128)S(1)} collective-permute-done((f32[2,16,5,64]{3,2,1,0:T(8,128)S(1)}, f32[2,16,5,64]{3,2,1,0:T(8,128)S(1)}, u32[]{:S(2)}, u32[]{:S(2)}) %collective-permute-start.5) | collective-permute-done | bytes 40992 | tf_op jit(solution)/shard_map/ppermute | solution.py:18
  38.8 1.2 collective-permute-start.6
  40.0 4.4 %collective-permute-start.7 = (f32[2,5,18,64]{3,2,1,0:T(8,128)}, f32[2,5,18,64]{3,2,1,0:T(8,128)}, u32[]{:S(2)}, u32[]{:S(2)}) collective-permute-start(f32[2,5,18,64]{3,2,1,0:T(8,128)} %get-tuple-element.46), channel_id=1, source_target_pairs={{0,496},{16,0},{32,16},{48,32},{64,48},{80,64},{96,80},{112,96},{1... | collective-permute-start | bytes 138248 | tf_op jit(solution)/shard_map/ppermute | solution.py:18
  44.4 1.1 collective-permute-done.6
  45.7 1.2 pad_maximum_fusion.1
  49.2 19.0 %all_gather.3 = f32[16,2,8,128]{3,2,0,1:T(8,128)S(1)} all-gather(f32[1,2,8,128]{3,2,0,1:T(8,128)S(1)} %pad_maximum_fusion.24), channel_id=1, replica_groups=mesh['row'=32,'col'=16] {'col'}, dimensions={0}, use_global_device_ids=true | all-gather | bytes 139264 | tf_op jit(solution)/shard_map/all_gather | solution.py:332
  68.5 3.8 %collective-permute-start.8 = (f32[16,2,4,128]{3,2,0,1:T(4,128)S(1)}, f32[16,2,4,128]{3,2,0,1:T(4,128)S(1)}, u32[]{:S(2)}, u32[]{:S(2)}) collective-permute-start(f32[16,2,4,128]{3,2,0,1:T(4,128)S(1)} %get-tuple-element.99), channel_id=1, source_target_pairs={{0,16},{16,32},{32,48},{48,64},{64,80},{80,96},{96,112},{112,128},... | collective-permute-start | bytes 196616 | tf_op jit(solution)/shard_map/ppermute | solution.py:18
  72.3 5.6 %collective-permute-start.9 = (f32[16,2,4,128]{3,2,0,1:T(4,128)S(1)}, f32[16,2,4,128]{3,2,0,1:T(4,128)S(1)}, u32[]{:S(2)}, u32[]{:S(2)}) collective-permute-start(f32[16,2,4,128]{3,2,0,1:T(4,128)S(1)} %get-tuple-element.100), channel_id=1, source_target_pairs={{0,496},{16,0},{32,16},{48,32},{64,48},{80,64},{96,80},{112,96},{1... | collective-permute-start | bytes 196616 | tf_op jit(solution)/shard_map/ppermute | solution.py:18
  82.7 1.9 %collective-permute-start.13 = (f32[2,4,512]{2,1,0:T(4,128)S(1)}, f32[2,4,512]{2,1,0:T(4,128)S(1)}, u32[]{:S(2)}, u32[]{:S(2)}) collective-permute-start(f32[2,4,512]{2,1,0:T(4,128)S(1)} %reshape.73), channel_id=1, source_target_pairs={{0,32},{16,48},{32,64},{48,80},{64,96},{80,112},{96,128},{112,144}... | collective-permute-start | bytes 49160 | tf_op jit(solution)/shard_map/ppermute | solution.py:18
  84.7 8.4 %collective-permute-start.11 = (f32[2,4,512]{2,1,0:T(4,128)S(1)}, f32[2,4,512]{2,1,0:T(4,128)S(1)}, u32[]{:S(2)}, u32[]{:S(2)}) collective-permute-start(f32[2,4,512]{2,1,0:T(4,128)S(1)} %reshape.73), channel_id=1, source_target_pairs={{0,480},{16,496},{32,0},{48,16},{64,32},{80,48},{96,64},{112,80},{... | collective-permute-start | bytes 49160 | tf_op jit(solution)/shard_map/ppermute | solution.py:18
  94.5 1.8 %collective-permute-done.10 = f32[2,4,512]{2,1,0:T(4,128)S(1)} collective-permute-done((f32[2,4,512]{2,1,0:T(4,128)S(1)}, f32[2,4,512]{2,1,0:T(4,128)S(1)}, u32[]{:S(2)}, u32[]{:S(2)}) %collective-permute-start.10) | collective-permute-done | bytes 16416 | tf_op jit(solution)/shard_map/ppermute | solution.py:18
  97.0 4.3 %collective-permute-start.15 = (f32[2,10,512]{2,1,0:T(8,128)}, f32[2,10,512]{2,1,0:T(8,128)}, u32[]{:S(2)}, u32[]{:S(2)}) collective-permute-start(f32[2,10,512]{2,1,0:T(8,128)} %get-tuple-element.107), channel_id=1, source_target_pairs={{0,432},{16,448},{32,464},{48,480},{64,496},{80,0},{96,16},{112,32... | collective-permute-start | bytes 122888 | tf_op jit(solution)/shard_map/ppermute | solution.py:18
  101.2 3.3 %collective-permute-start.12 = (f32[2,10,512]{2,1,0:T(8,128)S(1)}, f32[2,10,512]{2,1,0:T(8,128)}, u32[]{:S(2)}, u32[]{:S(2)}) collective-permute-start(f32[2,10,512]{2,1,0:T(8,128)S(1)} %get-tuple-element.108), channel_id=1, source_target_pairs={{0,80},{16,96},{32,112},{48,128},{64,144},{80,160},{96,176},{112,1... | collective-permute-start | bytes 122888 | tf_op jit(solution)/shard_map/ppermute | solution.py:18
  105.0 1.3 slice.1235
  106.3 3.3 %concatenate.252.refs_1_ = f32[2,20,512]{2,1,0:T(8,128)} concatenate(f32[2,4,512]{2,1,0:T(4,128)S(1)} %collective-permute-done.13, f32[2,4,512]{2,1,0:T(4,128)S(1)} %collective-permute-done.14, f32[2,4,512]{2,1,0:T(4,128)S(1)} %reshape.73, f32[2,4,512]{2,1,0:T(4,128)} %copy-done.46, f32[2,4,512]{2,1,0:T(4,128)} %copy-done.45), dimensions={1} | concatenate | bytes 163840 | tf_op jit(solution)/shard_map/concatenate | solution.py:239
  109.7 3.5 %collective-permute-done.12.refs_0_ = f32[2,10,512]{2,1,0:T(8,128)} collective-permute-done((f32[2,10,512]{2,1,0:T(8,128)S(1)}, f32[2,10,512]{2,1,0:T(8,128)}, u32[]{:S(2)}, u32[]{:S(2)}) %collective-permute-start.12) | collective-permute-done | bytes 40992 | tf_op jit(solution)/shard_map/ppermute | solution.py:18
  113.2 4.5 %shard_map.37 = f32[8,512]{1,0:T(8,128)} custom-call(f32[2,10,512]{2,1,0:T(8,128)} %collective-permute-done.12.refs_0_, f32[2,20,512]{2,1,0:T(8,128)} %concatenate.252.refs_1_, f32[2,10,512]{2,1,0:T(8,128)} %collective-permute-done.15.refs_2_), custom_call_target="tpu_custom_call" | custom-call | flops 13107200 | bytes 491520 | tf_op jit(solution)/shard_map/pallas_call | solution.py:313
  119.3 1.3 convolution_add_fusion
  124.0 1.7 %collective-permute-start.16 = (f32[16,2,128]{2,1,0:T(2,128)}, f32[16,2,128]{2,1,0:T(2,128)S(1)}, u32[]{:S(2)}, u32[]{:S(2)}) collective-permute-start(f32[16,2,128]{2,1,0:T(2,128)} %get-tuple-element.104), channel_id=1, source_target_pairs={{0,16},{16,32},{32,48},{48,64},{64,80},{80,96},{96,112},{112,128},... | collective-permute-start | bytes 49160 | tf_op jit(solution)/shard_map/ppermute | solution.py:18
  125.7 1.6 %collective-permute-done.17 = f32[16,2,128]{2,1,0:T(2,128)S(1)} collective-permute-done((f32[16,2,128]{2,1,0:T(2,128)}, f32[16,2,128]{2,1,0:T(2,128)S(1)}, u32[]{:S(2)}, u32[]{:S(2)}) %collective-permute-start.17) | collective-permute-done | bytes 16416 | tf_op jit(solution)/shard_map/ppermute | solution.py:18
  127.7 1.1 fusion.254
  129.2 1.0 slice_add_fusion
  133.5 0.9 fusion.28
  134.5 1.3 fusion.42
  (285 shorter events, 27.1 us)
Async XLA Ops:
  1.4 12.4 %collective-permute-start = (f32[3,32,4,128]{3,2,1,0:T(4,128)S(1)}, f32[3,32,4,128]{3,2,1,0:T(4,128)S(1)}, u32[]{:S(2)}, u32[]{:S(2)}) collective-permute-start(f32[3,32,4,128]{3,2,1,0:T(4,128)S(1)} %get-tuple-element.29), channel_id=1, source_target_pairs={{0,1},{1,2},{2,3},{3,4},{4,5},{5,6},{6,7},{7,8},{8,9},{9,10},{10,1... | collective-permute-start | bytes 589832 | tf_op jit(solution)/shard_map/ppermute | solution.py:18
  5.3 8.4 %collective-permute-start.1 = (f32[3,32,4,128]{3,2,1,0:T(4,128)S(1)}, f32[3,32,4,128]{3,2,1,0:T(4,128)S(1)}, u32[]{:S(2)}, u32[]{:S(2)}) collective-permute-start(f32[3,32,4,128]{3,2,1,0:T(4,128)S(1)} %get-tuple-element.30), channel_id=1, source_target_pairs={{0,15},{1,0},{2,1},{3,2},{4,3},{5,4},{6,5},{7,6},{8,7},{9,8},{10,9... | collective-permute-start | bytes 589832 | tf_op jit(solution)/shard_map/ppermute | solution.py:18
  11.0 15.2 %copy-start.58 = (pred[128]{0:T(512)(128)(4,1)}, pred[128]{0:T(512)(128)(4,1)S(1)}, u32[]{:S(2)}) copy-start(pred[128]{0:T(512)(128)(4,1)S(1)} %compare_and_fusion.3) | copy-start | bytes 388
  11.0 37.7 %copy-start.73 = (pred[64]{0:T(512)(128)(4,1)}, pred[64]{0:T(512)(128)(4,1)S(1)}, u32[]{:S(2)}) copy-start(pred[64]{0:T(512)(128)(4,1)S(1)} %compare_and_fusion.1) | copy-start | bytes 196
  11.1 15.1 %copy-start.60 = (s32[128]{0:T(128)}, s32[128]{0:T(128)S(1)}, u32[]{:S(2)}) copy-start(s32[128]{0:T(128)S(1)} %get-tuple-element.112) | copy-start | bytes 1540
  11.1 15.1 %copy-start.62 = (s32[128]{0:T(128)}, s32[128]{0:T(128)S(1)}, u32[]{:S(2)}) copy-start(s32[128]{0:T(128)S(1)} %get-tuple-element.113) | copy-start | bytes 1540
  11.1 37.6 %copy-start.67 = (s32[64]{0:T(128)}, s32[64]{0:T(128)S(1)}, u32[]{:S(2)}) copy-start(s32[64]{0:T(128)S(1)} %get-tuple-element.116) | copy-start | bytes 772
  11.1 37.6 %copy-start.69 = (s32[64]{0:T(128)}, s32[64]{0:T(128)S(1)}, u32[]{:S(2)}) copy-start(s32[64]{0:T(128)S(1)} %get-tuple-element.117) | copy-start | bytes 772
  13.8 7.7 %collective-permute-start.2 = (f32[3,4,24,128]{3,2,1,0:T(8,128)S(1)}, f32[3,4,24,128]{3,2,1,0:T(8,128)S(1)}, u32[]{:S(2)}, u32[]{:S(2)}) collective-permute-start(f32[3,4,24,128]{3,2,1,0:T(8,128)S(1)} %get-tuple-element.27), channel_id=1, source_target_pairs={{0,16},{16,32},{32,48},{48,64},{64,80},{80,96},{96,112},{112,128},... | collective-permute-start | bytes 442376 | tf_op jit(solution)/shard_map/ppermute | solution.py:18
  17.6 4.6 %collective-permute-start.3 = (f32[3,4,24,128]{3,2,1,0:T(8,128)S(1)}, f32[3,4,24,128]{3,2,1,0:T(8,128)S(1)}, u32[]{:S(2)}, u32[]{:S(2)}) collective-permute-start(f32[3,4,24,128]{3,2,1,0:T(8,128)S(1)} %get-tuple-element.28), channel_id=1, source_target_pairs={{0,496},{16,0},{32,16},{48,32},{64,48},{80,64},{96,80},{112,96},{1... | collective-permute-start | bytes 442376 | tf_op jit(solution)/shard_map/ppermute | solution.py:18
  20.7 61.2 %copy-start.48 = (pred[128]{0:T(512)(128)(4,1)}, pred[128]{0:T(512)(128)(4,1)S(1)}, u32[]{:S(2)}) copy-start(pred[128]{0:T(512)(128)(4,1)S(1)} %get-tuple-element.122) | copy-start | bytes 388
  20.7 61.2 %copy-start.50 = (pred[128]{0:T(512)(128)(4,1)}, pred[128]{0:T(512)(128)(4,1)S(1)}, u32[]{:S(2)}) copy-start(pred[128]{0:T(512)(128)(4,1)S(1)} %get-tuple-element.123) | copy-start | bytes 388
  20.7 61.7 %copy-start.52 = (s32[128]{0:T(128)}, s32[128]{0:T(128)S(1)}, u32[]{:S(2)}) copy-start(s32[128]{0:T(128)S(1)} %get-tuple-element.120) | copy-start | bytes 1540
  20.7 61.7 %copy-start.54 = (s32[128]{0:T(128)}, s32[128]{0:T(128)S(1)}, u32[]{:S(2)}) copy-start(s32[128]{0:T(128)S(1)} %get-tuple-element.121) | copy-start | bytes 1540
  26.8 9.8 %collective-permute-start.4 = (f32[2,16,5,64]{3,2,1,0:T(8,128)S(1)}, f32[2,16,5,64]{3,2,1,0:T(8,128)S(1)}, u32[]{:S(2)}, u32[]{:S(2)}) collective-permute-start(f32[2,16,5,64]{3,2,1,0:T(8,128)S(1)} %get-tuple-element.101), channel_id=1, source_target_pairs={{0,1},{1,2},{2,3},{3,4},{4,5},{5,6},{6,7},{7,8},{8,9},{9,10},{10,1... | collective-permute-start | bytes 122888 | tf_op jit(solution)/shard_map/ppermute | solution.py:18
  28.7 9.4 %collective-permute-start.5 = (f32[2,16,5,64]{3,2,1,0:T(8,128)S(1)}, f32[2,16,5,64]{3,2,1,0:T(8,128)S(1)}, u32[]{:S(2)}, u32[]{:S(2)}) collective-permute-start(f32[2,16,5,64]{3,2,1,0:T(8,128)S(1)} %get-tuple-element.102), channel_id=1, source_target_pairs={{0,15},{1,0},{2,1},{3,2},{4,3},{5,4},{6,5},{7,6},{8,7},{9,8},{10,9... | collective-permute-start | bytes 122888 | tf_op jit(solution)/shard_map/ppermute | solution.py:18
  36.2 46.2 %copy-start.70 = (s32[128]{0:T(128)}, s32[128]{0:T(128)S(1)}, u32[]{:S(2)}) copy-start(s32[128]{0:T(128)S(1)} %get-tuple-element.124) | copy-start | bytes 1540
  36.2 46.2 %copy-start.71 = (s32[128]{0:T(128)}, s32[128]{0:T(128)S(1)}, u32[]{:S(2)}) copy-start(s32[128]{0:T(128)S(1)} %get-tuple-element.125) | copy-start | bytes 1540
  38.8 6.7 %collective-permute-start.6 = (f32[2,5,18,64]{3,2,1,0:T(8,128)}, f32[2,5,18,64]{3,2,1,0:T(8,128)}, u32[]{:S(2)}, u32[]{:S(2)}) collective-permute-start(f32[2,5,18,64]{3,2,1,0:T(8,128)} %get-tuple-element.45), channel_id=1, source_target_pairs={{0,16},{16,32},{32,48},{48,64},{64,80},{80,96},{96,112},{112,128},... | collective-permute-start | bytes 138248 | tf_op jit(solution)/shard_map/ppermute | solution.py:18
  40.0 5.7 %collective-permute-start.7 = (f32[2,5,18,64]{3,2,1,0:T(8,128)}, f32[2,5,18,64]{3,2,1,0:T(8,128)}, u32[]{:S(2)}, u32[]{:S(2)}) collective-permute-start(f32[2,5,18,64]{3,2,1,0:T(8,128)} %get-tuple-element.46), channel_id=1, source_target_pairs={{0,496},{16,0},{32,16},{48,32},{64,48},{80,64},{96,80},{112,96},{1... | collective-permute-start | bytes 138248 | tf_op jit(solution)/shard_map/ppermute | solution.py:18
  44.3 38.1 %copy-start.56 = (pred[128]{0:T(512)(128)(4,1)}, pred[128]{0:T(512)(128)(4,1)S(1)}, u32[]{:S(2)}) copy-start(pred[128]{0:T(512)(128)(4,1)S(1)} %get-tuple-element.110) | copy-start | bytes 388
  44.3 38.1 %copy-start.72 = (pred[128]{0:T(512)(128)(4,1)}, pred[128]{0:T(512)(128)(4,1)S(1)}, u32[]{:S(2)}) copy-start(pred[128]{0:T(512)(128)(4,1)S(1)} %get-tuple-element.111) | copy-start | bytes 388
  68.5 10.1 %collective-permute-start.8 = (f32[16,2,4,128]{3,2,0,1:T(4,128)S(1)}, f32[16,2,4,128]{3,2,0,1:T(4,128)S(1)}, u32[]{:S(2)}, u32[]{:S(2)}) collective-permute-start(f32[16,2,4,128]{3,2,0,1:T(4,128)S(1)} %get-tuple-element.99), channel_id=1, source_target_pairs={{0,16},{16,32},{32,48},{48,64},{64,80},{80,96},{96,112},{112,128},... | collective-permute-start | bytes 196616 | tf_op jit(solution)/shard_map/ppermute | solution.py:18
  72.3 6.5 %collective-permute-start.9 = (f32[16,2,4,128]{3,2,0,1:T(4,128)S(1)}, f32[16,2,4,128]{3,2,0,1:T(4,128)S(1)}, u32[]{:S(2)}, u32[]{:S(2)}) collective-permute-start(f32[16,2,4,128]{3,2,0,1:T(4,128)S(1)} %get-tuple-element.100), channel_id=1, source_target_pairs={{0,496},{16,0},{32,16},{48,32},{64,48},{80,64},{96,80},{112,96},{1... | collective-permute-start | bytes 196616 | tf_op jit(solution)/shard_map/ppermute | solution.py:18
  82.7 11.8 %collective-permute-start.14 = (f32[2,4,512]{2,1,0:T(4,128)S(1)}, f32[2,4,512]{2,1,0:T(4,128)S(1)}, u32[]{:S(2)}, u32[]{:S(2)}) collective-permute-start(f32[2,4,512]{2,1,0:T(4,128)S(1)} %reshape.73), channel_id=1, source_target_pairs={{0,16},{16,32},{32,48},{48,64},{64,80},{80,96},{96,112},{112,128},... | collective-permute-start | bytes 49160 | tf_op jit(solution)/shard_map/ppermute | solution.py:18
  82.7 11.8 %collective-permute-start.13 = (f32[2,4,512]{2,1,0:T(4,128)S(1)}, f32[2,4,512]{2,1,0:T(4,128)S(1)}, u32[]{:S(2)}, u32[]{:S(2)}) collective-permute-start(f32[2,4,512]{2,1,0:T(4,128)S(1)} %reshape.73), channel_id=1, source_target_pairs={{0,32},{16,48},{32,64},{48,80},{64,96},{80,112},{96,128},{112,144}... | collective-permute-start | bytes 49160 | tf_op jit(solution)/shard_map/ppermute | solution.py:18
  84.7 9.8 %collective-permute-start.11 = (f32[2,4,512]{2,1,0:T(4,128)S(1)}, f32[2,4,512]{2,1,0:T(4,128)S(1)}, u32[]{:S(2)}, u32[]{:S(2)}) collective-permute-start(f32[2,4,512]{2,1,0:T(4,128)S(1)} %reshape.73), channel_id=1, source_target_pairs={{0,480},{16,496},{32,0},{48,16},{64,32},{80,48},{96,64},{112,80},{... | collective-permute-start | bytes 49160 | tf_op jit(solution)/shard_map/ppermute | solution.py:18
  93.1 3.2 %collective-permute-start.10 = (f32[2,4,512]{2,1,0:T(4,128)S(1)}, f32[2,4,512]{2,1,0:T(4,128)S(1)}, u32[]{:S(2)}, u32[]{:S(2)}) collective-permute-start(f32[2,4,512]{2,1,0:T(4,128)S(1)} %reshape.73), channel_id=1, source_target_pairs={{0,496},{16,0},{32,16},{48,32},{64,48},{80,64},{96,80},{112,96},{1... | collective-permute-start | bytes 49160 | tf_op jit(solution)/shard_map/ppermute | solution.py:18
  97.0 12.7 %collective-permute-start.15 = (f32[2,10,512]{2,1,0:T(8,128)}, f32[2,10,512]{2,1,0:T(8,128)}, u32[]{:S(2)}, u32[]{:S(2)}) collective-permute-start(f32[2,10,512]{2,1,0:T(8,128)} %get-tuple-element.107), channel_id=1, source_target_pairs={{0,432},{16,448},{32,464},{48,480},{64,496},{80,0},{96,16},{112,32... | collective-permute-start | bytes 122888 | tf_op jit(solution)/shard_map/ppermute | solution.py:18
  101.2 12.0 %collective-permute-start.12 = (f32[2,10,512]{2,1,0:T(8,128)S(1)}, f32[2,10,512]{2,1,0:T(8,128)}, u32[]{:S(2)}, u32[]{:S(2)}) collective-permute-start(f32[2,10,512]{2,1,0:T(8,128)S(1)} %get-tuple-element.108), channel_id=1, source_target_pairs={{0,80},{16,96},{32,112},{48,128},{64,144},{80,160},{96,176},{112,1... | collective-permute-start | bytes 122888 | tf_op jit(solution)/shard_map/ppermute | solution.py:18
  124.0 3.4 %collective-permute-start.17 = (f32[16,2,128]{2,1,0:T(2,128)}, f32[16,2,128]{2,1,0:T(2,128)S(1)}, u32[]{:S(2)}, u32[]{:S(2)}) collective-permute-start(f32[16,2,128]{2,1,0:T(2,128)} %get-tuple-element.103), channel_id=1, source_target_pairs={{0,496},{16,0},{32,16},{48,32},{64,48},{80,64},{96,80},{112,96},{1... | collective-permute-start | bytes 49160 | tf_op jit(solution)/shard_map/ppermute | solution.py:18
  124.0 3.3 %collective-permute-start.16 = (f32[16,2,128]{2,1,0:T(2,128)}, f32[16,2,128]{2,1,0:T(2,128)S(1)}, u32[]{:S(2)}, u32[]{:S(2)}) collective-permute-start(f32[16,2,128]{2,1,0:T(2,128)} %get-tuple-element.104), channel_id=1, source_target_pairs={{0,16},{16,32},{32,48},{48,64},{64,80},{80,96},{96,112},{112,128},... | collective-permute-start | bytes 49160 | tf_op jit(solution)/shard_map/ppermute | solution.py:18
  (60 other events, 156.3 us)

commit v8 on v7

--- a/solution.py
+++ b/solution.py
@@ -330,22 +330,21 @@
     _, size_y2, size_z2 = rhs.shape
     block = jnp.stack([perm, rhs]).reshape(2, rhs.shape[0], size_y2 * size_z2)
     band = lax.all_gather(block, "col", axis=0, tiled=False)
-    k2, b2 = jnp.moveaxis(rows_halo(band, 4, 2), 1, 0)
+    k2, b2 = jnp.moveaxis(rows_halo(band, 6, 2), 1, 0)
     ops = lane_band_ops(size_z2)
-    lev2 = LaneBand(ops, k2, scales[2], 3, b2, 4)
-    p = lev2.first_sweep(3)
-    s2 = lev2.sweep(p, 2)
-    rhs = band_coarsen(lev2.residual(s2[:, 1:-1]), size_y2, size_z2)
+    lev2 = LaneBand(ops, k2, scales[2], 5, b2, 6)
+    p = lev2.first_sweep(5)
+    s2 = lev2.sweep(p, 4)
+    rhs = band_coarsen(lev2.residual(s2[:, 3:-3]), size_y2, size_z2)
     perm = band_coarsen(band[:, 0], size_y2, size_z2)
     blocks, size_x3, lanes3 = rhs.shape
     pair = jnp.stack([rhs, perm], axis=1)
     pair = jnp.transpose(pair, (1, 2, 0, 3)).reshape(2, size_x3, blocks * lanes3)
     correction = coarse_solve(pair, size_z2 // 2, scales[3])
     correction = jnp.transpose(correction.reshape(-1, blocks, lanes3), (1, 0, 2))
-    q = s2 + band_prolong(correction, size_y2, size_z2)[:, 2:-2]
-    q = lev2.sweep(q, 1)
-    u2 = lev2.sweep(q, 0)
-    u2 = rows_halo(u2, 2, 1)
+    q = s2 + band_prolong(correction, size_y2, size_z2)
+    q = lev2.sweep(q, 3)
+    u2 = lev2.sweep(q, 2)
     u2 = jnp.concatenate([u2[-1:], u2, u2[:1]], axis=0)
     col = lax.axis_index("col")
     u2 = lax.dynamic_slice_in_dim(u2, col, 3, axis=0)

time: 138 us -> 134 us (0.971)
  waiting for transfers between devices: 12.3 us -> 8.89 us
  other arithmetic: 16.8 us -> 20.1 us
    ppermute x18 -> x16, waiting for transfers between devices: 12.3 us -> 8.89 us  [shift_from(): return lax.ppermute(x, axis, [(i, (i + k) % n) for i in range(n)])]
    slice x2 -> x1, local copies, waits for them, and re-layouts: 1.97 us -> 0.01 us  [on_device(): u2 = jnp.concatenate([u2[-1:], u2, u2[:1]], axis=0)]
    convert_element_type x4, other arithmetic: 0.62 us -> 2.54 us  [pairs(): return (i // 2 == j).astype(jnp.float32)]
    ppermute x18 -> x16, starting transfers between devices: 61.1 us -> 60.2 us  [shift_from(): return lax.ppermute(x, axis, [(i, (i + k) % n) for i in range(n)])]
    unnamed x148 -> x158, local copies, waits for them, and re-layouts: 2.43 us -> 3.22 us
  transfers between devices with their start and end apart: 18 -> 16, of which waited for: 11 -> 9; matrix products, arithmetic and copies ran while one was open for 6% -> 8% of each run, Pallas kernels for 0% -> 0%
where the time goes in v8:
time: 134 us; the launch traced here: 133 us
  starting transfers between devices  60.2 us (45%)
  other arithmetic  20.1 us (15%)
  blocking collectives  19 us (14%)
  local copies, waits for them, and re-layouts  11 us (8%)
  waiting for transfers between devices  8.89 us (7%)
  matrix products  7.87 us (6%)
  Pallas kernels  4.48 us (3%)
  between operations  1.6 us (1%)
    ppermute x16, starting transfers between devices, shift_from(): return lax.ppermute(x, axis, [(i, (i + k) % n) for i in range(n)])  60.2 us
    all_gather x1, blocking collectives, on_device(): band = lax.all_gather(block, 'col', axis=0, tiled=False)  19 us
    ppermute x16, waiting for transfers between devices, shift_from(): return lax.ppermute(x, axis, [(i, (i + k) % n) for i in range(n)])  8.89 us
    add x6, other arithmetic, sweep(): return v[1:-1, 1:-1] + OMEGA * residual / faces[6]  4.49 us
    pallas_call x1, Pallas kernels, coarse_solve(): return call(lower, near, upper)  4.48 us
    dot_general x9, matrix products, along_y(): jnp.einsum('xjy,xyz->xjz', batched, field, precision=lax.Precision.HIGHEST)  3.86 us
    concatenate x1, local copies, waits for them, and re-layouts, rows_around(): return jnp.concatenate(lower + [x] + upper, axis=axis)  3.31 us
    unnamed x158, local copies, waits for them, and re-layouts  3.22 us
  transfers between devices with their start and end apart: 16, of which 9 were waited for; matrix products, arithmetic and copies ran while one was open for 8% of the time, Pallas kernels for 0%

profile of v8, /device:TPU:1, one launch (start us, length us, event | category | flops | bytes accessed | tf_op | source)
XLA Modules:
  0.0 133.1 jit_solution(3530750792503861756)
XLA Ops:
  0.0 1.3 %pad_maximum_fusion.6 = (f32[3,32,4,128]{3,2,1,0:T(4,128)S(1)}, f32[3,32,4,128]{3,2,1,0:T(4,128)S(1)}) fusion(f32[1,32,16,128]{3,2,1,0:T(8,128)} %bitcast.88, f32[1,32,16,128]{3,2,1,0:T(8,128)} %bitcast.91, f32[1,32,16,128]{3,2,1,0:T(8,128)} %bitcast.84), kind=kLoop, calls=%fused_computation.119 | loop fusion | flops 196608 | bytes 1179648 | tf_op jit(solution)/shard_map/slice | solution.py:23
  1.4 3.9 %collective-permute-start = (f32[3,32,4,128]{3,2,1,0:T(4,128)S(1)}, f32[3,32,4,128]{3,2,1,0:T(4,128)S(1)}, u32[]{:S(2)}, u32[]{:S(2)}) collective-permute-start(f32[3,32,4,128]{3,2,1,0:T(4,128)S(1)} %get-tuple-element.29), channel_id=1, source_target_pairs={{0,1},{1,2},{2,3},{3,4},{4,5},{5,6},{6,7},{7,8},{8,9},{9,10},{10,1... | collective-permute-start | bytes 589832 | tf_op jit(solution)/shard_map/ppermute | solution.py:18
  5.3 5.6 %collective-permute-start.1 = (f32[3,32,4,128]{3,2,1,0:T(4,128)S(1)}, f32[3,32,4,128]{3,2,1,0:T(4,128)S(1)}, u32[]{:S(2)}, u32[]{:S(2)}) collective-permute-start(f32[3,32,4,128]{3,2,1,0:T(4,128)S(1)} %get-tuple-element.30), channel_id=1, source_target_pairs={{0,15},{1,0},{2,1},{3,2},{4,3},{5,4},{6,5},{7,6},{8,7},{9,8},{10,9... | collective-permute-start | bytes 589832 | tf_op jit(solution)/shard_map/ppermute | solution.py:18
  11.2 1.3 fusion.126
  13.6 4.0 %collective-permute-start.2 = (f32[3,4,24,128]{3,2,1,0:T(8,128)S(1)}, f32[3,4,24,128]{3,2,1,0:T(8,128)S(1)}, u32[]{:S(2)}, u32[]{:S(2)}) collective-permute-start(f32[3,4,24,128]{3,2,1,0:T(8,128)S(1)} %get-tuple-element.27), channel_id=1, source_target_pairs={{0,16},{16,32},{32,48},{48,64},{64,80},{80,96},{96,112},{112,128},... | collective-permute-start | bytes 442376 | tf_op jit(solution)/shard_map/ppermute | solution.py:18
  17.6 3.0 %collective-permute-start.3 = (f32[3,4,24,128]{3,2,1,0:T(8,128)S(1)}, f32[3,4,24,128]{3,2,1,0:T(8,128)S(1)}, u32[]{:S(2)}, u32[]{:S(2)}) collective-permute-start(f32[3,4,24,128]{3,2,1,0:T(8,128)S(1)} %get-tuple-element.28), channel_id=1, source_target_pairs={{0,496},{16,0},{32,16},{48,32},{64,48},{80,64},{96,80},{112,96},{1... | collective-permute-start | bytes 442376 | tf_op jit(solution)/shard_map/ppermute | solution.py:18
  24.6 0.9 fusion.18
  26.8 1.9 %collective-permute-start.4 = (f32[2,16,5,64]{3,2,1,0:T(8,128)S(1)}, f32[2,16,5,64]{3,2,1,0:T(8,128)S(1)}, u32[]{:S(2)}, u32[]{:S(2)}) collective-permute-start(f32[2,16,5,64]{3,2,1,0:T(8,128)S(1)} %get-tuple-element.103), channel_id=1, source_target_pairs={{0,1},{1,2},{2,3},{3,4},{4,5},{5,6},{6,7},{7,8},{8,9},{9,10},{10,1... | collective-permute-start | bytes 122888 | tf_op jit(solution)/shard_map/ppermute | solution.py:18
  28.7 7.4 %collective-permute-start.5 = (f32[2,16,5,64]{3,2,1,0:T(8,128)S(1)}, f32[2,16,5,64]{3,2,1,0:T(8,128)S(1)}, u32[]{:S(2)}, u32[]{:S(2)}) collective-permute-start(f32[2,16,5,64]{3,2,1,0:T(8,128)S(1)} %get-tuple-element.104), channel_id=1, source_target_pairs={{0,15},{1,0},{2,1},{3,2},{4,3},{5,4},{6,5},{7,6},{8,7},{9,8},{10,9... | collective-permute-start | bytes 122888 | tf_op jit(solution)/shard_map/ppermute | solution.py:18
  36.7 1.4 %collective-permute-done.5 = f32[2,16,5,64]{3,2,1,0:T(8,128)S(1)} collective-permute-done((f32[2,16,5,64]{3,2,1,0:T(8,128)S(1)}, f32[2,16,5,64]{3,2,1,0:T(8,128)S(1)}, u32[]{:S(2)}, u32[]{:S(2)}) %collective-permute-start.5) | collective-permute-done | bytes 40992 | tf_op jit(solution)/shard_map/ppermute | solution.py:18
  39.5 1.2 collective-permute-start.6
  40.7 4.4 %collective-permute-start.7 = (f32[2,5,18,64]{3,2,1,0:T(8,128)}, f32[2,5,18,64]{3,2,1,0:T(8,128)}, u32[]{:S(2)}, u32[]{:S(2)}) collective-permute-start(f32[2,5,18,64]{3,2,1,0:T(8,128)} %get-tuple-element.48), channel_id=1, source_target_pairs={{0,496},{16,0},{32,16},{48,32},{64,48},{80,64},{96,80},{112,96},{1... | collective-permute-start | bytes 138248 | tf_op jit(solution)/shard_map/ppermute | solution.py:18
  46.4 1.1 pad_maximum_fusion.1
  49.9 19.0 %all_gather.3 = f32[16,2,8,128]{3,2,0,1:T(8,128)S(1)} all-gather(f32[1,2,8,128]{3,2,0,1:T(8,128)S(1)} %pad_maximum_fusion.24), channel_id=1, replica_groups=mesh['row'=32,'col'=16] {'col'}, dimensions={0}, use_global_device_ids=true | all-gather | bytes 139264 | tf_op jit(solution)/shard_map/all_gather | solution.py:332
  69.1 3.8 %collective-permute-start.8 = (f32[16,2,6,128]{3,2,0,1:T(8,128)S(1)}, f32[16,2,6,128]{3,2,0,1:T(8,128)S(1)}, u32[]{:S(2)}, u32[]{:S(2)}) collective-permute-start(f32[16,2,6,128]{3,2,0,1:T(8,128)S(1)} %get-tuple-element.101), channel_id=1, source_target_pairs={{0,16},{16,32},{32,48},{48,64},{64,80},{80,96},{96,112},{112,128},... | collective-permute-start | bytes 294920 | tf_op jit(solution)/shard_map/ppermute | solution.py:18
  72.9 5.6 %collective-permute-start.9 = (f32[16,2,6,128]{3,2,0,1:T(8,128)S(1)}, f32[16,2,6,128]{3,2,0,1:T(8,128)S(1)}, u32[]{:S(2)}, u32[]{:S(2)}) collective-permute-start(f32[16,2,6,128]{3,2,0,1:T(8,128)S(1)} %get-tuple-element.102), channel_id=1, source_target_pairs={{0,496},{16,0},{32,16},{48,32},{64,48},{80,64},{96,80},{112,96},{1... | collective-permute-start | bytes 294920 | tf_op jit(solution)/shard_map/ppermute | solution.py:18
  83.7 1.9 %collective-permute-start.13 = (f32[2,4,512]{2,1,0:T(4,128)S(1)}, f32[2,4,512]{2,1,0:T(4,128)S(1)}, u32[]{:S(2)}, u32[]{:S(2)}) collective-permute-start(f32[2,4,512]{2,1,0:T(4,128)S(1)} %reshape.73), channel_id=1, source_target_pairs={{0,32},{16,48},{32,64},{48,80},{64,96},{80,112},{96,128},{112,144}... | collective-permute-start | bytes 49160 | tf_op jit(solution)/shard_map/ppermute | solution.py:18
  85.7 9.1 %collective-permute-start.11 = (f32[2,4,512]{2,1,0:T(4,128)S(1)}, f32[2,4,512]{2,1,0:T(4,128)S(1)}, u32[]{:S(2)}, u32[]{:S(2)}) collective-permute-start(f32[2,4,512]{2,1,0:T(4,128)S(1)} %reshape.73), channel_id=1, source_target_pairs={{0,480},{16,496},{32,0},{48,16},{64,32},{80,48},{96,64},{112,80},{... | collective-permute-start | bytes 49160 | tf_op jit(solution)/shard_map/ppermute | solution.py:18
  95.5 1.3 fusion.230
  96.8 1.1 collective-permute-done.10
  98.6 4.3 %collective-permute-start.15 = (f32[2,10,512]{2,1,0:T(8,128)}, f32[2,10,512]{2,1,0:T(8,128)}, u32[]{:S(2)}, u32[]{:S(2)}) collective-permute-start(f32[2,10,512]{2,1,0:T(8,128)} %get-tuple-element.107), channel_id=1, source_target_pairs={{0,432},{16,448},{32,464},{48,480},{64,496},{80,0},{96,16},{112,32... | collective-permute-start | bytes 122888 | tf_op jit(solution)/shard_map/ppermute | solution.py:18
  102.9 3.3 %collective-permute-start.12 = (f32[2,10,512]{2,1,0:T(8,128)S(1)}, f32[2,10,512]{2,1,0:T(8,128)}, u32[]{:S(2)}, u32[]{:S(2)}) collective-permute-start(f32[2,10,512]{2,1,0:T(8,128)S(1)} %get-tuple-element.108), channel_id=1, source_target_pairs={{0,80},{16,96},{32,112},{48,128},{64,144},{80,160},{96,176},{112,1... | collective-permute-start | bytes 122888 | tf_op jit(solution)/shard_map/ppermute | solution.py:18
  106.1 1.3 fusion.234
  107.4 3.3 %concatenate.255.refs_1_ = f32[2,20,512]{2,1,0:T(8,128)} concatenate(f32[2,4,512]{2,1,0:T(4,128)S(1)} %collective-permute-done.13, f32[2,4,512]{2,1,0:T(4,128)S(1)} %collective-permute-done.14, f32[2,4,512]{2,1,0:T(4,128)S(1)} %reshape.73, f32[2,4,512]{2,1,0:T(4,128)} %copy-done.45, f32[2,4,512]{2,1,0:T(4,128)} %copy-done.44), dimensions={1} | concatenate | bytes 163840 | tf_op jit(solution)/shard_map/concatenate | solution.py:239
  110.7 4.1 %collective-permute-done.12.refs_0_ = f32[2,10,512]{2,1,0:T(8,128)} collective-permute-done((f32[2,10,512]{2,1,0:T(8,128)S(1)}, f32[2,10,512]{2,1,0:T(8,128)}, u32[]{:S(2)}, u32[]{:S(2)}) %collective-permute-start.12) | collective-permute-done | bytes 40992 | tf_op jit(solution)/shard_map/ppermute | solution.py:18
  114.8 4.5 %shard_map.37 = f32[8,512]{1,0:T(8,128)} custom-call(f32[2,10,512]{2,1,0:T(8,128)} %collective-permute-done.12.refs_0_, f32[2,20,512]{2,1,0:T(8,128)} %concatenate.255.refs_1_, f32[2,10,512]{2,1,0:T(8,128)} %collective-permute-done.15.refs_2_), custom_call_target="tpu_custom_call" | custom-call | flops 13107200 | bytes 491520 | tf_op jit(solution)/shard_map/pallas_call | solution.py:313
  119.3 0.8 reshape.74
  120.1 0.9 fusion.171
  121.0 1.3 %convolution_add_fusion = f32[16,16,128]{2,1,0:T(8,128)S(1)} fusion(f32[16,16,128]{2,1,0:T(8,128)} %copy-done.10, f32[16,8,128]{2,1,0:T(8,128)S(1)} %fusion.171, f32[16,8]{0,1:T(8,128)} %fusion.234), kind=kOutput, calls=%fused_computation.1 | convolution fusion | flops 3178496 | bytes 328192 | tf_op jit(solution)/shard_map/xjy,xyz->xjz/dot_general | solution.py:108
  126.5 1.0 slice_add_fusion
  130.8 0.9 fusion.28
  131.8 1.3 fusion.42
  (290 shorter events, 25.5 us)
Async XLA Ops:
  0.0 13.5 %copy-start.12 = (f32[32,16,128]{2,1,0:T(8,128)S(1)}, f32[32,16,128]{2,1,0:T(8,128)}, u32[]{:S(2)}) copy-start(f32[32,16,128]{2,1,0:T(8,128)} %param.5) | copy-start | bytes 786436
  0.0 13.6 %copy-start.17 = (f32[32,16,128]{2,1,0:T(8,128)S(1)}, f32[32,16,128]{2,1,0:T(8,128)}, u32[]{:S(2)}) copy-start(f32[32,16,128]{2,1,0:T(8,128)} %param.4) | copy-start | bytes 786436
  0.0 13.6 %copy-start.18 = (f32[32,16,128]{2,1,0:T(8,128)S(1)}, f32[32,16,128]{2,1,0:T(8,128)}, u32[]{:S(2)}) copy-start(f32[32,16,128]{2,1,0:T(8,128)} %param.3) | copy-start | bytes 786436
  1.4 11.9 %collective-permute-start = (f32[3,32,4,128]{3,2,1,0:T(4,128)S(1)}, f32[3,32,4,128]{3,2,1,0:T(4,128)S(1)}, u32[]{:S(2)}, u32[]{:S(2)}) collective-permute-start(f32[3,32,4,128]{3,2,1,0:T(4,128)S(1)} %get-tuple-element.29), channel_id=1, source_target_pairs={{0,1},{1,2},{2,3},{3,4},{4,5},{5,6},{6,7},{7,8},{8,9},{9,10},{10,1... | collective-permute-start | bytes 589832 | tf_op jit(solution)/shard_map/ppermute | solution.py:18
  5.3 8.2 %collective-permute-start.1 = (f32[3,32,4,128]{3,2,1,0:T(4,128)S(1)}, f32[3,32,4,128]{3,2,1,0:T(4,128)S(1)}, u32[]{:S(2)}, u32[]{:S(2)}) collective-permute-start(f32[3,32,4,128]{3,2,1,0:T(4,128)S(1)} %get-tuple-element.30), channel_id=1, source_target_pairs={{0,15},{1,0},{2,1},{3,2},{4,3},{5,4},{6,5},{7,6},{8,7},{9,8},{10,9... | collective-permute-start | bytes 589832 | tf_op jit(solution)/shard_map/ppermute | solution.py:18
  11.0 15.2 %copy-start.58 = (pred[128]{0:T(512)(128)(4,1)}, pred[128]{0:T(512)(128)(4,1)S(1)}, u32[]{:S(2)}) copy-start(pred[128]{0:T(512)(128)(4,1)S(1)} %compare_and_fusion.3) | copy-start | bytes 388
  11.0 11.4 %copy-start.76 = (pred[64]{0:T(512)(128)(4,1)}, pred[64]{0:T(512)(128)(4,1)S(1)}, u32[]{:S(2)}) copy-start(pred[64]{0:T(512)(128)(4,1)S(1)} %compare_and_fusion.1) | copy-start | bytes 196
  11.0 11.4 %copy-start.64 = (pred[16]{0:T(512)(128)(4,1)}, pred[16]{0:T(512)(128)(4,1)S(1)}, u32[]{:S(2)}) copy-start(pred[16]{0:T(512)(128)(4,1)S(1)} %compare_and_fusion.4) | copy-start | bytes 52
  11.1 71.9 %copy-start.48 = (pred[128]{0:T(512)(128)(4,1)}, pred[128]{0:T(512)(128)(4,1)S(1)}, u32[]{:S(2)}) copy-start(pred[128]{0:T(512)(128)(4,1)S(1)} %get-tuple-element.122) | copy-start | bytes 388
  11.1 71.9 %copy-start.50 = (pred[128]{0:T(512)(128)(4,1)}, pred[128]{0:T(512)(128)(4,1)S(1)}, u32[]{:S(2)}) copy-start(pred[128]{0:T(512)(128)(4,1)S(1)} %get-tuple-element.123) | copy-start | bytes 388
  11.1 72.3 %copy-start.52 = (s32[128]{0:T(128)}, s32[128]{0:T(128)S(1)}, u32[]{:S(2)}) copy-start(s32[128]{0:T(128)S(1)} %get-tuple-element.120) | copy-start | bytes 1540
  11.1 72.3 %copy-start.54 = (s32[128]{0:T(128)}, s32[128]{0:T(128)S(1)}, u32[]{:S(2)}) copy-start(s32[128]{0:T(128)S(1)} %get-tuple-element.121) | copy-start | bytes 1540
  11.1 15.1 %copy-start.60 = (s32[128]{0:T(128)}, s32[128]{0:T(128)S(1)}, u32[]{:S(2)}) copy-start(s32[128]{0:T(128)S(1)} %get-tuple-element.112) | copy-start | bytes 1540
  11.2 15.1 %copy-start.62 = (s32[128]{0:T(128)}, s32[128]{0:T(128)S(1)}, u32[]{:S(2)}) copy-start(s32[128]{0:T(128)S(1)} %get-tuple-element.113) | copy-start | bytes 1540
  13.6 8.2 %collective-permute-start.2 = (f32[3,4,24,128]{3,2,1,0:T(8,128)S(1)}, f32[3,4,24,128]{3,2,1,0:T(8,128)S(1)}, u32[]{:S(2)}, u32[]{:S(2)}) collective-permute-start(f32[3,4,24,128]{3,2,1,0:T(8,128)S(1)} %get-tuple-element.27), channel_id=1, source_target_pairs={{0,16},{16,32},{32,48},{48,64},{64,80},{80,96},{96,112},{112,128},... | collective-permute-start | bytes 442376 | tf_op jit(solution)/shard_map/ppermute | solution.py:18
  17.6 4.6 %collective-permute-start.3 = (f32[3,4,24,128]{3,2,1,0:T(8,128)S(1)}, f32[3,4,24,128]{3,2,1,0:T(8,128)S(1)}, u32[]{:S(2)}, u32[]{:S(2)}) collective-permute-start(f32[3,4,24,128]{3,2,1,0:T(8,128)S(1)} %get-tuple-element.28), channel_id=1, source_target_pairs={{0,496},{16,0},{32,16},{48,32},{64,48},{80,64},{96,80},{112,96},{1... | collective-permute-start | bytes 442376 | tf_op jit(solution)/shard_map/ppermute | solution.py:18
  26.8 9.9 %collective-permute-start.4 = (f32[2,16,5,64]{3,2,1,0:T(8,128)S(1)}, f32[2,16,5,64]{3,2,1,0:T(8,128)S(1)}, u32[]{:S(2)}, u32[]{:S(2)}) collective-permute-start(f32[2,16,5,64]{3,2,1,0:T(8,128)S(1)} %get-tuple-element.103), channel_id=1, source_target_pairs={{0,1},{1,2},{2,3},{3,4},{4,5},{5,6},{6,7},{7,8},{8,9},{9,10},{10,1... | collective-permute-start | bytes 122888 | tf_op jit(solution)/shard_map/ppermute | solution.py:18
  28.7 9.4 %collective-permute-start.5 = (f32[2,16,5,64]{3,2,1,0:T(8,128)S(1)}, f32[2,16,5,64]{3,2,1,0:T(8,128)S(1)}, u32[]{:S(2)}, u32[]{:S(2)}) collective-permute-start(f32[2,16,5,64]{3,2,1,0:T(8,128)S(1)} %get-tuple-element.104), channel_id=1, source_target_pairs={{0,15},{1,0},{2,1},{3,2},{4,3},{5,4},{6,5},{7,6},{8,7},{9,8},{10,9... | collective-permute-start | bytes 122888 | tf_op jit(solution)/shard_map/ppermute | solution.py:18
  36.7 46.7 %copy-start.56 = (pred[128]{0:T(512)(128)(4,1)}, pred[128]{0:T(512)(128)(4,1)S(1)}, u32[]{:S(2)}) copy-start(pred[128]{0:T(512)(128)(4,1)S(1)} %get-tuple-element.110) | copy-start | bytes 388
  39.5 6.7 %collective-permute-start.6 = (f32[2,5,18,64]{3,2,1,0:T(8,128)}, f32[2,5,18,64]{3,2,1,0:T(8,128)}, u32[]{:S(2)}, u32[]{:S(2)}) collective-permute-start(f32[2,5,18,64]{3,2,1,0:T(8,128)} %get-tuple-element.47), channel_id=1, source_target_pairs={{0,16},{16,32},{32,48},{48,64},{64,80},{80,96},{96,112},{112,128},... | collective-permute-start | bytes 138248 | tf_op jit(solution)/shard_map/ppermute | solution.py:18
  40.7 5.7 %collective-permute-start.7 = (f32[2,5,18,64]{3,2,1,0:T(8,128)}, f32[2,5,18,64]{3,2,1,0:T(8,128)}, u32[]{:S(2)}, u32[]{:S(2)}) collective-permute-start(f32[2,5,18,64]{3,2,1,0:T(8,128)} %get-tuple-element.48), channel_id=1, source_target_pairs={{0,496},{16,0},{32,16},{48,32},{64,48},{80,64},{96,80},{112,96},{1... | collective-permute-start | bytes 138248 | tf_op jit(solution)/shard_map/ppermute | solution.py:18
  48.7 29.8 %copy-start.73 = (s32[128]{0:T(128)S(1)}, s32[128]{0:T(128)}, u32[]{:S(2)}) copy-start(s32[128]{0:T(128)} %get-tuple-element.124) | copy-start | bytes 1540
  48.7 29.8 %copy-start.74 = (s32[128]{0:T(128)S(1)}, s32[128]{0:T(128)}, u32[]{:S(2)}) copy-start(s32[128]{0:T(128)} %get-tuple-element.125) | copy-start | bytes 1540
  48.7 29.8 %copy-start.75 = (pred[128]{0:T(512)(128)(4,1)S(1)}, pred[128]{0:T(512)(128)(4,1)}, u32[]{:S(2)}) copy-start(pred[128]{0:T(512)(128)(4,1)} %get-tuple-element.111) | copy-start | bytes 388
  69.1 10.2 %collective-permute-start.8 = (f32[16,2,6,128]{3,2,0,1:T(8,128)S(1)}, f32[16,2,6,128]{3,2,0,1:T(8,128)S(1)}, u32[]{:S(2)}, u32[]{:S(2)}) collective-permute-start(f32[16,2,6,128]{3,2,0,1:T(8,128)S(1)} %get-tuple-element.101), channel_id=1, source_target_pairs={{0,16},{16,32},{32,48},{48,64},{64,80},{80,96},{96,112},{112,128},... | collective-permute-start | bytes 294920 | tf_op jit(solution)/shard_map/ppermute | solution.py:18
  72.9 6.6 %collective-permute-start.9 = (f32[16,2,6,128]{3,2,0,1:T(8,128)S(1)}, f32[16,2,6,128]{3,2,0,1:T(8,128)S(1)}, u32[]{:S(2)}, u32[]{:S(2)}) collective-permute-start(f32[16,2,6,128]{3,2,0,1:T(8,128)S(1)} %get-tuple-element.102), channel_id=1, source_target_pairs={{0,496},{16,0},{32,16},{48,32},{64,48},{80,64},{96,80},{112,96},{1... | collective-permute-start | bytes 294920 | tf_op jit(solution)/shard_map/ppermute | solution.py:18
  83.7 13.1 %collective-permute-start.14 = (f32[2,4,512]{2,1,0:T(4,128)S(1)}, f32[2,4,512]{2,1,0:T(4,128)S(1)}, u32[]{:S(2)}, u32[]{:S(2)}) collective-permute-start(f32[2,4,512]{2,1,0:T(4,128)S(1)} %reshape.73), channel_id=1, source_target_pairs={{0,16},{16,32},{32,48},{48,64},{64,80},{80,96},{96,112},{112,128},... | collective-permute-start | bytes 49160 | tf_op jit(solution)/shard_map/ppermute | solution.py:18
  83.7 13.0 %collective-permute-start.13 = (f32[2,4,512]{2,1,0:T(4,128)S(1)}, f32[2,4,512]{2,1,0:T(4,128)S(1)}, u32[]{:S(2)}, u32[]{:S(2)}) collective-permute-start(f32[2,4,512]{2,1,0:T(4,128)S(1)} %reshape.73), channel_id=1, source_target_pairs={{0,32},{16,48},{32,64},{48,80},{64,96},{80,112},{96,128},{112,144}... | collective-permute-start | bytes 49160 | tf_op jit(solution)/shard_map/ppermute | solution.py:18
  85.7 11.1 %collective-permute-start.11 = (f32[2,4,512]{2,1,0:T(4,128)S(1)}, f32[2,4,512]{2,1,0:T(4,128)S(1)}, u32[]{:S(2)}, u32[]{:S(2)}) collective-permute-start(f32[2,4,512]{2,1,0:T(4,128)S(1)} %reshape.73), channel_id=1, source_target_pairs={{0,480},{16,496},{32,0},{48,16},{64,32},{80,48},{96,64},{112,80},{... | collective-permute-start | bytes 49160 | tf_op jit(solution)/shard_map/ppermute | solution.py:18
  94.7 3.2 %collective-permute-start.10 = (f32[2,4,512]{2,1,0:T(4,128)S(1)}, f32[2,4,512]{2,1,0:T(4,128)S(1)}, u32[]{:S(2)}, u32[]{:S(2)}) collective-permute-start(f32[2,4,512]{2,1,0:T(4,128)S(1)} %reshape.73), channel_id=1, source_target_pairs={{0,496},{16,0},{32,16},{48,32},{64,48},{80,64},{96,80},{112,96},{1... | collective-permute-start | bytes 49160 | tf_op jit(solution)/shard_map/ppermute | solution.py:18
  98.6 12.1 %collective-permute-start.15 = (f32[2,10,512]{2,1,0:T(8,128)}, f32[2,10,512]{2,1,0:T(8,128)}, u32[]{:S(2)}, u32[]{:S(2)}) collective-permute-start(f32[2,10,512]{2,1,0:T(8,128)} %get-tuple-element.107), channel_id=1, source_target_pairs={{0,432},{16,448},{32,464},{48,480},{64,496},{80,0},{96,16},{112,32... | collective-permute-start | bytes 122888 | tf_op jit(solution)/shard_map/ppermute | solution.py:18
  102.9 12.0 %collective-permute-start.12 = (f32[2,10,512]{2,1,0:T(8,128)S(1)}, f32[2,10,512]{2,1,0:T(8,128)}, u32[]{:S(2)}, u32[]{:S(2)}) collective-permute-start(f32[2,10,512]{2,1,0:T(8,128)S(1)} %get-tuple-element.108), channel_id=1, source_target_pairs={{0,80},{16,96},{32,112},{48,128},{64,144},{80,160},{96,176},{112,1... | collective-permute-start | bytes 122888 | tf_op jit(solution)/shard_map/ppermute | solution.py:18
  (63 other events, 130.0 us)

commit v9 on v8

--- a/solution.py
+++ b/solution.py
@@ -239,12 +239,18 @@
     return jnp.concatenate(lower + [x] + upper, axis=axis)
 
 
-def coarse_kernel(scale, size_z, spans, keep, lower_ref, own_ref, upper_ref, out_ref, tile_ref):
-    span, extra = spans
-    for f in range(2):
-        tile_ref[f, 0:extra] = lower_ref[f]
-        tile_ref[f, extra : extra + span] = own_ref[f]
-        tile_ref[f, extra + span : 2 * extra + span] = upper_ref[f]
+def coarse_kernel(scale, size_z, keep, near_refs, lower_ref, upper_ref, out_ref, tile_ref):
+    size_x = near_refs[0].shape[1]
+    rows = tile_ref.shape[1]
+    reach = (rows - size_x) // 2
+    sources = [lower_ref.at[i] for i in range(3)] + list(near_refs) + [upper_ref.at[i] for i in range(3)]
+    for d, ref in zip(range(-5, 6), sources):
+        start = max(d * size_x, -reach)
+        end = min(d * size_x + size_x, size_x + reach)
+        if start >= end:
+            continue
+        for f in range(2):
+            tile_ref[f, start + reach : end + reach] = ref[f, start - d * size_x : end - d * size_x]
     b = tile_ref[0]
     k = tile_ref[1]
     rows, lanes = k.shape
@@ -292,25 +298,26 @@
 
 def coarse_solve(pair, size_z, scale):
     size_x, lanes = pair.shape[1:]
-    near = rows_around(pair, (1, 2), 1)
-    span = near.shape[1]
-    extra = CSWEEPS + 2 - (span - size_x) // 2
-    extra += (-(span + 2 * extra)) % 8 // 2
-    assert 0 < extra <= span
-    rows = span + 2 * extra
+    m1, p1 = shift_from(pair, "row", 1), shift_from(pair, "row", -1)
+    m2, p2 = shift_from(pair, "row", 2), shift_from(pair, "row", -2)
+    near = [m2, m1, pair, p1, p2]
+    lower = shift_from(jnp.stack([pair, p1, p2]), "row", 5)
+    upper = shift_from(jnp.stack([m2, m1, pair]), "row", -5)
+    reach = CSWEEPS + 2
+    reach += (-(size_x + 2 * reach)) % 8 // 2
+    assert reach <= 5 * size_x
+    rows = size_x + 2 * reach
     keep = 8
     assert (rows - keep) // 2 >= CSWEEPS
-    lower = shift_from(near[:, span - extra :], "row", 5)
-    upper = shift_from(near[:, :extra], "row", -5)
     call = pl.pallas_call(
-        lambda *refs: coarse_kernel(scale, size_z, (span, extra), keep, *refs),
+        lambda *refs: coarse_kernel(scale, size_z, keep, refs[:5], *refs[5:]),
         out_shape=jax.ShapeDtypeStruct((keep, lanes), jnp.float32),
         scratch_shapes=[pltpu.VMEM((2, rows, lanes), jnp.float32)],
         cost_estimate=pl.CostEstimate(
             flops=40 * CSWEEPS * rows * lanes, transcendentals=0, bytes_accessed=24 * rows * lanes
         ),
     )
-    return call(lower, near, upper)
+    return call(*near, lower, upper)
 
 
 def on_device(pressure_in, source, permeability):

time: 134 us -> 135 us (level)
  waiting for transfers between devices: 8.89 us -> 12.3 us
  local copies, waits for them, and re-layouts: 11 us -> 7.75 us
    ppermute x16, waiting for transfers between devices: 8.89 us -> 12.3 us  [shift_from(): return lax.ppermute(x, axis, [(i, (i + k) % n) for i in range(n)])]
    concatenate x1 -> x0, local copies, waits for them, and re-layouts: 3.31 us -> none  [rows_around(): return jnp.concatenate(lower + [x] + upper, axis=axis)]
    another operation x0 -> x1, other arithmetic: none -> 1.48 us  [coarse_solve(): upper = shift_from(jnp.stack([m2, m1, pair]), 'row', -5)]
  transfers between devices with their start and end apart: 16 -> 16, of which waited for: 9 -> 11; matrix products, arithmetic and copies ran while one was open for 8% -> 5% of each run, Pallas kernels for 0% -> 0%
where the time goes in v9:
time: 135 us; the launch traced here: 134 us
  starting transfers between devices  61.2 us (45%)
  other arithmetic  20 us (15%)
  blocking collectives  19 us (14%)
  waiting for transfers between devices  12.3 us (9%)
  matrix products  7.88 us (6%)
  local copies, waits for them, and re-layouts  7.75 us (6%)
  Pallas kernels  4.5 us (3%)
  between operations  1.57 us (1%)
    ppermute x16, starting transfers between devices, shift_from(): return lax.ppermute(x, axis, [(i, (i + k) % n) for i in range(n)])  61.2 us
    all_gather x1, blocking collectives, on_device(): band = lax.all_gather(block, 'col', axis=0, tiled=False)  19 us
    ppermute x16, waiting for transfers between devices, shift_from(): return lax.ppermute(x, axis, [(i, (i + k) % n) for i in range(n)])  12.3 us
    add x6, other arithmetic, sweep(): return v[1:-1, 1:-1] + OMEGA * residual / faces[6]  4.52 us
    pallas_call x1, Pallas kernels, coarse_solve(): return call(*near, lower, upper)  4.5 us
    dot_general x9, matrix products, along_y(): jnp.einsum('xjy,xyz->xjz', batched, field, precision=lax.Precision.HIGHEST)  3.86 us
    dot_general x6, matrix products, along_z(): out = jnp.dot(flat, matrix, precision=lax.Precision.HIGHEST)  2.83 us
  transfers between devices with their start and end apart: 16, of which 11 were waited for; matrix products, arithmetic and copies ran while one was open for 5% of the time, Pallas kernels for 0%

profile of v9, /device:TPU:1, one launch (start us, length us, event | category | flops | bytes accessed | tf_op | source)
XLA Modules:
  0.0 134.1 jit_solution(11888303301375815028)
XLA Ops:
  0.0 1.3 pad_maximum_fusion.6
  1.4 3.9 %collective-permute-start = (f32[3,32,4,128]{3,2,1,0:T(4,128)S(1)}, f32[3,32,4,128]{3,2,1,0:T(4,128)S(1)}, u32[]{:S(2)}, u32[]{:S(2)}) collective-permute-start(f32[3,32,4,128]{3,2,1,0:T(4,128)S(1)} %get-tuple-element.29), channel_id=1, source_target_pairs={{0,1},{1,2},{2,3},{3,4},{4,5},{5,6},{6,7},{7,8},{8,9},{9,10},{10,1... | collective-permute-start | bytes 589832 | tf_op jit(solution)/shard_map/ppermute | solution.py:18
  5.3 5.6 %collective-permute-start.1 = (f32[3,32,4,128]{3,2,1,0:T(4,128)S(1)}, f32[3,32,4,128]{3,2,1,0:T(4,128)S(1)}, u32[]{:S(2)}, u32[]{:S(2)}) collective-permute-start(f32[3,32,4,128]{3,2,1,0:T(4,128)S(1)} %get-tuple-element.30), channel_id=1, source_target_pairs={{0,15},{1,0},{2,1},{3,2},{4,3},{5,4},{6,5},{7,6},{8,7},{9,8},{10,9... | collective-permute-start | bytes 589832 | tf_op jit(solution)/shard_map/ppermute | solution.py:18
  11.2 1.3 fusion.126
  13.6 4.0 %collective-permute-start.2 = (f32[3,4,24,128]{3,2,1,0:T(8,128)S(1)}, f32[3,4,24,128]{3,2,1,0:T(8,128)S(1)}, u32[]{:S(2)}, u32[]{:S(2)}) collective-permute-start(f32[3,4,24,128]{3,2,1,0:T(8,128)S(1)} %get-tuple-element.27), channel_id=1, source_target_pairs={{0,16},{16,32},{32,48},{48,64},{64,80},{80,96},{96,112},{112,128},... | collective-permute-start | bytes 442376 | tf_op jit(solution)/shard_map/ppermute | solution.py:18
  17.6 3.0 %collective-permute-start.3 = (f32[3,4,24,128]{3,2,1,0:T(8,128)S(1)}, f32[3,4,24,128]{3,2,1,0:T(8,128)S(1)}, u32[]{:S(2)}, u32[]{:S(2)}) collective-permute-start(f32[3,4,24,128]{3,2,1,0:T(8,128)S(1)} %get-tuple-element.28), channel_id=1, source_target_pairs={{0,496},{16,0},{32,16},{48,32},{64,48},{80,64},{96,80},{112,96},{1... | collective-permute-start | bytes 442376 | tf_op jit(solution)/shard_map/ppermute | solution.py:18
  24.5 0.9 fusion.18
  26.8 1.9 %collective-permute-start.4 = (f32[2,16,5,64]{3,2,1,0:T(8,128)S(1)}, f32[2,16,5,64]{3,2,1,0:T(8,128)S(1)}, u32[]{:S(2)}, u32[]{:S(2)}) collective-permute-start(f32[2,16,5,64]{3,2,1,0:T(8,128)S(1)} %get-tuple-element.103), channel_id=1, source_target_pairs={{0,1},{1,2},{2,3},{3,4},{4,5},{5,6},{6,7},{7,8},{8,9},{9,10},{10,1... | collective-permute-start | bytes 122888 | tf_op jit(solution)/shard_map/ppermute | solution.py:18
  28.7 7.4 %collective-permute-start.5 = (f32[2,16,5,64]{3,2,1,0:T(8,128)S(1)}, f32[2,16,5,64]{3,2,1,0:T(8,128)S(1)}, u32[]{:S(2)}, u32[]{:S(2)}) collective-permute-start(f32[2,16,5,64]{3,2,1,0:T(8,128)S(1)} %get-tuple-element.104), channel_id=1, source_target_pairs={{0,15},{1,0},{2,1},{3,2},{4,3},{5,4},{6,5},{7,6},{8,7},{9,8},{10,9... | collective-permute-start | bytes 122888 | tf_op jit(solution)/shard_map/ppermute | solution.py:18
  36.6 1.5 %collective-permute-done.5 = f32[2,16,5,64]{3,2,1,0:T(8,128)S(1)} collective-permute-done((f32[2,16,5,64]{3,2,1,0:T(8,128)S(1)}, f32[2,16,5,64]{3,2,1,0:T(8,128)S(1)}, u32[]{:S(2)}, u32[]{:S(2)}) %collective-permute-start.5) | collective-permute-done | bytes 40992 | tf_op jit(solution)/shard_map/ppermute | solution.py:18
  38.8 1.2 collective-permute-start.6
  40.0 4.3 %collective-permute-start.7 = (f32[2,5,18,64]{3,2,1,0:T(8,128)}, f32[2,5,18,64]{3,2,1,0:T(8,128)}, u32[]{:S(2)}, u32[]{:S(2)}) collective-permute-start(f32[2,5,18,64]{3,2,1,0:T(8,128)} %get-tuple-element.48), channel_id=1, source_target_pairs={{0,496},{16,0},{32,16},{48,32},{64,48},{80,64},{96,80},{112,96},{1... | collective-permute-start | bytes 138248 | tf_op jit(solution)/shard_map/ppermute | solution.py:18
  45.7 1.2 pad_maximum_fusion.1
  49.2 19.0 %all_gather.3 = f32[16,2,8,128]{3,2,0,1:T(8,128)S(1)} all-gather(f32[1,2,8,128]{3,2,0,1:T(8,128)S(1)} %pad_maximum_fusion.22), channel_id=1, replica_groups=mesh['row'=32,'col'=16] {'col'}, dimensions={0}, use_global_device_ids=true | all-gather | bytes 139264 | tf_op jit(solution)/shard_map/all_gather | solution.py:339
  68.5 3.8 %collective-permute-start.8 = (f32[16,2,6,128]{3,2,0,1:T(8,128)S(1)}, f32[16,2,6,128]{3,2,0,1:T(8,128)S(1)}, u32[]{:S(2)}, u32[]{:S(2)}) collective-permute-start(f32[16,2,6,128]{3,2,0,1:T(8,128)S(1)} %get-tuple-element.101), channel_id=1, source_target_pairs={{0,16},{16,32},{32,48},{48,64},{64,80},{80,96},{96,112},{112,128},... | collective-permute-start | bytes 294920 | tf_op jit(solution)/shard_map/ppermute | solution.py:18
  72.3 5.5 %collective-permute-start.9 = (f32[16,2,6,128]{3,2,0,1:T(8,128)S(1)}, f32[16,2,6,128]{3,2,0,1:T(8,128)S(1)}, u32[]{:S(2)}, u32[]{:S(2)}) collective-permute-start(f32[16,2,6,128]{3,2,0,1:T(8,128)S(1)} %get-tuple-element.102), channel_id=1, source_target_pairs={{0,496},{16,0},{32,16},{48,32},{64,48},{80,64},{96,80},{112,96},{1... | collective-permute-start | bytes 294920 | tf_op jit(solution)/shard_map/ppermute | solution.py:18
  83.1 9.1 %collective-permute-start.13 = (f32[2,4,512]{2,1,0:T(4,128)S(1)}, f32[2,4,512]{2,1,0:T(4,128)S(1)}, u32[]{:S(2)}, u32[]{:S(2)}) collective-permute-start(f32[2,4,512]{2,1,0:T(4,128)S(1)} %reshape.73.refs_2_), channel_id=1, source_target_pairs={{0,480},{16,496},{32,0},{48,16},{64,32},{80,48},{96,64},{112,80},{... | collective-permute-start | bytes 49160 | tf_op jit(solution)/shard_map/ppermute | solution.py:18
  92.2 1.7 %collective-permute-start.11 = (f32[2,4,512]{2,1,0:T(4,128)S(1)}, f32[2,4,512]{2,1,0:T(4,128)}, u32[]{:S(2)}, u32[]{:S(2)}) collective-permute-start(f32[2,4,512]{2,1,0:T(4,128)S(1)} %reshape.73.refs_2_), channel_id=1, source_target_pairs={{0,16},{16,32},{32,48},{48,64},{64,80},{80,96},{96,112},{112,128},... | collective-permute-start | bytes 49160 | tf_op jit(solution)/shard_map/ppermute | solution.py:18
  93.9 1.9 %collective-permute-start.10 = (f32[2,4,512]{2,1,0:T(4,128)S(1)}, f32[2,4,512]{2,1,0:T(4,128)}, u32[]{:S(2)}, u32[]{:S(2)}) collective-permute-start(f32[2,4,512]{2,1,0:T(4,128)S(1)} %reshape.73.refs_2_), channel_id=1, source_target_pairs={{0,32},{16,48},{32,64},{48,80},{64,96},{80,112},{96,128},{112,144}... | collective-permute-start | bytes 49160 | tf_op jit(solution)/shard_map/ppermute | solution.py:18
  95.8 1.3 fusion.230
  97.8 1.9 %collective-permute-done.10.refs_0_ = f32[2,4,512]{2,1,0:T(4,128)} collective-permute-done((f32[2,4,512]{2,1,0:T(4,128)S(1)}, f32[2,4,512]{2,1,0:T(4,128)}, u32[]{:S(2)}, u32[]{:S(2)}) %collective-permute-start.10) | collective-permute-done | bytes 16416 | tf_op jit(solution)/shard_map/ppermute | solution.py:18
  99.7 1.5 %pad_maximum_fusion.20 = (f32[3,2,4,512]{3,2,1,0:T(4,128)}, f32[3,2,4,512]{3,2,1,0:T(4,128)}) fusion(f32[1,2,4,512]{3,2,1,0:T(4,128)} %stack_reshape.4, f32[1,2,4,512]{3,2,1,0:T(4,128)} %bitcast.33, f32[1,2,4,512]{3,2,1,0:T(4,128)} %bitcast.32, f32[1,2,4,512]{3,2,1,0:T(4,128)S(1)} %bitcast.108, f32[1,2,4,512]{3,2,1,0:T(4,128)S(1)} %bitcast.109), kind=kLoop, calls=%fused_computation.382 | loop fusion | flops 49152 | bytes 180224 | tf_op jit(solution)/shard_map/stack | solution.py:305
  101.2 5.4 %collective-permute-start.15 = (f32[3,2,4,512]{3,2,1,0:T(4,128)}, f32[3,2,4,512]{3,2,1,0:T(4,128)S(1)}, u32[]{:S(2)}, u32[]{:S(2)}) collective-permute-start(f32[3,2,4,512]{3,2,1,0:T(4,128)} %get-tuple-element.107), channel_id=1, source_target_pairs={{0,432},{16,448},{32,464},{48,480},{64,496},{80,0},{96,16},{112,32... | collective-permute-start | bytes 147464 | tf_op jit(solution)/shard_map/ppermute | solution.py:18
  106.6 2.2 %collective-permute-start.14 = (f32[3,2,4,512]{3,2,1,0:T(4,128)}, f32[3,2,4,512]{3,2,1,0:T(4,128)}, u32[]{:S(2)}, u32[]{:S(2)}) collective-permute-start(f32[3,2,4,512]{3,2,1,0:T(4,128)} %get-tuple-element.108), channel_id=1, source_target_pairs={{0,80},{16,96},{32,112},{48,128},{64,144},{80,160},{96,176},{112,1... | collective-permute-start | bytes 147464 | tf_op jit(solution)/shard_map/ppermute | solution.py:18
  108.7 1.3 fusion.234
  110.0 5.7 %collective-permute-done.14.refs_5_ = f32[3,2,4,512]{3,2,1,0:T(4,128)} collective-permute-done((f32[3,2,4,512]{3,2,1,0:T(4,128)}, f32[3,2,4,512]{3,2,1,0:T(4,128)}, u32[]{:S(2)}, u32[]{:S(2)}) %collective-permute-start.14) | collective-permute-done | bytes 49184 | tf_op jit(solution)/shard_map/ppermute | solution.py:18
  115.7 4.5 %shard_map.37 = f32[8,512]{1,0:T(8,128)} custom-call(f32[2,4,512]{2,1,0:T(4,128)} %collective-permute-done.10.refs_0_, f32[2,4,512]{2,1,0:T(4,128)} %collective-permute-done.11.refs_1_, f32[2,4,512]{2,1,0:T(4,128)} %copy-done.45, f32[2,4,512]{2,1,0:T(4,128)} %copy-done.47, f32[2,4,512]{2,1,0:T(4,128)} %copy-done.46, ...), custom_call_target="tpu_custom_call" | custom-call | flops 13107200 | bytes 491520 | tf_op jit(solution)/shard_map/pallas_call | solution.py:320
  121.0 0.9 fusion.171
  121.9 1.3 convolution_add_fusion
  127.4 1.0 slice_add_fusion
  131.7 0.9 fusion.28
  132.8 1.3 fusion.42
  (290 shorter events, 24.8 us)
Async XLA Ops:
  1.4 11.9 %collective-permute-start = (f32[3,32,4,128]{3,2,1,0:T(4,128)S(1)}, f32[3,32,4,128]{3,2,1,0:T(4,128)S(1)}, u32[]{:S(2)}, u32[]{:S(2)}) collective-permute-start(f32[3,32,4,128]{3,2,1,0:T(4,128)S(1)} %get-tuple-element.29), channel_id=1, source_target_pairs={{0,1},{1,2},{2,3},{3,4},{4,5},{5,6},{6,7},{7,8},{8,9},{9,10},{10,1... | collective-permute-start | bytes 589832 | tf_op jit(solution)/shard_map/ppermute | solution.py:18
  5.3 8.2 %collective-permute-start.1 = (f32[3,32,4,128]{3,2,1,0:T(4,128)S(1)}, f32[3,32,4,128]{3,2,1,0:T(4,128)S(1)}, u32[]{:S(2)}, u32[]{:S(2)}) collective-permute-start(f32[3,32,4,128]{3,2,1,0:T(4,128)S(1)} %get-tuple-element.30), channel_id=1, source_target_pairs={{0,15},{1,0},{2,1},{3,2},{4,3},{5,4},{6,5},{7,6},{8,7},{9,8},{10,9... | collective-permute-start | bytes 589832 | tf_op jit(solution)/shard_map/ppermute | solution.py:18
  11.0 15.2 %copy-start.61 = (pred[128]{0:T(512)(128)(4,1)}, pred[128]{0:T(512)(128)(4,1)S(1)}, u32[]{:S(2)}) copy-start(pred[128]{0:T(512)(128)(4,1)S(1)} %compare_and_fusion.3) | copy-start | bytes 388
  11.0 37.7 %copy-start.77 = (pred[64]{0:T(512)(128)(4,1)}, pred[64]{0:T(512)(128)(4,1)S(1)}, u32[]{:S(2)}) copy-start(pred[64]{0:T(512)(128)(4,1)S(1)} %compare_and_fusion.1) | copy-start | bytes 196
  11.1 71.2 %copy-start.51 = (pred[128]{0:T(512)(128)(4,1)}, pred[128]{0:T(512)(128)(4,1)S(1)}, u32[]{:S(2)}) copy-start(pred[128]{0:T(512)(128)(4,1)S(1)} %get-tuple-element.122) | copy-start | bytes 388
  11.1 71.2 %copy-start.53 = (pred[128]{0:T(512)(128)(4,1)}, pred[128]{0:T(512)(128)(4,1)S(1)}, u32[]{:S(2)}) copy-start(pred[128]{0:T(512)(128)(4,1)S(1)} %get-tuple-element.123) | copy-start | bytes 388
  11.1 71.7 %copy-start.55 = (s32[128]{0:T(128)}, s32[128]{0:T(128)S(1)}, u32[]{:S(2)}) copy-start(s32[128]{0:T(128)S(1)} %get-tuple-element.120) | copy-start | bytes 1540
  11.1 71.7 %copy-start.57 = (s32[128]{0:T(128)}, s32[128]{0:T(128)S(1)}, u32[]{:S(2)}) copy-start(s32[128]{0:T(128)S(1)} %get-tuple-element.121) | copy-start | bytes 1540
  11.1 15.0 %copy-start.63 = (s32[128]{0:T(128)}, s32[128]{0:T(128)S(1)}, u32[]{:S(2)}) copy-start(s32[128]{0:T(128)S(1)} %get-tuple-element.112) | copy-start | bytes 1540
  11.2 37.5 %copy-start.70 = (s32[64]{0:T(128)}, s32[64]{0:T(128)S(1)}, u32[]{:S(2)}) copy-start(s32[64]{0:T(128)S(1)} %get-tuple-element.116) | copy-start | bytes 772
  11.2 37.5 %copy-start.72 = (s32[64]{0:T(128)}, s32[64]{0:T(128)S(1)}, u32[]{:S(2)}) copy-start(s32[64]{0:T(128)S(1)} %get-tuple-element.117) | copy-start | bytes 772
  13.6 7.9 %collective-permute-start.2 = (f32[3,4,24,128]{3,2,1,0:T(8,128)S(1)}, f32[3,4,24,128]{3,2,1,0:T(8,128)S(1)}, u32[]{:S(2)}, u32[]{:S(2)}) collective-permute-start(f32[3,4,24,128]{3,2,1,0:T(8,128)S(1)} %get-tuple-element.27), channel_id=1, source_target_pairs={{0,16},{16,32},{32,48},{48,64},{64,80},{80,96},{96,112},{112,128},... | collective-permute-start | bytes 442376 | tf_op jit(solution)/shard_map/ppermute | solution.py:18
  17.6 4.6 %collective-permute-start.3 = (f32[3,4,24,128]{3,2,1,0:T(8,128)S(1)}, f32[3,4,24,128]{3,2,1,0:T(8,128)S(1)}, u32[]{:S(2)}, u32[]{:S(2)}) collective-permute-start(f32[3,4,24,128]{3,2,1,0:T(8,128)S(1)} %get-tuple-element.28), channel_id=1, source_target_pairs={{0,496},{16,0},{32,16},{48,32},{64,48},{80,64},{96,80},{112,96},{1... | collective-permute-start | bytes 442376 | tf_op jit(solution)/shard_map/ppermute | solution.py:18
  20.7 62.1 %copy-start.74 = (s32[128]{0:T(128)}, s32[128]{0:T(128)S(1)}, u32[]{:S(2)}) copy-start(s32[128]{0:T(128)S(1)} %get-tuple-element.124) | copy-start | bytes 1540
  20.7 62.1 %copy-start.75 = (s32[128]{0:T(128)}, s32[128]{0:T(128)S(1)}, u32[]{:S(2)}) copy-start(s32[128]{0:T(128)S(1)} %get-tuple-element.125) | copy-start | bytes 1540
  26.8 9.8 %collective-permute-start.4 = (f32[2,16,5,64]{3,2,1,0:T(8,128)S(1)}, f32[2,16,5,64]{3,2,1,0:T(8,128)S(1)}, u32[]{:S(2)}, u32[]{:S(2)}) collective-permute-start(f32[2,16,5,64]{3,2,1,0:T(8,128)S(1)} %get-tuple-element.103), channel_id=1, source_target_pairs={{0,1},{1,2},{2,3},{3,4},{4,5},{5,6},{6,7},{7,8},{8,9},{9,10},{10,1... | collective-permute-start | bytes 122888 | tf_op jit(solution)/shard_map/ppermute | solution.py:18
  28.7 9.4 %collective-permute-start.5 = (f32[2,16,5,64]{3,2,1,0:T(8,128)S(1)}, f32[2,16,5,64]{3,2,1,0:T(8,128)S(1)}, u32[]{:S(2)}, u32[]{:S(2)}) collective-permute-start(f32[2,16,5,64]{3,2,1,0:T(8,128)S(1)} %get-tuple-element.104), channel_id=1, source_target_pairs={{0,15},{1,0},{2,1},{3,2},{4,3},{5,4},{6,5},{7,6},{8,7},{9,8},{10,9... | collective-permute-start | bytes 122888 | tf_op jit(solution)/shard_map/ppermute | solution.py:18
  36.2 46.6 %copy-start.59 = (pred[128]{0:T(512)(128)(4,1)}, pred[128]{0:T(512)(128)(4,1)S(1)}, u32[]{:S(2)}) copy-start(pred[128]{0:T(512)(128)(4,1)S(1)} %get-tuple-element.110) | copy-start | bytes 388
  36.2 46.6 %copy-start.76 = (pred[128]{0:T(512)(128)(4,1)}, pred[128]{0:T(512)(128)(4,1)S(1)}, u32[]{:S(2)}) copy-start(pred[128]{0:T(512)(128)(4,1)S(1)} %get-tuple-element.111) | copy-start | bytes 388
  38.8 6.7 %collective-permute-start.6 = (f32[2,5,18,64]{3,2,1,0:T(8,128)}, f32[2,5,18,64]{3,2,1,0:T(8,128)}, u32[]{:S(2)}, u32[]{:S(2)}) collective-permute-start(f32[2,5,18,64]{3,2,1,0:T(8,128)} %get-tuple-element.47), channel_id=1, source_target_pairs={{0,16},{16,32},{32,48},{48,64},{64,80},{80,96},{96,112},{112,128},... | collective-permute-start | bytes 138248 | tf_op jit(solution)/shard_map/ppermute | solution.py:18
  40.0 5.6 %collective-permute-start.7 = (f32[2,5,18,64]{3,2,1,0:T(8,128)}, f32[2,5,18,64]{3,2,1,0:T(8,128)}, u32[]{:S(2)}, u32[]{:S(2)}) collective-permute-start(f32[2,5,18,64]{3,2,1,0:T(8,128)} %get-tuple-element.48), channel_id=1, source_target_pairs={{0,496},{16,0},{32,16},{48,32},{64,48},{80,64},{96,80},{112,96},{1... | collective-permute-start | bytes 138248 | tf_op jit(solution)/shard_map/ppermute | solution.py:18
  68.5 10.2 %collective-permute-start.8 = (f32[16,2,6,128]{3,2,0,1:T(8,128)S(1)}, f32[16,2,6,128]{3,2,0,1:T(8,128)S(1)}, u32[]{:S(2)}, u32[]{:S(2)}) collective-permute-start(f32[16,2,6,128]{3,2,0,1:T(8,128)S(1)} %get-tuple-element.101), channel_id=1, source_target_pairs={{0,16},{16,32},{32,48},{48,64},{64,80},{80,96},{96,112},{112,128},... | collective-permute-start | bytes 294920 | tf_op jit(solution)/shard_map/ppermute | solution.py:18
  72.3 6.5 %collective-permute-start.9 = (f32[16,2,6,128]{3,2,0,1:T(8,128)S(1)}, f32[16,2,6,128]{3,2,0,1:T(8,128)S(1)}, u32[]{:S(2)}, u32[]{:S(2)}) collective-permute-start(f32[16,2,6,128]{3,2,0,1:T(8,128)S(1)} %get-tuple-element.102), channel_id=1, source_target_pairs={{0,496},{16,0},{32,16},{48,32},{64,48},{80,64},{96,80},{112,96},{1... | collective-permute-start | bytes 294920 | tf_op jit(solution)/shard_map/ppermute | solution.py:18
  83.1 32.6 %copy-start.45 = (f32[2,4,512]{2,1,0:T(4,128)}, f32[2,4,512]{2,1,0:T(4,128)S(1)}, u32[]{:S(2)}) copy-start(f32[2,4,512]{2,1,0:T(4,128)S(1)} %reshape.73.refs_2_) | copy-start | bytes 49156
  83.1 14.7 %collective-permute-start.13 = (f32[2,4,512]{2,1,0:T(4,128)S(1)}, f32[2,4,512]{2,1,0:T(4,128)S(1)}, u32[]{:S(2)}, u32[]{:S(2)}) collective-permute-start(f32[2,4,512]{2,1,0:T(4,128)S(1)} %reshape.73.refs_2_), channel_id=1, source_target_pairs={{0,480},{16,496},{32,0},{48,16},{64,32},{80,48},{96,64},{112,80},{... | collective-permute-start | bytes 49160 | tf_op jit(solution)/shard_map/ppermute | solution.py:18
  92.2 5.6 %collective-permute-start.12 = (f32[2,4,512]{2,1,0:T(4,128)S(1)}, f32[2,4,512]{2,1,0:T(4,128)S(1)}, u32[]{:S(2)}, u32[]{:S(2)}) collective-permute-start(f32[2,4,512]{2,1,0:T(4,128)S(1)} %reshape.73.refs_2_), channel_id=1, source_target_pairs={{0,496},{16,0},{32,16},{48,32},{64,48},{80,64},{96,80},{112,96},{1... | collective-permute-start | bytes 49160 | tf_op jit(solution)/shard_map/ppermute | solution.py:18
  92.2 5.6 %collective-permute-start.11 = (f32[2,4,512]{2,1,0:T(4,128)S(1)}, f32[2,4,512]{2,1,0:T(4,128)}, u32[]{:S(2)}, u32[]{:S(2)}) collective-permute-start(f32[2,4,512]{2,1,0:T(4,128)S(1)} %reshape.73.refs_2_), channel_id=1, source_target_pairs={{0,16},{16,32},{32,48},{48,64},{64,80},{80,96},{96,112},{112,128},... | collective-permute-start | bytes 49160 | tf_op jit(solution)/shard_map/ppermute | solution.py:18
  93.9 5.8 %collective-permute-start.10 = (f32[2,4,512]{2,1,0:T(4,128)S(1)}, f32[2,4,512]{2,1,0:T(4,128)}, u32[]{:S(2)}, u32[]{:S(2)}) collective-permute-start(f32[2,4,512]{2,1,0:T(4,128)S(1)} %reshape.73.refs_2_), channel_id=1, source_target_pairs={{0,32},{16,48},{32,64},{48,80},{64,96},{80,112},{96,128},{112,144}... | collective-permute-start | bytes 49160 | tf_op jit(solution)/shard_map/ppermute | solution.py:18
  97.8 17.9 %copy-start.46 = (f32[2,4,512]{2,1,0:T(4,128)}, f32[2,4,512]{2,1,0:T(4,128)S(1)}, u32[]{:S(2)}) copy-start(f32[2,4,512]{2,1,0:T(4,128)S(1)} %collective-permute-done.13.refs_4_) | copy-start | bytes 49156
  97.8 17.9 %copy-start.47 = (f32[2,4,512]{2,1,0:T(4,128)}, f32[2,4,512]{2,1,0:T(4,128)S(1)}, u32[]{:S(2)}) copy-start(f32[2,4,512]{2,1,0:T(4,128)S(1)} %collective-permute-done.12.refs_3_) | copy-start | bytes 49156
  101.2 8.8 %collective-permute-start.15 = (f32[3,2,4,512]{3,2,1,0:T(4,128)}, f32[3,2,4,512]{3,2,1,0:T(4,128)S(1)}, u32[]{:S(2)}, u32[]{:S(2)}) collective-permute-start(f32[3,2,4,512]{3,2,1,0:T(4,128)} %get-tuple-element.107), channel_id=1, source_target_pairs={{0,432},{16,448},{32,464},{48,480},{64,496},{80,0},{96,16},{112,32... | collective-permute-start | bytes 147464 | tf_op jit(solution)/shard_map/ppermute | solution.py:18
  106.6 9.2 %collective-permute-start.14 = (f32[3,2,4,512]{3,2,1,0:T(4,128)}, f32[3,2,4,512]{3,2,1,0:T(4,128)}, u32[]{:S(2)}, u32[]{:S(2)}) collective-permute-start(f32[3,2,4,512]{3,2,1,0:T(4,128)} %get-tuple-element.108), channel_id=1, source_target_pairs={{0,80},{16,96},{32,112},{48,128},{64,144},{80,160},{96,176},{112,1... | collective-permute-start | bytes 147464 | tf_op jit(solution)/shard_map/ppermute | solution.py:18
  (63 other events, 167.8 us)

commit v10 on v9

--- a/solution.py
+++ b/solution.py
@@ -301,8 +301,8 @@
     m1, p1 = shift_from(pair, "row", 1), shift_from(pair, "row", -1)
     m2, p2 = shift_from(pair, "row", 2), shift_from(pair, "row", -2)
     near = [m2, m1, pair, p1, p2]
-    lower = shift_from(jnp.stack([pair, p1, p2]), "row", 5)
-    upper = shift_from(jnp.stack([m2, m1, pair]), "row", -5)
+    lower = shift_from(jnp.stack([m2, m1, pair]), "row", 3)
+    upper = shift_from(jnp.stack([pair, p1, p2]), "row", -3)
     reach = CSWEEPS + 2
     reach += (-(size_x + 2 * reach)) % 8 // 2
     assert reach <= 5 * size_x

time: 135 us -> 132 us (0.978)
  waiting for transfers between devices: 12.3 us -> 9.96 us
    ppermute x16, waiting for transfers between devices: 12.3 us -> 9.96 us  [shift_from(): return lax.ppermute(x, axis, [(i, (i + k) % n) for i in range(n)])]
where the time goes in v10:
time: 132 us; the launch traced here: 131 us
  starting transfers between devices  60.3 us (46%)
  other arithmetic  20 us (15%)
  blocking collectives  19 us (14%)
  waiting for transfers between devices  9.96 us (8%)
  matrix products  7.88 us (6%)
  local copies, waits for them, and re-layouts  7.75 us (6%)
  Pallas kernels  4.5 us (3%)
  between operations  1.57 us (1%)
    ppermute x16, starting transfers between devices, shift_from(): return lax.ppermute(x, axis, [(i, (i + k) % n) for i in range(n)])  60.3 us
    all_gather x1, blocking collectives, on_device(): band = lax.all_gather(block, 'col', axis=0, tiled=False)  19 us
    ppermute x16, waiting for transfers between devices, shift_from(): return lax.ppermute(x, axis, [(i, (i + k) % n) for i in range(n)])  9.96 us
    add x6, other arithmetic, sweep(): return v[1:-1, 1:-1] + OMEGA * residual / faces[6]  4.52 us
    pallas_call x1, Pallas kernels, coarse_solve(): return call(*near, lower, upper)  4.5 us
    dot_general x9, matrix products, along_y(): jnp.einsum('xjy,xyz->xjz', batched, field, precision=lax.Precision.HIGHEST)  3.86 us
    dot_general x6, matrix products, along_z(): out = jnp.dot(flat, matrix, precision=lax.Precision.HIGHEST)  2.83 us
  transfers between devices with their start and end apart: 16, of which 11 were waited for; matrix products, arithmetic and copies ran while one was open for 5% of the time, Pallas kernels for 0%

profile of v10, /device:TPU:1, one launch (start us, length us, event | category | flops | bytes accessed | tf_op | source)
XLA Modules:
  0.0 130.9 jit_solution(13143193299013521411)
XLA Ops:
  0.0 1.3 %pad_maximum_fusion.6 = (f32[3,32,4,128]{3,2,1,0:T(4,128)S(1)}, f32[3,32,4,128]{3,2,1,0:T(4,128)S(1)}) fusion(f32[1,32,16,128]{3,2,1,0:T(8,128)} %bitcast.94, f32[1,32,16,128]{3,2,1,0:T(8,128)} %bitcast.97, f32[1,32,16,128]{3,2,1,0:T(8,128)} %bitcast.90), kind=kLoop, calls=%fused_computation.119 | loop fusion | flops 196608 | bytes 1179648 | tf_op jit(solution)/shard_map/slice | solution.py:23
  1.4 3.9 %collective-permute-start = (f32[3,32,4,128]{3,2,1,0:T(4,128)S(1)}, f32[3,32,4,128]{3,2,1,0:T(4,128)S(1)}, u32[]{:S(2)}, u32[]{:S(2)}) collective-permute-start(f32[3,32,4,128]{3,2,1,0:T(4,128)S(1)} %get-tuple-element.29), channel_id=1, source_target_pairs={{0,1},{1,2},{2,3},{3,4},{4,5},{5,6},{6,7},{7,8},{8,9},{9,10},{10,1... | collective-permute-start | bytes 589832 | tf_op jit(solution)/shard_map/ppermute | solution.py:18
  5.3 5.6 %collective-permute-start.1 = (f32[3,32,4,128]{3,2,1,0:T(4,128)S(1)}, f32[3,32,4,128]{3,2,1,0:T(4,128)S(1)}, u32[]{:S(2)}, u32[]{:S(2)}) collective-permute-start(f32[3,32,4,128]{3,2,1,0:T(4,128)S(1)} %get-tuple-element.30), channel_id=1, source_target_pairs={{0,15},{1,0},{2,1},{3,2},{4,3},{5,4},{6,5},{7,6},{8,7},{9,8},{10,9... | collective-permute-start | bytes 589832 | tf_op jit(solution)/shard_map/ppermute | solution.py:18
  11.2 1.3 fusion.126
  13.6 4.0 %collective-permute-start.2 = (f32[3,4,24,128]{3,2,1,0:T(8,128)S(1)}, f32[3,4,24,128]{3,2,1,0:T(8,128)S(1)}, u32[]{:S(2)}, u32[]{:S(2)}) collective-permute-start(f32[3,4,24,128]{3,2,1,0:T(8,128)S(1)} %get-tuple-element.27), channel_id=1, source_target_pairs={{0,16},{16,32},{32,48},{48,64},{64,80},{80,96},{96,112},{112,128},... | collective-permute-start | bytes 442376 | tf_op jit(solution)/shard_map/ppermute | solution.py:18
  17.6 3.0 %collective-permute-start.3 = (f32[3,4,24,128]{3,2,1,0:T(8,128)S(1)}, f32[3,4,24,128]{3,2,1,0:T(8,128)S(1)}, u32[]{:S(2)}, u32[]{:S(2)}) collective-permute-start(f32[3,4,24,128]{3,2,1,0:T(8,128)S(1)} %get-tuple-element.28), channel_id=1, source_target_pairs={{0,496},{16,0},{32,16},{48,32},{64,48},{80,64},{96,80},{112,96},{1... | collective-permute-start | bytes 442376 | tf_op jit(solution)/shard_map/ppermute | solution.py:18
  24.5 0.9 fusion.18
  26.8 1.9 %collective-permute-start.4 = (f32[2,16,5,64]{3,2,1,0:T(8,128)S(1)}, f32[2,16,5,64]{3,2,1,0:T(8,128)S(1)}, u32[]{:S(2)}, u32[]{:S(2)}) collective-permute-start(f32[2,16,5,64]{3,2,1,0:T(8,128)S(1)} %get-tuple-element.103), channel_id=1, source_target_pairs={{0,1},{1,2},{2,3},{3,4},{4,5},{5,6},{6,7},{7,8},{8,9},{9,10},{10,1... | collective-permute-start | bytes 122888 | tf_op jit(solution)/shard_map/ppermute | solution.py:18
  28.7 7.4 %collective-permute-start.5 = (f32[2,16,5,64]{3,2,1,0:T(8,128)S(1)}, f32[2,16,5,64]{3,2,1,0:T(8,128)S(1)}, u32[]{:S(2)}, u32[]{:S(2)}) collective-permute-start(f32[2,16,5,64]{3,2,1,0:T(8,128)S(1)} %get-tuple-element.104), channel_id=1, source_target_pairs={{0,15},{1,0},{2,1},{3,2},{4,3},{5,4},{6,5},{7,6},{8,7},{9,8},{10,9... | collective-permute-start | bytes 122888 | tf_op jit(solution)/shard_map/ppermute | solution.py:18
  36.6 1.5 %collective-permute-done.5 = f32[2,16,5,64]{3,2,1,0:T(8,128)S(1)} collective-permute-done((f32[2,16,5,64]{3,2,1,0:T(8,128)S(1)}, f32[2,16,5,64]{3,2,1,0:T(8,128)S(1)}, u32[]{:S(2)}, u32[]{:S(2)}) %collective-permute-start.5) | collective-permute-done | bytes 40992 | tf_op jit(solution)/shard_map/ppermute | solution.py:18
  38.8 1.2 collective-permute-start.6
  40.0 4.3 %collective-permute-start.7 = (f32[2,5,18,64]{3,2,1,0:T(8,128)}, f32[2,5,18,64]{3,2,1,0:T(8,128)}, u32[]{:S(2)}, u32[]{:S(2)}) collective-permute-start(f32[2,5,18,64]{3,2,1,0:T(8,128)} %get-tuple-element.48), channel_id=1, source_target_pairs={{0,496},{16,0},{32,16},{48,32},{64,48},{80,64},{96,80},{112,96},{1... | collective-permute-start | bytes 138248 | tf_op jit(solution)/shard_map/ppermute | solution.py:18
  45.7 1.2 pad_maximum_fusion.1
  49.2 19.0 %all_gather.3 = f32[16,2,8,128]{3,2,0,1:T(8,128)S(1)} all-gather(f32[1,2,8,128]{3,2,0,1:T(8,128)S(1)} %pad_maximum_fusion.22), channel_id=1, replica_groups=mesh['row'=32,'col'=16] {'col'}, dimensions={0}, use_global_device_ids=true | all-gather | bytes 139264 | tf_op jit(solution)/shard_map/all_gather | solution.py:339
  68.5 3.8 %collective-permute-start.8 = (f32[16,2,6,128]{3,2,0,1:T(8,128)S(1)}, f32[16,2,6,128]{3,2,0,1:T(8,128)S(1)}, u32[]{:S(2)}, u32[]{:S(2)}) collective-permute-start(f32[16,2,6,128]{3,2,0,1:T(8,128)S(1)} %get-tuple-element.101), channel_id=1, source_target_pairs={{0,16},{16,32},{32,48},{48,64},{64,80},{80,96},{96,112},{112,128},... | collective-permute-start | bytes 294920 | tf_op jit(solution)/shard_map/ppermute | solution.py:18
  72.3 5.5 %collective-permute-start.9 = (f32[16,2,6,128]{3,2,0,1:T(8,128)S(1)}, f32[16,2,6,128]{3,2,0,1:T(8,128)S(1)}, u32[]{:S(2)}, u32[]{:S(2)}) collective-permute-start(f32[16,2,6,128]{3,2,0,1:T(8,128)S(1)} %get-tuple-element.102), channel_id=1, source_target_pairs={{0,496},{16,0},{32,16},{48,32},{64,48},{80,64},{96,80},{112,96},{1... | collective-permute-start | bytes 294920 | tf_op jit(solution)/shard_map/ppermute | solution.py:18
  83.1 9.1 %collective-permute-start.13 = (f32[2,4,512]{2,1,0:T(4,128)S(1)}, f32[2,4,512]{2,1,0:T(4,128)S(1)}, u32[]{:S(2)}, u32[]{:S(2)}) collective-permute-start(f32[2,4,512]{2,1,0:T(4,128)S(1)} %reshape.73.refs_2_), channel_id=1, source_target_pairs={{0,480},{16,496},{32,0},{48,16},{64,32},{80,48},{96,64},{112,80},{... | collective-permute-start | bytes 49160 | tf_op jit(solution)/shard_map/ppermute | solution.py:18
  92.2 1.7 %collective-permute-start.11 = (f32[2,4,512]{2,1,0:T(4,128)S(1)}, f32[2,4,512]{2,1,0:T(4,128)}, u32[]{:S(2)}, u32[]{:S(2)}) collective-permute-start(f32[2,4,512]{2,1,0:T(4,128)S(1)} %reshape.73.refs_2_), channel_id=1, source_target_pairs={{0,16},{16,32},{32,48},{48,64},{64,80},{80,96},{96,112},{112,128},... | collective-permute-start | bytes 49160 | tf_op jit(solution)/shard_map/ppermute | solution.py:18
  93.9 1.9 %collective-permute-start.10 = (f32[2,4,512]{2,1,0:T(4,128)S(1)}, f32[2,4,512]{2,1,0:T(4,128)}, u32[]{:S(2)}, u32[]{:S(2)}) collective-permute-start(f32[2,4,512]{2,1,0:T(4,128)S(1)} %reshape.73.refs_2_), channel_id=1, source_target_pairs={{0,32},{16,48},{32,64},{48,80},{64,96},{80,112},{96,128},{112,144}... | collective-permute-start | bytes 49160 | tf_op jit(solution)/shard_map/ppermute | solution.py:18
  95.8 1.3 fusion.230
  97.8 1.9 %collective-permute-done.10.refs_0_ = f32[2,4,512]{2,1,0:T(4,128)} collective-permute-done((f32[2,4,512]{2,1,0:T(4,128)S(1)}, f32[2,4,512]{2,1,0:T(4,128)}, u32[]{:S(2)}, u32[]{:S(2)}) %collective-permute-start.10) | collective-permute-done | bytes 16416 | tf_op jit(solution)/shard_map/ppermute | solution.py:18
  99.7 1.5 %pad_maximum_fusion.20 = (f32[3,2,4,512]{3,2,1,0:T(4,128)}, f32[3,2,4,512]{3,2,1,0:T(4,128)}) fusion(f32[1,2,4,512]{3,2,1,0:T(4,128)S(1)} %bitcast.108, f32[1,2,4,512]{3,2,1,0:T(4,128)S(1)} %bitcast.109, f32[1,2,4,512]{3,2,1,0:T(4,128)} %stack_reshape.4, f32[1,2,4,512]{3,2,1,0:T(4,128)} %bitcast.31, f32[1,2,4,512]{3,2,1,0:T(4,128)} %bitcast.30), kind=kLoop, calls=%fused_computation.382 | loop fusion | flops 49152 | bytes 180224 | tf_op jit(solution)/shard_map/stack | solution.py:305
  101.2 1.9 %collective-permute-start.15 = (f32[3,2,4,512]{3,2,1,0:T(4,128)}, f32[3,2,4,512]{3,2,1,0:T(4,128)S(1)}, u32[]{:S(2)}, u32[]{:S(2)}) collective-permute-start(f32[3,2,4,512]{3,2,1,0:T(4,128)} %get-tuple-element.107), channel_id=1, source_target_pairs={{0,464},{16,480},{32,496},{48,0},{64,16},{80,32},{96,48},{112,64},... | collective-permute-start | bytes 147464 | tf_op jit(solution)/shard_map/ppermute | solution.py:18
  103.1 4.7 %collective-permute-start.14 = (f32[3,2,4,512]{3,2,1,0:T(4,128)}, f32[3,2,4,512]{3,2,1,0:T(4,128)}, u32[]{:S(2)}, u32[]{:S(2)}) collective-permute-start(f32[3,2,4,512]{3,2,1,0:T(4,128)} %get-tuple-element.108), channel_id=1, source_target_pairs={{0,48},{16,64},{32,80},{48,96},{64,112},{80,128},{96,144},{112,160... | collective-permute-start | bytes 147464 | tf_op jit(solution)/shard_map/ppermute | solution.py:18
  107.8 1.3 fusion.234
  109.1 3.4 %collective-permute-done.14.refs_5_ = f32[3,2,4,512]{3,2,1,0:T(4,128)} collective-permute-done((f32[3,2,4,512]{3,2,1,0:T(4,128)}, f32[3,2,4,512]{3,2,1,0:T(4,128)}, u32[]{:S(2)}, u32[]{:S(2)}) %collective-permute-start.14) | collective-permute-done | bytes 49184 | tf_op jit(solution)/shard_map/ppermute | solution.py:18
  112.5 4.5 %shard_map.37 = f32[8,512]{1,0:T(8,128)} custom-call(f32[2,4,512]{2,1,0:T(4,128)} %collective-permute-done.10.refs_0_, f32[2,4,512]{2,1,0:T(4,128)} %collective-permute-done.11.refs_1_, f32[2,4,512]{2,1,0:T(4,128)} %copy-done.45, f32[2,4,512]{2,1,0:T(4,128)} %copy-done.47, f32[2,4,512]{2,1,0:T(4,128)} %copy-done.46, ...), custom_call_target="tpu_custom_call" | custom-call | flops 13107200 | bytes 491520 | tf_op jit(solution)/shard_map/pallas_call | solution.py:320
  117.8 0.9 fusion.171
  118.7 1.3 %convolution_add_fusion = f32[16,16,128]{2,1,0:T(8,128)S(1)} fusion(f32[16,16,128]{2,1,0:T(8,128)} %copy-done.10, f32[16,8,128]{2,1,0:T(8,128)S(1)} %fusion.171, f32[16,8]{0,1:T(8,128)} %fusion.234), kind=kOutput, calls=%fused_computation.1 | convolution fusion | flops 3178496 | bytes 328192 | tf_op jit(solution)/shard_map/xjy,xyz->xjz/dot_general | solution.py:108
  124.2 1.0 slice_add_fusion
  128.5 0.9 fusion.28
  129.6 1.3 fusion.42
  (290 shorter events, 24.8 us)
Async XLA Ops:
  1.4 11.9 %collective-permute-start = (f32[3,32,4,128]{3,2,1,0:T(4,128)S(1)}, f32[3,32,4,128]{3,2,1,0:T(4,128)S(1)}, u32[]{:S(2)}, u32[]{:S(2)}) collective-permute-start(f32[3,32,4,128]{3,2,1,0:T(4,128)S(1)} %get-tuple-element.29), channel_id=1, source_target_pairs={{0,1},{1,2},{2,3},{3,4},{4,5},{5,6},{6,7},{7,8},{8,9},{9,10},{10,1... | collective-permute-start | bytes 589832 | tf_op jit(solution)/shard_map/ppermute | solution.py:18
  5.3 8.2 %collective-permute-start.1 = (f32[3,32,4,128]{3,2,1,0:T(4,128)S(1)}, f32[3,32,4,128]{3,2,1,0:T(4,128)S(1)}, u32[]{:S(2)}, u32[]{:S(2)}) collective-permute-start(f32[3,32,4,128]{3,2,1,0:T(4,128)S(1)} %get-tuple-element.30), channel_id=1, source_target_pairs={{0,15},{1,0},{2,1},{3,2},{4,3},{5,4},{6,5},{7,6},{8,7},{9,8},{10,9... | collective-permute-start | bytes 589832 | tf_op jit(solution)/shard_map/ppermute | solution.py:18
  11.0 15.2 %copy-start.61 = (pred[128]{0:T(512)(128)(4,1)}, pred[128]{0:T(512)(128)(4,1)S(1)}, u32[]{:S(2)}) copy-start(pred[128]{0:T(512)(128)(4,1)S(1)} %compare_and_fusion.3) | copy-start | bytes 388
  11.0 37.7 %copy-start.77 = (pred[64]{0:T(512)(128)(4,1)}, pred[64]{0:T(512)(128)(4,1)S(1)}, u32[]{:S(2)}) copy-start(pred[64]{0:T(512)(128)(4,1)S(1)} %compare_and_fusion.1) | copy-start | bytes 196
  11.1 71.2 %copy-start.51 = (pred[128]{0:T(512)(128)(4,1)}, pred[128]{0:T(512)(128)(4,1)S(1)}, u32[]{:S(2)}) copy-start(pred[128]{0:T(512)(128)(4,1)S(1)} %get-tuple-element.122) | copy-start | bytes 388
  11.1 71.2 %copy-start.53 = (pred[128]{0:T(512)(128)(4,1)}, pred[128]{0:T(512)(128)(4,1)S(1)}, u32[]{:S(2)}) copy-start(pred[128]{0:T(512)(128)(4,1)S(1)} %get-tuple-element.123) | copy-start | bytes 388
  11.1 71.7 %copy-start.55 = (s32[128]{0:T(128)}, s32[128]{0:T(128)S(1)}, u32[]{:S(2)}) copy-start(s32[128]{0:T(128)S(1)} %get-tuple-element.120) | copy-start | bytes 1540
  11.1 71.7 %copy-start.57 = (s32[128]{0:T(128)}, s32[128]{0:T(128)S(1)}, u32[]{:S(2)}) copy-start(s32[128]{0:T(128)S(1)} %get-tuple-element.121) | copy-start | bytes 1540
  11.1 15.0 %copy-start.63 = (s32[128]{0:T(128)}, s32[128]{0:T(128)S(1)}, u32[]{:S(2)}) copy-start(s32[128]{0:T(128)S(1)} %get-tuple-element.112) | copy-start | bytes 1540
  11.2 15.0 %copy-start.65 = (s32[128]{0:T(128)}, s32[128]{0:T(128)S(1)}, u32[]{:S(2)}) copy-start(s32[128]{0:T(128)S(1)} %get-tuple-element.113) | copy-start | bytes 1540
  11.2 37.5 %copy-start.70 = (s32[64]{0:T(128)}, s32[64]{0:T(128)S(1)}, u32[]{:S(2)}) copy-start(s32[64]{0:T(128)S(1)} %get-tuple-element.116) | copy-start | bytes 772
  11.2 37.5 %copy-start.72 = (s32[64]{0:T(128)}, s32[64]{0:T(128)S(1)}, u32[]{:S(2)}) copy-start(s32[64]{0:T(128)S(1)} %get-tuple-element.117) | copy-start | bytes 772
  13.6 7.9 %collective-permute-start.2 = (f32[3,4,24,128]{3,2,1,0:T(8,128)S(1)}, f32[3,4,24,128]{3,2,1,0:T(8,128)S(1)}, u32[]{:S(2)}, u32[]{:S(2)}) collective-permute-start(f32[3,4,24,128]{3,2,1,0:T(8,128)S(1)} %get-tuple-element.27), channel_id=1, source_target_pairs={{0,16},{16,32},{32,48},{48,64},{64,80},{80,96},{96,112},{112,128},... | collective-permute-start | bytes 442376 | tf_op jit(solution)/shard_map/ppermute | solution.py:18
  17.6 4.6 %collective-permute-start.3 = (f32[3,4,24,128]{3,2,1,0:T(8,128)S(1)}, f32[3,4,24,128]{3,2,1,0:T(8,128)S(1)}, u32[]{:S(2)}, u32[]{:S(2)}) collective-permute-start(f32[3,4,24,128]{3,2,1,0:T(8,128)S(1)} %get-tuple-element.28), channel_id=1, source_target_pairs={{0,496},{16,0},{32,16},{48,32},{64,48},{80,64},{96,80},{112,96},{1... | collective-permute-start | bytes 442376 | tf_op jit(solution)/shard_map/ppermute | solution.py:18
  20.7 62.1 %copy-start.74 = (s32[128]{0:T(128)}, s32[128]{0:T(128)S(1)}, u32[]{:S(2)}) copy-start(s32[128]{0:T(128)S(1)} %get-tuple-element.124) | copy-start | bytes 1540
  20.7 62.1 %copy-start.75 = (s32[128]{0:T(128)}, s32[128]{0:T(128)S(1)}, u32[]{:S(2)}) copy-start(s32[128]{0:T(128)S(1)} %get-tuple-element.125) | copy-start | bytes 1540
  26.8 9.8 %collective-permute-start.4 = (f32[2,16,5,64]{3,2,1,0:T(8,128)S(1)}, f32[2,16,5,64]{3,2,1,0:T(8,128)S(1)}, u32[]{:S(2)}, u32[]{:S(2)}) collective-permute-start(f32[2,16,5,64]{3,2,1,0:T(8,128)S(1)} %get-tuple-element.103), channel_id=1, source_target_pairs={{0,1},{1,2},{2,3},{3,4},{4,5},{5,6},{6,7},{7,8},{8,9},{9,10},{10,1... | collective-permute-start | bytes 122888 | tf_op jit(solution)/shard_map/ppermute | solution.py:18
  28.7 9.4 %collective-permute-start.5 = (f32[2,16,5,64]{3,2,1,0:T(8,128)S(1)}, f32[2,16,5,64]{3,2,1,0:T(8,128)S(1)}, u32[]{:S(2)}, u32[]{:S(2)}) collective-permute-start(f32[2,16,5,64]{3,2,1,0:T(8,128)S(1)} %get-tuple-element.104), channel_id=1, source_target_pairs={{0,15},{1,0},{2,1},{3,2},{4,3},{5,4},{6,5},{7,6},{8,7},{9,8},{10,9... | collective-permute-start | bytes 122888 | tf_op jit(solution)/shard_map/ppermute | solution.py:18
  36.2 46.6 %copy-start.59 = (pred[128]{0:T(512)(128)(4,1)}, pred[128]{0:T(512)(128)(4,1)S(1)}, u32[]{:S(2)}) copy-start(pred[128]{0:T(512)(128)(4,1)S(1)} %get-tuple-element.110) | copy-start | bytes 388
  36.2 46.6 %copy-start.76 = (pred[128]{0:T(512)(128)(4,1)}, pred[128]{0:T(512)(128)(4,1)S(1)}, u32[]{:S(2)}) copy-start(pred[128]{0:T(512)(128)(4,1)S(1)} %get-tuple-element.111) | copy-start | bytes 388
  38.8 6.7 %collective-permute-start.6 = (f32[2,5,18,64]{3,2,1,0:T(8,128)}, f32[2,5,18,64]{3,2,1,0:T(8,128)}, u32[]{:S(2)}, u32[]{:S(2)}) collective-permute-start(f32[2,5,18,64]{3,2,1,0:T(8,128)} %get-tuple-element.47), channel_id=1, source_target_pairs={{0,16},{16,32},{32,48},{48,64},{64,80},{80,96},{96,112},{112,128},... | collective-permute-start | bytes 138248 | tf_op jit(solution)/shard_map/ppermute | solution.py:18
  40.0 5.6 %collective-permute-start.7 = (f32[2,5,18,64]{3,2,1,0:T(8,128)}, f32[2,5,18,64]{3,2,1,0:T(8,128)}, u32[]{:S(2)}, u32[]{:S(2)}) collective-permute-start(f32[2,5,18,64]{3,2,1,0:T(8,128)} %get-tuple-element.48), channel_id=1, source_target_pairs={{0,496},{16,0},{32,16},{48,32},{64,48},{80,64},{96,80},{112,96},{1... | collective-permute-start | bytes 138248 | tf_op jit(solution)/shard_map/ppermute | solution.py:18
  68.5 10.2 %collective-permute-start.8 = (f32[16,2,6,128]{3,2,0,1:T(8,128)S(1)}, f32[16,2,6,128]{3,2,0,1:T(8,128)S(1)}, u32[]{:S(2)}, u32[]{:S(2)}) collective-permute-start(f32[16,2,6,128]{3,2,0,1:T(8,128)S(1)} %get-tuple-element.101), channel_id=1, source_target_pairs={{0,16},{16,32},{32,48},{48,64},{64,80},{80,96},{96,112},{112,128},... | collective-permute-start | bytes 294920 | tf_op jit(solution)/shard_map/ppermute | solution.py:18
  72.3 6.5 %collective-permute-start.9 = (f32[16,2,6,128]{3,2,0,1:T(8,128)S(1)}, f32[16,2,6,128]{3,2,0,1:T(8,128)S(1)}, u32[]{:S(2)}, u32[]{:S(2)}) collective-permute-start(f32[16,2,6,128]{3,2,0,1:T(8,128)S(1)} %get-tuple-element.102), channel_id=1, source_target_pairs={{0,496},{16,0},{32,16},{48,32},{64,48},{80,64},{96,80},{112,96},{1... | collective-permute-start | bytes 294920 | tf_op jit(solution)/shard_map/ppermute | solution.py:18
  83.1 29.4 %copy-start.45 = (f32[2,4,512]{2,1,0:T(4,128)}, f32[2,4,512]{2,1,0:T(4,128)S(1)}, u32[]{:S(2)}) copy-start(f32[2,4,512]{2,1,0:T(4,128)S(1)} %reshape.73.refs_2_) | copy-start | bytes 49156
  83.1 14.7 %collective-permute-start.13 = (f32[2,4,512]{2,1,0:T(4,128)S(1)}, f32[2,4,512]{2,1,0:T(4,128)S(1)}, u32[]{:S(2)}, u32[]{:S(2)}) collective-permute-start(f32[2,4,512]{2,1,0:T(4,128)S(1)} %reshape.73.refs_2_), channel_id=1, source_target_pairs={{0,480},{16,496},{32,0},{48,16},{64,32},{80,48},{96,64},{112,80},{... | collective-permute-start | bytes 49160 | tf_op jit(solution)/shard_map/ppermute | solution.py:18
  92.2 5.6 %collective-permute-start.12 = (f32[2,4,512]{2,1,0:T(4,128)S(1)}, f32[2,4,512]{2,1,0:T(4,128)S(1)}, u32[]{:S(2)}, u32[]{:S(2)}) collective-permute-start(f32[2,4,512]{2,1,0:T(4,128)S(1)} %reshape.73.refs_2_), channel_id=1, source_target_pairs={{0,496},{16,0},{32,16},{48,32},{64,48},{80,64},{96,80},{112,96},{1... | collective-permute-start | bytes 49160 | tf_op jit(solution)/shard_map/ppermute | solution.py:18
  92.2 5.6 %collective-permute-start.11 = (f32[2,4,512]{2,1,0:T(4,128)S(1)}, f32[2,4,512]{2,1,0:T(4,128)}, u32[]{:S(2)}, u32[]{:S(2)}) collective-permute-start(f32[2,4,512]{2,1,0:T(4,128)S(1)} %reshape.73.refs_2_), channel_id=1, source_target_pairs={{0,16},{16,32},{32,48},{48,64},{64,80},{80,96},{96,112},{112,128},... | collective-permute-start | bytes 49160 | tf_op jit(solution)/shard_map/ppermute | solution.py:18
  93.9 5.8 %collective-permute-start.10 = (f32[2,4,512]{2,1,0:T(4,128)S(1)}, f32[2,4,512]{2,1,0:T(4,128)}, u32[]{:S(2)}, u32[]{:S(2)}) collective-permute-start(f32[2,4,512]{2,1,0:T(4,128)S(1)} %reshape.73.refs_2_), channel_id=1, source_target_pairs={{0,32},{16,48},{32,64},{48,80},{64,96},{80,112},{96,128},{112,144}... | collective-permute-start | bytes 49160 | tf_op jit(solution)/shard_map/ppermute | solution.py:18
  97.8 14.7 %copy-start.46 = (f32[2,4,512]{2,1,0:T(4,128)}, f32[2,4,512]{2,1,0:T(4,128)S(1)}, u32[]{:S(2)}) copy-start(f32[2,4,512]{2,1,0:T(4,128)S(1)} %collective-permute-done.13.refs_4_) | copy-start | bytes 49156
  101.2 7.9 %collective-permute-start.15 = (f32[3,2,4,512]{3,2,1,0:T(4,128)}, f32[3,2,4,512]{3,2,1,0:T(4,128)S(1)}, u32[]{:S(2)}, u32[]{:S(2)}) collective-permute-start(f32[3,2,4,512]{3,2,1,0:T(4,128)} %get-tuple-element.107), channel_id=1, source_target_pairs={{0,464},{16,480},{32,496},{48,0},{64,16},{80,32},{96,48},{112,64},... | collective-permute-start | bytes 147464 | tf_op jit(solution)/shard_map/ppermute | solution.py:18
  103.1 9.4 %collective-permute-start.14 = (f32[3,2,4,512]{3,2,1,0:T(4,128)}, f32[3,2,4,512]{3,2,1,0:T(4,128)}, u32[]{:S(2)}, u32[]{:S(2)}) collective-permute-start(f32[3,2,4,512]{3,2,1,0:T(4,128)} %get-tuple-element.108), channel_id=1, source_target_pairs={{0,48},{16,64},{32,80},{48,96},{64,112},{80,128},{96,144},{112,160... | collective-permute-start | bytes 147464 | tf_op jit(solution)/shard_map/ppermute | solution.py:18
  (63 other events, 165.1 us)

commit v11 on v10

--- a/solution.py
+++ b/solution.py
@@ -292,7 +292,7 @@
         return v + OMEGA * (b - (diagonal * v - beside_all)) / diagonal
 
     v = OMEGA * b / diagonal
-    v = lax.fori_loop(1, CSWEEPS, one_sweep, v)
+    v = lax.fori_loop(1, CSWEEPS, one_sweep, v, unroll=True)
     out_ref[...] = v[(rows - keep) // 2 : (rows + keep) // 2]
 
 

time: 132 us -> 131 us (level)
  no operation moved by 1% of the time
where the time goes in v11:
time: 131 us; the launch traced here: 130 us
  starting transfers between devices  60.3 us (46%)
  other arithmetic  20 us (15%)
  blocking collectives  19 us (15%)
  waiting for transfers between devices  9.96 us (8%)
  matrix products  7.88 us (6%)
  local copies, waits for them, and re-layouts  7.75 us (6%)
  Pallas kernels  3.98 us (3%)
  between operations  1.57 us (1%)
    ppermute x16, starting transfers between devices, shift_from(): return lax.ppermute(x, axis, [(i, (i + k) % n) for i in range(n)])  60.3 us
    all_gather x1, blocking collectives, on_device(): band = lax.all_gather(block, 'col', axis=0, tiled=False)  19 us
    ppermute x16, waiting for transfers between devices, shift_from(): return lax.ppermute(x, axis, [(i, (i + k) % n) for i in range(n)])  9.96 us
    add x6, other arithmetic, sweep(): return v[1:-1, 1:-1] + OMEGA * residual / faces[6]  4.52 us
    pallas_call x1, Pallas kernels, coarse_solve(): return call(*near, lower, upper)  3.98 us
    dot_general x9, matrix products, along_y(): jnp.einsum('xjy,xyz->xjz', batched, field, precision=lax.Precision.HIGHEST)  3.86 us
    dot_general x6, matrix products, along_z(): out = jnp.dot(flat, matrix, precision=lax.Precision.HIGHEST)  2.83 us
  transfers between devices with their start and end apart: 16, of which 11 were waited for; matrix products, arithmetic and copies ran while one was open for 5% of the time, Pallas kernels for 0%

profile of v11, /device:TPU:1, one launch (start us, length us, event | category | flops | bytes accessed | tf_op | source)
XLA Modules:
  0.0 130.4 jit_solution(14807585560726840883)
XLA Ops:
  0.0 1.3 %pad_maximum_fusion.6 = (f32[3,32,4,128]{3,2,1,0:T(4,128)S(1)}, f32[3,32,4,128]{3,2,1,0:T(4,128)S(1)}) fusion(f32[1,32,16,128]{3,2,1,0:T(8,128)} %bitcast.94, f32[1,32,16,128]{3,2,1,0:T(8,128)} %bitcast.97, f32[1,32,16,128]{3,2,1,0:T(8,128)} %bitcast.90), kind=kLoop, calls=%fused_computation.119 | loop fusion | flops 196608 | bytes 1179648 | tf_op jit(solution)/shard_map/slice | solution.py:23
  1.4 3.9 %collective-permute-start = (f32[3,32,4,128]{3,2,1,0:T(4,128)S(1)}, f32[3,32,4,128]{3,2,1,0:T(4,128)S(1)}, u32[]{:S(2)}, u32[]{:S(2)}) collective-permute-start(f32[3,32,4,128]{3,2,1,0:T(4,128)S(1)} %get-tuple-element.29), channel_id=1, source_target_pairs={{0,1},{1,2},{2,3},{3,4},{4,5},{5,6},{6,7},{7,8},{8,9},{9,10},{10,1... | collective-permute-start | bytes 589832 | tf_op jit(solution)/shard_map/ppermute | solution.py:18
  5.3 5.6 %collective-permute-start.1 = (f32[3,32,4,128]{3,2,1,0:T(4,128)S(1)}, f32[3,32,4,128]{3,2,1,0:T(4,128)S(1)}, u32[]{:S(2)}, u32[]{:S(2)}) collective-permute-start(f32[3,32,4,128]{3,2,1,0:T(4,128)S(1)} %get-tuple-element.30), channel_id=1, source_target_pairs={{0,15},{1,0},{2,1},{3,2},{4,3},{5,4},{6,5},{7,6},{8,7},{9,8},{10,9... | collective-permute-start | bytes 589832 | tf_op jit(solution)/shard_map/ppermute | solution.py:18
  11.2 1.3 fusion.126
  13.6 4.0 %collective-permute-start.2 = (f32[3,4,24,128]{3,2,1,0:T(8,128)S(1)}, f32[3,4,24,128]{3,2,1,0:T(8,128)S(1)}, u32[]{:S(2)}, u32[]{:S(2)}) collective-permute-start(f32[3,4,24,128]{3,2,1,0:T(8,128)S(1)} %get-tuple-element.27), channel_id=1, source_target_pairs={{0,16},{16,32},{32,48},{48,64},{64,80},{80,96},{96,112},{112,128},... | collective-permute-start | bytes 442376 | tf_op jit(solution)/shard_map/ppermute | solution.py:18
  17.6 3.0 %collective-permute-start.3 = (f32[3,4,24,128]{3,2,1,0:T(8,128)S(1)}, f32[3,4,24,128]{3,2,1,0:T(8,128)S(1)}, u32[]{:S(2)}, u32[]{:S(2)}) collective-permute-start(f32[3,4,24,128]{3,2,1,0:T(8,128)S(1)} %get-tuple-element.28), channel_id=1, source_target_pairs={{0,496},{16,0},{32,16},{48,32},{64,48},{80,64},{96,80},{112,96},{1... | collective-permute-start | bytes 442376 | tf_op jit(solution)/shard_map/ppermute | solution.py:18
  24.5 0.9 fusion.18
  26.8 1.9 %collective-permute-start.4 = (f32[2,16,5,64]{3,2,1,0:T(8,128)S(1)}, f32[2,16,5,64]{3,2,1,0:T(8,128)S(1)}, u32[]{:S(2)}, u32[]{:S(2)}) collective-permute-start(f32[2,16,5,64]{3,2,1,0:T(8,128)S(1)} %get-tuple-element.103), channel_id=1, source_target_pairs={{0,1},{1,2},{2,3},{3,4},{4,5},{5,6},{6,7},{7,8},{8,9},{9,10},{10,1... | collective-permute-start | bytes 122888 | tf_op jit(solution)/shard_map/ppermute | solution.py:18
  28.7 7.4 %collective-permute-start.5 = (f32[2,16,5,64]{3,2,1,0:T(8,128)S(1)}, f32[2,16,5,64]{3,2,1,0:T(8,128)S(1)}, u32[]{:S(2)}, u32[]{:S(2)}) collective-permute-start(f32[2,16,5,64]{3,2,1,0:T(8,128)S(1)} %get-tuple-element.104), channel_id=1, source_target_pairs={{0,15},{1,0},{2,1},{3,2},{4,3},{5,4},{6,5},{7,6},{8,7},{9,8},{10,9... | collective-permute-start | bytes 122888 | tf_op jit(solution)/shard_map/ppermute | solution.py:18
  36.6 1.5 %collective-permute-done.5 = f32[2,16,5,64]{3,2,1,0:T(8,128)S(1)} collective-permute-done((f32[2,16,5,64]{3,2,1,0:T(8,128)S(1)}, f32[2,16,5,64]{3,2,1,0:T(8,128)S(1)}, u32[]{:S(2)}, u32[]{:S(2)}) %collective-permute-start.5) | collective-permute-done | bytes 40992 | tf_op jit(solution)/shard_map/ppermute | solution.py:18
  38.8 1.2 collective-permute-start.6
  40.0 4.3 %collective-permute-start.7 = (f32[2,5,18,64]{3,2,1,0:T(8,128)}, f32[2,5,18,64]{3,2,1,0:T(8,128)}, u32[]{:S(2)}, u32[]{:S(2)}) collective-permute-start(f32[2,5,18,64]{3,2,1,0:T(8,128)} %get-tuple-element.48), channel_id=1, source_target_pairs={{0,496},{16,0},{32,16},{48,32},{64,48},{80,64},{96,80},{112,96},{1... | collective-permute-start | bytes 138248 | tf_op jit(solution)/shard_map/ppermute | solution.py:18
  45.7 1.2 pad_maximum_fusion.1
  49.2 19.0 %all_gather.3 = f32[16,2,8,128]{3,2,0,1:T(8,128)S(1)} all-gather(f32[1,2,8,128]{3,2,0,1:T(8,128)S(1)} %pad_maximum_fusion.22), channel_id=1, replica_groups=mesh['row'=32,'col'=16] {'col'}, dimensions={0}, use_global_device_ids=true | all-gather | bytes 139264 | tf_op jit(solution)/shard_map/all_gather | solution.py:339
  68.5 3.8 %collective-permute-start.8 = (f32[16,2,6,128]{3,2,0,1:T(8,128)S(1)}, f32[16,2,6,128]{3,2,0,1:T(8,128)S(1)}, u32[]{:S(2)}, u32[]{:S(2)}) collective-permute-start(f32[16,2,6,128]{3,2,0,1:T(8,128)S(1)} %get-tuple-element.101), channel_id=1, source_target_pairs={{0,16},{16,32},{32,48},{48,64},{64,80},{80,96},{96,112},{112,128},... | collective-permute-start | bytes 294920 | tf_op jit(solution)/shard_map/ppermute | solution.py:18
  72.3 5.5 %collective-permute-start.9 = (f32[16,2,6,128]{3,2,0,1:T(8,128)S(1)}, f32[16,2,6,128]{3,2,0,1:T(8,128)S(1)}, u32[]{:S(2)}, u32[]{:S(2)}) collective-permute-start(f32[16,2,6,128]{3,2,0,1:T(8,128)S(1)} %get-tuple-element.102), channel_id=1, source_target_pairs={{0,496},{16,0},{32,16},{48,32},{64,48},{80,64},{96,80},{112,96},{1... | collective-permute-start | bytes 294920 | tf_op jit(solution)/shard_map/ppermute | solution.py:18
  83.1 9.1 %collective-permute-start.13 = (f32[2,4,512]{2,1,0:T(4,128)S(1)}, f32[2,4,512]{2,1,0:T(4,128)S(1)}, u32[]{:S(2)}, u32[]{:S(2)}) collective-permute-start(f32[2,4,512]{2,1,0:T(4,128)S(1)} %reshape.73.refs_2_), channel_id=1, source_target_pairs={{0,480},{16,496},{32,0},{48,16},{64,32},{80,48},{96,64},{112,80},{... | collective-permute-start | bytes 49160 | tf_op jit(solution)/shard_map/ppermute | solution.py:18
  92.2 1.7 %collective-permute-start.11 = (f32[2,4,512]{2,1,0:T(4,128)S(1)}, f32[2,4,512]{2,1,0:T(4,128)}, u32[]{:S(2)}, u32[]{:S(2)}) collective-permute-start(f32[2,4,512]{2,1,0:T(4,128)S(1)} %reshape.73.refs_2_), channel_id=1, source_target_pairs={{0,16},{16,32},{32,48},{48,64},{64,80},{80,96},{96,112},{112,128},... | collective-permute-start | bytes 49160 | tf_op jit(solution)/shard_map/ppermute | solution.py:18
  93.9 1.9 %collective-permute-start.10 = (f32[2,4,512]{2,1,0:T(4,128)S(1)}, f32[2,4,512]{2,1,0:T(4,128)}, u32[]{:S(2)}, u32[]{:S(2)}) collective-permute-start(f32[2,4,512]{2,1,0:T(4,128)S(1)} %reshape.73.refs_2_), channel_id=1, source_target_pairs={{0,32},{16,48},{32,64},{48,80},{64,96},{80,112},{96,128},{112,144}... | collective-permute-start | bytes 49160 | tf_op jit(solution)/shard_map/ppermute | solution.py:18
  95.8 1.3 fusion.230
  97.8 1.9 %collective-permute-done.10.refs_0_ = f32[2,4,512]{2,1,0:T(4,128)} collective-permute-done((f32[2,4,512]{2,1,0:T(4,128)S(1)}, f32[2,4,512]{2,1,0:T(4,128)}, u32[]{:S(2)}, u32[]{:S(2)}) %collective-permute-start.10) | collective-permute-done | bytes 16416 | tf_op jit(solution)/shard_map/ppermute | solution.py:18
  99.7 1.5 %pad_maximum_fusion.20 = (f32[3,2,4,512]{3,2,1,0:T(4,128)}, f32[3,2,4,512]{3,2,1,0:T(4,128)}) fusion(f32[1,2,4,512]{3,2,1,0:T(4,128)S(1)} %bitcast.108, f32[1,2,4,512]{3,2,1,0:T(4,128)S(1)} %bitcast.109, f32[1,2,4,512]{3,2,1,0:T(4,128)} %stack_reshape.4, f32[1,2,4,512]{3,2,1,0:T(4,128)} %bitcast.31, f32[1,2,4,512]{3,2,1,0:T(4,128)} %bitcast.30), kind=kLoop, calls=%fused_computation.382 | loop fusion | flops 49152 | bytes 180224 | tf_op jit(solution)/shard_map/stack | solution.py:305
  101.2 1.9 %collective-permute-start.15 = (f32[3,2,4,512]{3,2,1,0:T(4,128)}, f32[3,2,4,512]{3,2,1,0:T(4,128)S(1)}, u32[]{:S(2)}, u32[]{:S(2)}) collective-permute-start(f32[3,2,4,512]{3,2,1,0:T(4,128)} %get-tuple-element.107), channel_id=1, source_target_pairs={{0,464},{16,480},{32,496},{48,0},{64,16},{80,32},{96,48},{112,64},... | collective-permute-start | bytes 147464 | tf_op jit(solution)/shard_map/ppermute | solution.py:18
  103.1 4.7 %collective-permute-start.14 = (f32[3,2,4,512]{3,2,1,0:T(4,128)}, f32[3,2,4,512]{3,2,1,0:T(4,128)}, u32[]{:S(2)}, u32[]{:S(2)}) collective-permute-start(f32[3,2,4,512]{3,2,1,0:T(4,128)} %get-tuple-element.108), channel_id=1, source_target_pairs={{0,48},{16,64},{32,80},{48,96},{64,112},{80,128},{96,144},{112,160... | collective-permute-start | bytes 147464 | tf_op jit(solution)/shard_map/ppermute | solution.py:18
  107.8 1.3 fusion.234
  109.1 3.4 %collective-permute-done.14.refs_5_ = f32[3,2,4,512]{3,2,1,0:T(4,128)} collective-permute-done((f32[3,2,4,512]{3,2,1,0:T(4,128)}, f32[3,2,4,512]{3,2,1,0:T(4,128)}, u32[]{:S(2)}, u32[]{:S(2)}) %collective-permute-start.14) | collective-permute-done | bytes 49184 | tf_op jit(solution)/shard_map/ppermute | solution.py:18
  112.5 4.0 %shard_map.37 = f32[8,512]{1,0:T(8,128)} custom-call(f32[2,4,512]{2,1,0:T(4,128)} %collective-permute-done.10.refs_0_, f32[2,4,512]{2,1,0:T(4,128)} %collective-permute-done.11.refs_1_, f32[2,4,512]{2,1,0:T(4,128)} %copy-done.45, f32[2,4,512]{2,1,0:T(4,128)} %copy-done.47, f32[2,4,512]{2,1,0:T(4,128)} %copy-done.46, ...), custom_call_target="tpu_custom_call" | custom-call | flops 13107200 | bytes 491520 | tf_op jit(solution)/shard_map/pallas_call | solution.py:320
  117.3 0.9 fusion.171
  118.1 1.3 %convolution_add_fusion = f32[16,16,128]{2,1,0:T(8,128)S(1)} fusion(f32[16,16,128]{2,1,0:T(8,128)} %copy-done.10, f32[16,8,128]{2,1,0:T(8,128)S(1)} %fusion.171, f32[16,8]{0,1:T(8,128)} %fusion.234), kind=kOutput, calls=%fused_computation.1 | convolution fusion | flops 3178496 | bytes 328192 | tf_op jit(solution)/shard_map/xjy,xyz->xjz/dot_general | solution.py:108
  123.6 1.0 slice_add_fusion
  128.0 0.9 fusion.28
  129.0 1.3 %fusion.42 = f32[32,16,128]{2,1,0:T(8,128)} fusion(f32[34,18,128]{2,1,0:T(8,128)S(1)} %fusion.28, f32[32,16,127]{2,1,0:T(8,128)S(1)} %get-tuple-element.44, f32[32,16,127]{2,1,0:T(8,128)S(1)} %get-tuple-element.43, f32[38,22,128]{2,1,0:T(8,128)S(1)} %copy-done.1, f32[38,22,128]{2,1,0:T(8,128)S(1)} %get-tuple-element.22, ...), kind=kLoop, calls=%fused_computation.91 | loop fusion | flops 1245184 | bytes 4097296 | tf_op jit(solution)/shard_map/add | solution.py:83
  (290 shorter events, 24.8 us)
Async XLA Ops:
  1.4 11.9 %collective-permute-start = (f32[3,32,4,128]{3,2,1,0:T(4,128)S(1)}, f32[3,32,4,128]{3,2,1,0:T(4,128)S(1)}, u32[]{:S(2)}, u32[]{:S(2)}) collective-permute-start(f32[3,32,4,128]{3,2,1,0:T(4,128)S(1)} %get-tuple-element.29), channel_id=1, source_target_pairs={{0,1},{1,2},{2,3},{3,4},{4,5},{5,6},{6,7},{7,8},{8,9},{9,10},{10,1... | collective-permute-start | bytes 589832 | tf_op jit(solution)/shard_map/ppermute | solution.py:18
  5.3 8.2 %collective-permute-start.1 = (f32[3,32,4,128]{3,2,1,0:T(4,128)S(1)}, f32[3,32,4,128]{3,2,1,0:T(4,128)S(1)}, u32[]{:S(2)}, u32[]{:S(2)}) collective-permute-start(f32[3,32,4,128]{3,2,1,0:T(4,128)S(1)} %get-tuple-element.30), channel_id=1, source_target_pairs={{0,15},{1,0},{2,1},{3,2},{4,3},{5,4},{6,5},{7,6},{8,7},{9,8},{10,9... | collective-permute-start | bytes 589832 | tf_op jit(solution)/shard_map/ppermute | solution.py:18
  11.0 15.2 %copy-start.61 = (pred[128]{0:T(512)(128)(4,1)}, pred[128]{0:T(512)(128)(4,1)S(1)}, u32[]{:S(2)}) copy-start(pred[128]{0:T(512)(128)(4,1)S(1)} %compare_and_fusion.3) | copy-start | bytes 388
  11.0 37.7 %copy-start.77 = (pred[64]{0:T(512)(128)(4,1)}, pred[64]{0:T(512)(128)(4,1)S(1)}, u32[]{:S(2)}) copy-start(pred[64]{0:T(512)(128)(4,1)S(1)} %compare_and_fusion.1) | copy-start | bytes 196
  11.1 71.2 %copy-start.51 = (pred[128]{0:T(512)(128)(4,1)}, pred[128]{0:T(512)(128)(4,1)S(1)}, u32[]{:S(2)}) copy-start(pred[128]{0:T(512)(128)(4,1)S(1)} %get-tuple-element.122) | copy-start | bytes 388
  11.1 71.2 %copy-start.53 = (pred[128]{0:T(512)(128)(4,1)}, pred[128]{0:T(512)(128)(4,1)S(1)}, u32[]{:S(2)}) copy-start(pred[128]{0:T(512)(128)(4,1)S(1)} %get-tuple-element.123) | copy-start | bytes 388
  11.1 71.7 %copy-start.55 = (s32[128]{0:T(128)}, s32[128]{0:T(128)S(1)}, u32[]{:S(2)}) copy-start(s32[128]{0:T(128)S(1)} %get-tuple-element.120) | copy-start | bytes 1540
  11.1 71.7 %copy-start.57 = (s32[128]{0:T(128)}, s32[128]{0:T(128)S(1)}, u32[]{:S(2)}) copy-start(s32[128]{0:T(128)S(1)} %get-tuple-element.121) | copy-start | bytes 1540
  11.1 15.0 %copy-start.63 = (s32[128]{0:T(128)}, s32[128]{0:T(128)S(1)}, u32[]{:S(2)}) copy-start(s32[128]{0:T(128)S(1)} %get-tuple-element.112) | copy-start | bytes 1540
  11.2 15.0 %copy-start.65 = (s32[128]{0:T(128)}, s32[128]{0:T(128)S(1)}, u32[]{:S(2)}) copy-start(s32[128]{0:T(128)S(1)} %get-tuple-element.113) | copy-start | bytes 1540
  11.2 37.5 %copy-start.70 = (s32[64]{0:T(128)}, s32[64]{0:T(128)S(1)}, u32[]{:S(2)}) copy-start(s32[64]{0:T(128)S(1)} %get-tuple-element.116) | copy-start | bytes 772
  11.2 37.5 %copy-start.72 = (s32[64]{0:T(128)}, s32[64]{0:T(128)S(1)}, u32[]{:S(2)}) copy-start(s32[64]{0:T(128)S(1)} %get-tuple-element.117) | copy-start | bytes 772
  13.6 7.9 %collective-permute-start.2 = (f32[3,4,24,128]{3,2,1,0:T(8,128)S(1)}, f32[3,4,24,128]{3,2,1,0:T(8,128)S(1)}, u32[]{:S(2)}, u32[]{:S(2)}) collective-permute-start(f32[3,4,24,128]{3,2,1,0:T(8,128)S(1)} %get-tuple-element.27), channel_id=1, source_target_pairs={{0,16},{16,32},{32,48},{48,64},{64,80},{80,96},{96,112},{112,128},... | collective-permute-start | bytes 442376 | tf_op jit(solution)/shard_map/ppermute | solution.py:18
  17.6 4.6 %collective-permute-start.3 = (f32[3,4,24,128]{3,2,1,0:T(8,128)S(1)}, f32[3,4,24,128]{3,2,1,0:T(8,128)S(1)}, u32[]{:S(2)}, u32[]{:S(2)}) collective-permute-start(f32[3,4,24,128]{3,2,1,0:T(8,128)S(1)} %get-tuple-element.28), channel_id=1, source_target_pairs={{0,496},{16,0},{32,16},{48,32},{64,48},{80,64},{96,80},{112,96},{1... | collective-permute-start | bytes 442376 | tf_op jit(solution)/shard_map/ppermute | solution.py:18
  20.7 62.1 %copy-start.74 = (s32[128]{0:T(128)}, s32[128]{0:T(128)S(1)}, u32[]{:S(2)}) copy-start(s32[128]{0:T(128)S(1)} %get-tuple-element.124) | copy-start | bytes 1540
  20.7 62.1 %copy-start.75 = (s32[128]{0:T(128)}, s32[128]{0:T(128)S(1)}, u32[]{:S(2)}) copy-start(s32[128]{0:T(128)S(1)} %get-tuple-element.125) | copy-start | bytes 1540
  26.8 9.8 %collective-permute-start.4 = (f32[2,16,5,64]{3,2,1,0:T(8,128)S(1)}, f32[2,16,5,64]{3,2,1,0:T(8,128)S(1)}, u32[]{:S(2)}, u32[]{:S(2)}) collective-permute-start(f32[2,16,5,64]{3,2,1,0:T(8,128)S(1)} %get-tuple-element.103), channel_id=1, source_target_pairs={{0,1},{1,2},{2,3},{3,4},{4,5},{5,6},{6,7},{7,8},{8,9},{9,10},{10,1... | collective-permute-start | bytes 122888 | tf_op jit(solution)/shard_map/ppermute | solution.py:18
  28.7 9.4 %collective-permute-start.5 = (f32[2,16,5,64]{3,2,1,0:T(8,128)S(1)}, f32[2,16,5,64]{3,2,1,0:T(8,128)S(1)}, u32[]{:S(2)}, u32[]{:S(2)}) collective-permute-start(f32[2,16,5,64]{3,2,1,0:T(8,128)S(1)} %get-tuple-element.104), channel_id=1, source_target_pairs={{0,15},{1,0},{2,1},{3,2},{4,3},{5,4},{6,5},{7,6},{8,7},{9,8},{10,9... | collective-permute-start | bytes 122888 | tf_op jit(solution)/shard_map/ppermute | solution.py:18
  36.2 46.6 %copy-start.59 = (pred[128]{0:T(512)(128)(4,1)}, pred[128]{0:T(512)(128)(4,1)S(1)}, u32[]{:S(2)}) copy-start(pred[128]{0:T(512)(128)(4,1)S(1)} %get-tuple-element.110) | copy-start | bytes 388
  36.2 46.6 %copy-start.76 = (pred[128]{0:T(512)(128)(4,1)}, pred[128]{0:T(512)(128)(4,1)S(1)}, u32[]{:S(2)}) copy-start(pred[128]{0:T(512)(128)(4,1)S(1)} %get-tuple-element.111) | copy-start | bytes 388
  38.8 6.7 %collective-permute-start.6 = (f32[2,5,18,64]{3,2,1,0:T(8,128)}, f32[2,5,18,64]{3,2,1,0:T(8,128)}, u32[]{:S(2)}, u32[]{:S(2)}) collective-permute-start(f32[2,5,18,64]{3,2,1,0:T(8,128)} %get-tuple-element.47), channel_id=1, source_target_pairs={{0,16},{16,32},{32,48},{48,64},{64,80},{80,96},{96,112},{112,128},... | collective-permute-start | bytes 138248 | tf_op jit(solution)/shard_map/ppermute | solution.py:18
  40.0 5.6 %collective-permute-start.7 = (f32[2,5,18,64]{3,2,1,0:T(8,128)}, f32[2,5,18,64]{3,2,1,0:T(8,128)}, u32[]{:S(2)}, u32[]{:S(2)}) collective-permute-start(f32[2,5,18,64]{3,2,1,0:T(8,128)} %get-tuple-element.48), channel_id=1, source_target_pairs={{0,496},{16,0},{32,16},{48,32},{64,48},{80,64},{96,80},{112,96},{1... | collective-permute-start | bytes 138248 | tf_op jit(solution)/shard_map/ppermute | solution.py:18
  68.5 10.2 %collective-permute-start.8 = (f32[16,2,6,128]{3,2,0,1:T(8,128)S(1)}, f32[16,2,6,128]{3,2,0,1:T(8,128)S(1)}, u32[]{:S(2)}, u32[]{:S(2)}) collective-permute-start(f32[16,2,6,128]{3,2,0,1:T(8,128)S(1)} %get-tuple-element.101), channel_id=1, source_target_pairs={{0,16},{16,32},{32,48},{48,64},{64,80},{80,96},{96,112},{112,128},... | collective-permute-start | bytes 294920 | tf_op jit(solution)/shard_map/ppermute | solution.py:18
  72.3 6.5 %collective-permute-start.9 = (f32[16,2,6,128]{3,2,0,1:T(8,128)S(1)}, f32[16,2,6,128]{3,2,0,1:T(8,128)S(1)}, u32[]{:S(2)}, u32[]{:S(2)}) collective-permute-start(f32[16,2,6,128]{3,2,0,1:T(8,128)S(1)} %get-tuple-element.102), channel_id=1, source_target_pairs={{0,496},{16,0},{32,16},{48,32},{64,48},{80,64},{96,80},{112,96},{1... | collective-permute-start | bytes 294920 | tf_op jit(solution)/shard_map/ppermute | solution.py:18
  83.1 29.4 %copy-start.45 = (f32[2,4,512]{2,1,0:T(4,128)}, f32[2,4,512]{2,1,0:T(4,128)S(1)}, u32[]{:S(2)}) copy-start(f32[2,4,512]{2,1,0:T(4,128)S(1)} %reshape.73.refs_2_) | copy-start | bytes 49156
  83.1 14.7 %collective-permute-start.13 = (f32[2,4,512]{2,1,0:T(4,128)S(1)}, f32[2,4,512]{2,1,0:T(4,128)S(1)}, u32[]{:S(2)}, u32[]{:S(2)}) collective-permute-start(f32[2,4,512]{2,1,0:T(4,128)S(1)} %reshape.73.refs_2_), channel_id=1, source_target_pairs={{0,480},{16,496},{32,0},{48,16},{64,32},{80,48},{96,64},{112,80},{... | collective-permute-start | bytes 49160 | tf_op jit(solution)/shard_map/ppermute | solution.py:18
  92.2 5.6 %collective-permute-start.12 = (f32[2,4,512]{2,1,0:T(4,128)S(1)}, f32[2,4,512]{2,1,0:T(4,128)S(1)}, u32[]{:S(2)}, u32[]{:S(2)}) collective-permute-start(f32[2,4,512]{2,1,0:T(4,128)S(1)} %reshape.73.refs_2_), channel_id=1, source_target_pairs={{0,496},{16,0},{32,16},{48,32},{64,48},{80,64},{96,80},{112,96},{1... | collective-permute-start | bytes 49160 | tf_op jit(solution)/shard_map/ppermute | solution.py:18
  92.2 5.6 %collective-permute-start.11 = (f32[2,4,512]{2,1,0:T(4,128)S(1)}, f32[2,4,512]{2,1,0:T(4,128)}, u32[]{:S(2)}, u32[]{:S(2)}) collective-permute-start(f32[2,4,512]{2,1,0:T(4,128)S(1)} %reshape.73.refs_2_), channel_id=1, source_target_pairs={{0,16},{16,32},{32,48},{48,64},{64,80},{80,96},{96,112},{112,128},... | collective-permute-start | bytes 49160 | tf_op jit(solution)/shard_map/ppermute | solution.py:18
  93.9 5.8 %collective-permute-start.10 = (f32[2,4,512]{2,1,0:T(4,128)S(1)}, f32[2,4,512]{2,1,0:T(4,128)}, u32[]{:S(2)}, u32[]{:S(2)}) collective-permute-start(f32[2,4,512]{2,1,0:T(4,128)S(1)} %reshape.73.refs_2_), channel_id=1, source_target_pairs={{0,32},{16,48},{32,64},{48,80},{64,96},{80,112},{96,128},{112,144}... | collective-permute-start | bytes 49160 | tf_op jit(solution)/shard_map/ppermute | solution.py:18
  97.8 14.7 %copy-start.46 = (f32[2,4,512]{2,1,0:T(4,128)}, f32[2,4,512]{2,1,0:T(4,128)S(1)}, u32[]{:S(2)}) copy-start(f32[2,4,512]{2,1,0:T(4,128)S(1)} %collective-permute-done.13.refs_4_) | copy-start | bytes 49156
  101.2 7.9 %collective-permute-start.15 = (f32[3,2,4,512]{3,2,1,0:T(4,128)}, f32[3,2,4,512]{3,2,1,0:T(4,128)S(1)}, u32[]{:S(2)}, u32[]{:S(2)}) collective-permute-start(f32[3,2,4,512]{3,2,1,0:T(4,128)} %get-tuple-element.107), channel_id=1, source_target_pairs={{0,464},{16,480},{32,496},{48,0},{64,16},{80,32},{96,48},{112,64},... | collective-permute-start | bytes 147464 | tf_op jit(solution)/shard_map/ppermute | solution.py:18
  103.1 9.4 %collective-permute-start.14 = (f32[3,2,4,512]{3,2,1,0:T(4,128)}, f32[3,2,4,512]{3,2,1,0:T(4,128)}, u32[]{:S(2)}, u32[]{:S(2)}) collective-permute-start(f32[3,2,4,512]{3,2,1,0:T(4,128)} %get-tuple-element.108), channel_id=1, source_target_pairs={{0,48},{16,64},{32,80},{48,96},{64,112},{80,128},{96,144},{112,160... | collective-permute-start | bytes 147464 | tf_op jit(solution)/shard_map/ppermute | solution.py:18
  (63 other events, 165.1 us)
